TPU v7x, 32 devices: a whole 2x2x4 slice. The times are simulated.
32 devices in a mesh: dp: 4 (over z), expert: 4 (over y, core), etp: 2 (over x).
Axes of the slice: x: 2, y: 2, z: 4, core: 2. Of those that a mesh axis runs over, the one named last changes fastest.
Arguments:
- grad_out: bfloat16 [2048, 4096], P(('dp', 'expert')), may hold values from -3 to 3
- routes: int32 [2048, 8], P(('dp', 'expert')), may hold values from 0 to 15, all different within a row; in each aligned block of 128 rows (0 to 127, 128 to 255, ...) at most 80 rows name the same one
- gates: bfloat16 [2048, 8], P(('dp', 'expert')), may hold values from 0.099609375 to 1
- hidden_saved: bfloat16 [4, 16, 320, 1536], P('dp', 'expert', None, 'etp'), may hold values from -1.5 to 1.5
- down_weight: bfloat16 [16, 1536, 4096], P('expert', 'etp', 'dp'), may hold values from -0.15625 to 0.15625
Outputs:
- weight_grad: bfloat16 [16, 1536, 4096], P('expert', 'etp', 'dp')
- hidden_grad: bfloat16 [4, 16, 320, 1536], P('dp', 'expert', None, 'etp')
- gate_grad: float32 [2048, 8], P(('dp', 'expert'))
Inputs may be any that keep to these rules, and one draw needn't show every extreme that they name: `routes`: each row names 8 different experts. Within the rows of one device (aligned blocks of 128 rows) no expert is named more than 80 times, a bound that some block reaches.
All inputs are finite; a program needn't handle non-finite values.
Results may differ from a plain program's by a relative error of at most 0.005.
Values may be sent and summed in bfloat16 or wider, within the bound.
No kernel may reach another device: no remote copies, remote signals or barrier semaphores. Data moves between devices by JAX's collectives and lax.ppermute only.
A program may use at most 192 MiB of HBM per device.

v0:
```python
import jax
import jax.numpy as jnp
from jax import lax
from jax.sharding import PartitionSpec as P


def body(grad_out, routes, gates, hidden_saved, down_weight):
    token_count = grad_out.shape[0]
    top_count = routes.shape[1]
    exp_dev, ff_part, quarter = down_weight.shape
    groups = lax.axis_size("dp")
    senders = lax.axis_size("expert")
    slot_rows_all = hidden_saved.shape[2]
    capacity = slot_rows_all // senders
    experts = exp_dev * senders
    columns = lax.all_to_all(grad_out, "dp", split_axis=1, concat_axis=0, tiled=True)
    all_routes, all_gates = (
        lax.all_gather(routes, "dp", axis=0, tiled=True),
        lax.all_gather(gates, "dp", axis=0, tiled=True),
    )
    pair_routes = all_routes.reshape(groups, token_count * top_count)
    expert_ids = jnp.arange(experts, dtype=jnp.int32)
    onehot = (pair_routes[:, :, None] == expert_ids[None, None, :]).astype(jnp.int32)
    before = jnp.cumsum(onehot, axis=1) - onehot
    slot_ids = jnp.sum(before * onehot, axis=2)
    group_ids = jnp.arange(groups, dtype=jnp.int32)[:, None]
    position = ((group_ids * experts + pair_routes) * capacity + slot_ids).reshape(-1)
    source_rows = (
        group_ids * token_count
        + jnp.arange(token_count * top_count, dtype=jnp.int32)[None, :] // top_count
    ).reshape(-1)
    row_table = (
        jnp.zeros((groups * experts * capacity,), jnp.int32).at[position].set(source_rows + 1)
    )
    gate_table = (
        jnp.zeros((groups * experts * capacity,), gates.dtype)
        .at[position]
        .set(all_gates.reshape(-1))
    )
    row_table = (
        row_table.reshape(groups, senders, exp_dev, capacity).transpose(2, 0, 1, 3).reshape(-1)
    )
    gate_table = gate_table.reshape(groups, senders, exp_dev, capacity).transpose(2, 0, 1, 3)
    filled = row_table > 0
    safe_rows = jnp.maximum(row_table - 1, 0)
    picked = jnp.where(filled[:, None], columns[safe_rows], jnp.zeros((1, quarter), columns.dtype))
    picked = picked.reshape(exp_dev, groups, senders, capacity, quarter)
    received, got_gates = (
        lax.all_to_all(picked, "expert", split_axis=2, concat_axis=2, tiled=True),
        lax.all_to_all(gate_table, "expert", split_axis=2, concat_axis=2, tiled=True),
    )
    received = received.reshape(exp_dev, groups, slot_rows_all, quarter)
    got_gates = got_gates.reshape(exp_dev, groups, slot_rows_all)
    slot_rows = received
    slot_gates = got_gates.astype(jnp.float32)
    scaled = (
        jnp.moveaxis(slot_gates, 0, 1)[..., None]
        * lax.all_gather(hidden_saved, "dp", axis=0, tiled=True).astype(jnp.float32)
    ).astype(jnp.bfloat16)
    weight_sum = jnp.einsum("nerf,enrd->efd", scaled, slot_rows, preferred_element_type=jnp.float32)
    weight_grad = weight_sum.astype(jnp.bfloat16)
    slot_rows = received
    expert_grad = lax.psum_scatter(
        jnp.einsum("enrd,efd->nerf", slot_rows, down_weight, preferred_element_type=jnp.float32),
        "dp",
        scatter_dimension=0,
        tiled=True,
    )
    own_gates = jnp.moveaxis(
        lax.dynamic_slice_in_dim(got_gates, lax.axis_index("dp"), 1, 1), 0, 1
    ).astype(jnp.float32)
    hidden_grad = (own_gates[..., None] * expert_grad).astype(jnp.bfloat16)
    slot_dots = jnp.sum(hidden_saved.astype(jnp.float32) * expert_grad, axis=3)
    slot_dots = slot_dots.reshape(exp_dev, senders, capacity)
    slot_dots = lax.psum(slot_dots, "etp")
    returned = lax.all_to_all(slot_dots, "expert", split_axis=1, concat_axis=1, tiled=True)
    own_slots = lax.dynamic_slice_in_dim(slot_ids, lax.axis_index("dp"), 1, 0).reshape(
        token_count, top_count
    )
    lookup = (routes % exp_dev * senders + routes // exp_dev) * capacity + own_slots
    gate_grad = returned.reshape(-1)[lookup]
    return (weight_grad, hidden_grad, gate_grad)


def solution(mesh):
    in_specs = (
        P(("dp", "expert"), None),
        P(("dp", "expert"), None),
        P(("dp", "expert"), None),
        P("dp", "expert", None, "etp"),
        P("expert", "etp", "dp"),
    )
    out_specs = (
        P("expert", "etp", "dp"),
        P("dp", "expert", None, "etp"),
        P(("dp", "expert"), None),
    )
    return jax.shard_map(body, mesh=mesh, in_specs=in_specs, out_specs=out_specs, check_vma=False)
```

profile of v0, /device:TPU:29, one launch (start us, length us, event | category | flops | bytes accessed | tf_op | source)
XLA Modules:
  0.0 950.5 jit_solution(11956927413460439206)
XLA Ops:
  7.2 2.3 copy.112
  9.4 4.5 all-to-all-start.1
  14.0 27.4 %all_gather.9 = s32[512,8]{0,1:T(8,128)S(1)} all-gather(s32[128,8]{0,1:T(8,128)} %param.6), channel_id=1, replica_groups=mesh['dp'=4,'expert'=4,'etp'=2] {'dp'}, dimensions={0}, use_global_device_ids=true | all-gather | bytes 20480 | tf_op jit(solution)/shard_map/all_gather | solution.py:18
  42.3 18.0 %reduce-window.6 = s32[4,16,8,128]{3,2,1,0:T(8,128)S(1)} reduce-window(s32[4,16,8,128]{3,2,1,0:T(8,128)S(1)} %fusion.11, s32[]{:T(128)} %constant.65.clone.1), window={size=1x1x1x128 pad=0_0x0_0x0_0x127_0}, to_apply=%region_0.0 | reduce-window | flops 8323072 | bytes 524292 | tf_op jit(solution)/shard_map/reduce-window
  61.2 15.5 %scatter_custom_fusion.1 = s32[5120]{0:T(1024)S(1)} fusion(s32[4096]{0:T(1024)S(1)} %bitcast.80, s32[4096]{0:T(1024)S(1)} %bitcast.79, s32[]{:T(128)} %constant.65.clone.1), kind=kCustom, calls=%fused_computation.46 | custom fusion | bytes 20484 | tf_op jit(solution)/shard_map/scatter | solution.py:33
  77.1 22.6 %gather_fusion = bf16[5120,1024]{1,0:T(8,128)(2,1)} fusion(bf16[512,1024]{1,0:T(8,128)(2,1)S(1)} %bitcast.67, s32[5120]{0:T(1024)S(1)} %broadcast_clamp_fusion), kind=kCustom, calls=%fused_computation | custom fusion | bytes 20992000 | tf_op jit(solution)/shard_map/gather | solution.py:46
  99.7 6.3 copy_select_fusion
  106.0 121.2 %all_to_all.34 = bf16[4,4,4,80,1024]{4,3,0,1,2:T(8,128)(2,1)} all-to-all(bf16[4,4,4,80,1024]{4,3,0,1,2:T(8,128)(2,1)S(1)} %copy_select_fusion), channel_id=1, replica_groups=mesh['dp'=4,'expert'=4,'etp'=2] {'expert'}, dimensions={2} | all-to-all | bytes 20971520 | tf_op jit(solution)/shard_map/all_to_all | solution.py:49
  227.2 10.1 %copy.83 = bf16[4,4,4,80,1024]{4,3,2,0,1:T(8,128)(2,1)} copy(bf16[4,4,4,80,1024]{4,3,0,1,2:T(8,128)(2,1)} %all_to_all.34) | data formatting | bytes 20971520 | tf_op jit(solution)/shard_map/all_to_all | solution.py:49
  237.3 16.0 %fusion.2 = f32[4,4,320,768]{3,2,0,1:T(8,128)} fusion(bf16[4,4,320,1024]{3,2,0,1:T(8,128)(2,1)} %bitcast.69, bf16[4,768,1024]{2,1,0:T(8,128)(2,1)} %param.9), kind=kOutput, calls=%fused_computation.9 | convolution fusion | flops 8053063680 | bytes 32505856 | tf_op jit(solution)/shard_map/enrd,efd->nerf/dot_general | solution.py:64
  253.4 0.7 all-gather.2.cloned.1.call-update
  254.1 8.9 all_gather.10
  263.3 28.6 %scatter_custom_fusion = bf16[5120]{0:T(1024)(128)(2,1)S(1)} fusion(s32[4096]{0:T(1024)S(1)} %bitcast.81, bf16[4096]{0:T(1024)(128)(2,1)S(1)} %reshape.225, bf16[]{:T(256)} %constant.62.clone.1), kind=kCustom, calls=%fused_computation.55 | custom fusion | bytes 10242 | tf_op jit(solution)/shard_map/scatter | solution.py:38
  292.0 0.6 copy.76
  292.6 12.6 %all-to-all-start = ((bf16[4,4,4,80]{3,0,1,2:T(4,128)(2,1)}), bf16[4,4,4,80]{3,0,1,2:T(4,128)(2,1)S(1)}, u32[]{:S(2)}, u32[]{:S(2)}) async-start(bf16[4,4,4,80]{3,0,1,2:T(4,128)(2,1)} %copy.76), calls=%async_computation | async-start | bytes 32768 | tf_op jit(solution)/shard_map/all_to_all | solution.py:50
  306.2 0.9 all-to-all-done
  307.3 473.0 %all-reduce.3.cloned.1.call-done = f32[4,4,320,768]{3,2,0,1:T(8,128)} async-done(((f32[4,4,320,768]{3,2,0,1:T(8,128)}), f32[4,4,320,768]{3,2,0,1:T(8,128)}) %all-reduce.3.cloned.1.call-update) | async-done | bytes 15728656
  780.3 4.7 multiply_reduce_fusion
  785.1 3.8 psum.7
  789.5 4.8 all-to-all-start.3
  794.3 126.8 %all-gather.2.cloned.1.call-done = bf16[4,4,320,768]{3,2,1,0:T(8,128)(2,1)} async-done(((bf16[1,4,320,768]{3,2,1,0:T(8,128)(2,1)}), bf16[4,4,320,768]{3,2,1,0:T(8,128)(2,1)}) %all-gather.2.cloned.1.call-update) | async-done | bytes 7864336 | tf_op jit(solution)/shard_map/all_gather | solution.py:58
  921.2 15.5 %bitcast_convert_fusion = bf16[4,768,1024]{2,1,0:T(8,128)(2,1)} fusion(bf16[4,4,320,1024]{3,2,0,1:T(8,128)(2,1)} %bitcast.70, bf16[4,4,320,768]{3,2,1,0:T(8,128)(2,1)} %all-gather.2.cloned.1.call-done, f32[4,4,320]{2,1,0:T(4,128)S(1)} %copy.78), kind=kOutput, calls=%fused_computation.5 | convolution fusion | flops 8068005888 | bytes 24662016 | tf_op jit(solution)/shard_map/nerf,enrd->efd/dot_general | solution.py:60
  936.8 6.2 gather_fusion.1
  943.0 0.7 copy.93
  (63 shorter events, 4.3 us)
Async XLA Ops:
  9.4 67.6 %all-to-all-start.1 = ((bf16[128,4,1024]{2,0,1:T(8,128)(2,1)}), bf16[128,4,1024]{2,0,1:T(8,128)(2,1)S(1)}, u32[]{:S(2)}, u32[]{:S(2)}) async-start(bf16[128,4,1024]{2,0,1:T(8,128)(2,1)} %bitcast.62), calls=%async_computation.1 | async-start | bytes 2097152 | tf_op jit(solution)/shard_map/all_to_all | solution.py:16
  14.0 766.3 %all-reduce.3.cloned.1.call-start = ((), (), s32[]{:S(2)}) async-start(), calls=%async_computation.5 | async-start | bytes 31457280
  253.3 0.8 copy-start.2
  253.3 51.9 %copy-start.1 = (s32[128,8]{0,1:T(8,128)S(1)}, s32[128,8]{0,1:T(8,128)}, u32[]{:S(2)}) copy-start(s32[128,8]{0,1:T(8,128)} %param.6) | copy-start | bytes 12292
  253.3 52.3 %copy-start.3 = (u32[32]{0:T(128)S(1)}, u32[32]{0:T(128)}, u32[]{:S(2)}) copy-start(u32[32]{0:T(128)} %constant.80) | copy-start | bytes 388
  253.3 527.0 %copy-start = (bf16[1,4,320,768]{3,2,1,0:T(8,128)(2,1)S(1)}, bf16[1,4,320,768]{3,2,1,0:T(8,128)(2,1)}, u32[]{:S(2)}) copy-start(bf16[1,4,320,768]{3,2,1,0:T(8,128)(2,1)} %param.8) | copy-start | bytes 5898244
  253.3 667.8 %all-gather.2.cloned.1.call-start = ((), (), s32[]{:S(2)}) async-start(), calls=%async_computation.4 | async-start | bytes 9830400 | tf_op jit(solution)/shard_map/all_gather | solution.py:58
  292.6 14.5 %all-to-all-start = ((bf16[4,4,4,80]{3,0,1,2:T(4,128)(2,1)}), bf16[4,4,4,80]{3,0,1,2:T(4,128)(2,1)S(1)}, u32[]{:S(2)}, u32[]{:S(2)}) async-start(bf16[4,4,4,80]{3,0,1,2:T(4,128)(2,1)} %copy.76), calls=%async_computation | async-start | bytes 32768 | tf_op jit(solution)/shard_map/all_to_all | solution.py:50
  789.5 147.2 %all-to-all-start.3 = ((f32[4,4,80]{2,0,1:T(4,128)}), f32[4,4,80]{2,0,1:T(4,128)S(1)}, u32[]{:S(2)}, u32[]{:S(2)}) async-start(f32[4,4,80]{2,0,1:T(4,128)} %copy.86), calls=%async_computation.3 | async-start | bytes 16384 | tf_op jit(solution)/shard_map/all_to_all | solution.py:76
Sparse Core Ops, SparseCore 0:
  253.5 526.7 all-reduce.2
  781.9 139.2 all-gather.1
where the time goes:
time: 955 us; the launch traced here: 951 us
  waiting for transfers between devices  601 us (63%)
  blocking collectives  161 us (17%)
  local copies, waits for them, and re-layouts  90.3 us (9%)
  matrix products  31.6 us (3%)
  other arithmetic  29.6 us (3%)
  starting transfers between devices  22 us (2%)
  between operations  14.3 us (1%)
    unnamed x3, waiting for transfers between devices  474 us
    all_gather x1, waiting for transfers between devices, body(): lax.all_gather(hidden_saved, 'dp', axis=0, tiled=True).astype(jnp.float32)  127 us
    all_to_all x1, blocking collectives, body(): lax.all_to_all(picked, 'expert', split_axis=2, concat_axis=2, tiled=True)  121 us
    scatter x1, local copies, waits for them, and re-layouts, body(): gate_table = jnp.zeros((groups * experts * capacity,), gates.dtype).at[po...  28.6 us
    all_gather x1, blocking collectives, body(): lax.all_gather(routes, 'dp', axis=0, tiled=True)  27.4 us
    gather x1, local copies, waits for them, and re-layouts, body(): columns[safe_rows]  22.6 us
  transfers between devices with their start and end apart: 5, of which 3 were waited for; matrix products, arithmetic and copies ran while one was open for 9% of the time, Pallas kernels for 0%

commit v1 on v0

--- a/solution.py
+++ b/solution.py
@@ -13,6 +13,7 @@
     slot_rows_all = hidden_saved.shape[2]
     capacity = slot_rows_all // senders
     experts = exp_dev * senders
+    hidden_all = lax.all_gather(hidden_saved, "dp", axis=0, tiled=True)
     columns = lax.all_to_all(grad_out, "dp", split_axis=1, concat_axis=0, tiled=True)
     all_routes, all_gates = (
         lax.all_gather(routes, "dp", axis=0, tiled=True),
@@ -45,6 +46,7 @@
     safe_rows = jnp.maximum(row_table - 1, 0)
     picked = jnp.where(filled[:, None], columns[safe_rows], jnp.zeros((1, quarter), columns.dtype))
     picked = picked.reshape(exp_dev, groups, senders, capacity, quarter)
+    hidden_all, picked = lax.optimization_barrier((hidden_all, picked))
     received, got_gates = (
         lax.all_to_all(picked, "expert", split_axis=2, concat_axis=2, tiled=True),
         lax.all_to_all(gate_table, "expert", split_axis=2, concat_axis=2, tiled=True),
@@ -53,26 +55,24 @@
     got_gates = got_gates.reshape(exp_dev, groups, slot_rows_all)
     slot_rows = received
     slot_gates = got_gates.astype(jnp.float32)
-    scaled = (
-        jnp.moveaxis(slot_gates, 0, 1)[..., None]
-        * lax.all_gather(hidden_saved, "dp", axis=0, tiled=True).astype(jnp.float32)
-    ).astype(jnp.bfloat16)
+    hidden_rows = hidden_all.astype(jnp.float32)
+    scaled = (jnp.moveaxis(slot_gates, 0, 1)[..., None] * hidden_rows).astype(jnp.bfloat16)
     weight_sum = jnp.einsum("nerf,enrd->efd", scaled, slot_rows, preferred_element_type=jnp.float32)
     weight_grad = weight_sum.astype(jnp.bfloat16)
-    slot_rows = received
-    expert_grad = lax.psum_scatter(
-        jnp.einsum("enrd,efd->nerf", slot_rows, down_weight, preferred_element_type=jnp.float32),
-        "dp",
-        scatter_dimension=0,
-        tiled=True,
-    )
-    own_gates = jnp.moveaxis(
-        lax.dynamic_slice_in_dim(got_gates, lax.axis_index("dp"), 1, 1), 0, 1
-    ).astype(jnp.float32)
-    hidden_grad = (own_gates[..., None] * expert_grad).astype(jnp.bfloat16)
-    slot_dots = jnp.sum(hidden_saved.astype(jnp.float32) * expert_grad, axis=3)
+    partial = jnp.einsum("enrd,efd->nerf", slot_rows, down_weight, preferred_element_type=jnp.float32)
+    dot_part = jnp.sum(hidden_rows * partial, axis=3)
+    me = lax.axis_index("dp")
+    sent = partial.astype(jnp.bfloat16)
+    expert_grad = lax.dynamic_index_in_dim(partial, me, 0, keepdims=False)
+    for shift in range(1, groups):
+        chunk = lax.dynamic_index_in_dim(sent, (me + shift) % groups, 0, keepdims=False)
+        pairs = [(i, (i + shift) % groups) for i in range(groups)]
+        expert_grad = expert_grad + lax.ppermute(chunk, "dp", pairs).astype(jnp.float32)
+    own_gates = lax.dynamic_index_in_dim(got_gates, me, 1, keepdims=False).astype(jnp.float32)
+    hidden_grad = (own_gates[..., None] * expert_grad).astype(jnp.bfloat16)[None]
+    slot_dots = lax.psum(dot_part, ("dp", "etp"))
+    slot_dots = lax.dynamic_index_in_dim(slot_dots, me, 0, keepdims=False)
     slot_dots = slot_dots.reshape(exp_dev, senders, capacity)
-    slot_dots = lax.psum(slot_dots, "etp")
     returned = lax.all_to_all(slot_dots, "expert", split_axis=1, concat_axis=1, tiled=True)
     own_slots = lax.dynamic_slice_in_dim(slot_ids, lax.axis_index("dp"), 1, 0).reshape(
         token_count, top_count

time: 955 us -> 586 us (0.61)
  waiting for transfers between devices: 601 us -> 114 us
  blocking collectives: 161 us -> 255 us
  other arithmetic: 29.6 us -> 43.2 us
    unnamed x3 -> x1, waiting for transfers between devices: 474 us -> 0.68 us
    psum x1, blocking collectives: 3.83 us -> 176 us  [body(): slot_dots = lax.psum(dot_part, ('dp', 'etp'))]
    all_gather x1, waiting for transfers between devices: 127 us -> 0.01 us  [body(): hidden_all = lax.all_gather(hidden_saved, 'dp', axis=0, tiled=True)]
    all_to_all x1 -> x0, blocking collectives: 121 us -> none  [body(): lax.all_to_all(picked, 'expert', split_axis=2, concat_axis=2, tiled=True)]
    all_to_all x0 -> x1, waiting for transfers between devices: none -> 113 us  [body(): lax.all_to_all(picked, 'expert', split_axis=2, concat_axis=2, tiled=True)]
    all_gather x1, blocking collectives: 27.4 us -> 61 us  [body(): lax.all_gather(routes, 'dp', axis=0, tiled=True)]
  transfers between devices with their start and end apart: 5 -> 8, of which waited for: 3 -> 1; matrix products, arithmetic and copies ran while one was open for 9% -> 23% of each run, Pallas kernels for 0% -> 0%
where the time goes in v1:
time: 586 us; the launch traced here: 581 us
  blocking collectives  255 us (44%)
  waiting for transfers between devices  114 us (19%)
  local copies, waits for them, and re-layouts  94.9 us (16%)
  other arithmetic  43.2 us (7%)
  matrix products  33 us (6%)
  starting transfers between devices  27.2 us (5%)
  between operations  14.4 us (2%)
    psum x1, blocking collectives, body(): slot_dots = lax.psum(dot_part, ('dp', 'etp'))  176 us
    all_to_all x1, waiting for transfers between devices, body(): lax.all_to_all(picked, 'expert', split_axis=2, concat_axis=2, tiled=True)  113 us
    all_gather x1, blocking collectives, body(): lax.all_gather(routes, 'dp', axis=0, tiled=True)  61 us
    scatter x1, local copies, waits for them, and re-layouts, body(): gate_table = jnp.zeros((groups * experts * capacity,), gates.dtype).at[po...  28.6 us
    gather x1, local copies, waits for them, and re-layouts, body(): columns[safe_rows]  22.6 us
    another operation x3, other arithmetic  18.2 us
    all_gather x1, blocking collectives, body(): lax.all_gather(gates, 'dp', axis=0, tiled=True)  17.4 us
    dot_general x1, matrix products, body(): jnp.einsum('enrd,efd->nerf', slot_rows, down_weight, preferred_element_ty...  17.3 us
  transfers between devices with their start and end apart: 8, of which 1 were waited for; matrix products, arithmetic and copies ran while one was open for 23% of the time, Pallas kernels for 0%

profile of v1, /device:TPU:29, one launch (start us, length us, event | category | flops | bytes accessed | tf_op | source)
XLA Modules:
  0.0 581.1 jit_solution(11124000495688380727)
XLA Ops:
  7.2 0.7 all-gather.2.cloned.1.call-update
  7.9 2.3 copy.91
  10.2 4.5 all-to-all-start.1
  14.7 61.0 %all_gather.9 = s32[512,8]{0,1:T(8,128)S(1)} all-gather(s32[128,8]{0,1:T(8,128)} %param.6), channel_id=1, replica_groups=mesh['dp'=4,'expert'=4,'etp'=2] {'dp'}, dimensions={0}, use_global_device_ids=true | all-gather | bytes 20480 | tf_op jit(solution)/shard_map/all_gather | solution.py:19
  76.4 18.0 %reduce-window.6 = s32[4,16,8,128]{3,2,1,0:T(8,128)S(1)} reduce-window(s32[4,16,8,128]{3,2,1,0:T(8,128)S(1)} %fusion.16, s32[]{:T(128)} %constant.102.clone.1), window={size=1x1x1x128 pad=0_0x0_0x0_0x127_0}, to_apply=%region_0.0 | reduce-window | flops 8323072 | bytes 524292 | tf_op jit(solution)/shard_map/reduce-window
  95.5 15.5 %scatter_custom_fusion.1 = s32[5120]{0:T(1024)S(1)} fusion(s32[4096]{0:T(1024)S(1)} %bitcast.92, s32[4096]{0:T(1024)S(1)} %bitcast.91, s32[]{:T(128)} %constant.102.clone.1), kind=kCustom, calls=%fused_computation.54 | custom fusion | bytes 20484 | tf_op jit(solution)/shard_map/scatter | solution.py:34
  111.4 17.4 %all_gather.10 = bf16[512,8]{0,1:T(8,128)(2,1)S(1)} all-gather(bf16[128,8]{0,1:T(8,128)(2,1)S(1)} %copy-done.1), channel_id=1, replica_groups=mesh['dp'=4,'expert'=4,'etp'=2] {'dp'}, dimensions={0}, use_global_device_ids=true | all-gather | bytes 10240 | tf_op jit(solution)/shard_map/all_gather | solution.py:20
  129.1 28.6 %scatter_custom_fusion = bf16[5120]{0:T(1024)(128)(2,1)S(1)} fusion(s32[4096]{0:T(1024)S(1)} %bitcast.93, bf16[4096]{0:T(1024)(128)(2,1)S(1)} %reshape.221, bf16[]{:T(256)} %constant.99.clone.1), kind=kCustom, calls=%fused_computation.64 | custom fusion | bytes 10242 | tf_op jit(solution)/shard_map/scatter | solution.py:39
  158.4 3.8 all-to-all-start
  162.2 22.6 %gather_fusion = bf16[5120,1024]{1,0:T(8,128)(2,1)} fusion(bf16[512,1024]{1,0:T(8,128)(2,1)S(1)} %bitcast.77, s32[5120]{0:T(1024)S(1)} %broadcast_clamp_fusion), kind=kCustom, calls=%fused_computation | custom fusion | bytes 20992000 | tf_op jit(solution)/shard_map/gather | solution.py:47
  184.8 10.0 %copy_select_fusion = bf16[4,4,4,80,1024]{4,3,1,0,2:T(8,128)(2,1)} fusion(bf16[4,4,4,80,1024]{4,3,2,1,0:T(8,128)(2,1)} %bitcast.78, pred[4,4,4,80]{3,1,0,2:T(4,128)(4,1)S(1)} %copy.68), kind=kLoop, calls=%fused_computation.10 | loop fusion | flops 5242880 | bytes 20976640 | tf_op jit(solution)/shard_map/jit(_where)/select_n | solution.py:47
  194.8 6.2 %all-to-all-start.2 = ((bf16[4,4,4,80,1024]{4,3,1,0,2:T(8,128)(2,1)}), bf16[4,4,4,80,1024]{4,3,1,0,2:T(8,128)(2,1)}, u32[]{:S(2)}, u32[]{:S(2)}) async-start(bf16[4,4,4,80,1024]{4,3,1,0,2:T(8,128)(2,1)} %copy_select_fusion), calls=%async_computation.2 | async-start | bytes 20971520 | tf_op jit(solution)/shard_map/all_to_all | solution.py:51
  201.7 113.1 %all-to-all-done.2 = bf16[4,4,4,80,1024]{4,3,1,0,2:T(8,128)(2,1)} async-done(((bf16[4,4,4,80,1024]{4,3,1,0,2:T(8,128)(2,1)}), bf16[4,4,4,80,1024]{4,3,1,0,2:T(8,128)(2,1)}, u32[]{:S(2)}, u32[]{:S(2)}) %all-to-all-start.2) | async-done | bytes 10485792 | tf_op jit(solution)/shard_map/all_to_all | solution.py:51
  314.7 10.2 %copy.72 = bf16[4,4,4,80,1024]{4,3,2,1,0:T(8,128)(2,1)} copy(bf16[4,4,4,80,1024]{4,3,1,0,2:T(8,128)(2,1)} %all-to-all-done.2) | data formatting | bytes 20971520 | tf_op jit(solution)/shard_map/all_to_all | solution.py:51
  325.0 17.3 %bitcast_convert_fusion = (bf16[4,4,320,768]{3,2,0,1:T(8,128)(2,1)}, f32[4,4,320,768]{3,2,1,0:T(8,128)}) fusion(bf16[4,4,320,1024]{3,2,1,0:T(8,128)(2,1)} %bitcast.79, bf16[4,768,1024]{2,1,0:T(8,128)(2,1)} %param.9), kind=kOutput, calls=%fused_computation.8 | convolution fusion | flops 8056995840 | bytes 40370176 | tf_op jit(solution)/shard_map/enrd,efd->nerf/dot_general | solution.py:62
  342.3 5.1 dynamic-slice_bitcast_fusion.2
  347.4 1.5 collective-permute-start.2
  348.8 8.5 %fusion.1 = f32[4,4,320]{2,0,1:T(4,128)S(1)} fusion(bf16[4,4,320,768]{3,2,0,1:T(8,128)(2,1)} %all-gather.2.cloned.1.call-done, f32[4,4,320,768]{3,2,1,0:T(8,128)} %get-tuple-element.23), kind=kLoop, calls=%fused_computation.7 | loop fusion | flops 11791360 | bytes 23613440 | tf_op jit(solution)/shard_map/reduce_sum | solution.py:63
  357.3 176.3 %psum.7 = f32[4,4,320]{2,0,1:T(4,128)S(1)} all-reduce(f32[4,4,320]{2,0,1:T(4,128)S(1)} %fusion.1), channel_id=1, replica_groups=mesh['dp'=4,'expert'=4,'etp'=2] {'dp','etp'}, use_global_device_ids=true, to_apply=%region_6.7 | all-reduce | flops 5120 | bytes 40960 | tf_op jit(solution)/shard_map/psum | solution.py:73
  534.3 11.2 %all-to-all-start.3 = ((f32[4,4,80]{2,0,1:T(4,128)}), f32[4,4,80]{2,0,1:T(4,128)S(1)}, u32[]{:S(2)}, u32[]{:S(2)}) async-start(f32[4,4,80]{2,0,1:T(4,128)} %copy.73), calls=%async_computation.3 | async-start | bytes 16384 | tf_op jit(solution)/shard_map/all_to_all | solution.py:76
  545.5 15.6 %bitcast_convert_fusion.1 = bf16[4,768,1024]{2,1,0:T(8,128)(2,1)} fusion(bf16[4,4,320,1024]{3,2,1,0:T(8,128)(2,1)} %bitcast.80, bf16[4,4,320,768]{3,2,0,1:T(8,128)(2,1)} %all-gather.2.cloned.1.call-done, f32[4,4,320]{2,0,1:T(4,128)S(1)} %convert_bitcast_fusion), kind=kOutput, calls=%fused_computation.9 | convolution fusion | flops 8068005888 | bytes 24662016 | tf_op jit(solution)/shard_map/nerf,enrd->efd/dot_general | solution.py:60
  561.2 6.2 %gather_fusion.1 = f32[1024]{0:T(1024)S(1)} fusion(f32[1280]{0:T(1024)S(1)} %reshape.198, s32[1024]{0:T(1024)S(1)} %broadcast_clamp_fusion.1), kind=kCustom, calls=%fused_computation.1 | custom fusion | bytes 12288 | tf_op jit(solution)/shard_map/gather | solution.py:81
  567.5 0.7 copy.79
  568.1 6.1 %fusion.13 = bf16[1,4,320,768]{3,2,1,0:T(8,128)(2,1)} fusion(bf16[4,320,768]{2,1,0:T(8,128)(2,1)} %collective-permute-done.2, bf16[4,320,768]{2,1,0:T(8,128)(2,1)} %collective-permute-done.1, bf16[4,320,768]{2,1,0:T(8,128)(2,1)} %collective-permute-done, f32[4,4,320,768]{3,2,1,0:T(8,128)} %get-tuple-element.23, s32[]{:T(128)S(6)} %select_n.78, ...), kind=kLoop, calls=%fused_computation.20 | loop fusion | flops 7864320 | bytes 11801604 | tf_op jit(solution)/shard_map/broadcast_in_dim | solution.py:72
  (65 shorter events, 4.4 us)
Async XLA Ops:
  7.2 104.3 %copy-start.1 = (bf16[128,8]{0,1:T(8,128)(2,1)S(1)}, bf16[128,8]{0,1:T(8,128)(2,1)}, u32[]{:S(2)}) copy-start(bf16[128,8]{0,1:T(8,128)(2,1)} %param.7) | copy-start | bytes 6148
  7.2 187.6 %all-gather.2.cloned.1.call-start = ((), (), s32[]{:S(2)}) async-start(), calls=%async_computation.4 | async-start | bytes 9830400 | tf_op jit(solution)/shard_map/all_gather | solution.py:16
  10.2 148.2 %all-to-all-start.1 = ((bf16[128,4,1024]{2,0,1:T(8,128)(2,1)}), bf16[128,4,1024]{2,0,1:T(8,128)(2,1)S(1)}, u32[]{:S(2)}, u32[]{:S(2)}) async-start(bf16[128,4,1024]{2,0,1:T(8,128)(2,1)} %bitcast.74), calls=%async_computation.1 | async-start | bytes 2097152 | tf_op jit(solution)/shard_map/all_to_all | solution.py:17
  158.4 36.4 %all-to-all-start = ((bf16[4,4,4,80]{3,0,1,2:T(4,128)(2,1)}), bf16[4,4,4,80]{3,0,1,2:T(4,128)(2,1)S(1)}, u32[]{:S(2)}, u32[]{:S(2)}) async-start(bf16[4,4,4,80]{3,0,1,2:T(4,128)(2,1)} %copy.65), calls=%async_computation | async-start | bytes 32768 | tf_op jit(solution)/shard_map/all_to_all | solution.py:52
  194.8 6.3 %copy-start = (s32[128,8]{0,1:T(8,128)S(1)}, s32[128,8]{0,1:T(8,128)}, u32[]{:S(2)}) copy-start(s32[128,8]{0,1:T(8,128)} %param.6) | copy-start | bytes 12292
  194.8 119.9 %all-to-all-start.2 = ((bf16[4,4,4,80,1024]{4,3,1,0,2:T(8,128)(2,1)}), bf16[4,4,4,80,1024]{4,3,1,0,2:T(8,128)(2,1)}, u32[]{:S(2)}, u32[]{:S(2)}) async-start(bf16[4,4,4,80,1024]{4,3,1,0,2:T(8,128)(2,1)} %copy_select_fusion), calls=%async_computation.2 | async-start | bytes 20971520 | tf_op jit(solution)/shard_map/all_to_all | solution.py:51
  347.3 220.8 %collective-permute-start = (bf16[4,320,768]{2,1,0:T(8,128)(2,1)}, bf16[4,320,768]{2,1,0:T(8,128)(2,1)}, u32[]{:S(2)}, u32[]{:S(2)}) collective-permute-start(bf16[4,320,768]{2,1,0:T(8,128)(2,1)} %get-tuple-element.19), channel_id=1, source_target_pairs={{0,8},{8,16},{16,24},{24,0},{1,9},{9,17},{17,25},{25,1},{2,10},{10... | collective-permute-start | bytes 5898248 | tf_op jit(solution)/shard_map/ppermute | solution.py:70
  347.4 220.8 %collective-permute-start.1 = (bf16[4,320,768]{2,1,0:T(8,128)(2,1)}, bf16[4,320,768]{2,1,0:T(8,128)(2,1)}, u32[]{:S(2)}, u32[]{:S(2)}) collective-permute-start(bf16[4,320,768]{2,1,0:T(8,128)(2,1)} %get-tuple-element.21), channel_id=1, source_target_pairs={{0,16},{8,24},{16,0},{24,8},{1,17},{9,25},{17,1},{25,9},{2,18},{10... | collective-permute-start | bytes 5898248 | tf_op jit(solution)/shard_map/ppermute | solution.py:70
  347.4 220.8 %collective-permute-start.2 = (bf16[4,320,768]{2,1,0:T(8,128)(2,1)S(1)}, bf16[4,320,768]{2,1,0:T(8,128)(2,1)}, u32[]{:S(2)}, u32[]{:S(2)}) collective-permute-start(bf16[4,320,768]{2,1,0:T(8,128)(2,1)S(1)} %get-tuple-element.20), channel_id=1, source_target_pairs={{0,24},{8,0},{16,8},{24,16},{1,25},{9,1},{17,9},{25,17},{2,26},{10... | collective-permute-start | bytes 5898248 | tf_op jit(solution)/shard_map/ppermute | solution.py:70
  534.3 26.8 %all-to-all-start.3 = ((f32[4,4,80]{2,0,1:T(4,128)}), f32[4,4,80]{2,0,1:T(4,128)S(1)}, u32[]{:S(2)}, u32[]{:S(2)}) async-start(f32[4,4,80]{2,0,1:T(4,128)} %copy.73), calls=%async_computation.3 | async-start | bytes 16384 | tf_op jit(solution)/shard_map/all_to_all | solution.py:76
Sparse Core Ops, SparseCore 0:
  9.6 156.7 all-gather.1

commit v2 on v1

--- a/solution.py
+++ b/solution.py
@@ -13,12 +13,13 @@
     slot_rows_all = hidden_saved.shape[2]
     capacity = slot_rows_all // senders
     experts = exp_dev * senders
+    meta = jnp.concatenate([routes.astype(jnp.float32), gates.astype(jnp.float32)], axis=1)
+    all_meta = lax.all_gather(meta, "dp", axis=0, tiled=True)
+    hidden_saved, all_meta = lax.optimization_barrier((hidden_saved, all_meta))
     hidden_all = lax.all_gather(hidden_saved, "dp", axis=0, tiled=True)
+    all_routes = all_meta[:, :top_count].astype(jnp.int32)
+    all_gates = all_meta[:, top_count:].astype(gates.dtype)
     columns = lax.all_to_all(grad_out, "dp", split_axis=1, concat_axis=0, tiled=True)
-    all_routes, all_gates = (
-        lax.all_gather(routes, "dp", axis=0, tiled=True),
-        lax.all_gather(gates, "dp", axis=0, tiled=True),
-    )
     pair_routes = all_routes.reshape(groups, token_count * top_count)
     expert_ids = jnp.arange(experts, dtype=jnp.int32)
     onehot = (pair_routes[:, :, None] == expert_ids[None, None, :]).astype(jnp.int32)
@@ -46,12 +47,12 @@
     safe_rows = jnp.maximum(row_table - 1, 0)
     picked = jnp.where(filled[:, None], columns[safe_rows], jnp.zeros((1, quarter), columns.dtype))
     picked = picked.reshape(exp_dev, groups, senders, capacity, quarter)
-    hidden_all, picked = lax.optimization_barrier((hidden_all, picked))
     received, got_gates = (
         lax.all_to_all(picked, "expert", split_axis=2, concat_axis=2, tiled=True),
         lax.all_to_all(gate_table, "expert", split_axis=2, concat_axis=2, tiled=True),
     )
     received = received.reshape(exp_dev, groups, slot_rows_all, quarter)
+    hidden_all, received = lax.optimization_barrier((hidden_all, received))
     got_gates = got_gates.reshape(exp_dev, groups, slot_rows_all)
     slot_rows = received
     slot_gates = got_gates.astype(jnp.float32)
@@ -70,6 +71,7 @@
         expert_grad = expert_grad + lax.ppermute(chunk, "dp", pairs).astype(jnp.float32)
     own_gates = lax.dynamic_index_in_dim(got_gates, me, 1, keepdims=False).astype(jnp.float32)
     hidden_grad = (own_gates[..., None] * expert_grad).astype(jnp.bfloat16)[None]
+    expert_grad, dot_part, weight_grad = lax.optimization_barrier((expert_grad, dot_part, weight_grad))
     slot_dots = lax.psum(dot_part, ("dp", "etp"))
     slot_dots = lax.dynamic_index_in_dim(slot_dots, me, 0, keepdims=False)
     slot_dots = slot_dots.reshape(exp_dev, senders, capacity)

time: 586 us -> 522 us (0.89)
  blocking collectives: 255 us -> 75.2 us
  waiting for transfers between devices: 114 us -> 219 us
  starting transfers between devices: 27.2 us -> 34.1 us
    psum x1, blocking collectives: 176 us -> 65 us  [body(): slot_dots = lax.psum(dot_part, ('dp', 'etp'))]
    ppermute x3, waiting for transfers between devices: 0.01 us -> 105 us  [body(): lax.ppermute(chunk, 'dp', pairs).astype(jnp.float32)]
    all_gather x2 -> x1, blocking collectives: 78.4 us -> 10.2 us  [body(): all_meta = lax.all_gather(meta, 'dp', axis=0, tiled=True)]
  transfers between devices with their start and end apart: 8 -> 8, of which waited for: 1 -> 4; matrix products, arithmetic and copies ran while one was open for 23% -> 26% of each run, Pallas kernels for 0% -> 0%
where the time goes in v2:
time: 522 us; the launch traced here: 514 us
  waiting for transfers between devices  219 us (42%)
  local copies, waits for them, and re-layouts  95.1 us (18%)
  blocking collectives  75.2 us (14%)
  other arithmetic  44.1 us (8%)
  starting transfers between devices  34.1 us (7%)
  matrix products  31.1 us (6%)
  between operations  14.4 us (3%)
    all_to_all x1, waiting for transfers between devices, body(): lax.all_to_all(picked, 'expert', split_axis=2, concat_axis=2, tiled=True)  113 us
    ppermute x3, waiting for transfers between devices, body(): lax.ppermute(chunk, 'dp', pairs).astype(jnp.float32)  105 us
    psum x1, blocking collectives, body(): slot_dots = lax.psum(dot_part, ('dp', 'etp'))  65 us
    scatter x1, local copies, waits for them, and re-layouts, body(): gate_table = jnp.zeros((groups * experts * capacity,), gates.dtype).at[po...  28.6 us
    gather x1, local copies, waits for them, and re-layouts, body(): columns[safe_rows]  22.6 us
    another operation x3, other arithmetic  18.2 us
    dot_general x1, matrix products, body(): jnp.einsum('enrd,efd->nerf', slot_rows, down_weight, preferred_element_ty...  17.3 us
    scatter x1, local copies, waits for them, and re-layouts, body(): jnp.zeros((groups * experts * capacity,), jnp.int32).at[position]  15.5 us
  transfers between devices with their start and end apart: 8, of which 4 were waited for; matrix products, arithmetic and copies ran while one was open for 26% of the time, Pallas kernels for 0%

profile of v2, /device:TPU:29, one launch (start us, length us, event | category | flops | bytes accessed | tf_op | source)
XLA Modules:
  0.0 513.6 jit_solution(5603916048965349323)
XLA Ops:
  8.6 10.2 %all_gather.6 = f32[512,16]{0,1:T(8,128)S(1)} all-gather(f32[128,16]{0,1:T(8,128)S(1)} %pad_maximum_fusion), channel_id=1, replica_groups=mesh['dp'=4,'expert'=4,'etp'=2] {'dp'}, dimensions={0}, use_global_device_ids=true | all-gather | bytes 40960 | tf_op jit(solution)/shard_map/all_gather | solution.py:17
  18.8 2.3 copy.90
  21.1 4.5 all-to-all-start
  26.3 18.0 %reduce-window.6 = s32[4,16,8,128]{3,2,1,0:T(8,128)S(1)} reduce-window(s32[4,16,8,128]{3,2,1,0:T(8,128)S(1)} %fusion.14, s32[]{:T(128)} %constant.99.clone.1), window={size=1x1x1x128 pad=0_0x0_0x0_0x127_0}, to_apply=%region_0.0 | reduce-window | flops 8323072 | bytes 524292 | tf_op jit(solution)/shard_map/reduce-window
  45.7 28.6 %scatter_custom_fusion.1 = bf16[5120]{0:T(1024)(128)(2,1)S(1)} fusion(s32[4096]{0:T(1024)S(1)} %bitcast.89, bf16[4096]{0:T(1024)(128)(2,1)S(1)} %reshape.229, bf16[]{:T(256)} %constant.108.clone.1), kind=kCustom, calls=%fused_computation.66 | custom fusion | bytes 10242 | tf_op jit(solution)/shard_map/scatter | solution.py:40
  75.0 15.5 %scatter_custom_fusion = s32[5120]{0:T(1024)S(1)} fusion(s32[4096]{0:T(1024)S(1)} %bitcast.90, s32[4096]{0:T(1024)S(1)} %bitcast.88, s32[]{:T(128)} %constant.99.clone.1), kind=kCustom, calls=%fused_computation.55 | custom fusion | bytes 20484 | tf_op jit(solution)/shard_map/scatter | solution.py:35
  91.0 7.5 %all-to-all-start.2 = ((bf16[4,4,4,80]{3,0,1,2:T(4,128)(2,1)}), bf16[4,4,4,80]{3,0,1,2:T(4,128)(2,1)S(1)}, u32[]{:S(2)}, u32[]{:S(2)}) async-start(bf16[4,4,4,80]{3,0,1,2:T(4,128)(2,1)} %copy.70), calls=%async_computation.2 | async-start | bytes 32768 | tf_op jit(solution)/shard_map/all_to_all | solution.py:52
  98.4 22.6 %gather_fusion = bf16[5120,1024]{1,0:T(8,128)(2,1)} fusion(bf16[512,1024]{1,0:T(8,128)(2,1)S(1)} %bitcast.72, s32[5120]{0:T(1024)S(1)} %broadcast_clamp_fusion), kind=kCustom, calls=%fused_computation | custom fusion | bytes 20992000 | tf_op jit(solution)/shard_map/gather | solution.py:48
  121.0 10.1 %copy_select_fusion = bf16[4,4,4,80,1024]{4,3,1,0,2:T(8,128)(2,1)} fusion(bf16[4,4,4,80,1024]{4,3,2,1,0:T(8,128)(2,1)} %bitcast.73, pred[4,4,4,80]{3,1,0,2:T(4,128)(4,1)S(1)} %copy.64), kind=kLoop, calls=%fused_computation.10 | loop fusion | flops 5242880 | bytes 20976640 | tf_op jit(solution)/shard_map/jit(_where)/select_n | solution.py:48
  131.1 6.4 %all-to-all-start.1 = ((bf16[4,4,4,80,1024]{4,3,1,0,2:T(8,128)(2,1)}), bf16[4,4,4,80,1024]{4,3,1,0,2:T(8,128)(2,1)}, u32[]{:S(2)}, u32[]{:S(2)}) async-start(bf16[4,4,4,80,1024]{4,3,1,0,2:T(8,128)(2,1)} %copy_select_fusion), calls=%async_computation.1 | async-start | bytes 20971520 | tf_op jit(solution)/shard_map/all_to_all | solution.py:51
  138.0 113.1 %all-to-all-done.1 = bf16[4,4,4,80,1024]{4,3,1,0,2:T(8,128)(2,1)} async-done(((bf16[4,4,4,80,1024]{4,3,1,0,2:T(8,128)(2,1)}), bf16[4,4,4,80,1024]{4,3,1,0,2:T(8,128)(2,1)}, u32[]{:S(2)}, u32[]{:S(2)}) %all-to-all-start.1) | async-done | bytes 10485792 | tf_op jit(solution)/shard_map/all_to_all | solution.py:51
  251.1 10.2 %copy.68 = bf16[4,4,4,80,1024]{4,3,2,1,0:T(8,128)(2,1)} copy(bf16[4,4,4,80,1024]{4,3,1,0,2:T(8,128)(2,1)} %all-to-all-done.1) | data formatting | bytes 20971520 | tf_op jit(solution)/shard_map/all_to_all | solution.py:51
  261.3 17.3 %bitcast_convert_fusion = (bf16[4,4,320,768]{3,2,0,1:T(8,128)(2,1)}, f32[4,4,320,768]{3,2,1,0:T(8,128)}) fusion(bf16[4,4,320,1024]{3,2,1,0:T(8,128)(2,1)} %bitcast.74, bf16[4,768,1024]{2,1,0:T(8,128)(2,1)} %param.9), kind=kOutput, calls=%fused_computation.8 | convolution fusion | flops 8056995840 | bytes 40370176 | tf_op jit(solution)/shard_map/enrd,efd->nerf/dot_general | solution.py:63
  278.7 5.3 %dynamic-slice_bitcast_fusion.2 = (bf16[4,320,768]{2,1,0:T(8,128)(2,1)S(1)}, bf16[4,320,768]{2,1,0:T(8,128)(2,1)}, bf16[4,320,768]{2,1,0:T(8,128)(2,1)}) fusion(bf16[4,4,320,768]{3,2,0,1:T(8,128)(2,1)} %get-tuple-element.32, s32[]{:T(128)S(6)} %select_n.80, s32[]{:T(128)S(6)} %select_n.84, s32[]{:T(128)S(6)} %select_n.82), kind=kLoop, calls=%fused_computation.22 | loop fusion | bytes 11796492 | tf_op jit(solution)/shard_map/jit(dynamic_index_in_dim)/squeeze | solution.py:69
  284.2 3.0 collective-permute-start
  287.2 8.0 %fusion = f32[4,4,320]{2,0,1:T(4,128)S(1)} fusion(bf16[4,4,320,768]{3,2,0,1:T(8,128)(2,1)S(1)} %copy-done, f32[4,4,320,768]{3,2,1,0:T(8,128)} %get-tuple-element.33), kind=kLoop, calls=%fused_computation.6 | loop fusion | flops 11791360 | bytes 23613440 | tf_op jit(solution)/shard_map/reduce_sum | solution.py:64
  295.2 13.8 %bitcast_convert_fusion.1 = bf16[4,768,1024]{2,1,0:T(8,128)(2,1)} fusion(bf16[4,4,320,1024]{3,2,1,0:T(8,128)(2,1)S(1)} %bitcast.77, bf16[4,4,320,768]{3,2,0,1:T(8,128)(2,1)} %all-gather.2.cloned.1.call-done, f32[4,4,320]{2,0,1:T(4,128)S(1)} %convert_bitcast_fusion), kind=kOutput, calls=%fused_computation.9 | convolution fusion | flops 8068005888 | bytes 24662016 | tf_op jit(solution)/shard_map/nerf,enrd->efd/dot_general | solution.py:61
  309.0 20.9 %collective-permute-done.2 = bf16[4,320,768]{2,1,0:T(8,128)(2,1)} collective-permute-done((bf16[4,320,768]{2,1,0:T(8,128)(2,1)}, bf16[4,320,768]{2,1,0:T(8,128)(2,1)}, u32[]{:S(2)}, u32[]{:S(2)}) %collective-permute-start.2) | collective-permute-done | bytes 1966112 | tf_op jit(solution)/shard_map/ppermute | solution.py:71
  329.9 83.9 %collective-permute-done.1 = bf16[4,320,768]{2,1,0:T(8,128)(2,1)} collective-permute-done((bf16[4,320,768]{2,1,0:T(8,128)(2,1)}, bf16[4,320,768]{2,1,0:T(8,128)(2,1)}, u32[]{:S(2)}, u32[]{:S(2)}) %collective-permute-start.1) | collective-permute-done | bytes 1966112 | tf_op jit(solution)/shard_map/ppermute | solution.py:71
  413.8 6.1 %fusion.11 = bf16[1,4,320,768]{3,2,1,0:T(8,128)(2,1)} fusion(f32[4,320]{1,0:T(4,128)S(1)} %bitcast.87, bf16[4,320,768]{2,1,0:T(8,128)(2,1)} %collective-permute-done.2, bf16[4,320,768]{2,1,0:T(8,128)(2,1)} %collective-permute-done.1, bf16[4,320,768]{2,1,0:T(8,128)(2,1)} %collective-permute-done, f32[4,4,320,768]{3,2,1,0:T(8,128)} %get-tuple-element.33, ...), kind=kLoop, calls=%fused_computation.19 | loop fusion | flops 7864320 | bytes 11801604 | tf_op jit(solution)/shard_map/broadcast_in_dim | solution.py:73
  420.0 65.0 %psum.7 = f32[4,4,320]{2,0,1:T(4,128)S(1)} all-reduce(f32[4,4,320]{2,0,1:T(4,128)S(1)} %fusion), channel_id=1, replica_groups=mesh['dp'=4,'expert'=4,'etp'=2] {'dp','etp'}, use_global_device_ids=true, to_apply=%region_6.7 | all-reduce | flops 5120 | bytes 40960 | tf_op jit(solution)/shard_map/psum | solution.py:75
  485.7 12.5 %all-to-all-start.3 = ((f32[4,4,80]{2,0,1:T(4,128)}), f32[4,4,80]{2,0,1:T(4,128)S(1)}, u32[]{:S(2)}, u32[]{:S(2)}) async-start(f32[4,4,80]{2,0,1:T(4,128)} %copy.72), calls=%async_computation.3 | async-start | bytes 16384 | tf_op jit(solution)/shard_map/all_to_all | solution.py:78
  498.2 1.5 all-to-all-done.3
  499.8 6.2 %gather_fusion.1 = f32[1024]{0:T(1024)S(1)} fusion(f32[1280]{0:T(1024)S(1)} %reshape.198, s32[1024]{0:T(1024)S(1)} %broadcast_clamp_fusion.1), kind=kCustom, calls=%fused_computation.1 | custom fusion | bytes 12288 | tf_op jit(solution)/shard_map/gather | solution.py:83
  (76 shorter events, 6.8 us)
Async XLA Ops:
  7.2 254.2 %all-gather.2.cloned.1.call-start = ((), (), s32[]{:S(2)}) async-start(), calls=%async_computation.4 | async-start | bytes 9830400 | tf_op jit(solution)/shard_map/all_gather | solution.py:19
  21.1 69.8 %all-to-all-start = ((bf16[128,4,1024]{2,0,1:T(8,128)(2,1)}), bf16[128,4,1024]{2,0,1:T(8,128)(2,1)S(1)}, u32[]{:S(2)}, u32[]{:S(2)}) async-start(bf16[128,4,1024]{2,0,1:T(8,128)(2,1)} %bitcast.69), calls=%async_computation | async-start | bytes 2097152 | tf_op jit(solution)/shard_map/all_to_all | solution.py:22
  91.0 40.1 %all-to-all-start.2 = ((bf16[4,4,4,80]{3,0,1,2:T(4,128)(2,1)}), bf16[4,4,4,80]{3,0,1,2:T(4,128)(2,1)S(1)}, u32[]{:S(2)}, u32[]{:S(2)}) async-start(bf16[4,4,4,80]{3,0,1,2:T(4,128)(2,1)} %copy.70), calls=%async_computation.2 | async-start | bytes 32768 | tf_op jit(solution)/shard_map/all_to_all | solution.py:52
  131.1 6.4 %copy-start.1 = (s32[128,8]{0,1:T(8,128)S(1)}, s32[128,8]{0,1:T(8,128)}, u32[]{:S(2)}) copy-start(s32[128,8]{0,1:T(8,128)} %param.6) | copy-start | bytes 12292
  131.1 120.1 %all-to-all-start.1 = ((bf16[4,4,4,80,1024]{4,3,1,0,2:T(8,128)(2,1)}), bf16[4,4,4,80,1024]{4,3,1,0,2:T(8,128)(2,1)}, u32[]{:S(2)}, u32[]{:S(2)}) async-start(bf16[4,4,4,80,1024]{4,3,1,0,2:T(8,128)(2,1)} %copy_select_fusion), calls=%async_computation.1 | async-start | bytes 20971520 | tf_op jit(solution)/shard_map/all_to_all | solution.py:51
  278.7 8.5 %copy-start = (bf16[4,4,320,768]{3,2,0,1:T(8,128)(2,1)S(1)}, bf16[4,4,320,768]{3,2,0,1:T(8,128)(2,1)}, u32[]{:S(2)}) copy-start(bf16[4,4,320,768]{3,2,0,1:T(8,128)(2,1)} %all-gather.2.cloned.1.call-done) | copy-start | bytes 23592964
  278.7 16.5 %slice-start = ((s8[10485760]{0:T(1024)(128)(4,1)}), s8[4194304]{0:T(1024)(128)(4,1)S(1)}, s32[]{:S(2)}) async-start(s8[10485760]{0:T(1024)(128)(4,1)} %bitcast.75), calls=%async_computation.5 | async-start | bytes 8388608
  283.9 46.0 %collective-permute-start.2 = (bf16[4,320,768]{2,1,0:T(8,128)(2,1)}, bf16[4,320,768]{2,1,0:T(8,128)(2,1)}, u32[]{:S(2)}, u32[]{:S(2)}) collective-permute-start(bf16[4,320,768]{2,1,0:T(8,128)(2,1)} %get-tuple-element.30), channel_id=1, source_target_pairs={{0,24},{8,0},{16,8},{24,16},{1,25},{9,1},{17,9},{25,17},{2,26},{10... | collective-permute-start | bytes 5898248 | tf_op jit(solution)/shard_map/ppermute | solution.py:71
  284.2 129.6 %collective-permute-start.1 = (bf16[4,320,768]{2,1,0:T(8,128)(2,1)}, bf16[4,320,768]{2,1,0:T(8,128)(2,1)}, u32[]{:S(2)}, u32[]{:S(2)}) collective-permute-start(bf16[4,320,768]{2,1,0:T(8,128)(2,1)} %get-tuple-element.31), channel_id=1, source_target_pairs={{0,16},{8,24},{16,0},{24,8},{1,17},{9,25},{17,1},{25,9},{2,18},{10... | collective-permute-start | bytes 5898248 | tf_op jit(solution)/shard_map/ppermute | solution.py:71
  284.2 129.6 %collective-permute-start = (bf16[4,320,768]{2,1,0:T(8,128)(2,1)S(1)}, bf16[4,320,768]{2,1,0:T(8,128)(2,1)}, u32[]{:S(2)}, u32[]{:S(2)}) collective-permute-start(bf16[4,320,768]{2,1,0:T(8,128)(2,1)S(1)} %get-tuple-element.29), channel_id=1, source_target_pairs={{0,8},{8,16},{16,24},{24,0},{1,9},{9,17},{17,25},{25,1},{2,10},{10... | collective-permute-start | bytes 5898248 | tf_op jit(solution)/shard_map/ppermute | solution.py:71
  287.2 8.0 %slice-start.1 = ((s8[10485760]{0:T(1024)(128)(4,1)}), s8[4194304]{0:T(1024)(128)(4,1)S(1)}, s32[]{:S(2)}) async-start(s8[10485760]{0:T(1024)(128)(4,1)} %bitcast.75), calls=%async_computation.6 | async-start | bytes 8388608
  287.2 8.0 %slice-start.2 = ((s8[10485760]{0:T(1024)(128)(4,1)}), s8[2097152]{0:T(1024)(128)(4,1)S(1)}, s32[]{:S(2)}) async-start(s8[10485760]{0:T(1024)(128)(4,1)} %bitcast.75), calls=%async_computation.7 | async-start | bytes 4194304
  485.7 14.0 %all-to-all-start.3 = ((f32[4,4,80]{2,0,1:T(4,128)}), f32[4,4,80]{2,0,1:T(4,128)S(1)}, u32[]{:S(2)}, u32[]{:S(2)}) async-start(f32[4,4,80]{2,0,1:T(4,128)} %copy.72), calls=%async_computation.3 | async-start | bytes 16384 | tf_op jit(solution)/shard_map/all_to_all | solution.py:78
Sparse Core Ops, SparseCore 0:
  19.0 157.8 all-gather.1

commit v3 on v2

--- a/solution.py
+++ b/solution.py
@@ -20,33 +20,32 @@
     all_routes = all_meta[:, :top_count].astype(jnp.int32)
     all_gates = all_meta[:, top_count:].astype(gates.dtype)
     columns = lax.all_to_all(grad_out, "dp", split_axis=1, concat_axis=0, tiled=True)
-    pair_routes = all_routes.reshape(groups, token_count * top_count)
+    pair_count = token_count * top_count
+    pair_routes = all_routes.reshape(groups, pair_count)
     expert_ids = jnp.arange(experts, dtype=jnp.int32)
-    onehot = (pair_routes[:, :, None] == expert_ids[None, None, :]).astype(jnp.int32)
-    before = jnp.cumsum(onehot, axis=1) - onehot
-    slot_ids = jnp.sum(before * onehot, axis=2)
-    group_ids = jnp.arange(groups, dtype=jnp.int32)[:, None]
-    position = ((group_ids * experts + pair_routes) * capacity + slot_ids).reshape(-1)
-    source_rows = (
-        group_ids * token_count
-        + jnp.arange(token_count * top_count, dtype=jnp.int32)[None, :] // top_count
-    ).reshape(-1)
-    row_table = (
-        jnp.zeros((groups * experts * capacity,), jnp.int32).at[position].set(source_rows + 1)
+    onehot = (pair_routes[:, :, None] == expert_ids[None, None, :]).astype(jnp.bfloat16)
+    pair_ids = jnp.arange(pair_count, dtype=jnp.int32)
+    earlier = (pair_ids[:, None] > pair_ids[None, :]).astype(jnp.bfloat16)
+    before = jnp.einsum("jk,gke->gje", earlier, onehot, preferred_element_type=jnp.float32)
+    slot_ids = jnp.sum(before * onehot.astype(jnp.float32), axis=2).astype(jnp.int32)
+    rows = exp_dev * senders * capacity
+    position = (pair_routes % exp_dev * senders + pair_routes // exp_dev) * capacity + slot_ids
+    position = position.reshape(groups, token_count, top_count)
+    row_ids = jnp.arange(rows, dtype=jnp.int32)
+    select = (position[..., None] == row_ids).astype(jnp.bfloat16)
+    gate_rows = all_gates.reshape(groups, token_count, top_count).astype(jnp.float32)
+    gate_table = jnp.einsum("gtk,gtkr->gr", gate_rows, select.astype(jnp.float32))
+    token_select = jnp.sum(select, axis=2)
+    picked = jnp.einsum(
+        "gtr,gtd->grd",
+        token_select,
+        columns.reshape(groups, token_count, quarter),
+        preferred_element_type=jnp.float32,
+    ).astype(columns.dtype)
+    picked = picked.reshape(groups, exp_dev, senders, capacity, quarter).transpose(1, 0, 2, 3, 4)
+    gate_table = (
+        gate_table.reshape(groups, exp_dev, senders, capacity).transpose(1, 0, 2, 3).astype(gates.dtype)
     )
-    gate_table = (
-        jnp.zeros((groups * experts * capacity,), gates.dtype)
-        .at[position]
-        .set(all_gates.reshape(-1))
-    )
-    row_table = (
-        row_table.reshape(groups, senders, exp_dev, capacity).transpose(2, 0, 1, 3).reshape(-1)
-    )
-    gate_table = gate_table.reshape(groups, senders, exp_dev, capacity).transpose(2, 0, 1, 3)
-    filled = row_table > 0
-    safe_rows = jnp.maximum(row_table - 1, 0)
-    picked = jnp.where(filled[:, None], columns[safe_rows], jnp.zeros((1, quarter), columns.dtype))
-    picked = picked.reshape(exp_dev, groups, senders, capacity, quarter)
     received, got_gates = (
         lax.all_to_all(picked, "expert", split_axis=2, concat_axis=2, tiled=True),
         lax.all_to_all(gate_table, "expert", split_axis=2, concat_axis=2, tiled=True),
@@ -76,11 +75,8 @@
     slot_dots = lax.dynamic_index_in_dim(slot_dots, me, 0, keepdims=False)
     slot_dots = slot_dots.reshape(exp_dev, senders, capacity)
     returned = lax.all_to_all(slot_dots, "expert", split_axis=1, concat_axis=1, tiled=True)
-    own_slots = lax.dynamic_slice_in_dim(slot_ids, lax.axis_index("dp"), 1, 0).reshape(
-        token_count, top_count
-    )
-    lookup = (routes % exp_dev * senders + routes // exp_dev) * capacity + own_slots
-    gate_grad = returned.reshape(-1)[lookup]
+    own_select = lax.dynamic_index_in_dim(select, me, 0, keepdims=False).astype(jnp.float32)
+    gate_grad = jnp.sum(own_select * returned.reshape(1, 1, rows), axis=2)
     return (weight_grad, hidden_grad, gate_grad)
 
 

time: 522 us -> 485 us (0.929)
  local copies, waits for them, and re-layouts: 95.1 us -> 32.1 us
  waiting for transfers between devices: 219 us -> 240 us
  other arithmetic: 44.1 us -> 30.2 us
  matrix products: 31.1 us -> 43 us
  starting transfers between devices: 34.1 us -> 44.3 us
    scatter x2 -> x0, local copies, waits for them, and re-layouts: 44.1 us -> none  [the longest x1 28.6 us: body(): gate_table = jnp.zeros((groups * experts * capacity,), gates.dtype).at[po...]
    gather x3 -> x0, local copies, waits for them, and re-layouts: 28.8 us -> none  [the longest x1 22.6 us: body(): columns[safe_rows]]
    all_to_all x1, waiting for transfers between devices: 0.01 us -> 21.9 us  [body(): lax.all_to_all(grad_out, 'dp', split_axis=1, concat_axis=0, tiled=True)]
    another operation x3 -> x0, other arithmetic: 18.2 us -> none
    dot_general x0 -> x3, matrix products: none -> 11.8 us  [the longest x1 5.63 us: body(): jnp.einsum('gtr,gtd->grd', token_select, columns.reshape(groups, token_co...]
    all_to_all x1, starting transfers between devices: 7.47 us -> 17.7 us  [body(): lax.all_to_all(gate_table, 'expert', split_axis=2, concat_axis=2, tiled=T...]
    select_n x4 -> x0, other arithmetic: 10.2 us -> none  [the longest x1 10.1 us: body(): jnp.where(filled[:, None], columns[safe_rows], jnp.zeros((1, quarter), co...]
    reshape x5 -> x3, local copies, waits for them, and re-layouts: 0.58 us -> 10.3 us  [the longest x1 10.1 us: body(): picked.reshape(groups, exp_dev, senders, capacity, quarter)]
  transfers between devices with their start and end apart: 8 -> 8, of which waited for: 4 -> 4; matrix products, arithmetic and copies ran while one was open for 26% -> 15% of each run, Pallas kernels for 0% -> 0%
where the time goes in v3:
time: 485 us; the launch traced here: 479 us
  waiting for transfers between devices  240 us (49%)
  blocking collectives  75.2 us (16%)
  starting transfers between devices  44.3 us (9%)
  matrix products  43 us (9%)
  local copies, waits for them, and re-layouts  32.1 us (7%)
  other arithmetic  30.2 us (6%)
  between operations  14.2 us (3%)
    all_to_all x1, waiting for transfers between devices, body(): lax.all_to_all(picked, 'expert', split_axis=2, concat_axis=2, tiled=True)  114 us
    ppermute x3, waiting for transfers between devices, body(): lax.ppermute(chunk, 'dp', pairs).astype(jnp.float32)  104 us
    psum x1, blocking collectives, body(): slot_dots = lax.psum(dot_part, ('dp', 'etp'))  65 us
    all_to_all x1, waiting for transfers between devices, body(): lax.all_to_all(grad_out, 'dp', split_axis=1, concat_axis=0, tiled=True)  21.9 us
    all_to_all x1, starting transfers between devices, body(): lax.all_to_all(gate_table, 'expert', split_axis=2, concat_axis=2, tiled=T...  17.7 us
    dot_general x1, matrix products, body(): jnp.einsum('enrd,efd->nerf', slot_rows, down_weight, preferred_element_ty...  17.3 us
    dot_general x1, matrix products, body(): jnp.einsum('nerf,enrd->efd', scaled, slot_rows, preferred_element_type=jn...  13.8 us
    all_to_all x1, starting transfers between devices, body(): lax.all_to_all(slot_dots, 'expert', split_axis=1, concat_axis=1, tiled=True)  12.5 us
  transfers between devices with their start and end apart: 8, of which 4 were waited for; matrix products, arithmetic and copies ran while one was open for 15% of the time, Pallas kernels for 0%

profile of v3, /device:TPU:29, one launch (start us, length us, event | category | flops | bytes accessed | tf_op | source)
XLA Modules:
  0.0 478.8 jit_solution(11054668556376574342)
XLA Ops:
  8.6 10.2 %all_gather.6 = f32[512,16]{0,1:T(8,128)S(1)} all-gather(f32[128,16]{0,1:T(8,128)S(1)} %pad_maximum_fusion), channel_id=1, replica_groups=mesh['dp'=4,'expert'=4,'etp'=2] {'dp'}, dimensions={0}, use_global_device_ids=true | all-gather | bytes 40960 | tf_op jit(solution)/shard_map/all_gather | solution.py:17
  18.8 1.6 copy.39
  21.8 4.5 all-to-all-start
  27.9 5.6 %fusion = bf16[4,1,1280,1]{2,1,3,0:T(2,128)(2,1)S(1)} fusion(bf16[4,128,8,1]{2,3,1,0:T(2,128)(2,1)S(1)} %copy.51, s32[4,128,8]{2,1,0:T(8,128)S(1)} %fusion.33), kind=kOutput, calls=%fused_computation.1 | convolution fusion | flops 15728640 | bytes 34816 | tf_op jit(solution)/shard_map/gtk,gtkr->gr/dot_general | solution.py:37
  34.2 6.3 %fusion.18 = bf16[4,128,1280]{2,1,0:T(8,128)(2,1)S(1)} fusion(s32[4,128,8]{2,1,0:T(8,128)S(1)} %fusion.33), kind=kLoop, calls=%fused_computation.25 | loop fusion | flops 15073280 | bytes 1327104 | tf_op jit(solution)/shard_map/reduce_sum | solution.py:38
  40.5 21.9 %all-to-all-done = bf16[128,4,1024]{2,0,1:T(8,128)(2,1)S(1)} async-done(((bf16[128,4,1024]{2,0,1:T(8,128)(2,1)}), bf16[128,4,1024]{2,0,1:T(8,128)(2,1)S(1)}, u32[]{:S(2)}, u32[]{:S(2)}) %all-to-all-start) | async-done | bytes 1048608 | tf_op jit(solution)/shard_map/all_to_all | solution.py:22
  62.5 17.7 %all-to-all-start.2 = ((bf16[4,4,4,80]{3,0,1,2:T(4,128)(2,1)}), bf16[4,4,4,80]{3,0,1,2:T(4,128)(2,1)S(1)}, u32[]{:S(2)}, u32[]{:S(2)}) async-start(bf16[4,4,4,80]{3,0,1,2:T(4,128)(2,1)} %copy.44), calls=%async_computation.2 | async-start | bytes 32768 | tf_op jit(solution)/shard_map/all_to_all | solution.py:51
  80.2 5.6 %convolution_convert_fusion = bf16[4,1280,1024]{2,1,0:T(8,128)(2,1)} fusion(bf16[4,128,1280]{2,1,0:T(8,128)(2,1)S(1)} %fusion.18, bf16[128,4,1024]{2,0,1:T(8,128)(2,1)S(1)} %all-to-all-done), kind=kOutput, calls=%fused_computation.8 | convolution fusion | flops 1347420160 | bytes 12845056 | tf_op jit(solution)/shard_map/gtr,gtd->grd/dot_general | solution.py:39
  85.8 10.1 %copy.58 = bf16[4,4,4,80,1024]{4,3,1,0,2:T(8,128)(2,1)} copy(bf16[4,4,4,80,1024]{4,3,2,1,0:T(8,128)(2,1)} %bitcast.74) | data formatting | bytes 20971520 | tf_op jit(solution)/shard_map/reshape | solution.py:45
  95.9 6.2 %all-to-all-start.1 = ((bf16[4,4,4,80,1024]{4,3,0,1,2:T(8,128)(2,1)}), bf16[4,4,4,80,1024]{4,3,0,1,2:T(8,128)(2,1)}, u32[]{:S(2)}, u32[]{:S(2)}) async-start(bf16[4,4,4,80,1024]{4,3,0,1,2:T(8,128)(2,1)} %bitcast.75), calls=%async_computation.1 | async-start | bytes 20971520 | tf_op jit(solution)/shard_map/all_to_all | solution.py:50
  102.3 113.6 %all-to-all-done.1 = bf16[4,4,4,80,1024]{4,3,0,1,2:T(8,128)(2,1)} async-done(((bf16[4,4,4,80,1024]{4,3,0,1,2:T(8,128)(2,1)}), bf16[4,4,4,80,1024]{4,3,0,1,2:T(8,128)(2,1)}, u32[]{:S(2)}, u32[]{:S(2)}) %all-to-all-start.1) | async-done | bytes 10485792 | tf_op jit(solution)/shard_map/all_to_all | solution.py:50
  215.9 10.2 %copy.43 = bf16[4,4,4,80,1024]{4,3,2,1,0:T(8,128)(2,1)} copy(bf16[4,4,4,80,1024]{4,3,0,1,2:T(8,128)(2,1)} %all-to-all-done.1) | data formatting | bytes 20971520 | tf_op jit(solution)/shard_map/all_to_all | solution.py:50
  226.1 17.3 %bitcast_convert_fusion = (bf16[4,4,320,768]{3,2,0,1:T(8,128)(2,1)}, f32[4,4,320,768]{3,2,1,0:T(8,128)}) fusion(bf16[4,4,320,1024]{3,2,1,0:T(8,128)(2,1)} %bitcast.76, bf16[4,768,1024]{2,1,0:T(8,128)(2,1)} %param.9), kind=kOutput, calls=%fused_computation.7 | convolution fusion | flops 8056995840 | bytes 40370176 | tf_op jit(solution)/shard_map/enrd,efd->nerf/dot_general | solution.py:62
  243.4 6.0 %dynamic-slice_bitcast_fusion.2 = (bf16[4,320,768]{2,1,0:T(8,128)(2,1)}, bf16[4,320,768]{2,1,0:T(8,128)(2,1)}, bf16[4,320,768]{2,1,0:T(8,128)(2,1)}) fusion(bf16[4,4,320,768]{3,2,0,1:T(8,128)(2,1)} %get-tuple-element.23, s32[]{:T(128)S(6)} %select_n.58, s32[]{:T(128)S(6)} %select_n.62, s32[]{:T(128)S(6)} %select_n.60), kind=kLoop, calls=%fused_computation.29 | loop fusion | bytes 11796492 | tf_op jit(solution)/shard_map/jit(dynamic_index_in_dim)/squeeze | solution.py:68
  250.9 1.8 collective-permute-start
  252.7 8.0 %fusion.2 = f32[4,4,320]{2,0,1:T(4,128)S(1)} fusion(bf16[4,4,320,768]{3,2,0,1:T(8,128)(2,1)S(1)} %copy-done, f32[4,4,320,768]{3,2,1,0:T(8,128)} %get-tuple-element.24), kind=kLoop, calls=%fused_computation.5 | loop fusion | flops 11791360 | bytes 23613440 | tf_op jit(solution)/shard_map/reduce_sum | solution.py:63
  260.7 13.8 %bitcast_convert_fusion.1 = bf16[4,768,1024]{2,1,0:T(8,128)(2,1)} fusion(bf16[4,4,320,1024]{3,2,1,0:T(8,128)(2,1)S(1)} %bitcast.79, bf16[4,4,320,768]{3,2,0,1:T(8,128)(2,1)} %all-gather.2.cloned.1.call-done, f32[4,4,320]{2,0,1:T(4,128)S(1)} %convert_bitcast_fusion), kind=kOutput, calls=%fused_computation.9 | convolution fusion | flops 8068005888 | bytes 24662016 | tf_op jit(solution)/shard_map/nerf,enrd->efd/dot_general | solution.py:60
  274.5 20.9 %collective-permute-done.2 = bf16[4,320,768]{2,1,0:T(8,128)(2,1)} collective-permute-done((bf16[4,320,768]{2,1,0:T(8,128)(2,1)}, bf16[4,320,768]{2,1,0:T(8,128)(2,1)}, u32[]{:S(2)}, u32[]{:S(2)}) %collective-permute-start.2) | collective-permute-done | bytes 1966112 | tf_op jit(solution)/shard_map/ppermute | solution.py:70
  295.4 83.3 %collective-permute-done.1 = bf16[4,320,768]{2,1,0:T(8,128)(2,1)} collective-permute-done((bf16[4,320,768]{2,1,0:T(8,128)(2,1)}, bf16[4,320,768]{2,1,0:T(8,128)(2,1)}, u32[]{:S(2)}, u32[]{:S(2)}) %collective-permute-start.1) | collective-permute-done | bytes 1966112 | tf_op jit(solution)/shard_map/ppermute | solution.py:70
  378.8 6.1 %fusion.19 = bf16[1,4,320,768]{3,2,1,0:T(8,128)(2,1)} fusion(f32[4,320]{1,0:T(4,128)S(1)} %bitcast.85, bf16[4,320,768]{2,1,0:T(8,128)(2,1)} %collective-permute-done.2, bf16[4,320,768]{2,1,0:T(8,128)(2,1)} %collective-permute-done.1, bf16[4,320,768]{2,1,0:T(8,128)(2,1)} %collective-permute-done, f32[4,4,320,768]{3,2,1,0:T(8,128)} %get-tuple-element.24, ...), kind=kLoop, calls=%fused_computation.26 | loop fusion | flops 7864320 | bytes 11801604 | tf_op jit(solution)/shard_map/broadcast_in_dim | solution.py:72
  384.9 65.0 %psum.7 = f32[4,4,320]{2,0,1:T(4,128)S(1)} all-reduce(f32[4,4,320]{2,0,1:T(4,128)S(1)} %fusion.2), channel_id=1, replica_groups=mesh['dp'=4,'expert'=4,'etp'=2] {'dp','etp'}, use_global_device_ids=true, to_apply=%region_3.4 | all-reduce | flops 5120 | bytes 40960 | tf_op jit(solution)/shard_map/psum | solution.py:74
  450.6 12.5 %all-to-all-start.3 = ((f32[4,4,80]{2,0,1:T(4,128)}), f32[4,4,80]{2,0,1:T(4,128)S(1)}, u32[]{:S(2)}, u32[]{:S(2)}) async-start(f32[4,4,80]{2,0,1:T(4,128)} %copy.46), calls=%async_computation.3 | async-start | bytes 16384 | tf_op jit(solution)/shard_map/all_to_all | solution.py:77
  463.1 5.7 %fusion.1 = bf16[4,128,8,1280]{3,2,1,0:T(8,128)(2,1)} fusion(s32[4,128,8]{2,1,0:T(8,128)S(1)} %fusion.33), kind=kLoop, calls=%fused_computation.2 | loop fusion | flops 10485760 | bytes 10502144 | tf_op jit(solution)/shard_map/convert_element_type | solution.py:35
  468.9 2.3 fusion.10
  (44 shorter events, 8.0 us)
Async XLA Ops:
  7.2 218.9 %all-gather.2.cloned.1.call-start = ((), (), s32[]{:S(2)}) async-start(), calls=%async_computation.4 | async-start | bytes 9830400 | tf_op jit(solution)/shard_map/all_gather | solution.py:19
  21.8 40.7 %all-to-all-start = ((bf16[128,4,1024]{2,0,1:T(8,128)(2,1)}), bf16[128,4,1024]{2,0,1:T(8,128)(2,1)S(1)}, u32[]{:S(2)}, u32[]{:S(2)}) async-start(bf16[128,4,1024]{2,0,1:T(8,128)(2,1)} %copy.40), calls=%async_computation | async-start | bytes 2097152 | tf_op jit(solution)/shard_map/all_to_all | solution.py:22
  62.5 33.5 %all-to-all-start.2 = ((bf16[4,4,4,80]{3,0,1,2:T(4,128)(2,1)}), bf16[4,4,4,80]{3,0,1,2:T(4,128)(2,1)S(1)}, u32[]{:S(2)}, u32[]{:S(2)}) async-start(bf16[4,4,4,80]{3,0,1,2:T(4,128)(2,1)} %copy.44), calls=%async_computation.2 | async-start | bytes 32768 | tf_op jit(solution)/shard_map/all_to_all | solution.py:51
  95.9 120.0 %all-to-all-start.1 = ((bf16[4,4,4,80,1024]{4,3,0,1,2:T(8,128)(2,1)}), bf16[4,4,4,80,1024]{4,3,0,1,2:T(8,128)(2,1)}, u32[]{:S(2)}, u32[]{:S(2)}) async-start(bf16[4,4,4,80,1024]{4,3,0,1,2:T(8,128)(2,1)} %bitcast.75), calls=%async_computation.1 | async-start | bytes 20971520 | tf_op jit(solution)/shard_map/all_to_all | solution.py:50
  243.4 9.3 %copy-start = (bf16[4,4,320,768]{3,2,0,1:T(8,128)(2,1)S(1)}, bf16[4,4,320,768]{3,2,0,1:T(8,128)(2,1)}, u32[]{:S(2)}) copy-start(bf16[4,4,320,768]{3,2,0,1:T(8,128)(2,1)} %all-gather.2.cloned.1.call-done) | copy-start | bytes 23592964
  243.4 17.3 %slice-start = ((s8[10485760]{0:T(1024)(128)(4,1)}), s8[4194304]{0:T(1024)(128)(4,1)S(1)}, s32[]{:S(2)}) async-start(s8[10485760]{0:T(1024)(128)(4,1)} %bitcast.77), calls=%async_computation.5 | async-start | bytes 8388608
  249.4 46.0 %collective-permute-start.2 = (bf16[4,320,768]{2,1,0:T(8,128)(2,1)}, bf16[4,320,768]{2,1,0:T(8,128)(2,1)}, u32[]{:S(2)}, u32[]{:S(2)}) collective-permute-start(bf16[4,320,768]{2,1,0:T(8,128)(2,1)} %get-tuple-element.21), channel_id=1, source_target_pairs={{0,24},{8,0},{16,8},{24,16},{1,25},{9,1},{17,9},{25,17},{2,26},{10... | collective-permute-start | bytes 5898248 | tf_op jit(solution)/shard_map/ppermute | solution.py:70
  249.4 129.4 %collective-permute-start.1 = (bf16[4,320,768]{2,1,0:T(8,128)(2,1)}, bf16[4,320,768]{2,1,0:T(8,128)(2,1)}, u32[]{:S(2)}, u32[]{:S(2)}) collective-permute-start(bf16[4,320,768]{2,1,0:T(8,128)(2,1)} %get-tuple-element.22), channel_id=1, source_target_pairs={{0,16},{8,24},{16,0},{24,8},{1,17},{9,25},{17,1},{25,9},{2,18},{10... | collective-permute-start | bytes 5898248 | tf_op jit(solution)/shard_map/ppermute | solution.py:70
  250.9 127.9 %collective-permute-start = (bf16[4,320,768]{2,1,0:T(8,128)(2,1)}, bf16[4,320,768]{2,1,0:T(8,128)(2,1)}, u32[]{:S(2)}, u32[]{:S(2)}) collective-permute-start(bf16[4,320,768]{2,1,0:T(8,128)(2,1)} %get-tuple-element.20), channel_id=1, source_target_pairs={{0,8},{8,16},{16,24},{24,0},{1,9},{9,17},{17,25},{25,1},{2,10},{10... | collective-permute-start | bytes 5898248 | tf_op jit(solution)/shard_map/ppermute | solution.py:70
  252.7 8.0 %slice-start.1 = ((s8[10485760]{0:T(1024)(128)(4,1)}), s8[4194304]{0:T(1024)(128)(4,1)S(1)}, s32[]{:S(2)}) async-start(s8[10485760]{0:T(1024)(128)(4,1)} %bitcast.77), calls=%async_computation.6 | async-start | bytes 8388608
  252.7 8.0 %slice-start.2 = ((s8[10485760]{0:T(1024)(128)(4,1)}), s8[2097152]{0:T(1024)(128)(4,1)S(1)}, s32[]{:S(2)}) async-start(s8[10485760]{0:T(1024)(128)(4,1)} %bitcast.77), calls=%async_computation.7 | async-start | bytes 4194304
  450.6 18.3 %all-to-all-start.3 = ((f32[4,4,80]{2,0,1:T(4,128)}), f32[4,4,80]{2,0,1:T(4,128)S(1)}, u32[]{:S(2)}, u32[]{:S(2)}) async-start(f32[4,4,80]{2,0,1:T(4,128)} %copy.46), calls=%async_computation.3 | async-start | bytes 16384 | tf_op jit(solution)/shard_map/all_to_all | solution.py:77
Sparse Core Ops, SparseCore 0:
  19.0 158.5 all-gather.1

commit v4 on v3

--- a/solution.py
+++ b/solution.py
@@ -15,11 +15,11 @@
     experts = exp_dev * senders
     meta = jnp.concatenate([routes.astype(jnp.float32), gates.astype(jnp.float32)], axis=1)
     all_meta = lax.all_gather(meta, "dp", axis=0, tiled=True)
-    hidden_saved, all_meta = lax.optimization_barrier((hidden_saved, all_meta))
+    columns = lax.all_to_all(grad_out, "dp", split_axis=1, concat_axis=0, tiled=True)
+    hidden_saved, all_meta, columns = lax.optimization_barrier((hidden_saved, all_meta, columns))
     hidden_all = lax.all_gather(hidden_saved, "dp", axis=0, tiled=True)
     all_routes = all_meta[:, :top_count].astype(jnp.int32)
     all_gates = all_meta[:, top_count:].astype(gates.dtype)
-    columns = lax.all_to_all(grad_out, "dp", split_axis=1, concat_axis=0, tiled=True)
     pair_count = token_count * top_count
     pair_routes = all_routes.reshape(groups, pair_count)
     expert_ids = jnp.arange(experts, dtype=jnp.int32)
@@ -46,31 +46,39 @@
     gate_table = (
         gate_table.reshape(groups, exp_dev, senders, capacity).transpose(1, 0, 2, 3).astype(gates.dtype)
     )
-    received, got_gates = (
-        lax.all_to_all(picked, "expert", split_axis=2, concat_axis=2, tiled=True),
-        lax.all_to_all(gate_table, "expert", split_axis=2, concat_axis=2, tiled=True),
-    )
-    received = received.reshape(exp_dev, groups, slot_rows_all, quarter)
-    hidden_all, received = lax.optimization_barrier((hidden_all, received))
+    got_gates = lax.all_to_all(gate_table, "expert", split_axis=2, concat_axis=2, tiled=True)
     got_gates = got_gates.reshape(exp_dev, groups, slot_rows_all)
-    slot_rows = received
     slot_gates = got_gates.astype(jnp.float32)
-    hidden_rows = hidden_all.astype(jnp.float32)
-    scaled = (jnp.moveaxis(slot_gates, 0, 1)[..., None] * hidden_rows).astype(jnp.bfloat16)
-    weight_sum = jnp.einsum("nerf,enrd->efd", scaled, slot_rows, preferred_element_type=jnp.float32)
-    weight_grad = weight_sum.astype(jnp.bfloat16)
-    partial = jnp.einsum("enrd,efd->nerf", slot_rows, down_weight, preferred_element_type=jnp.float32)
-    dot_part = jnp.sum(hidden_rows * partial, axis=3)
     me = lax.axis_index("dp")
-    sent = partial.astype(jnp.bfloat16)
-    expert_grad = lax.dynamic_index_in_dim(partial, me, 0, keepdims=False)
-    for shift in range(1, groups):
-        chunk = lax.dynamic_index_in_dim(sent, (me + shift) % groups, 0, keepdims=False)
-        pairs = [(i, (i + shift) % groups) for i in range(groups)]
-        expert_grad = expert_grad + lax.ppermute(chunk, "dp", pairs).astype(jnp.float32)
     own_gates = lax.dynamic_index_in_dim(got_gates, me, 1, keepdims=False).astype(jnp.float32)
-    hidden_grad = (own_gates[..., None] * expert_grad).astype(jnp.bfloat16)[None]
-    expert_grad, dot_part, weight_grad = lax.optimization_barrier((expert_grad, dot_part, weight_grad))
+    chunks = 2 if exp_dev % 2 == 0 else 1
+    per = exp_dev // chunks
+    grads, dots, hidden_parts = [], [], []
+    for c in range(chunks):
+        local = slice(c * per, (c + 1) * per)
+        received = lax.all_to_all(picked[local], "expert", split_axis=2, concat_axis=2, tiled=True)
+        received = received.reshape(per, groups, slot_rows_all, quarter)
+        if c == chunks - 1:
+            hidden_all, received = lax.optimization_barrier((hidden_all, received))
+        partial = jnp.einsum(
+            "enrd,efd->nerf", received, down_weight[local], preferred_element_type=jnp.float32
+        )
+        sent = partial.astype(jnp.bfloat16)
+        expert_grad = lax.dynamic_index_in_dim(partial, me, 0, keepdims=False)
+        for shift in range(1, groups):
+            chunk = lax.dynamic_index_in_dim(sent, (me + shift) % groups, 0, keepdims=False)
+            pairs = [(i, (i + shift) % groups) for i in range(groups)]
+            expert_grad = expert_grad + lax.ppermute(chunk, "dp", pairs).astype(jnp.float32)
+        hidden_rows = hidden_all[:, local].astype(jnp.float32)
+        dots.append(jnp.sum(hidden_rows * partial, axis=3))
+        scaled = (jnp.moveaxis(slot_gates[local], 0, 1)[..., None] * hidden_rows).astype(jnp.bfloat16)
+        weight_sum = jnp.einsum("nerf,enrd->efd", scaled, received, preferred_element_type=jnp.float32)
+        grads.append(weight_sum.astype(jnp.bfloat16))
+        hidden_parts.append((own_gates[local][..., None] * expert_grad).astype(jnp.bfloat16))
+    weight_grad = jnp.concatenate(grads, axis=0)
+    dot_part = jnp.concatenate(dots, axis=1)
+    hidden_grad = jnp.concatenate(hidden_parts, axis=0)[None]
+    hidden_grad, dot_part, weight_grad = lax.optimization_barrier((hidden_grad, dot_part, weight_grad))
     slot_dots = lax.psum(dot_part, ("dp", "etp"))
     slot_dots = lax.dynamic_index_in_dim(slot_dots, me, 0, keepdims=False)
     slot_dots = slot_dots.reshape(exp_dev, senders, capacity)

time: 485 us -> 429 us (0.88)
  waiting for transfers between devices: 240 us -> 139 us
  blocking collectives: 75.2 us -> 116 us
  starting transfers between devices: 44.3 us -> 35 us
  local copies, waits for them, and re-layouts: 32.1 us -> 38 us
  matrix products: 43 us -> 48.7 us
    all_to_all x1, waiting for transfers between devices: 114 us -> 40.9 us  [body(): lax.all_to_all(picked[local], 'expert', split_axis=2, concat_axis=2, tile...]
    all_to_all x0 -> x1, blocking collectives: none -> 64 us  [body(): lax.all_to_all(picked[local], 'expert', split_axis=2, concat_axis=2, tile...]
    psum x1, blocking collectives: 65 us -> 25.3 us  [body(): slot_dots = lax.psum(dot_part, ('dp', 'etp'))]
    all_to_all x1, waiting for transfers between devices: 21.9 us -> 0.01 us  [body(): lax.all_to_all(grad_out, 'dp', split_axis=1, concat_axis=0, tiled=True)]
    all_gather x1, blocking collectives: 10.2 us -> 26.2 us  [body(): all_meta = lax.all_gather(meta, 'dp', axis=0, tiled=True)]
    all_to_all x1, starting transfers between devices: 17.7 us -> 6.81 us  [body(): lax.all_to_all(gate_table, 'expert', split_axis=2, concat_axis=2, tiled=T...]
    slice x0 -> x2, local copies, waits for them, and re-layouts: none -> 10.5 us  [the longest x1 10.5 us: body(): picked[local]]
    ppermute x3 -> x6, waiting for transfers between devices: 104 us -> 97.9 us  [body(): lax.ppermute(chunk, 'dp', pairs).astype(jnp.float32)]
  transfers between devices with their start and end apart: 8 -> 11, of which waited for: 4 -> 5; matrix products, arithmetic and copies ran while one was open for 15% -> 24% of each run, Pallas kernels for 0% -> 0%
where the time goes in v4:
time: 429 us; the launch traced here: 423 us
  waiting for transfers between devices  139 us (32%)
  blocking collectives  116 us (27%)
  matrix products  48.7 us (11%)
  local copies, waits for them, and re-layouts  38 us (9%)
  starting transfers between devices  35 us (8%)
  other arithmetic  32.1 us (7%)
  between operations  14.2 us (3%)
    ppermute x6, waiting for transfers between devices, body(): lax.ppermute(chunk, 'dp', pairs).astype(jnp.float32)  97.9 us
    all_to_all x1, blocking collectives, body(): lax.all_to_all(picked[local], 'expert', split_axis=2, concat_axis=2, tile...  64 us
    all_to_all x1, waiting for transfers between devices, body(): lax.all_to_all(picked[local], 'expert', split_axis=2, concat_axis=2, tile...  40.9 us
    all_gather x1, blocking collectives, body(): all_meta = lax.all_gather(meta, 'dp', axis=0, tiled=True)  26.2 us
    psum x1, blocking collectives, body(): slot_dots = lax.psum(dot_part, ('dp', 'etp'))  25.3 us
    dot_general x2, matrix products, body(): jnp.einsum('nerf,enrd->efd', scaled, received, preferred_element_type=jnp...  19.6 us
    dot_general x2, matrix products, body(): jnp.einsum('enrd,efd->nerf', received, down_weight[local], preferred_elem...  17.4 us
    all_to_all x1, starting transfers between devices, body(): lax.all_to_all(slot_dots, 'expert', split_axis=1, concat_axis=1, tiled=True)  11.8 us
  transfers between devices with their start and end apart: 11, of which 5 were waited for; matrix products, arithmetic and copies ran while one was open for 24% of the time, Pallas kernels for 0%

profile of v4, /device:TPU:29, one launch (start us, length us, event | category | flops | bytes accessed | tf_op | source)
XLA Modules:
  0.0 422.5 jit_solution(1807356731623169667)
XLA Ops:
  9.4 4.5 %all-to-all-start = ((bf16[128,4,1024]{0,2,1:T(8,128)(2,1)}), bf16[128,4,1024]{0,2,1:T(8,128)(2,1)S(1)}, u32[]{:S(2)}, u32[]{:S(2)}) async-start(bf16[128,4,1024]{0,2,1:T(8,128)(2,1)} %bitcast), calls=%async_computation | async-start | bytes 2097152 | tf_op jit(solution)/shard_map/all_to_all | solution.py:18
  15.3 26.2 %all_gather.6 = f32[512,16]{0,1:T(8,128)S(1)} all-gather(f32[128,16]{0,1:T(8,128)S(1)} %pad_maximum_fusion.2), channel_id=1, replica_groups=mesh['dp'=4,'expert'=4,'etp'=2] {'dp'}, dimensions={0}, use_global_device_ids=true | all-gather | bytes 40960 | tf_op jit(solution)/shard_map/all_gather | solution.py:17
  43.7 5.6 %fusion.1 = bf16[4,1,1280,1]{2,1,3,0:T(2,128)(2,1)S(1)} fusion(bf16[4,128,8,1]{2,3,1,0:T(2,128)(2,1)S(1)} %copy.60, s32[4,128,8]{2,1,0:T(8,128)S(1)} %fusion.50), kind=kOutput, calls=%fused_computation.2 | convolution fusion | flops 15728640 | bytes 34816 | tf_op jit(solution)/shard_map/gtk,gtkr->gr/dot_general | solution.py:37
  50.0 6.8 %all-to-all-start.1 = ((bf16[4,4,4,80]{3,0,1,2:T(4,128)(2,1)}), bf16[4,4,4,80]{3,0,1,2:T(4,128)(2,1)S(1)}, u32[]{:S(2)}, u32[]{:S(2)}) async-start(bf16[4,4,4,80]{3,0,1,2:T(4,128)(2,1)} %copy.50), calls=%async_computation.1 | async-start | bytes 32768 | tf_op jit(solution)/shard_map/all_to_all | solution.py:49
  56.9 6.3 %fusion.25 = bf16[4,128,1280]{2,1,0:T(8,128)(2,1)S(1)} fusion(s32[4,128,8]{2,1,0:T(8,128)S(1)} %fusion.50), kind=kLoop, calls=%fused_computation.36 | loop fusion | flops 15073280 | bytes 1327104 | tf_op jit(solution)/shard_map/reduce_sum | solution.py:38
  63.2 5.5 %convolution_convert_fusion = bf16[4,1280,1024]{2,1,0:T(8,128)(2,1)} fusion(bf16[4,128,1280]{2,1,0:T(8,128)(2,1)S(1)} %fusion.25, bf16[4,128,1024]{2,1,0:T(8,128)(2,1)S(1)} %copy.47), kind=kOutput, calls=%fused_computation.3 | convolution fusion | flops 1347420160 | bytes 12845056 | tf_op jit(solution)/shard_map/gtr,gtd->grd/dot_general | solution.py:39
  68.7 10.3 %copy.73 = bf16[4,4,4,80,1024]{4,3,1,0,2:T(8,128)(2,1)} copy(bf16[4,4,4,80,1024]{4,3,2,1,0:T(8,128)(2,1)} %bitcast.113) | data formatting | bytes 20971520 | tf_op jit(solution)/shard_map/reshape | solution.py:45
  79.0 10.5 %fusion.58 = (bf16[2,4,4,80,1024]{4,3,0,1,2:T(8,128)(2,1)}, bf16[2,4,4,80,1024]{4,3,0,1,2:T(8,128)(2,1)}) fusion(bf16[4,4,4,80,1024]{4,3,0,1,2:T(8,128)(2,1)} %bitcast.114), kind=kLoop, calls=%fused_computation.86 | loop fusion | bytes 20971520 | tf_op jit(solution)/shard_map/slice | solution.py:59
  89.5 64.0 %all_to_all.39 = bf16[2,4,4,80,1024]{4,3,0,1,2:T(8,128)(2,1)} all-to-all(bf16[2,4,4,80,1024]{4,3,0,1,2:T(8,128)(2,1)} %get-tuple-element.22), channel_id=1, replica_groups=mesh['dp'=4,'expert'=4,'etp'=2] {'expert'}, dimensions={2} | all-to-all | bytes 10485760 | tf_op jit(solution)/shard_map/all_to_all | solution.py:59
  153.6 6.9 %all-to-all-start.3 = ((bf16[2,4,4,80,1024]{4,3,0,1,2:T(8,128)(2,1)}), bf16[2,4,4,80,1024]{4,3,0,1,2:T(8,128)(2,1)}, u32[]{:S(2)}, u32[]{:S(2)}) async-start(bf16[2,4,4,80,1024]{4,3,0,1,2:T(8,128)(2,1)} %get-tuple-element.23), calls=%async_computation.3 | async-start | bytes 10485760 | tf_op jit(solution)/shard_map/all_to_all | solution.py:59
  163.6 10.2 %bitcast_convert_fusion.1 = (bf16[4,2,320,768]{3,2,0,1:T(8,128)(2,1)S(1)}, f32[2,4,320,768]{3,2,1,0:T(8,128)}) fusion(bf16[2,4,320,1024]{3,2,1,0:T(8,128)(2,1)S(1)} %bitcast.117, bf16[4,768,1024]{2,1,0:T(8,128)(2,1)} %param.9), kind=kOutput, calls=%fused_computation.15 | convolution fusion | flops 4028497920 | bytes 20185088 | tf_op jit(solution)/shard_map/enrd,efd->nerf/dot_general | solution.py:63
  177.1 40.9 %all-to-all-done.3 = bf16[2,4,4,80,1024]{4,3,0,1,2:T(8,128)(2,1)} async-done(((bf16[2,4,4,80,1024]{4,3,0,1,2:T(8,128)(2,1)}), bf16[2,4,4,80,1024]{4,3,0,1,2:T(8,128)(2,1)}, u32[]{:S(2)}, u32[]{:S(2)}) %all-to-all-start.3) | async-done | bytes 5242912 | tf_op jit(solution)/shard_map/all_to_all | solution.py:59
  217.9 5.8 %copy.56 = bf16[2,4,4,80,1024]{4,3,2,1,0:T(8,128)(2,1)} copy(bf16[2,4,4,80,1024]{4,3,0,1,2:T(8,128)(2,1)} %all-to-all-done.3) | data formatting | bytes 10485760 | tf_op jit(solution)/shard_map/all_to_all | solution.py:59
  226.1 42.4 %collective-permute-done.1 = bf16[2,320,768]{2,1,0:T(8,128)(2,1)} collective-permute-done((bf16[2,320,768]{2,1,0:T(8,128)(2,1)S(1)}, bf16[2,320,768]{2,1,0:T(8,128)(2,1)}, u32[]{:S(2)}, u32[]{:S(2)}) %collective-permute-start.1) | collective-permute-done | bytes 983072 | tf_op jit(solution)/shard_map/ppermute | solution.py:71
  270.9 7.2 %bitcast_convert_fusion = (bf16[4,2,320,768]{3,2,0,1:T(8,128)(2,1)S(1)}, f32[2,4,320,768]{3,2,1,0:T(8,128)S(1)}) fusion(bf16[2,4,320,1024]{3,2,1,0:T(8,128)(2,1)} %bitcast.119, bf16[4,768,1024]{2,1,0:T(8,128)(2,1)} %param.9), kind=kOutput, calls=%fused_computation.14 | convolution fusion | flops 4028497920 | bytes 20185088 | tf_op jit(solution)/shard_map/enrd,efd->nerf/dot_general | solution.py:63
  282.6 9.9 %bitcast_convert_fusion.2 = bf16[2,768,1024]{2,1,0:T(8,128)(2,1)} fusion(bf16[2,4,320,1024]{3,2,1,0:T(8,128)(2,1)} %bitcast.120, f32[4,2,320]{2,0,1:T(4,128)S(1)} %get-tuple-element.31, bf16[4,4,320,768]{3,2,0,1:T(8,128)(2,1)} %all-gather.2.cloned.1.call-done), kind=kOutput, calls=%fused_computation.17 | convolution fusion | flops 4034002944 | bytes 12331008 | tf_op jit(solution)/shard_map/nerf,enrd->efd/dot_general | solution.py:75
  292.5 4.2 fusion.3
  296.8 9.7 %bitcast_convert_fusion.3 = bf16[2,768,1024]{2,1,0:T(8,128)(2,1)} fusion(bf16[2,4,320,1024]{3,2,1,0:T(8,128)(2,1)} %bitcast.118, f32[4,2,320]{2,0,1:T(4,128)S(1)} %get-tuple-element.30, bf16[4,4,320,768]{3,2,0,1:T(8,128)(2,1)} %all-gather.2.cloned.1.call-done), kind=kOutput, calls=%fused_computation.18 | convolution fusion | flops 4034002944 | bytes 12331008 | tf_op jit(solution)/shard_map/nerf,enrd->efd/dot_general | solution.py:75
  306.5 6.1 %pad_maximum_fusion = bf16[4,768,1024]{2,1,0:T(8,128)(2,1)} fusion(bf16[2,768,1024]{2,1,0:T(8,128)(2,1)} %bitcast_convert_fusion.2, bf16[2,768,1024]{2,1,0:T(8,128)(2,1)} %bitcast_convert_fusion.3), kind=kLoop, calls=%fused_computation.16 | loop fusion | flops 3145728 | bytes 12582912 | tf_op jit(solution)/shard_map/concatenate | solution.py:78
  312.5 13.0 %collective-permute-done.5 = bf16[2,320,768]{2,1,0:T(8,128)(2,1)} collective-permute-done((bf16[2,320,768]{2,1,0:T(8,128)(2,1)S(1)}, bf16[2,320,768]{2,1,0:T(8,128)(2,1)}, u32[]{:S(2)}, u32[]{:S(2)}) %collective-permute-start.5) | collective-permute-done | bytes 983072 | tf_op jit(solution)/shard_map/ppermute | solution.py:71
  325.5 40.1 %collective-permute-done.4 = bf16[2,320,768]{2,1,0:T(8,128)(2,1)} collective-permute-done((bf16[2,320,768]{2,1,0:T(8,128)(2,1)S(1)}, bf16[2,320,768]{2,1,0:T(8,128)(2,1)}, u32[]{:S(2)}, u32[]{:S(2)}) %collective-permute-start.4) | collective-permute-done | bytes 983072 | tf_op jit(solution)/shard_map/ppermute | solution.py:71
  369.1 25.3 %psum.7 = f32[4,4,320]{2,0,1:T(4,128)S(1)} all-reduce(f32[4,4,320]{2,0,1:T(4,128)S(1)} %pad_maximum_fusion.1), channel_id=1, replica_groups=mesh['dp'=4,'expert'=4,'etp'=2] {'dp','etp'}, use_global_device_ids=true, to_apply=%region_4.5 | all-reduce | flops 5120 | bytes 40960 | tf_op jit(solution)/shard_map/psum | solution.py:82
  395.1 11.8 %all-to-all-start.4 = ((f32[4,4,80]{2,0,1:T(4,128)}), f32[4,4,80]{2,0,1:T(4,128)S(1)}, u32[]{:S(2)}, u32[]{:S(2)}) async-start(f32[4,4,80]{2,0,1:T(4,128)} %copy.57), calls=%async_computation.4 | async-start | bytes 16384 | tf_op jit(solution)/shard_map/all_to_all | solution.py:85
  406.9 5.7 %fusion = bf16[4,128,8,1280]{3,2,1,0:T(8,128)(2,1)} fusion(s32[4,128,8]{2,1,0:T(8,128)S(1)} %fusion.50), kind=kLoop, calls=%fused_computation.1 | loop fusion | flops 10485760 | bytes 10502144 | tf_op jit(solution)/shard_map/convert_element_type | solution.py:35
  (60 shorter events, 29.2 us)
Async XLA Ops:
  9.4 32.2 %all-to-all-start = ((bf16[128,4,1024]{0,2,1:T(8,128)(2,1)}), bf16[128,4,1024]{0,2,1:T(8,128)(2,1)S(1)}, u32[]{:S(2)}, u32[]{:S(2)}) async-start(bf16[128,4,1024]{0,2,1:T(8,128)(2,1)} %bitcast), calls=%async_computation | async-start | bytes 2097152 | tf_op jit(solution)/shard_map/all_to_all | solution.py:18
  14.0 256.9 %all-gather.2.cloned.1.call-start = ((), (), s32[]{:S(2)}) async-start(), calls=%async_computation.5 | async-start | bytes 9830400 | tf_op jit(solution)/shard_map/all_gather | solution.py:20
  50.0 39.5 %all-to-all-start.1 = ((bf16[4,4,4,80]{3,0,1,2:T(4,128)(2,1)}), bf16[4,4,4,80]{3,0,1,2:T(4,128)(2,1)S(1)}, u32[]{:S(2)}, u32[]{:S(2)}) async-start(bf16[4,4,4,80]{3,0,1,2:T(4,128)(2,1)} %copy.50), calls=%async_computation.1 | async-start | bytes 32768 | tf_op jit(solution)/shard_map/all_to_all | solution.py:49
  153.6 64.4 %all-to-all-start.3 = ((bf16[2,4,4,80,1024]{4,3,0,1,2:T(8,128)(2,1)}), bf16[2,4,4,80,1024]{4,3,0,1,2:T(8,128)(2,1)}, u32[]{:S(2)}, u32[]{:S(2)}) async-start(bf16[2,4,4,80,1024]{4,3,0,1,2:T(8,128)(2,1)} %get-tuple-element.23), calls=%async_computation.3 | async-start | bytes 10485760 | tf_op jit(solution)/shard_map/all_to_all | solution.py:59
  163.6 10.2 %copy-start = (bf16[2,4,4,80,1024]{4,3,2,1,0:T(8,128)(2,1)}, bf16[2,4,4,80,1024]{4,3,2,1,0:T(8,128)(2,1)S(1)}, u32[]{:S(2)}) copy-start(bf16[2,4,4,80,1024]{4,3,2,1,0:T(8,128)(2,1)S(1)} %copy.54) | copy-start | bytes 15728644
  175.3 48.5 %collective-permute-start = (bf16[2,320,768]{2,1,0:T(8,128)(2,1)}, bf16[2,320,768]{2,1,0:T(8,128)(2,1)S(1)}, u32[]{:S(2)}, u32[]{:S(2)}) collective-permute-start(bf16[2,320,768]{2,1,0:T(8,128)(2,1)} %get-tuple-element.24), channel_id=1, source_target_pairs={{0,8},{8,16},{16,24},{24,0},{1,9},{9,17},{17,25},{25,1},{2,10},{10... | collective-permute-start | bytes 2949128 | tf_op jit(solution)/shard_map/ppermute | solution.py:71
  176.1 50.0 %collective-permute-start.2 = (bf16[2,320,768]{2,1,0:T(8,128)(2,1)}, bf16[2,320,768]{2,1,0:T(8,128)(2,1)S(1)}, u32[]{:S(2)}, u32[]{:S(2)}) collective-permute-start(bf16[2,320,768]{2,1,0:T(8,128)(2,1)} %get-tuple-element.25), channel_id=1, source_target_pairs={{0,24},{8,0},{16,8},{24,16},{1,25},{9,1},{17,9},{25,17},{2,26},{10... | collective-permute-start | bytes 2949128 | tf_op jit(solution)/shard_map/ppermute | solution.py:71
  176.7 91.8 %collective-permute-start.1 = (bf16[2,320,768]{2,1,0:T(8,128)(2,1)S(1)}, bf16[2,320,768]{2,1,0:T(8,128)(2,1)}, u32[]{:S(2)}, u32[]{:S(2)}) collective-permute-start(bf16[2,320,768]{2,1,0:T(8,128)(2,1)S(1)} %get-tuple-element.26), channel_id=1, source_target_pairs={{0,16},{8,24},{16,0},{24,8},{1,17},{9,25},{17,1},{25,9},{2,18},{10... | collective-permute-start | bytes 2949128 | tf_op jit(solution)/shard_map/ppermute | solution.py:71
  278.1 14.4 %slice-start = ((s8[7864320]{0:T(1024)(128)(4,1)}), s8[4194304]{0:T(1024)(128)(4,1)S(1)}, s32[]{:S(2)}) async-start(s8[7864320]{0:T(1024)(128)(4,1)} %bitcast.115), calls=%async_computation.6 | async-start | bytes 8388608
  279.3 33.3 %collective-permute-start.3 = (bf16[2,320,768]{2,1,0:T(8,128)(2,1)}, bf16[2,320,768]{2,1,0:T(8,128)(2,1)S(1)}, u32[]{:S(2)}, u32[]{:S(2)}) collective-permute-start(bf16[2,320,768]{2,1,0:T(8,128)(2,1)} %get-tuple-element.27), channel_id=1, source_target_pairs={{0,8},{8,16},{16,24},{24,0},{1,9},{9,17},{17,25},{25,1},{2,10},{10... | collective-permute-start | bytes 2949128 | tf_op jit(solution)/shard_map/ppermute | solution.py:71
  282.3 43.2 %collective-permute-start.5 = (bf16[2,320,768]{2,1,0:T(8,128)(2,1)S(1)}, bf16[2,320,768]{2,1,0:T(8,128)(2,1)}, u32[]{:S(2)}, u32[]{:S(2)}) collective-permute-start(bf16[2,320,768]{2,1,0:T(8,128)(2,1)S(1)} %get-tuple-element.28), channel_id=1, source_target_pairs={{0,24},{8,0},{16,8},{24,16},{1,25},{9,1},{17,9},{25,17},{2,26},{10... | collective-permute-start | bytes 2949128 | tf_op jit(solution)/shard_map/ppermute | solution.py:71
  282.3 83.3 %collective-permute-start.4 = (bf16[2,320,768]{2,1,0:T(8,128)(2,1)S(1)}, bf16[2,320,768]{2,1,0:T(8,128)(2,1)}, u32[]{:S(2)}, u32[]{:S(2)}) collective-permute-start(bf16[2,320,768]{2,1,0:T(8,128)(2,1)S(1)} %get-tuple-element.29), channel_id=1, source_target_pairs={{0,16},{8,24},{16,0},{24,8},{1,17},{9,25},{17,1},{25,9},{2,18},{10... | collective-permute-start | bytes 2949128 | tf_op jit(solution)/shard_map/ppermute | solution.py:71
  282.6 9.9 %slice-start.1 = ((s8[7864320]{0:T(1024)(128)(4,1)}), s8[3670016]{0:T(1024)(128)(4,1)S(1)}, s32[]{:S(2)}) async-start(s8[7864320]{0:T(1024)(128)(4,1)} %bitcast.115), calls=%async_computation.7 | async-start | bytes 7340032
  395.1 17.5 %all-to-all-start.4 = ((f32[4,4,80]{2,0,1:T(4,128)}), f32[4,4,80]{2,0,1:T(4,128)S(1)}, u32[]{:S(2)}, u32[]{:S(2)}) async-start(f32[4,4,80]{2,0,1:T(4,128)} %copy.57), calls=%async_computation.4 | async-start | bytes 16384 | tf_op jit(solution)/shard_map/all_to_all | solution.py:85
Sparse Core Ops, SparseCore 0:
  42.3 147.3 all-gather.1

commit v5 on v4

--- a/solution.py
+++ b/solution.py
@@ -78,10 +78,18 @@
     weight_grad = jnp.concatenate(grads, axis=0)
     dot_part = jnp.concatenate(dots, axis=1)
     hidden_grad = jnp.concatenate(hidden_parts, axis=0)[None]
-    hidden_grad, dot_part, weight_grad = lax.optimization_barrier((hidden_grad, dot_part, weight_grad))
-    slot_dots = lax.psum(dot_part, ("dp", "etp"))
-    slot_dots = lax.dynamic_index_in_dim(slot_dots, me, 0, keepdims=False)
-    slot_dots = slot_dots.reshape(exp_dev, senders, capacity)
+    own_dots = lax.dynamic_index_in_dim(dot_part, me, 0, keepdims=False)
+    for shift in range(1, groups):
+        chunk = lax.dynamic_index_in_dim(dot_part, (me + shift) % groups, 0, keepdims=False)
+        pairs = [(i, (i + shift) % groups) for i in range(groups)]
+        own_dots = own_dots + lax.ppermute(chunk, "dp", pairs)
+    halves = lax.axis_size("etp")
+    half_dots = own_dots
+    for shift in range(1, halves):
+        pairs = [(i, (i + shift) % halves) for i in range(halves)]
+        own_dots = own_dots + lax.ppermute(half_dots, "etp", pairs)
+    hidden_grad, own_dots, weight_grad = lax.optimization_barrier((hidden_grad, own_dots, weight_grad))
+    slot_dots = own_dots.reshape(exp_dev, senders, capacity)
     returned = lax.all_to_all(slot_dots, "expert", split_axis=1, concat_axis=1, tiled=True)
     own_select = lax.dynamic_index_in_dim(select, me, 0, keepdims=False).astype(jnp.float32)
     gate_grad = jnp.sum(own_select * returned.reshape(1, 1, rows), axis=2)

time: 429 us -> 423 us (0.986)
  blocking collectives: 116 us -> 90.1 us
  waiting for transfers between devices: 139 us -> 152 us
    psum x1 -> x0, blocking collectives: 25.3 us -> none  [body(): slot_dots = lax.psum(dot_part, ('dp', 'etp'))]
    ppermute x6, waiting for transfers between devices: 97.9 us -> 111 us  [body(): lax.ppermute(chunk, 'dp', pairs).astype(jnp.float32)]
    all_to_all x1, starting transfers between devices: 11.8 us -> 5.41 us  [body(): lax.all_to_all(slot_dots, 'expert', split_axis=1, concat_axis=1, tiled=True)]
    ppermute x0 -> x4, starting transfers between devices: none -> 4.7 us  [the longest x3 3.45 us: body(): own_dots = own_dots + lax.ppermute(chunk, 'dp', pairs)]
  transfers between devices with their start and end apart: 11 -> 15, of which waited for: 5 -> 6; matrix products, arithmetic and copies ran while one was open for 24% -> 21% of each run, Pallas kernels for 0% -> 0%
where the time goes in v5:
time: 423 us; the launch traced here: 415 us
  waiting for transfers between devices  152 us (36%)
  blocking collectives  90.1 us (21%)
  matrix products  51.4 us (12%)
  local copies, waits for them, and re-layouts  38.8 us (9%)
  other arithmetic  34.3 us (8%)
  starting transfers between devices  33.5 us (8%)
  between operations  14.8 us (3%)
    ppermute x6, waiting for transfers between devices, body(): lax.ppermute(chunk, 'dp', pairs).astype(jnp.float32)  111 us
    all_to_all x1, blocking collectives, body(): lax.all_to_all(picked[local], 'expert', split_axis=2, concat_axis=2, tile...  63.9 us
    all_to_all x1, waiting for transfers between devices, body(): lax.all_to_all(picked[local], 'expert', split_axis=2, concat_axis=2, tile...  41 us
    all_gather x1, blocking collectives, body(): all_meta = lax.all_gather(meta, 'dp', axis=0, tiled=True)  26.2 us
    dot_general x2, matrix products, body(): jnp.einsum('enrd,efd->nerf', received, down_weight[local], preferred_elem...  20 us
    dot_general x2, matrix products, body(): jnp.einsum('nerf,enrd->efd', scaled, received, preferred_element_type=jnp...  19.6 us
    slice x1, local copies, waits for them, and re-layouts, body(): picked[local]  10.5 us
    reshape x1, local copies, waits for them, and re-layouts, body(): picked.reshape(groups, exp_dev, senders, capacity, quarter)  10.3 us
  transfers between devices with their start and end apart: 15, of which 6 were waited for; matrix products, arithmetic and copies ran while one was open for 21% of the time, Pallas kernels for 0%

profile of v5, /device:TPU:29, one launch (start us, length us, event | category | flops | bytes accessed | tf_op | source)
XLA Modules:
  0.0 414.8 jit_solution(2129813750016875675)
XLA Ops:
  9.4 4.5 %all-to-all-start = ((bf16[128,4,1024]{0,2,1:T(8,128)(2,1)}), bf16[128,4,1024]{0,2,1:T(8,128)(2,1)S(1)}, u32[]{:S(2)}, u32[]{:S(2)}) async-start(bf16[128,4,1024]{0,2,1:T(8,128)(2,1)} %bitcast), calls=%async_computation | async-start | bytes 2097152 | tf_op jit(solution)/shard_map/all_to_all | solution.py:18
  15.3 26.2 %all_gather.6 = f32[512,16]{0,1:T(8,128)S(1)} all-gather(f32[128,16]{0,1:T(8,128)S(1)} %pad_maximum_fusion.1), channel_id=1, replica_groups=mesh['dp'=4,'expert'=4,'etp'=2] {'dp'}, dimensions={0}, use_global_device_ids=true | all-gather | bytes 40960 | tf_op jit(solution)/shard_map/all_gather | solution.py:17
  43.7 5.6 %fusion.1 = bf16[4,1,1280,1]{2,1,3,0:T(2,128)(2,1)S(1)} fusion(bf16[4,128,8,1]{2,3,1,0:T(2,128)(2,1)S(1)} %copy.60, s32[4,128,8]{2,1,0:T(8,128)S(1)} %fusion.50), kind=kOutput, calls=%fused_computation.2 | convolution fusion | flops 15728640 | bytes 34816 | tf_op jit(solution)/shard_map/gtk,gtkr->gr/dot_general | solution.py:37
  50.0 7.0 %all-to-all-start.1 = ((bf16[4,4,4,80]{3,0,1,2:T(4,128)(2,1)}), bf16[4,4,4,80]{3,0,1,2:T(4,128)(2,1)S(1)}, u32[]{:S(2)}, u32[]{:S(2)}) async-start(bf16[4,4,4,80]{3,0,1,2:T(4,128)(2,1)} %copy.50), calls=%async_computation.1 | async-start | bytes 32768 | tf_op jit(solution)/shard_map/all_to_all | solution.py:49
  57.0 6.3 %fusion.25 = bf16[4,128,1280]{2,1,0:T(8,128)(2,1)S(1)} fusion(s32[4,128,8]{2,1,0:T(8,128)S(1)} %fusion.50), kind=kLoop, calls=%fused_computation.36 | loop fusion | flops 15073280 | bytes 1327104 | tf_op jit(solution)/shard_map/reduce_sum | solution.py:38
  63.4 5.5 %convolution_convert_fusion = bf16[4,1280,1024]{2,1,0:T(8,128)(2,1)} fusion(bf16[4,128,1280]{2,1,0:T(8,128)(2,1)S(1)} %fusion.25, bf16[4,128,1024]{2,1,0:T(8,128)(2,1)S(1)} %copy.47), kind=kOutput, calls=%fused_computation.3 | convolution fusion | flops 1347420160 | bytes 12845056 | tf_op jit(solution)/shard_map/gtr,gtd->grd/dot_general | solution.py:39
  68.9 10.3 %copy.81 = bf16[4,4,4,80,1024]{4,3,1,0,2:T(8,128)(2,1)} copy(bf16[4,4,4,80,1024]{4,3,2,1,0:T(8,128)(2,1)} %bitcast.128) | data formatting | bytes 20971520 | tf_op jit(solution)/shard_map/reshape | solution.py:45
  79.2 10.5 %fusion.64 = (bf16[2,4,4,80,1024]{4,3,0,1,2:T(8,128)(2,1)}, bf16[2,4,4,80,1024]{4,3,0,1,2:T(8,128)(2,1)}) fusion(bf16[4,4,4,80,1024]{4,3,0,1,2:T(8,128)(2,1)} %bitcast.129), kind=kLoop, calls=%fused_computation.102 | loop fusion | bytes 20971520 | tf_op jit(solution)/shard_map/slice | solution.py:59
  89.7 63.9 %all_to_all.39 = bf16[2,4,4,80,1024]{4,3,0,1,2:T(8,128)(2,1)} all-to-all(bf16[2,4,4,80,1024]{4,3,0,1,2:T(8,128)(2,1)} %get-tuple-element.22), channel_id=1, replica_groups=mesh['dp'=4,'expert'=4,'etp'=2] {'expert'}, dimensions={2} | all-to-all | bytes 10485760 | tf_op jit(solution)/shard_map/all_to_all | solution.py:59
  153.6 7.2 %all-to-all-start.3 = ((bf16[2,4,4,80,1024]{4,3,0,1,2:T(8,128)(2,1)}), bf16[2,4,4,80,1024]{4,3,0,1,2:T(8,128)(2,1)}, u32[]{:S(2)}, u32[]{:S(2)}) async-start(bf16[2,4,4,80,1024]{4,3,0,1,2:T(8,128)(2,1)} %get-tuple-element.23), calls=%async_computation.3 | async-start | bytes 10485760 | tf_op jit(solution)/shard_map/all_to_all | solution.py:59
  160.8 3.1 copy.54
  163.9 10.1 %bitcast_convert_fusion.1 = (bf16[4,2,320,768]{3,2,0,1:T(8,128)(2,1)S(1)}, f32[2,4,320,768]{3,2,1,0:T(8,128)}) fusion(bf16[2,4,320,1024]{3,2,1,0:T(8,128)(2,1)S(1)} %bitcast.132, bf16[4,768,1024]{2,1,0:T(8,128)(2,1)} %param.9), kind=kOutput, calls=%fused_computation.15 | convolution fusion | flops 4028497920 | bytes 20185088 | tf_op jit(solution)/shard_map/enrd,efd->nerf/dot_general | solution.py:63
  177.3 41.0 %all-to-all-done.3 = bf16[2,4,4,80,1024]{4,3,0,1,2:T(8,128)(2,1)} async-done(((bf16[2,4,4,80,1024]{4,3,0,1,2:T(8,128)(2,1)}), bf16[2,4,4,80,1024]{4,3,0,1,2:T(8,128)(2,1)}, u32[]{:S(2)}, u32[]{:S(2)}) %all-to-all-start.3) | async-done | bytes 5242912 | tf_op jit(solution)/shard_map/all_to_all | solution.py:59
  218.3 5.8 %copy.56 = bf16[2,4,4,80,1024]{4,3,2,1,0:T(8,128)(2,1)} copy(bf16[2,4,4,80,1024]{4,3,0,1,2:T(8,128)(2,1)} %all-to-all-done.3) | data formatting | bytes 10485760 | tf_op jit(solution)/shard_map/all_to_all | solution.py:59
  226.1 42.4 %collective-permute-done.1 = bf16[2,320,768]{2,1,0:T(8,128)(2,1)} collective-permute-done((bf16[2,320,768]{2,1,0:T(8,128)(2,1)S(1)}, bf16[2,320,768]{2,1,0:T(8,128)(2,1)}, u32[]{:S(2)}, u32[]{:S(2)}) %collective-permute-start.1) | collective-permute-done | bytes 983072 | tf_op jit(solution)/shard_map/ppermute | solution.py:71
  270.9 9.9 %bitcast_convert_fusion = (bf16[4,2,320,768]{3,2,0,1:T(8,128)(2,1)}, f32[2,4,320,768]{3,2,1,0:T(8,128)S(1)}) fusion(bf16[2,4,320,1024]{3,2,1,0:T(8,128)(2,1)} %bitcast.134, bf16[4,768,1024]{2,1,0:T(8,128)(2,1)} %param.9), kind=kOutput, calls=%fused_computation.14 | convolution fusion | flops 4028497920 | bytes 20185088 | tf_op jit(solution)/shard_map/enrd,efd->nerf/dot_general | solution.py:63
  280.8 9.9 %bitcast_convert_fusion.2 = bf16[2,768,1024]{2,1,0:T(8,128)(2,1)} fusion(bf16[2,4,320,1024]{3,2,1,0:T(8,128)(2,1)} %bitcast.135, f32[4,2,320]{2,0,1:T(4,128)S(1)} %get-tuple-element.31, bf16[4,4,320,768]{3,2,0,1:T(8,128)(2,1)} %all-gather.2.cloned.1.call-done), kind=kOutput, calls=%fused_computation.17 | convolution fusion | flops 4034002944 | bytes 12331008 | tf_op jit(solution)/shard_map/nerf,enrd->efd/dot_general | solution.py:75
  299.0 3.3 collective-permute-start.7
  305.4 9.7 %bitcast_convert_fusion.3 = bf16[2,768,1024]{2,1,0:T(8,128)(2,1)} fusion(bf16[2,4,320,1024]{3,2,1,0:T(8,128)(2,1)} %bitcast.133, f32[4,2,320]{2,0,1:T(4,128)S(1)} %get-tuple-element.30, bf16[4,4,320,768]{3,2,0,1:T(8,128)(2,1)} %all-gather.2.cloned.1.call-done), kind=kOutput, calls=%fused_computation.18 | convolution fusion | flops 4034002944 | bytes 12331008 | tf_op jit(solution)/shard_map/nerf,enrd->efd/dot_general | solution.py:75
  316.4 6.1 %pad_maximum_fusion = bf16[4,768,1024]{2,1,0:T(8,128)(2,1)} fusion(bf16[2,768,1024]{2,1,0:T(8,128)(2,1)} %bitcast_convert_fusion.2, bf16[2,768,1024]{2,1,0:T(8,128)(2,1)} %bitcast_convert_fusion.3), kind=kLoop, calls=%fused_computation.16 | loop fusion | flops 3145728 | bytes 12582912 | tf_op jit(solution)/shard_map/concatenate | solution.py:78
  324.8 21.8 %collective-permute-done.5 = bf16[2,320,768]{2,1,0:T(8,128)(2,1)} collective-permute-done((bf16[2,320,768]{2,1,0:T(8,128)(2,1)S(1)}, bf16[2,320,768]{2,1,0:T(8,128)(2,1)}, u32[]{:S(2)}, u32[]{:S(2)}) %collective-permute-start.5) | collective-permute-done | bytes 983072 | tf_op jit(solution)/shard_map/ppermute | solution.py:71
  346.6 42.3 %collective-permute-done.4 = bf16[2,320,768]{2,1,0:T(8,128)(2,1)} collective-permute-done((bf16[2,320,768]{2,1,0:T(8,128)(2,1)S(1)}, bf16[2,320,768]{2,1,0:T(8,128)(2,1)}, u32[]{:S(2)}, u32[]{:S(2)}) %collective-permute-start.4) | collective-permute-done | bytes 983072 | tf_op jit(solution)/shard_map/ppermute | solution.py:71
  393.3 5.4 %all-to-all-start.4 = ((f32[4,4,80]{2,0,1:T(4,128)}), f32[4,4,80]{2,0,1:T(4,128)S(1)}, u32[]{:S(2)}, u32[]{:S(2)}) async-start(f32[4,4,80]{2,0,1:T(4,128)} %copy.57), calls=%async_computation.4 | async-start | bytes 16384 | tf_op jit(solution)/shard_map/all_to_all | solution.py:93
  398.7 5.7 %fusion = bf16[4,128,8,1280]{3,2,1,0:T(8,128)(2,1)} fusion(s32[4,128,8]{2,1,0:T(8,128)S(1)} %fusion.50), kind=kLoop, calls=%fused_computation.1 | loop fusion | flops 10485760 | bytes 10502144 | tf_op jit(solution)/shard_map/convert_element_type | solution.py:35
  (72 shorter events, 36.5 us)
Async XLA Ops:
  9.4 32.2 %all-to-all-start = ((bf16[128,4,1024]{0,2,1:T(8,128)(2,1)}), bf16[128,4,1024]{0,2,1:T(8,128)(2,1)S(1)}, u32[]{:S(2)}, u32[]{:S(2)}) async-start(bf16[128,4,1024]{0,2,1:T(8,128)(2,1)} %bitcast), calls=%async_computation | async-start | bytes 2097152 | tf_op jit(solution)/shard_map/all_to_all | solution.py:18
  14.0 256.9 %all-gather.2.cloned.1.call-start = ((), (), s32[]{:S(2)}) async-start(), calls=%async_computation.5 | async-start | bytes 9830400 | tf_op jit(solution)/shard_map/all_gather | solution.py:20
  50.0 39.7 %all-to-all-start.1 = ((bf16[4,4,4,80]{3,0,1,2:T(4,128)(2,1)}), bf16[4,4,4,80]{3,0,1,2:T(4,128)(2,1)S(1)}, u32[]{:S(2)}, u32[]{:S(2)}) async-start(bf16[4,4,4,80]{3,0,1,2:T(4,128)(2,1)} %copy.50), calls=%async_computation.1 | async-start | bytes 32768 | tf_op jit(solution)/shard_map/all_to_all | solution.py:49
  153.6 64.7 %all-to-all-start.3 = ((bf16[2,4,4,80,1024]{4,3,0,1,2:T(8,128)(2,1)}), bf16[2,4,4,80,1024]{4,3,0,1,2:T(8,128)(2,1)}, u32[]{:S(2)}, u32[]{:S(2)}) async-start(bf16[2,4,4,80,1024]{4,3,0,1,2:T(8,128)(2,1)} %get-tuple-element.23), calls=%async_computation.3 | async-start | bytes 10485760 | tf_op jit(solution)/shard_map/all_to_all | solution.py:59
  163.9 10.2 %copy-start = (bf16[2,4,4,80,1024]{4,3,2,1,0:T(8,128)(2,1)}, bf16[2,4,4,80,1024]{4,3,2,1,0:T(8,128)(2,1)S(1)}, u32[]{:S(2)}) copy-start(bf16[2,4,4,80,1024]{4,3,2,1,0:T(8,128)(2,1)S(1)} %copy.54) | copy-start | bytes 15728644
  175.5 48.5 %collective-permute-start = (bf16[2,320,768]{2,1,0:T(8,128)(2,1)}, bf16[2,320,768]{2,1,0:T(8,128)(2,1)S(1)}, u32[]{:S(2)}, u32[]{:S(2)}) collective-permute-start(bf16[2,320,768]{2,1,0:T(8,128)(2,1)} %get-tuple-element.24), channel_id=1, source_target_pairs={{0,8},{8,16},{16,24},{24,0},{1,9},{9,17},{17,25},{25,1},{2,10},{10... | collective-permute-start | bytes 2949128 | tf_op jit(solution)/shard_map/ppermute | solution.py:71
  176.4 49.7 %collective-permute-start.2 = (bf16[2,320,768]{2,1,0:T(8,128)(2,1)}, bf16[2,320,768]{2,1,0:T(8,128)(2,1)S(1)}, u32[]{:S(2)}, u32[]{:S(2)}) collective-permute-start(bf16[2,320,768]{2,1,0:T(8,128)(2,1)} %get-tuple-element.25), channel_id=1, source_target_pairs={{0,24},{8,0},{16,8},{24,16},{1,25},{9,1},{17,9},{25,17},{2,26},{10... | collective-permute-start | bytes 2949128 | tf_op jit(solution)/shard_map/ppermute | solution.py:71
  177.0 91.5 %collective-permute-start.1 = (bf16[2,320,768]{2,1,0:T(8,128)(2,1)S(1)}, bf16[2,320,768]{2,1,0:T(8,128)(2,1)}, u32[]{:S(2)}, u32[]{:S(2)}) collective-permute-start(bf16[2,320,768]{2,1,0:T(8,128)(2,1)S(1)} %get-tuple-element.26), channel_id=1, source_target_pairs={{0,16},{8,24},{16,0},{24,8},{1,17},{9,25},{17,1},{25,9},{2,18},{10... | collective-permute-start | bytes 2949128 | tf_op jit(solution)/shard_map/ppermute | solution.py:71
  270.9 22.7 %slice-start = ((s8[7864320]{0:T(1024)(128)(4,1)}), s8[4194304]{0:T(1024)(128)(4,1)S(1)}, s32[]{:S(2)}) async-start(s8[7864320]{0:T(1024)(128)(4,1)} %bitcast.130), calls=%async_computation.6 | async-start | bytes 8388608
  280.8 12.9 %slice-start.1 = ((s8[7864320]{0:T(1024)(128)(4,1)}), s8[3670016]{0:T(1024)(128)(4,1)S(1)}, s32[]{:S(2)}) async-start(s8[7864320]{0:T(1024)(128)(4,1)} %bitcast.130), calls=%async_computation.7 | async-start | bytes 7340032
  296.8 7.2 %collective-permute-start.8 = (f32[4,320]{1,0:T(4,128)S(1)}, f32[4,320]{1,0:T(4,128)S(1)}, u32[]{:S(2)}, u32[]{:S(2)}) collective-permute-start(f32[4,320]{1,0:T(4,128)S(1)} %bitcast.142), channel_id=1, source_target_pairs={{0,24},{8,0},{16,8},{24,16},{1,25},{9,1},{17,9},{25,17},{2,26},{10... | collective-permute-start | bytes 15368 | tf_op jit(solution)/shard_map/ppermute | solution.py:85
  299.0 16.1 %collective-permute-start.7 = (f32[4,320]{1,0:T(4,128)S(1)}, f32[4,320]{1,0:T(4,128)S(1)}, u32[]{:S(2)}, u32[]{:S(2)}) collective-permute-start(f32[4,320]{1,0:T(4,128)S(1)} %bitcast.143), channel_id=1, source_target_pairs={{0,16},{8,24},{16,0},{24,8},{1,17},{9,25},{17,1},{25,9},{2,18},{10... | collective-permute-start | bytes 15368 | tf_op jit(solution)/shard_map/ppermute | solution.py:85
  302.2 12.8 %collective-permute-start.6 = (f32[4,320]{1,0:T(4,128)S(1)}, f32[4,320]{1,0:T(4,128)S(1)}, u32[]{:S(2)}, u32[]{:S(2)}) collective-permute-start(f32[4,320]{1,0:T(4,128)S(1)} %bitcast.141), channel_id=1, source_target_pairs={{0,8},{8,16},{16,24},{24,0},{1,9},{9,17},{17,25},{25,1},{2,10},{10... | collective-permute-start | bytes 15368 | tf_op jit(solution)/shard_map/ppermute | solution.py:85
  302.3 22.5 %collective-permute-start.3 = (bf16[2,320,768]{2,1,0:T(8,128)(2,1)S(1)}, bf16[2,320,768]{2,1,0:T(8,128)(2,1)}, u32[]{:S(2)}, u32[]{:S(2)}) collective-permute-start(bf16[2,320,768]{2,1,0:T(8,128)(2,1)S(1)} %get-tuple-element.27), channel_id=1, source_target_pairs={{0,8},{8,16},{16,24},{24,0},{1,9},{9,17},{17,25},{25,1},{2,10},{10... | collective-permute-start | bytes 2949128 | tf_op jit(solution)/shard_map/ppermute | solution.py:71
  303.5 43.1 %collective-permute-start.5 = (bf16[2,320,768]{2,1,0:T(8,128)(2,1)S(1)}, bf16[2,320,768]{2,1,0:T(8,128)(2,1)}, u32[]{:S(2)}, u32[]{:S(2)}) collective-permute-start(bf16[2,320,768]{2,1,0:T(8,128)(2,1)S(1)} %get-tuple-element.28), channel_id=1, source_target_pairs={{0,24},{8,0},{16,8},{24,16},{1,25},{9,1},{17,9},{25,17},{2,26},{10... | collective-permute-start | bytes 2949128 | tf_op jit(solution)/shard_map/ppermute | solution.py:71
  304.0 84.9 %collective-permute-start.4 = (bf16[2,320,768]{2,1,0:T(8,128)(2,1)S(1)}, bf16[2,320,768]{2,1,0:T(8,128)(2,1)}, u32[]{:S(2)}, u32[]{:S(2)}) collective-permute-start(bf16[2,320,768]{2,1,0:T(8,128)(2,1)S(1)} %get-tuple-element.29), channel_id=1, source_target_pairs={{0,16},{8,24},{16,0},{24,8},{1,17},{9,25},{17,1},{25,9},{2,18},{10... | collective-permute-start | bytes 2949128 | tf_op jit(solution)/shard_map/ppermute | solution.py:71
  315.1 7.3 %collective-permute-start.9 = (f32[4,320]{1,0:T(4,128)S(1)}, f32[4,320]{1,0:T(4,128)S(1)}, u32[]{:S(2)}, u32[]{:S(2)}) collective-permute-start(f32[4,320]{1,0:T(4,128)S(1)} %fusion.63), channel_id=1, source_target_pairs={{0,1},{1,0},{2,3},{3,2},{4,5},{5,4},{6,7},{7,6},{8,9},{9,8},{10,11... | collective-permute-start | bytes 15368 | tf_op jit(solution)/shard_map/ppermute | solution.py:90
  393.3 11.2 %all-to-all-start.4 = ((f32[4,4,80]{2,0,1:T(4,128)}), f32[4,4,80]{2,0,1:T(4,128)S(1)}, u32[]{:S(2)}, u32[]{:S(2)}) async-start(f32[4,4,80]{2,0,1:T(4,128)} %copy.57), calls=%async_computation.4 | async-start | bytes 16384 | tf_op jit(solution)/shard_map/all_to_all | solution.py:93
Sparse Core Ops, SparseCore 0:
  42.3 147.3 all-gather.1

commit v6 on v5

--- a/solution.py
+++ b/solution.py
@@ -36,13 +36,8 @@
     gate_rows = all_gates.reshape(groups, token_count, top_count).astype(jnp.float32)
     gate_table = jnp.einsum("gtk,gtkr->gr", gate_rows, select.astype(jnp.float32))
     token_select = jnp.sum(select, axis=2)
-    picked = jnp.einsum(
-        "gtr,gtd->grd",
-        token_select,
-        columns.reshape(groups, token_count, quarter),
-        preferred_element_type=jnp.float32,
-    ).astype(columns.dtype)
-    picked = picked.reshape(groups, exp_dev, senders, capacity, quarter).transpose(1, 0, 2, 3, 4)
+    token_select = token_select.reshape(groups, token_count, exp_dev, senders, capacity)
+    token_columns = columns.reshape(groups, token_count, quarter)
     gate_table = (
         gate_table.reshape(groups, exp_dev, senders, capacity).transpose(1, 0, 2, 3).astype(gates.dtype)
     )
@@ -56,13 +51,18 @@
     grads, dots, hidden_parts = [], [], []
     for c in range(chunks):
         local = slice(c * per, (c + 1) * per)
-        received = lax.all_to_all(picked[local], "expert", split_axis=2, concat_axis=2, tiled=True)
-        received = received.reshape(per, groups, slot_rows_all, quarter)
+        picked = jnp.einsum(
+            "gtlqs,gtd->qglsd",
+            token_select[:, :, local],
+            token_columns,
+            preferred_element_type=jnp.float32,
+        ).astype(columns.dtype)
+        received = lax.all_to_all(picked, "expert", split_axis=0, concat_axis=0, tiled=True)
         if c == chunks - 1:
             hidden_all, received = lax.optimization_barrier((hidden_all, received))
         partial = jnp.einsum(
-            "enrd,efd->nerf", received, down_weight[local], preferred_element_type=jnp.float32
-        )
+            "qglsd,lfd->glqsf", received, down_weight[local], preferred_element_type=jnp.float32
+        ).reshape(groups, per, slot_rows_all, ff_part)
         sent = partial.astype(jnp.bfloat16)
         expert_grad = lax.dynamic_index_in_dim(partial, me, 0, keepdims=False)
         for shift in range(1, groups):
@@ -72,7 +72,8 @@
         hidden_rows = hidden_all[:, local].astype(jnp.float32)
         dots.append(jnp.sum(hidden_rows * partial, axis=3))
         scaled = (jnp.moveaxis(slot_gates[local], 0, 1)[..., None] * hidden_rows).astype(jnp.bfloat16)
-        weight_sum = jnp.einsum("nerf,enrd->efd", scaled, received, preferred_element_type=jnp.float32)
+        scaled = scaled.reshape(groups, per, senders, capacity, ff_part)
+        weight_sum = jnp.einsum("glqsf,qglsd->lfd", scaled, received, preferred_element_type=jnp.float32)
         grads.append(weight_sum.astype(jnp.bfloat16))
         hidden_parts.append((own_gates[local][..., None] * expert_grad).astype(jnp.bfloat16))
     weight_grad = jnp.concatenate(grads, axis=0)

time: 423 us -> 413 us (0.976); the launches traced: 415 us -> 410 us
  blocking collectives: 90.1 us -> 26.2 us
  waiting for transfers between devices: 152 us -> 193 us
  starting transfers between devices: 33.5 us -> 61.4 us
  local copies, waits for them, and re-layouts: 38.8 us -> 27.7 us
  other arithmetic: 34.3 us -> 44.8 us
  matrix products: 51.4 us -> 41.6 us
    all_to_all x1 -> x0, blocking collectives: 63.9 us -> none  [body(): lax.all_to_all(picked[local], 'expert', split_axis=2, concat_axis=2, tile...]
    ppermute x3, waiting for transfers between devices: 0.01 us -> 38.9 us  [body(): own_dots = own_dots + lax.ppermute(chunk, 'dp', pairs)]
    ppermute x3, starting transfers between devices: 3.45 us -> 24.7 us  [body(): own_dots = own_dots + lax.ppermute(chunk, 'dp', pairs)]
    convert_element_type x0 -> x6, other arithmetic: none -> 15.4 us  [the longest x2 8.27 us: body(): (jnp.moveaxis(slot_gates[local], 0, 1)[..., None] * hidden_rows).astype(j...]
    dot_general x5 -> x4, matrix products: 45.2 us -> 32.3 us  [the longest x2 18 us: body(): jnp.einsum('glqsf,qglsd->lfd', scaled, received, preferred_element_type=j...]
    convert_element_type x0 -> x2, local copies, waits for them, and re-layouts: none -> 11.6 us  [body(): picked = jnp.einsum('gtlqs,gtd->qglsd', token_select[:, :, local], token_...]
    slice x1, local copies, waits for them, and re-layouts: 10.5 us -> 0.1 us  [body(): token_select[:, :, local]]
    reshape x1 -> x0, local copies, waits for them, and re-layouts: 10.3 us -> none  [body(): picked.reshape(groups, exp_dev, senders, capacity, quarter)]
  transfers between devices with their start and end apart: 15 -> 16, of which waited for: 6 -> 5; matrix products, arithmetic and copies ran while one was open for 21% -> 22% of each run, Pallas kernels for 0% -> 0%
where the time goes in v6:
time: 413 us; the launch traced here: 410 us
  waiting for transfers between devices  193 us (47%)
  starting transfers between devices  61.4 us (15%)
  other arithmetic  44.8 us (11%)
  matrix products  41.6 us (10%)
  local copies, waits for them, and re-layouts  27.7 us (7%)
  blocking collectives  26.2 us (6%)
  between operations  14.6 us (4%)
    ppermute x6, waiting for transfers between devices, body(): lax.ppermute(chunk, 'dp', pairs).astype(jnp.float32)  107 us
    all_to_all x2, waiting for transfers between devices, body(): lax.all_to_all(picked, 'expert', split_axis=0, concat_axis=0, tiled=True)  47.1 us
    ppermute x3, waiting for transfers between devices, body(): own_dots = own_dots + lax.ppermute(chunk, 'dp', pairs)  38.9 us
    all_gather x1, blocking collectives, body(): all_meta = lax.all_gather(meta, 'dp', axis=0, tiled=True)  26.2 us
    ppermute x3, starting transfers between devices, body(): own_dots = own_dots + lax.ppermute(chunk, 'dp', pairs)  24.7 us
    dot_general x2, matrix products, body(): jnp.einsum('glqsf,qglsd->lfd', scaled, received, preferred_element_type=j...  18 us
    dot_general x2, matrix products, body(): jnp.einsum('qglsd,lfd->glqsf', received, down_weight[local], preferred_el...  14.3 us
    all_to_all x2, starting transfers between devices, body(): lax.all_to_all(picked, 'expert', split_axis=0, concat_axis=0, tiled=True)  12.2 us
  transfers between devices with their start and end apart: 16, of which 5 were waited for; matrix products, arithmetic and copies ran while one was open for 22% of the time, Pallas kernels for 0%

profile of v6, /device:TPU:29, one launch (start us, length us, event | category | flops | bytes accessed | tf_op | source)
XLA Modules:
  0.0 409.6 jit_solution(17525988731408793967)
XLA Ops:
  9.4 4.5 %all-to-all-start = ((bf16[128,4,1024]{0,2,1:T(8,128)(2,1)}), bf16[128,4,1024]{0,2,1:T(8,128)(2,1)S(1)}, u32[]{:S(2)}, u32[]{:S(2)}) async-start(bf16[128,4,1024]{0,2,1:T(8,128)(2,1)} %bitcast), calls=%async_computation | async-start | bytes 2097152 | tf_op jit(solution)/shard_map/all_to_all | solution.py:18
  15.3 26.2 %all_gather.6 = f32[512,16]{0,1:T(8,128)S(1)} all-gather(f32[128,16]{0,1:T(8,128)S(1)} %pad_maximum_fusion.1), channel_id=1, replica_groups=mesh['dp'=4,'expert'=4,'etp'=2] {'dp'}, dimensions={0}, use_global_device_ids=true | all-gather | bytes 40960 | tf_op jit(solution)/shard_map/all_gather | solution.py:17
  43.7 5.6 %fusion.1 = bf16[4,1,1280,1]{2,1,3,0:T(2,128)(2,1)S(1)} fusion(bf16[4,128,8,1]{2,3,1,0:T(2,128)(2,1)S(1)} %copy.83, s32[4,128,8]{2,1,0:T(8,128)S(1)} %fusion.58), kind=kOutput, calls=%fused_computation.2 | convolution fusion | flops 15728640 | bytes 34816 | tf_op jit(solution)/shard_map/gtk,gtkr->gr/dot_general | solution.py:37
  50.0 7.3 %all-to-all-start.1 = ((bf16[4,4,4,80]{3,0,1,2:T(4,128)(2,1)}), bf16[4,4,4,80]{3,0,1,2:T(4,128)(2,1)S(1)}, u32[]{:S(2)}, u32[]{:S(2)}) async-start(bf16[4,4,4,80]{3,0,1,2:T(4,128)(2,1)} %copy.67), calls=%async_computation.1 | async-start | bytes 32768 | tf_op jit(solution)/shard_map/all_to_all | solution.py:44
  57.4 7.4 %fusion.33 = bf16[4,128,1280]{2,1,0:T(8,128)(2,1)} fusion(s32[4,128,8]{2,1,0:T(8,128)S(1)} %fusion.58), kind=kLoop, calls=%fused_computation.36 | loop fusion | flops 15073280 | bytes 1327104 | tf_op jit(solution)/shard_map/reduce_sum | solution.py:38
  71.4 5.8 %copy.70 = bf16[4,4,2,80,1024]{4,3,2,1,0:T(8,128)(2,1)} copy(bf16[4,4,2,80,1024]{4,3,0,2,1:T(8,128)(2,1)} %convert_bitcast_fusion.1) | data formatting | bytes 10485760 | tf_op jit(solution)/shard_map/convert_element_type | solution.py:59
  77.1 5.2 %all-to-all-start.2 = ((bf16[4,4,2,80,1024]{4,3,2,1,0:T(8,128)(2,1)}), bf16[4,4,2,80,1024]{4,3,2,1,0:T(8,128)(2,1)}, u32[]{:S(2)}, u32[]{:S(2)}) async-start(bf16[4,4,2,80,1024]{4,3,2,1,0:T(8,128)(2,1)} %copy.70), calls=%async_computation.2 | async-start | bytes 10485760 | tf_op jit(solution)/shard_map/all_to_all | solution.py:60
  87.1 5.8 %copy.73 = bf16[4,4,2,80,1024]{4,3,2,1,0:T(8,128)(2,1)} copy(bf16[4,4,2,80,1024]{4,3,0,2,1:T(8,128)(2,1)} %convert_bitcast_fusion) | data formatting | bytes 10485760 | tf_op jit(solution)/shard_map/convert_element_type | solution.py:59
  92.9 47.1 %all-to-all-done.2 = bf16[4,4,2,80,1024]{4,3,2,1,0:T(8,128)(2,1)} async-done(((bf16[4,4,2,80,1024]{4,3,2,1,0:T(8,128)(2,1)}), bf16[4,4,2,80,1024]{4,3,2,1,0:T(8,128)(2,1)}, u32[]{:S(2)}, u32[]{:S(2)}) %all-to-all-start.2) | async-done | bytes 5242912 | tf_op jit(solution)/shard_map/all_to_all | solution.py:60
  139.9 6.9 %all-to-all-start.3 = ((bf16[4,4,2,80,1024]{4,3,2,1,0:T(8,128)(2,1)}), bf16[4,4,2,80,1024]{4,3,2,1,0:T(8,128)(2,1)}, u32[]{:S(2)}, u32[]{:S(2)}) async-start(bf16[4,4,2,80,1024]{4,3,2,1,0:T(8,128)(2,1)} %copy.73), calls=%async_computation.3 | async-start | bytes 10485760 | tf_op jit(solution)/shard_map/all_to_all | solution.py:60
  146.9 7.2 %fusion.23 = f32[4,2,4,80,768]{4,3,0,2,1:T(8,128)S(1)} fusion(bf16[4,768,1024]{2,1,0:T(8,128)(2,1)} %param.9, bf16[4,4,2,80,1024]{4,3,2,1,0:T(8,128)(2,1)} %all-to-all-done.2), kind=kOutput, calls=%fused_computation.34 | convolution fusion | flops 4026531840 | bytes 16252928 | tf_op jit(solution)/shard_map/qglsd,lfd->glqsf/dot_general | solution.py:63
  161.0 44.1 %collective-permute-done = bf16[2,320,768]{2,1,0:T(8,128)(2,1)S(1)} collective-permute-done((bf16[2,320,768]{2,1,0:T(8,128)(2,1)}, bf16[2,320,768]{2,1,0:T(8,128)(2,1)S(1)}, u32[]{:S(2)}, u32[]{:S(2)}) %collective-permute-start) | collective-permute-done | bytes 983072 | tf_op jit(solution)/shard_map/ppermute | solution.py:71
  205.1 21.0 %collective-permute-done.2 = bf16[2,320,768]{2,1,0:T(8,128)(2,1)} collective-permute-done((bf16[2,320,768]{2,1,0:T(8,128)(2,1)S(1)}, bf16[2,320,768]{2,1,0:T(8,128)(2,1)}, u32[]{:S(2)}, u32[]{:S(2)}) %collective-permute-start.2) | collective-permute-done | bytes 983072 | tf_op jit(solution)/shard_map/ppermute | solution.py:71
  226.1 42.1 %collective-permute-done.1 = bf16[2,320,768]{2,1,0:T(8,128)(2,1)} collective-permute-done((bf16[2,320,768]{2,1,0:T(8,128)(2,1)S(1)}, bf16[2,320,768]{2,1,0:T(8,128)(2,1)}, u32[]{:S(2)}, u32[]{:S(2)}) %collective-permute-start.1) | collective-permute-done | bytes 983072 | tf_op jit(solution)/shard_map/ppermute | solution.py:71
  270.9 7.2 %fusion.28 = f32[4,2,4,80,768]{4,3,0,2,1:T(8,128)S(1)} fusion(bf16[4,768,1024]{2,1,0:T(8,128)(2,1)} %param.9, bf16[4,4,2,80,1024]{4,3,2,1,0:T(8,128)(2,1)} %all-to-all-done.3), kind=kOutput, calls=%fused_computation.35 | convolution fusion | flops 4026531840 | bytes 16252928 | tf_op jit(solution)/shard_map/qglsd,lfd->glqsf/dot_general | solution.py:63
  284.1 4.9 %fusion.6 = (bf16[4,2,320,768]{3,2,1,0:T(8,128)(2,1)}, f32[4,2,320]{2,1,0:T(2,128)S(1)}) fusion(f32[4,2,320]{2,1,0:T(2,128)S(1)} %copy.78, bf16[4,4,320,768]{3,2,1,0:T(8,128)(2,1)} %all-gather.2.cloned.1.call-done, f32[4,2,320,768]{3,2,1,0:T(8,128)S(1)} %bitcast.139), kind=kLoop, calls=%fused_computation.11 | loop fusion | flops 9827840 | bytes 15749120 | tf_op jit(solution)/shard_map/convert_element_type | solution.py:74
  290.0 3.4 fusion.4
  296.5 9.8 %bitcast_convert_fusion = bf16[2,768,1024]{2,1,0:T(8,128)(2,1)} fusion(bf16[4,2,4,80,768]{4,3,2,1,0:T(8,128)(2,1)} %bitcast.150, bf16[4,4,2,80,1024]{4,3,2,1,0:T(8,128)(2,1)} %all-to-all-done.3), kind=kOutput, calls=%fused_computation.13 | convolution fusion | flops 4028104704 | bytes 12320768 | tf_op jit(solution)/shard_map/glqsf,qglsd->lfd/dot_general | solution.py:76
  307.7 38.9 %collective-permute-done.6 = f32[4,320]{1,0:T(4,128)S(1)} collective-permute-done((f32[4,320]{1,0:T(4,128)S(1)}, f32[4,320]{1,0:T(4,128)S(1)}, u32[]{:S(2)}, u32[]{:S(2)}) %collective-permute-start.6) | collective-permute-done | bytes 5152 | tf_op jit(solution)/shard_map/ppermute | solution.py:86
  346.6 20.2 %collective-permute-start.8 = (f32[4,320]{1,0:T(4,128)S(1)}, f32[4,320]{1,0:T(4,128)S(1)}, u32[]{:S(2)}, u32[]{:S(2)}) collective-permute-start(f32[4,320]{1,0:T(4,128)S(1)} %get-tuple-element.38), channel_id=1, source_target_pairs={{0,24},{8,0},{16,8},{24,16},{1,25},{9,1},{17,9},{25,17},{2,26},{10... | collective-permute-start | bytes 15368 | tf_op jit(solution)/shard_map/ppermute | solution.py:86
  366.8 8.2 %bitcast_convert_fusion.1 = bf16[2,768,1024]{2,1,0:T(8,128)(2,1)} fusion(bf16[4,2,4,80,768]{4,3,2,1,0:T(8,128)(2,1)S(1)} %bitcast.149, bf16[4,4,2,80,1024]{4,3,2,1,0:T(8,128)(2,1)} %all-to-all-done.2), kind=kOutput, calls=%fused_computation.14 | convolution fusion | flops 4028104704 | bytes 12320768 | tf_op jit(solution)/shard_map/glqsf,qglsd->lfd/dot_general | solution.py:76
  376.3 6.1 %pad_maximum_fusion = bf16[4,768,1024]{2,1,0:T(8,128)(2,1)} fusion(bf16[2,768,1024]{2,1,0:T(8,128)(2,1)} %bitcast_convert_fusion, bf16[2,768,1024]{2,1,0:T(8,128)(2,1)} %bitcast_convert_fusion.1), kind=kLoop, calls=%fused_computation.12 | loop fusion | flops 3145728 | bytes 12582912 | tf_op jit(solution)/shard_map/concatenate | solution.py:79
  387.5 6.1 %all-to-all-start.4 = ((f32[4,4,80]{2,0,1:T(4,128)}), f32[4,4,80]{2,0,1:T(4,128)S(1)}, u32[]{:S(2)}, u32[]{:S(2)}) async-start(f32[4,4,80]{2,0,1:T(4,128)} %copy.80), calls=%async_computation.4 | async-start | bytes 16384 | tf_op jit(solution)/shard_map/all_to_all | solution.py:94
  393.6 5.8 %fusion = bf16[4,128,8,1280]{3,2,1,0:T(8,128)(2,1)} fusion(s32[4,128,8]{2,1,0:T(8,128)S(1)} %fusion.58), kind=kLoop, calls=%fused_computation.1 | loop fusion | flops 10485760 | bytes 10502144 | tf_op jit(solution)/shard_map/convert_element_type | solution.py:35
  (88 shorter events, 48.1 us)
Async XLA Ops:
  9.4 32.2 %all-to-all-start = ((bf16[128,4,1024]{0,2,1:T(8,128)(2,1)}), bf16[128,4,1024]{0,2,1:T(8,128)(2,1)S(1)}, u32[]{:S(2)}, u32[]{:S(2)}) async-start(bf16[128,4,1024]{0,2,1:T(8,128)(2,1)} %bitcast), calls=%async_computation | async-start | bytes 2097152 | tf_op jit(solution)/shard_map/all_to_all | solution.py:18
  14.0 256.9 %all-gather.2.cloned.1.call-start = ((), (), s32[]{:S(2)}) async-start(), calls=%async_computation.5 | async-start | bytes 9830400 | tf_op jit(solution)/shard_map/all_gather | solution.py:20
  50.0 27.1 %all-to-all-start.1 = ((bf16[4,4,4,80]{3,0,1,2:T(4,128)(2,1)}), bf16[4,4,4,80]{3,0,1,2:T(4,128)(2,1)S(1)}, u32[]{:S(2)}, u32[]{:S(2)}) async-start(bf16[4,4,4,80]{3,0,1,2:T(4,128)(2,1)} %copy.67), calls=%async_computation.1 | async-start | bytes 32768 | tf_op jit(solution)/shard_map/all_to_all | solution.py:44
  77.1 62.8 %all-to-all-start.2 = ((bf16[4,4,2,80,1024]{4,3,2,1,0:T(8,128)(2,1)}), bf16[4,4,2,80,1024]{4,3,2,1,0:T(8,128)(2,1)}, u32[]{:S(2)}, u32[]{:S(2)}) async-start(bf16[4,4,2,80,1024]{4,3,2,1,0:T(8,128)(2,1)} %copy.70), calls=%async_computation.2 | async-start | bytes 10485760 | tf_op jit(solution)/shard_map/all_to_all | solution.py:60
  139.9 130.9 %all-to-all-start.3 = ((bf16[4,4,2,80,1024]{4,3,2,1,0:T(8,128)(2,1)}), bf16[4,4,2,80,1024]{4,3,2,1,0:T(8,128)(2,1)}, u32[]{:S(2)}, u32[]{:S(2)}) async-start(bf16[4,4,2,80,1024]{4,3,2,1,0:T(8,128)(2,1)} %copy.73), calls=%async_computation.3 | async-start | bytes 10485760 | tf_op jit(solution)/shard_map/all_to_all | solution.py:60
  154.8 3.1 copy-start
  159.1 46.0 %collective-permute-start = (bf16[2,320,768]{2,1,0:T(8,128)(2,1)}, bf16[2,320,768]{2,1,0:T(8,128)(2,1)S(1)}, u32[]{:S(2)}, u32[]{:S(2)}) collective-permute-start(bf16[2,320,768]{2,1,0:T(8,128)(2,1)} %get-tuple-element.26), channel_id=1, source_target_pairs={{0,8},{8,16},{16,24},{24,0},{1,9},{9,17},{17,25},{25,1},{2,10},{10... | collective-permute-start | bytes 2949128 | tf_op jit(solution)/shard_map/ppermute | solution.py:71
  160.2 65.9 %collective-permute-start.2 = (bf16[2,320,768]{2,1,0:T(8,128)(2,1)S(1)}, bf16[2,320,768]{2,1,0:T(8,128)(2,1)}, u32[]{:S(2)}, u32[]{:S(2)}) collective-permute-start(bf16[2,320,768]{2,1,0:T(8,128)(2,1)S(1)} %get-tuple-element.27), channel_id=1, source_target_pairs={{0,24},{8,0},{16,8},{24,16},{1,25},{9,1},{17,9},{25,17},{2,26},{10... | collective-permute-start | bytes 2949128 | tf_op jit(solution)/shard_map/ppermute | solution.py:71
  160.5 107.7 %collective-permute-start.1 = (bf16[2,320,768]{2,1,0:T(8,128)(2,1)S(1)}, bf16[2,320,768]{2,1,0:T(8,128)(2,1)}, u32[]{:S(2)}, u32[]{:S(2)}) collective-permute-start(bf16[2,320,768]{2,1,0:T(8,128)(2,1)S(1)} %get-tuple-element.28), channel_id=1, source_target_pairs={{0,16},{8,24},{16,0},{24,8},{1,17},{9,25},{17,1},{25,9},{2,18},{10... | collective-permute-start | bytes 2949128 | tf_op jit(solution)/shard_map/ppermute | solution.py:71
  278.6 10.3 %slice-start.2 = ((s8[7864320]{0:T(1024)(128)(4,1)}), s8[4194304]{0:T(1024)(128)(4,1)S(1)}, s32[]{:S(2)}) async-start(s8[7864320]{0:T(1024)(128)(4,1)} %bitcast.143), calls=%async_computation.8 | async-start | bytes 8388608
  279.0 9.9 %slice-start.3 = ((s8[7864320]{0:T(1024)(128)(4,1)}), s8[3670016]{0:T(1024)(128)(4,1)S(1)}, s32[]{:S(2)}) async-start(s8[7864320]{0:T(1024)(128)(4,1)} %bitcast.143), calls=%async_computation.9 | async-start | bytes 7340032
  280.5 101.9 %collective-permute-start.3 = (bf16[2,320,768]{2,1,0:T(8,128)(2,1)}, bf16[2,320,768]{2,1,0:T(8,128)(2,1)S(1)}, u32[]{:S(2)}, u32[]{:S(2)}) collective-permute-start(bf16[2,320,768]{2,1,0:T(8,128)(2,1)} %get-tuple-element.29), channel_id=1, source_target_pairs={{0,8},{8,16},{16,24},{24,0},{1,9},{9,17},{17,25},{25,1},{2,10},{10... | collective-permute-start | bytes 2949128 | tf_op jit(solution)/shard_map/ppermute | solution.py:71
  283.6 98.8 %collective-permute-start.5 = (bf16[2,320,768]{2,1,0:T(8,128)(2,1)}, bf16[2,320,768]{2,1,0:T(8,128)(2,1)S(1)}, u32[]{:S(2)}, u32[]{:S(2)}) collective-permute-start(bf16[2,320,768]{2,1,0:T(8,128)(2,1)} %get-tuple-element.30), channel_id=1, source_target_pairs={{0,24},{8,0},{16,8},{24,16},{1,25},{9,1},{17,9},{25,17},{2,26},{10... | collective-permute-start | bytes 2949128 | tf_op jit(solution)/shard_map/ppermute | solution.py:71
  283.8 98.7 %collective-permute-start.4 = (bf16[2,320,768]{2,1,0:T(8,128)(2,1)S(1)}, bf16[2,320,768]{2,1,0:T(8,128)(2,1)}, u32[]{:S(2)}, u32[]{:S(2)}) collective-permute-start(bf16[2,320,768]{2,1,0:T(8,128)(2,1)S(1)} %get-tuple-element.31), channel_id=1, source_target_pairs={{0,16},{8,24},{16,0},{24,8},{1,17},{9,25},{17,1},{25,9},{2,18},{10... | collective-permute-start | bytes 2949128 | tf_op jit(solution)/shard_map/ppermute | solution.py:71
  284.1 4.9 %slice-start = ((s8[7864320]{0:T(1024)(128)(4,1)}), s8[4194304]{0:T(1024)(128)(4,1)S(1)}, s32[]{:S(2)}) async-start(s8[7864320]{0:T(1024)(128)(4,1)} %bitcast.136), calls=%async_computation.6 | async-start | bytes 8388608
  284.1 5.9 %slice-start.1 = ((s8[7864320]{0:T(1024)(128)(4,1)}), s8[3670016]{0:T(1024)(128)(4,1)S(1)}, s32[]{:S(2)}) async-start(s8[7864320]{0:T(1024)(128)(4,1)} %bitcast.136), calls=%async_computation.7 | async-start | bytes 7340032
  293.4 53.2 %collective-permute-start.6 = (f32[4,320]{1,0:T(4,128)S(1)}, f32[4,320]{1,0:T(4,128)S(1)}, u32[]{:S(2)}, u32[]{:S(2)}) collective-permute-start(f32[4,320]{1,0:T(4,128)S(1)} %get-tuple-element.36), channel_id=1, source_target_pairs={{0,8},{8,16},{16,24},{24,0},{1,9},{9,17},{17,25},{25,1},{2,10},{10... | collective-permute-start | bytes 15368 | tf_op jit(solution)/shard_map/ppermute | solution.py:86
  296.5 70.4 %copy-start.1 = (bf16[4,2,320,768]{3,2,1,0:T(8,128)(2,1)S(1)}, bf16[4,2,320,768]{3,2,1,0:T(8,128)(2,1)}, u32[]{:S(2)}) copy-start(bf16[4,2,320,768]{3,2,1,0:T(8,128)(2,1)} %get-tuple-element.22) | copy-start | bytes 11796484
  306.2 68.8 %collective-permute-start.7 = (f32[4,320]{1,0:T(4,128)S(1)}, f32[4,320]{1,0:T(4,128)S(1)}, u32[]{:S(2)}, u32[]{:S(2)}) collective-permute-start(f32[4,320]{1,0:T(4,128)S(1)} %get-tuple-element.37), channel_id=1, source_target_pairs={{0,16},{8,24},{16,0},{24,8},{1,17},{9,25},{17,1},{25,9},{2,18},{10... | collective-permute-start | bytes 15368 | tf_op jit(solution)/shard_map/ppermute | solution.py:86
  346.6 28.4 %collective-permute-start.8 = (f32[4,320]{1,0:T(4,128)S(1)}, f32[4,320]{1,0:T(4,128)S(1)}, u32[]{:S(2)}, u32[]{:S(2)}) collective-permute-start(f32[4,320]{1,0:T(4,128)S(1)} %get-tuple-element.38), channel_id=1, source_target_pairs={{0,24},{8,0},{16,8},{24,16},{1,25},{9,1},{17,9},{25,17},{2,26},{10... | collective-permute-start | bytes 15368 | tf_op jit(solution)/shard_map/ppermute | solution.py:86
  375.0 7.4 %collective-permute-start.9 = (f32[4,320]{1,0:T(4,128)S(1)}, f32[4,320]{1,0:T(4,128)S(1)}, u32[]{:S(2)}, u32[]{:S(2)}) collective-permute-start(f32[4,320]{1,0:T(4,128)S(1)} %fusion.72), channel_id=1, source_target_pairs={{0,1},{1,0},{2,3},{3,2},{4,5},{5,4},{6,7},{7,6},{8,9},{9,8},{10,11... | collective-permute-start | bytes 15368 | tf_op jit(solution)/shard_map/ppermute | solution.py:91
  382.5 0.9 copy-start.2
  387.5 11.9 %all-to-all-start.4 = ((f32[4,4,80]{2,0,1:T(4,128)}), f32[4,4,80]{2,0,1:T(4,128)S(1)}, u32[]{:S(2)}, u32[]{:S(2)}) async-start(f32[4,4,80]{2,0,1:T(4,128)} %copy.80), calls=%async_computation.4 | async-start | bytes 16384 | tf_op jit(solution)/shard_map/all_to_all | solution.py:94
Sparse Core Ops, SparseCore 0:
  42.3 162.5 all-gather.1

commit v7 on v6

--- a/solution.py
+++ b/solution.py
@@ -63,12 +63,8 @@
         partial = jnp.einsum(
             "qglsd,lfd->glqsf", received, down_weight[local], preferred_element_type=jnp.float32
         ).reshape(groups, per, slot_rows_all, ff_part)
-        sent = partial.astype(jnp.bfloat16)
-        expert_grad = lax.dynamic_index_in_dim(partial, me, 0, keepdims=False)
-        for shift in range(1, groups):
-            chunk = lax.dynamic_index_in_dim(sent, (me + shift) % groups, 0, keepdims=False)
-            pairs = [(i, (i + shift) % groups) for i in range(groups)]
-            expert_grad = expert_grad + lax.ppermute(chunk, "dp", pairs).astype(jnp.float32)
+        arrived = lax.all_to_all(partial.astype(jnp.bfloat16), "dp", split_axis=0, concat_axis=0, tiled=True)
+        expert_grad = jnp.sum(arrived.astype(jnp.float32), axis=0)
         hidden_rows = hidden_all[:, local].astype(jnp.float32)
         dots.append(jnp.sum(hidden_rows * partial, axis=3))
         scaled = (jnp.moveaxis(slot_gates[local], 0, 1)[..., None] * hidden_rows).astype(jnp.bfloat16)

time: 413 us -> 434 us (1.051)
  waiting for transfers between devices: 193 us -> 231 us
  starting transfers between devices: 61.4 us -> 45.5 us
    ppermute x6 -> x0, waiting for transfers between devices: 107 us -> none  [body(): lax.ppermute(chunk, 'dp', pairs).astype(jnp.float32)]
    all_to_all x0 -> x2, waiting for transfers between devices: none -> 60.9 us  [body(): lax.all_to_all(partial.astype(jnp.bfloat16), 'dp', split_axis=0, concat_a...]
    all_to_all x2, waiting for transfers between devices: 47.1 us -> 90.6 us  [body(): lax.all_to_all(picked, 'expert', split_axis=0, concat_axis=0, tiled=True)]
    ppermute x3, starting transfers between devices: 24.7 us -> 1.8 us  [body(): own_dots = own_dots + lax.ppermute(chunk, 'dp', pairs)]
    all_gather x1, waiting for transfers between devices: 0.02 us -> 22.8 us  [body(): hidden_all = lax.all_gather(hidden_saved, 'dp', axis=0, tiled=True)]
    ppermute x3, waiting for transfers between devices: 38.9 us -> 56.2 us  [body(): own_dots = own_dots + lax.ppermute(chunk, 'dp', pairs)]
    all_to_all x0 -> x2, starting transfers between devices: none -> 13.7 us  [body(): lax.all_to_all(partial.astype(jnp.bfloat16), 'dp', split_axis=0, concat_a...]
    reduce_sum x0 -> x2, other arithmetic: none -> 6.01 us  [body(): expert_grad = jnp.sum(arrived.astype(jnp.float32), axis=0)]
  transfers between devices with their start and end apart: 16 -> 12, of which waited for: 5 -> 6; matrix products, arithmetic and copies ran while one was open for 22% -> 19% of each run, Pallas kernels for 0% -> 0%
where the time goes in v7:
time: 434 us; the launch traced here: 431 us
  waiting for transfers between devices  231 us (53%)
  other arithmetic  46 us (11%)
  starting transfers between devices  45.5 us (10%)
  matrix products  37.7 us (9%)
  local copies, waits for them, and re-layouts  29.9 us (7%)
  blocking collectives  26.2 us (6%)
  between operations  14.3 us (3%)
    all_to_all x2, waiting for transfers between devices, body(): lax.all_to_all(picked, 'expert', split_axis=0, concat_axis=0, tiled=True)  90.6 us
    all_to_all x2, waiting for transfers between devices, body(): lax.all_to_all(partial.astype(jnp.bfloat16), 'dp', split_axis=0, concat_a...  60.9 us
    ppermute x3, waiting for transfers between devices, body(): own_dots = own_dots + lax.ppermute(chunk, 'dp', pairs)  56.2 us
    all_gather x1, blocking collectives, body(): all_meta = lax.all_gather(meta, 'dp', axis=0, tiled=True)  26.2 us
    all_gather x1, waiting for transfers between devices, body(): hidden_all = lax.all_gather(hidden_saved, 'dp', axis=0, tiled=True)  22.8 us
    dot_general x2, matrix products, body(): jnp.einsum('qglsd,lfd->glqsf', received, down_weight[local], preferred_el...  14.3 us
    dot_general x2, matrix products, body(): jnp.einsum('glqsf,qglsd->lfd', scaled, received, preferred_element_type=j...  14.1 us
    all_to_all x2, starting transfers between devices, body(): lax.all_to_all(partial.astype(jnp.bfloat16), 'dp', split_axis=0, concat_a...  13.7 us
  transfers between devices with their start and end apart: 12, of which 6 were waited for; matrix products, arithmetic and copies ran while one was open for 19% of the time, Pallas kernels for 0%

profile of v7, /device:TPU:29, one launch (start us, length us, event | category | flops | bytes accessed | tf_op | source)
XLA Modules:
  0.0 430.8 jit_solution(16285758022632227555)
XLA Ops:
  9.4 4.5 %all-to-all-start = ((bf16[128,4,1024]{0,2,1:T(8,128)(2,1)}), bf16[128,4,1024]{0,2,1:T(8,128)(2,1)S(1)}, u32[]{:S(2)}, u32[]{:S(2)}) async-start(bf16[128,4,1024]{0,2,1:T(8,128)(2,1)} %bitcast), calls=%async_computation | async-start | bytes 2097152 | tf_op jit(solution)/shard_map/all_to_all | solution.py:18
  15.3 26.2 %all_gather.6 = f32[512,16]{0,1:T(8,128)S(1)} all-gather(f32[128,16]{0,1:T(8,128)S(1)} %pad_maximum_fusion.1), channel_id=1, replica_groups=mesh['dp'=4,'expert'=4,'etp'=2] {'dp'}, dimensions={0}, use_global_device_ids=true | all-gather | bytes 40960 | tf_op jit(solution)/shard_map/all_gather | solution.py:17
  43.7 6.3 %fusion.33 = bf16[4,128,1280]{2,1,0:T(8,128)(2,1)S(1)} fusion(s32[4,128,8]{2,1,0:T(8,128)S(1)} %fusion.50), kind=kLoop, calls=%fused_computation.38 | loop fusion | flops 15073280 | bytes 1327104 | tf_op jit(solution)/shard_map/reduce_sum | solution.py:38
  50.0 5.6 %fusion.1 = bf16[4,1,1280,1]{2,1,3,0:T(2,128)(2,1)S(1)} fusion(bf16[4,128,8,1]{2,3,1,0:T(2,128)(2,1)S(1)} %copy.83, s32[4,128,8]{2,1,0:T(8,128)S(1)} %fusion.50), kind=kOutput, calls=%fused_computation.2 | convolution fusion | flops 15728640 | bytes 34816 | tf_op jit(solution)/shard_map/gtk,gtkr->gr/dot_general | solution.py:37
  56.4 6.8 %all-to-all-start.1 = ((bf16[4,4,4,80]{3,0,1,2:T(4,128)(2,1)}), bf16[4,4,4,80]{3,0,1,2:T(4,128)(2,1)S(1)}, u32[]{:S(2)}, u32[]{:S(2)}) async-start(bf16[4,4,4,80]{3,0,1,2:T(4,128)(2,1)} %copy.67), calls=%async_computation.1 | async-start | bytes 32768 | tf_op jit(solution)/shard_map/all_to_all | solution.py:44
  70.7 5.8 %copy.70 = bf16[4,4,2,80,1024]{4,3,2,1,0:T(8,128)(2,1)} copy(bf16[4,4,2,80,1024]{4,3,0,2,1:T(8,128)(2,1)} %convert_bitcast_fusion.1) | data formatting | bytes 10485760 | tf_op jit(solution)/shard_map/convert_element_type | solution.py:59
  76.5 5.2 %all-to-all-start.2 = ((bf16[4,4,2,80,1024]{4,3,2,1,0:T(8,128)(2,1)}), bf16[4,4,2,80,1024]{4,3,2,1,0:T(8,128)(2,1)}, u32[]{:S(2)}, u32[]{:S(2)}) async-start(bf16[4,4,2,80,1024]{4,3,2,1,0:T(8,128)(2,1)} %copy.70), calls=%async_computation.2 | async-start | bytes 10485760 | tf_op jit(solution)/shard_map/all_to_all | solution.py:60
  87.1 5.8 %copy.73 = bf16[4,4,2,80,1024]{4,3,2,1,0:T(8,128)(2,1)} copy(bf16[4,4,2,80,1024]{4,3,0,2,1:T(8,128)(2,1)} %convert_bitcast_fusion) | data formatting | bytes 10485760 | tf_op jit(solution)/shard_map/convert_element_type | solution.py:59
  92.9 46.4 %all-to-all-done.2 = bf16[4,4,2,80,1024]{4,3,2,1,0:T(8,128)(2,1)} async-done(((bf16[4,4,2,80,1024]{4,3,2,1,0:T(8,128)(2,1)}), bf16[4,4,2,80,1024]{4,3,2,1,0:T(8,128)(2,1)}, u32[]{:S(2)}, u32[]{:S(2)}) %all-to-all-start.2) | async-done | bytes 5242912 | tf_op jit(solution)/shard_map/all_to_all | solution.py:60
  139.3 7.0 %all-to-all-start.4 = ((bf16[4,4,2,80,1024]{4,3,2,1,0:T(8,128)(2,1)}), bf16[4,4,2,80,1024]{4,3,2,1,0:T(8,128)(2,1)}, u32[]{:S(2)}, u32[]{:S(2)}) async-start(bf16[4,4,2,80,1024]{4,3,2,1,0:T(8,128)(2,1)} %copy.73), calls=%async_computation.4 | async-start | bytes 10485760 | tf_op jit(solution)/shard_map/all_to_all | solution.py:60
  146.3 7.2 %fusion.23 = f32[4,2,4,80,768]{4,3,0,2,1:T(8,128)S(1)} fusion(bf16[4,768,1024]{2,1,0:T(8,128)(2,1)} %param.9, bf16[4,4,2,80,1024]{4,3,2,1,0:T(8,128)(2,1)} %all-to-all-done.2), kind=kOutput, calls=%fused_computation.36 | convolution fusion | flops 4026531840 | bytes 16252928 | tf_op jit(solution)/shard_map/qglsd,lfd->glqsf/dot_general | solution.py:63
  159.6 44.2 %all-to-all-done.4 = bf16[4,4,2,80,1024]{4,3,2,1,0:T(8,128)(2,1)} async-done(((bf16[4,4,2,80,1024]{4,3,2,1,0:T(8,128)(2,1)}), bf16[4,4,2,80,1024]{4,3,2,1,0:T(8,128)(2,1)}, u32[]{:S(2)}, u32[]{:S(2)}) %all-to-all-start.4) | async-done | bytes 5242912 | tf_op jit(solution)/shard_map/all_to_all | solution.py:60
  203.9 5.9 %all-to-all-start.3 = ((bf16[4,2,320,768]{3,2,1,0:T(8,128)(2,1)}), bf16[4,2,320,768]{3,2,1,0:T(8,128)(2,1)}, u32[]{:S(2)}, u32[]{:S(2)}) async-start(bf16[4,2,320,768]{3,2,1,0:T(8,128)(2,1)} %bitcast_convert_fusion.4), calls=%async_computation.3 | async-start | bytes 7864320 | tf_op jit(solution)/shard_map/all_to_all | solution.py:66
  209.9 22.8 %all-gather.2.cloned.1.call-done = bf16[4,4,320,768]{3,2,1,0:T(8,128)(2,1)} async-done(((bf16[1,4,320,768]{3,2,1,0:T(8,128)(2,1)}), bf16[4,4,320,768]{3,2,1,0:T(8,128)(2,1)}) %all-gather.2.cloned.1.call-update) | async-done | bytes 7864336 | tf_op jit(solution)/shard_map/all_gather | solution.py:20
  232.7 7.2 %fusion.28 = f32[4,2,4,80,768]{4,3,0,2,1:T(8,128)S(1)} fusion(bf16[4,768,1024]{2,1,0:T(8,128)(2,1)} %param.9, bf16[4,4,2,80,1024]{4,3,2,1,0:T(8,128)(2,1)} %all-to-all-done.4), kind=kOutput, calls=%fused_computation.37 | convolution fusion | flops 4026531840 | bytes 16252928 | tf_op jit(solution)/shard_map/qglsd,lfd->glqsf/dot_general | solution.py:63
  246.1 60.9 %all-to-all-done.3 = bf16[4,2,320,768]{3,2,1,0:T(8,128)(2,1)} async-done(((bf16[4,2,320,768]{3,2,1,0:T(8,128)(2,1)}), bf16[4,2,320,768]{3,2,1,0:T(8,128)(2,1)}, u32[]{:S(2)}, u32[]{:S(2)}) %all-to-all-start.3) | async-done | bytes 3932192 | tf_op jit(solution)/shard_map/all_to_all | solution.py:66
  306.9 7.8 %all-to-all-start.5 = ((bf16[4,2,320,768]{3,2,1,0:T(8,128)(2,1)}), bf16[4,2,320,768]{3,2,1,0:T(8,128)(2,1)}, u32[]{:S(2)}, u32[]{:S(2)}) async-start(bf16[4,2,320,768]{3,2,1,0:T(8,128)(2,1)} %bitcast_convert_fusion.3), calls=%async_computation.5 | async-start | bytes 7864320 | tf_op jit(solution)/shard_map/all_to_all | solution.py:66
  318.1 5.6 %fusion.6 = (bf16[4,2,320,768]{3,2,1,0:T(8,128)(2,1)S(1)}, f32[4,2,320]{2,1,0:T(2,128)S(1)}) fusion(f32[4,2,320]{2,1,0:T(2,128)S(1)} %copy.78, bf16[4,4,320,768]{3,2,1,0:T(8,128)(2,1)} %all-gather.2.cloned.1.call-done, f32[4,2,320,768]{3,2,1,0:T(8,128)} %bitcast.106), kind=kLoop, calls=%fused_computation.11 | loop fusion | flops 9827840 | bytes 15749120 | tf_op jit(solution)/shard_map/convert_element_type | solution.py:70
  329.9 7.0 %bitcast_convert_fusion = bf16[2,768,1024]{2,1,0:T(8,128)(2,1)S(1)} fusion(bf16[4,2,4,80,768]{4,3,2,1,0:T(8,128)(2,1)S(1)} %bitcast.115, bf16[4,4,2,80,1024]{4,3,2,1,0:T(8,128)(2,1)} %all-to-all-done.4), kind=kOutput, calls=%fused_computation.15 | convolution fusion | flops 4028104704 | bytes 12320768 | tf_op jit(solution)/shard_map/glqsf,qglsd->lfd/dot_general | solution.py:72
  336.9 7.0 %bitcast_convert_fusion.1 = bf16[2,768,1024]{2,1,0:T(8,128)(2,1)S(1)} fusion(bf16[4,2,4,80,768]{4,3,2,1,0:T(8,128)(2,1)S(1)} %bitcast.116, bf16[4,4,2,80,1024]{4,3,2,1,0:T(8,128)(2,1)} %all-to-all-done.2), kind=kOutput, calls=%fused_computation.16 | convolution fusion | flops 4028104704 | bytes 12320768 | tf_op jit(solution)/shard_map/glqsf,qglsd->lfd/dot_general | solution.py:72
  344.0 33.7 %collective-permute-done = f32[4,320]{1,0:T(4,128)S(1)} collective-permute-done((f32[4,320]{1,0:T(4,128)S(1)}, f32[4,320]{1,0:T(4,128)S(1)}, u32[]{:S(2)}, u32[]{:S(2)}) %collective-permute-start) | collective-permute-done | bytes 5152 | tf_op jit(solution)/shard_map/ppermute | solution.py:82
  377.7 22.4 %collective-permute-done.1 = f32[4,320]{1,0:T(4,128)S(1)} collective-permute-done((f32[4,320]{1,0:T(4,128)S(1)}, f32[4,320]{1,0:T(4,128)S(1)}, u32[]{:S(2)}, u32[]{:S(2)}) %collective-permute-start.1) | collective-permute-done | bytes 5152 | tf_op jit(solution)/shard_map/ppermute | solution.py:82
  410.0 5.1 %all-to-all-start.6 = ((f32[4,4,80]{2,0,1:T(4,128)}), f32[4,4,80]{2,0,1:T(4,128)S(1)}, u32[]{:S(2)}, u32[]{:S(2)}) async-start(f32[4,4,80]{2,0,1:T(4,128)} %copy.80), calls=%async_computation.6 | async-start | bytes 16384 | tf_op jit(solution)/shard_map/all_to_all | solution.py:90
  415.1 5.7 %fusion = bf16[4,128,8,1280]{3,2,1,0:T(8,128)(2,1)} fusion(s32[4,128,8]{2,1,0:T(8,128)S(1)} %fusion.50), kind=kLoop, calls=%fused_computation.1 | loop fusion | flops 10485760 | bytes 10502144 | tf_op jit(solution)/shard_map/convert_element_type | solution.py:35
  (78 shorter events, 54.0 us)
Async XLA Ops:
  9.4 32.2 %all-to-all-start = ((bf16[128,4,1024]{0,2,1:T(8,128)(2,1)}), bf16[128,4,1024]{0,2,1:T(8,128)(2,1)S(1)}, u32[]{:S(2)}, u32[]{:S(2)}) async-start(bf16[128,4,1024]{0,2,1:T(8,128)(2,1)} %bitcast), calls=%async_computation | async-start | bytes 2097152 | tf_op jit(solution)/shard_map/all_to_all | solution.py:18
  56.4 20.1 %all-to-all-start.1 = ((bf16[4,4,4,80]{3,0,1,2:T(4,128)(2,1)}), bf16[4,4,4,80]{3,0,1,2:T(4,128)(2,1)S(1)}, u32[]{:S(2)}, u32[]{:S(2)}) async-start(bf16[4,4,4,80]{3,0,1,2:T(4,128)(2,1)} %copy.67), calls=%async_computation.1 | async-start | bytes 32768 | tf_op jit(solution)/shard_map/all_to_all | solution.py:44
  76.5 62.8 %all-to-all-start.2 = ((bf16[4,4,2,80,1024]{4,3,2,1,0:T(8,128)(2,1)}), bf16[4,4,2,80,1024]{4,3,2,1,0:T(8,128)(2,1)}, u32[]{:S(2)}, u32[]{:S(2)}) async-start(bf16[4,4,2,80,1024]{4,3,2,1,0:T(8,128)(2,1)} %copy.70), calls=%async_computation.2 | async-start | bytes 10485760 | tf_op jit(solution)/shard_map/all_to_all | solution.py:60
  81.7 151.0 %all-gather.2.cloned.1.call-start = ((), (), s32[]{:S(2)}) async-start(), calls=%async_computation.7 | async-start | bytes 9830400 | tf_op jit(solution)/shard_map/all_gather | solution.py:20
  139.3 64.6 %all-to-all-start.4 = ((bf16[4,4,2,80,1024]{4,3,2,1,0:T(8,128)(2,1)}), bf16[4,4,2,80,1024]{4,3,2,1,0:T(8,128)(2,1)}, u32[]{:S(2)}, u32[]{:S(2)}) async-start(bf16[4,4,2,80,1024]{4,3,2,1,0:T(8,128)(2,1)} %copy.73), calls=%async_computation.4 | async-start | bytes 10485760 | tf_op jit(solution)/shard_map/all_to_all | solution.py:60
  154.2 3.2 copy-start
  203.9 103.1 %all-to-all-start.3 = ((bf16[4,2,320,768]{3,2,1,0:T(8,128)(2,1)}), bf16[4,2,320,768]{3,2,1,0:T(8,128)(2,1)}, u32[]{:S(2)}, u32[]{:S(2)}) async-start(bf16[4,2,320,768]{3,2,1,0:T(8,128)(2,1)} %bitcast_convert_fusion.4), calls=%async_computation.3 | async-start | bytes 7864320 | tf_op jit(solution)/shard_map/all_to_all | solution.py:66
  240.6 3.2 copy-start.1
  306.9 97.8 %all-to-all-start.5 = ((bf16[4,2,320,768]{3,2,1,0:T(8,128)(2,1)}), bf16[4,2,320,768]{3,2,1,0:T(8,128)(2,1)}, u32[]{:S(2)}, u32[]{:S(2)}) async-start(bf16[4,2,320,768]{3,2,1,0:T(8,128)(2,1)} %bitcast_convert_fusion.3), calls=%async_computation.5 | async-start | bytes 7864320 | tf_op jit(solution)/shard_map/all_to_all | solution.py:66
  314.8 8.9 %slice-start.2 = ((s8[7864320]{0:T(1024)(128)(4,1)}), s8[4194304]{0:T(1024)(128)(4,1)S(1)}, s32[]{:S(2)}) async-start(s8[7864320]{0:T(1024)(128)(4,1)} %bitcast.109), calls=%async_computation.10 | async-start | bytes 8388608
  318.1 5.6 %slice-start = ((s8[7864320]{0:T(1024)(128)(4,1)}), s8[4194304]{0:T(1024)(128)(4,1)S(1)}, s32[]{:S(2)}) async-start(s8[7864320]{0:T(1024)(128)(4,1)} %bitcast.103), calls=%async_computation.8 | async-start | bytes 8388608
  318.1 6.7 %slice-start.1 = ((s8[7864320]{0:T(1024)(128)(4,1)}), s8[3670016]{0:T(1024)(128)(4,1)S(1)}, s32[]{:S(2)}) async-start(s8[7864320]{0:T(1024)(128)(4,1)} %bitcast.103), calls=%async_computation.9 | async-start | bytes 7340032
  318.1 7.7 %slice-start.3 = ((s8[7864320]{0:T(1024)(128)(4,1)}), s8[3670016]{0:T(1024)(128)(4,1)S(1)}, s32[]{:S(2)}) async-start(s8[7864320]{0:T(1024)(128)(4,1)} %bitcast.109), calls=%async_computation.11 | async-start | bytes 7340032
  328.1 49.6 %collective-permute-start = (f32[4,320]{1,0:T(4,128)S(1)}, f32[4,320]{1,0:T(4,128)S(1)}, u32[]{:S(2)}, u32[]{:S(2)}) collective-permute-start(f32[4,320]{1,0:T(4,128)S(1)} %get-tuple-element.30), channel_id=1, source_target_pairs={{0,8},{8,16},{16,24},{24,0},{1,9},{9,17},{17,25},{25,1},{2,10},{10... | collective-permute-start | bytes 15368 | tf_op jit(solution)/shard_map/ppermute | solution.py:82
  328.2 71.9 %collective-permute-start.1 = (f32[4,320]{1,0:T(4,128)S(1)}, f32[4,320]{1,0:T(4,128)S(1)}, u32[]{:S(2)}, u32[]{:S(2)}) collective-permute-start(f32[4,320]{1,0:T(4,128)S(1)} %get-tuple-element.31), channel_id=1, source_target_pairs={{0,16},{8,24},{16,0},{24,8},{1,17},{9,25},{17,1},{25,9},{2,18},{10... | collective-permute-start | bytes 15368 | tf_op jit(solution)/shard_map/ppermute | solution.py:82
  329.6 70.5 %collective-permute-start.2 = (f32[4,320]{1,0:T(4,128)S(1)}, f32[4,320]{1,0:T(4,128)S(1)}, u32[]{:S(2)}, u32[]{:S(2)}) collective-permute-start(f32[4,320]{1,0:T(4,128)S(1)} %get-tuple-element.32), channel_id=1, source_target_pairs={{0,24},{8,0},{16,8},{24,16},{1,25},{9,1},{17,9},{25,17},{2,26},{10... | collective-permute-start | bytes 15368 | tf_op jit(solution)/shard_map/ppermute | solution.py:82
  400.2 4.5 %collective-permute-start.3 = (f32[4,320]{1,0:T(4,128)S(1)}, f32[4,320]{1,0:T(4,128)S(1)}, u32[]{:S(2)}, u32[]{:S(2)}) collective-permute-start(f32[4,320]{1,0:T(4,128)S(1)} %fusion.64), channel_id=1, source_target_pairs={{0,1},{1,0},{2,3},{3,2},{4,5},{5,4},{6,7},{7,6},{8,9},{9,8},{10,11... | collective-permute-start | bytes 15368 | tf_op jit(solution)/shard_map/ppermute | solution.py:87
  410.0 10.9 %all-to-all-start.6 = ((f32[4,4,80]{2,0,1:T(4,128)}), f32[4,4,80]{2,0,1:T(4,128)S(1)}, u32[]{:S(2)}, u32[]{:S(2)}) async-start(f32[4,4,80]{2,0,1:T(4,128)} %copy.80), calls=%async_computation.6 | async-start | bytes 16384 | tf_op jit(solution)/shard_map/all_to_all | solution.py:90
Sparse Core Ops, SparseCore 0:
  84.1 148.5 all-gather.1

commit v8 on v6

--- a/solution.py
+++ b/solution.py
@@ -49,6 +49,7 @@
     chunks = 2 if exp_dev % 2 == 0 else 1
     per = exp_dev // chunks
     grads, dots, hidden_parts = [], [], []
+    incoming, partials = [], []
     for c in range(chunks):
         local = slice(c * per, (c + 1) * per)
         picked = jnp.einsum(
@@ -58,11 +59,16 @@
             preferred_element_type=jnp.float32,
         ).astype(columns.dtype)
         received = lax.all_to_all(picked, "expert", split_axis=0, concat_axis=0, tiled=True)
-        if c == chunks - 1:
-            hidden_all, received = lax.optimization_barrier((hidden_all, received))
-        partial = jnp.einsum(
-            "qglsd,lfd->glqsf", received, down_weight[local], preferred_element_type=jnp.float32
-        ).reshape(groups, per, slot_rows_all, ff_part)
+        incoming.append(received)
+        partials.append(
+            jnp.einsum(
+                "qglsd,lfd->glqsf", received, down_weight[local], preferred_element_type=jnp.float32
+            ).reshape(groups, per, slot_rows_all, ff_part)
+        )
+    partials = list(lax.optimization_barrier(tuple(partials)))
+    for c in range(chunks):
+        local = slice(c * per, (c + 1) * per)
+        partial, received = partials[c], incoming[c]
         sent = partial.astype(jnp.bfloat16)
         expert_grad = lax.dynamic_index_in_dim(partial, me, 0, keepdims=False)
         for shift in range(1, groups):

time: 413 us -> 439 us (1.063)
  waiting for transfers between devices: 193 us -> 236 us
  starting transfers between devices: 61.4 us -> 40.7 us
  other arithmetic: 44.8 us -> 52.4 us
    all_to_all x2, waiting for transfers between devices: 47.1 us -> 93.7 us  [body(): lax.all_to_all(picked, 'expert', split_axis=0, concat_axis=0, tiled=True)]
    ppermute x3, waiting for transfers between devices: 38.9 us -> 0.01 us  [body(): own_dots = own_dots + lax.ppermute(chunk, 'dp', pairs)]
    ppermute x6, waiting for transfers between devices: 107 us -> 143 us  [body(): lax.ppermute(chunk, 'dp', pairs).astype(jnp.float32)]
    ppermute x3, starting transfers between devices: 24.7 us -> 1.74 us  [body(): own_dots = own_dots + lax.ppermute(chunk, 'dp', pairs)]
    convert_element_type x2 -> x1, other arithmetic: 8.27 us -> 18.5 us  [body(): (jnp.moveaxis(slot_gates[local], 0, 1)[..., None] * hidden_rows).astype(j...]
    transpose x2, local copies, waits for them, and re-layouts: 1.23 us -> 7.24 us  [body(): jnp.einsum('qglsd,lfd->glqsf', received, down_weight[local], preferred_el...]
    unnamed x17 -> x7, local copies, waits for them, and re-layouts: 7.62 us -> 2.94 us
  transfers between devices with their start and end apart: 16 -> 16, of which waited for: 5 -> 7; matrix products, arithmetic and copies ran while one was open for 22% -> 20% of each run, Pallas kernels for 0% -> 0%
where the time goes in v8:
time: 439 us; the launch traced here: 435 us
  waiting for transfers between devices  236 us (54%)
  other arithmetic  52.4 us (12%)
  starting transfers between devices  40.7 us (9%)
  matrix products  37.8 us (9%)
  local copies, waits for them, and re-layouts  27.6 us (6%)
  blocking collectives  26.2 us (6%)
  between operations  14.3 us (3%)
    ppermute x6, waiting for transfers between devices, body(): lax.ppermute(chunk, 'dp', pairs).astype(jnp.float32)  143 us
    all_to_all x2, waiting for transfers between devices, body(): lax.all_to_all(picked, 'expert', split_axis=0, concat_axis=0, tiled=True)  93.7 us
    all_gather x1, blocking collectives, body(): all_meta = lax.all_gather(meta, 'dp', axis=0, tiled=True)  26.2 us
    convert_element_type x1, other arithmetic, body(): (jnp.moveaxis(slot_gates[local], 0, 1)[..., None] * hidden_rows).astype(j...  18.5 us
    dot_general x2, matrix products, body(): jnp.einsum('qglsd,lfd->glqsf', received, down_weight[local], preferred_el...  14.4 us
    dot_general x2, matrix products, body(): jnp.einsum('glqsf,qglsd->lfd', scaled, received, preferred_element_type=j...  14.2 us
    all_to_all x2, starting transfers between devices, body(): lax.all_to_all(picked, 'expert', split_axis=0, concat_axis=0, tiled=True)  12.4 us
    convert_element_type x2, local copies, waits for them, and re-layouts, body(): picked = jnp.einsum('gtlqs,gtd->qglsd', token_select[:, :, local], token_...  11.4 us
  transfers between devices with their start and end apart: 16, of which 7 were waited for; matrix products, arithmetic and copies ran while one was open for 20% of the time, Pallas kernels for 0%

profile of v8, /device:TPU:29, one launch (start us, length us, event | category | flops | bytes accessed | tf_op | source)
XLA Modules:
  0.0 435.4 jit_solution(660928245325358197)
XLA Ops:
  9.4 4.5 %all-to-all-start = ((bf16[128,4,1024]{0,2,1:T(8,128)(2,1)}), bf16[128,4,1024]{0,2,1:T(8,128)(2,1)S(1)}, u32[]{:S(2)}, u32[]{:S(2)}) async-start(bf16[128,4,1024]{0,2,1:T(8,128)(2,1)} %bitcast), calls=%async_computation | async-start | bytes 2097152 | tf_op jit(solution)/shard_map/all_to_all | solution.py:18
  15.3 26.2 %all_gather.6 = f32[512,16]{0,1:T(8,128)S(1)} all-gather(f32[128,16]{0,1:T(8,128)S(1)} %pad_maximum_fusion.1), channel_id=1, replica_groups=mesh['dp'=4,'expert'=4,'etp'=2] {'dp'}, dimensions={0}, use_global_device_ids=true | all-gather | bytes 40960 | tf_op jit(solution)/shard_map/all_gather | solution.py:17
  43.7 5.6 %fusion.1 = bf16[4,1,1280,1]{2,1,3,0:T(2,128)(2,1)S(1)} fusion(bf16[4,128,8,1]{2,3,1,0:T(2,128)(2,1)S(1)} %copy.83, s32[4,128,8]{2,1,0:T(8,128)S(1)} %fusion.58), kind=kOutput, calls=%fused_computation.2 | convolution fusion | flops 15728640 | bytes 34816 | tf_op jit(solution)/shard_map/gtk,gtkr->gr/dot_general | solution.py:37
  50.0 6.8 %all-to-all-start.1 = ((bf16[4,4,4,80]{3,0,1,2:T(4,128)(2,1)}), bf16[4,4,4,80]{3,0,1,2:T(4,128)(2,1)S(1)}, u32[]{:S(2)}, u32[]{:S(2)}) async-start(bf16[4,4,4,80]{3,0,1,2:T(4,128)(2,1)} %copy.67), calls=%async_computation.1 | async-start | bytes 32768 | tf_op jit(solution)/shard_map/all_to_all | solution.py:44
  56.9 7.4 %fusion.33 = bf16[4,128,1280]{2,1,0:T(8,128)(2,1)} fusion(s32[4,128,8]{2,1,0:T(8,128)S(1)} %fusion.58), kind=kLoop, calls=%fused_computation.36 | loop fusion | flops 15073280 | bytes 1327104 | tf_op jit(solution)/shard_map/reduce_sum | solution.py:38
  70.9 5.7 %copy.70 = bf16[4,4,2,80,1024]{4,3,2,1,0:T(8,128)(2,1)} copy(bf16[4,4,2,80,1024]{4,3,0,2,1:T(8,128)(2,1)} %convert_bitcast_fusion.1) | data formatting | bytes 10485760 | tf_op jit(solution)/shard_map/convert_element_type | solution.py:60
  76.6 5.3 %all-to-all-start.2 = ((bf16[4,4,2,80,1024]{4,3,2,1,0:T(8,128)(2,1)}), bf16[4,4,2,80,1024]{4,3,2,1,0:T(8,128)(2,1)}, u32[]{:S(2)}, u32[]{:S(2)}) async-start(bf16[4,4,2,80,1024]{4,3,2,1,0:T(8,128)(2,1)} %copy.70), calls=%async_computation.2 | async-start | bytes 10485760 | tf_op jit(solution)/shard_map/all_to_all | solution.py:61
  86.6 5.7 %copy.73 = bf16[4,4,2,80,1024]{4,3,2,1,0:T(8,128)(2,1)} copy(bf16[4,4,2,80,1024]{4,3,0,2,1:T(8,128)(2,1)} %convert_bitcast_fusion) | data formatting | bytes 10485760 | tf_op jit(solution)/shard_map/convert_element_type | solution.py:60
  92.3 47.1 %all-to-all-done.2 = bf16[4,4,2,80,1024]{4,3,2,1,0:T(8,128)(2,1)} async-done(((bf16[4,4,2,80,1024]{4,3,2,1,0:T(8,128)(2,1)}), bf16[4,4,2,80,1024]{4,3,2,1,0:T(8,128)(2,1)}, u32[]{:S(2)}, u32[]{:S(2)}) %all-to-all-start.2) | async-done | bytes 5242912 | tf_op jit(solution)/shard_map/all_to_all | solution.py:61
  139.4 7.1 %all-to-all-start.3 = ((bf16[4,4,2,80,1024]{4,3,2,1,0:T(8,128)(2,1)}), bf16[4,4,2,80,1024]{4,3,2,1,0:T(8,128)(2,1)}, u32[]{:S(2)}, u32[]{:S(2)}) async-start(bf16[4,4,2,80,1024]{4,3,2,1,0:T(8,128)(2,1)} %copy.73), calls=%async_computation.3 | async-start | bytes 10485760 | tf_op jit(solution)/shard_map/all_to_all | solution.py:61
  146.7 7.2 %fusion.23 = f32[4,2,4,80,768]{4,3,0,2,1:T(8,128)S(1)} fusion(bf16[4,768,1024]{2,1,0:T(8,128)(2,1)} %param.9, bf16[4,4,2,80,1024]{4,3,2,1,0:T(8,128)(2,1)} %all-to-all-done.2), kind=kOutput, calls=%fused_computation.34 | convolution fusion | flops 4026531840 | bytes 16252928 | tf_op jit(solution)/shard_map/qglsd,lfd->glqsf/dot_general | solution.py:64
  157.4 46.6 %all-to-all-done.3 = bf16[4,4,2,80,1024]{4,3,2,1,0:T(8,128)(2,1)} async-done(((bf16[4,4,2,80,1024]{4,3,2,1,0:T(8,128)(2,1)}), bf16[4,4,2,80,1024]{4,3,2,1,0:T(8,128)(2,1)}, u32[]{:S(2)}, u32[]{:S(2)}) %all-to-all-start.3) | async-done | bytes 5242912 | tf_op jit(solution)/shard_map/all_to_all | solution.py:61
  204.1 7.2 %fusion.28 = f32[4,2,4,80,768]{4,3,0,2,1:T(8,128)S(1)} fusion(bf16[4,768,1024]{2,1,0:T(8,128)(2,1)} %param.9, bf16[4,4,2,80,1024]{4,3,2,1,0:T(8,128)(2,1)} %all-to-all-done.3), kind=kOutput, calls=%fused_computation.35 | convolution fusion | flops 4026531840 | bytes 16252928 | tf_op jit(solution)/shard_map/qglsd,lfd->glqsf/dot_general | solution.py:64
  211.2 3.7 copy.75
  214.9 18.5 %fusion.4 = (bf16[4,2,320,768]{3,2,1,0:T(8,128)(2,1)}, bf16[4,2,320,768]{3,2,1,0:T(8,128)(2,1)}, f32[4,2,320]{2,1,0:T(2,128)S(1)}, f32[4,2,320]{2,1,0:T(2,128)S(...) fusion(f32[4,2,320]{2,1,0:T(2,128)S(1)} %copy.76, ...), kind=kLoop, calls=%fused_computation.9 | loop fusion | flops 23587840 | bytes 39362560 | tf_op jit(solution)/shard_map/convert_element_type | solution.py:80
  244.2 7.2 %bitcast_convert_fusion.1 = bf16[2,768,1024]{2,1,0:T(8,128)(2,1)S(1)} fusion(bf16[4,2,4,80,768]{4,3,2,1,0:T(8,128)(2,1)S(1)} %bitcast.144, bf16[4,4,2,80,1024]{4,3,2,1,0:T(8,128)(2,1)} %all-to-all-done.2), kind=kOutput, calls=%fused_computation.14 | convolution fusion | flops 4028104704 | bytes 12320768 | tf_op jit(solution)/shard_map/glqsf,qglsd->lfd/dot_general | solution.py:82
  251.5 8.4 %collective-permute-done.3 = bf16[2,320,768]{2,1,0:T(8,128)(2,1)S(1)} collective-permute-done((bf16[2,320,768]{2,1,0:T(8,128)(2,1)}, bf16[2,320,768]{2,1,0:T(8,128)(2,1)S(1)}, u32[]{:S(2)}, u32[]{:S(2)}) %collective-permute-start.3) | collective-permute-done | bytes 983072 | tf_op jit(solution)/shard_map/ppermute | solution.py:77
  260.9 7.0 %bitcast_convert_fusion = bf16[2,768,1024]{2,1,0:T(8,128)(2,1)S(1)} fusion(bf16[4,2,4,80,768]{4,3,2,1,0:T(8,128)(2,1)S(1)} %bitcast.143, bf16[4,4,2,80,1024]{4,3,2,1,0:T(8,128)(2,1)} %all-to-all-done.3), kind=kOutput, calls=%fused_computation.13 | convolution fusion | flops 4028104704 | bytes 12320768 | tf_op jit(solution)/shard_map/glqsf,qglsd->lfd/dot_general | solution.py:82
  271.2 10.6 %collective-permute-done.5 = bf16[2,320,768]{2,1,0:T(8,128)(2,1)} collective-permute-done((bf16[2,320,768]{2,1,0:T(8,128)(2,1)S(1)}, bf16[2,320,768]{2,1,0:T(8,128)(2,1)}, u32[]{:S(2)}, u32[]{:S(2)}) %collective-permute-start.5) | collective-permute-done | bytes 983072 | tf_op jit(solution)/shard_map/ppermute | solution.py:77
  281.9 42.0 %collective-permute-done.4 = bf16[2,320,768]{2,1,0:T(8,128)(2,1)} collective-permute-done((bf16[2,320,768]{2,1,0:T(8,128)(2,1)S(1)}, bf16[2,320,768]{2,1,0:T(8,128)(2,1)}, u32[]{:S(2)}, u32[]{:S(2)}) %collective-permute-start.4) | collective-permute-done | bytes 983072 | tf_op jit(solution)/shard_map/ppermute | solution.py:77
  326.5 18.6 %collective-permute-done.2 = bf16[2,320,768]{2,1,0:T(8,128)(2,1)} collective-permute-done((bf16[2,320,768]{2,1,0:T(8,128)(2,1)S(1)}, bf16[2,320,768]{2,1,0:T(8,128)(2,1)}, u32[]{:S(2)}, u32[]{:S(2)}) %collective-permute-start.2) | collective-permute-done | bytes 983072 | tf_op jit(solution)/shard_map/ppermute | solution.py:77
  345.1 63.0 %collective-permute-done.1 = bf16[2,320,768]{2,1,0:T(8,128)(2,1)} collective-permute-done((bf16[2,320,768]{2,1,0:T(8,128)(2,1)S(1)}, bf16[2,320,768]{2,1,0:T(8,128)(2,1)}, u32[]{:S(2)}, u32[]{:S(2)}) %collective-permute-start.1) | collective-permute-done | bytes 983072 | tf_op jit(solution)/shard_map/ppermute | solution.py:77
  413.2 6.5 %all-to-all-start.4 = ((f32[4,4,80]{2,0,1:T(4,128)}), f32[4,4,80]{2,0,1:T(4,128)S(1)}, u32[]{:S(2)}, u32[]{:S(2)}) async-start(f32[4,4,80]{2,0,1:T(4,128)} %copy.80), calls=%async_computation.4 | async-start | bytes 16384 | tf_op jit(solution)/shard_map/all_to_all | solution.py:100
  419.7 5.8 %fusion = bf16[4,128,8,1280]{3,2,1,0:T(8,128)(2,1)} fusion(s32[4,128,8]{2,1,0:T(8,128)S(1)} %fusion.58), kind=kLoop, calls=%fused_computation.1 | loop fusion | flops 10485760 | bytes 10502144 | tf_op jit(solution)/shard_map/convert_element_type | solution.py:35
  (73 shorter events, 47.2 us)
Async XLA Ops:
  9.4 32.2 %all-to-all-start = ((bf16[128,4,1024]{0,2,1:T(8,128)(2,1)}), bf16[128,4,1024]{0,2,1:T(8,128)(2,1)S(1)}, u32[]{:S(2)}, u32[]{:S(2)}) async-start(bf16[128,4,1024]{0,2,1:T(8,128)(2,1)} %bitcast), calls=%async_computation | async-start | bytes 2097152 | tf_op jit(solution)/shard_map/all_to_all | solution.py:18
  14.0 201.0 %all-gather.2.cloned.1.call-start = ((), (), s32[]{:S(2)}) async-start(), calls=%async_computation.5 | async-start | bytes 9830400 | tf_op jit(solution)/shard_map/all_gather | solution.py:20
  50.0 26.6 %all-to-all-start.1 = ((bf16[4,4,4,80]{3,0,1,2:T(4,128)(2,1)}), bf16[4,4,4,80]{3,0,1,2:T(4,128)(2,1)S(1)}, u32[]{:S(2)}, u32[]{:S(2)}) async-start(bf16[4,4,4,80]{3,0,1,2:T(4,128)(2,1)} %copy.67), calls=%async_computation.1 | async-start | bytes 32768 | tf_op jit(solution)/shard_map/all_to_all | solution.py:44
  76.6 62.8 %all-to-all-start.2 = ((bf16[4,4,2,80,1024]{4,3,2,1,0:T(8,128)(2,1)}), bf16[4,4,2,80,1024]{4,3,2,1,0:T(8,128)(2,1)}, u32[]{:S(2)}, u32[]{:S(2)}) async-start(bf16[4,4,2,80,1024]{4,3,2,1,0:T(8,128)(2,1)} %copy.70), calls=%async_computation.2 | async-start | bytes 10485760 | tf_op jit(solution)/shard_map/all_to_all | solution.py:61
  139.4 64.7 %all-to-all-start.3 = ((bf16[4,4,2,80,1024]{4,3,2,1,0:T(8,128)(2,1)}), bf16[4,4,2,80,1024]{4,3,2,1,0:T(8,128)(2,1)}, u32[]{:S(2)}, u32[]{:S(2)}) async-start(bf16[4,4,2,80,1024]{4,3,2,1,0:T(8,128)(2,1)} %copy.73), calls=%async_computation.3 | async-start | bytes 10485760 | tf_op jit(solution)/shard_map/all_to_all | solution.py:61
  233.5 10.7 %copy-start.1 = (bf16[4,2,320,768]{3,2,1,0:T(8,128)(2,1)S(1)}, bf16[4,2,320,768]{3,2,1,0:T(8,128)(2,1)}, u32[]{:S(2)}) copy-start(bf16[4,2,320,768]{3,2,1,0:T(8,128)(2,1)} %get-tuple-element.24) | copy-start | bytes 11796484
  234.6 4.7 %collective-permute-start.6 = (f32[4,320]{1,0:T(4,128)S(1)}, f32[4,320]{1,0:T(4,128)S(1)}, u32[]{:S(2)}, u32[]{:S(2)}) collective-permute-start(f32[4,320]{1,0:T(4,128)S(1)} %get-tuple-element.40), channel_id=1, source_target_pairs={{0,8},{8,16},{16,24},{24,0},{1,9},{9,17},{17,25},{25,1},{2,10},{10... | collective-permute-start | bytes 15368 | tf_op jit(solution)/shard_map/ppermute | solution.py:92
  235.8 4.4 %collective-permute-start.7 = (f32[4,320]{1,0:T(4,128)S(1)}, f32[4,320]{1,0:T(4,128)S(1)}, u32[]{:S(2)}, u32[]{:S(2)}) collective-permute-start(f32[4,320]{1,0:T(4,128)S(1)} %get-tuple-element.41), channel_id=1, source_target_pairs={{0,16},{8,24},{16,0},{24,8},{1,17},{9,25},{17,1},{25,9},{2,18},{10... | collective-permute-start | bytes 15368 | tf_op jit(solution)/shard_map/ppermute | solution.py:92
  235.8 7.1 %collective-permute-start.8 = (f32[4,320]{1,0:T(4,128)S(1)}, f32[4,320]{1,0:T(4,128)S(1)}, u32[]{:S(2)}, u32[]{:S(2)}) collective-permute-start(f32[4,320]{1,0:T(4,128)S(1)} %get-tuple-element.42), channel_id=1, source_target_pairs={{0,24},{8,0},{16,8},{24,16},{1,25},{9,1},{17,9},{25,17},{2,26},{10... | collective-permute-start | bytes 15368 | tf_op jit(solution)/shard_map/ppermute | solution.py:92
  236.6 23.3 %collective-permute-start.3 = (bf16[2,320,768]{2,1,0:T(8,128)(2,1)}, bf16[2,320,768]{2,1,0:T(8,128)(2,1)S(1)}, u32[]{:S(2)}, u32[]{:S(2)}) collective-permute-start(bf16[2,320,768]{2,1,0:T(8,128)(2,1)} %get-tuple-element.33), channel_id=1, source_target_pairs={{0,8},{8,16},{16,24},{24,0},{1,9},{9,17},{17,25},{25,1},{2,10},{10... | collective-permute-start | bytes 2949128 | tf_op jit(solution)/shard_map/ppermute | solution.py:77
  239.3 42.5 %collective-permute-start.5 = (bf16[2,320,768]{2,1,0:T(8,128)(2,1)S(1)}, bf16[2,320,768]{2,1,0:T(8,128)(2,1)}, u32[]{:S(2)}, u32[]{:S(2)}) collective-permute-start(bf16[2,320,768]{2,1,0:T(8,128)(2,1)S(1)} %get-tuple-element.34), channel_id=1, source_target_pairs={{0,24},{8,0},{16,8},{24,16},{1,25},{9,1},{17,9},{25,17},{2,26},{10... | collective-permute-start | bytes 2949128 | tf_op jit(solution)/shard_map/ppermute | solution.py:77
  239.3 84.5 %collective-permute-start.4 = (bf16[2,320,768]{2,1,0:T(8,128)(2,1)S(1)}, bf16[2,320,768]{2,1,0:T(8,128)(2,1)}, u32[]{:S(2)}, u32[]{:S(2)}) collective-permute-start(bf16[2,320,768]{2,1,0:T(8,128)(2,1)S(1)} %get-tuple-element.35), channel_id=1, source_target_pairs={{0,16},{8,24},{16,0},{24,8},{1,17},{9,25},{17,1},{25,9},{2,18},{10... | collective-permute-start | bytes 2949128 | tf_op jit(solution)/shard_map/ppermute | solution.py:77
  240.2 86.2 %collective-permute-start = (bf16[2,320,768]{2,1,0:T(8,128)(2,1)S(1)}, bf16[2,320,768]{2,1,0:T(8,128)(2,1)}, u32[]{:S(2)}, u32[]{:S(2)}) collective-permute-start(bf16[2,320,768]{2,1,0:T(8,128)(2,1)S(1)} %get-tuple-element.30), channel_id=1, source_target_pairs={{0,8},{8,16},{16,24},{24,0},{1,9},{9,17},{17,25},{25,1},{2,10},{10... | collective-permute-start | bytes 2949128 | tf_op jit(solution)/shard_map/ppermute | solution.py:77
  242.9 8.5 %collective-permute-start.9 = (f32[4,320]{1,0:T(4,128)S(1)}, f32[4,320]{1,0:T(4,128)S(1)}, u32[]{:S(2)}, u32[]{:S(2)}) collective-permute-start(f32[4,320]{1,0:T(4,128)S(1)} %fusion.72), channel_id=1, source_target_pairs={{0,1},{1,0},{2,3},{3,2},{4,5},{5,4},{6,7},{7,6},{8,9},{9,8},{10,11... | collective-permute-start | bytes 15368 | tf_op jit(solution)/shard_map/ppermute | solution.py:97
  244.2 16.7 %copy-start = (bf16[4,2,320,768]{3,2,1,0:T(8,128)(2,1)S(1)}, bf16[4,2,320,768]{3,2,1,0:T(8,128)(2,1)}, u32[]{:S(2)}) copy-start(bf16[4,2,320,768]{3,2,1,0:T(8,128)(2,1)} %get-tuple-element.25) | copy-start | bytes 11796484
  251.4 93.7 %collective-permute-start.2 = (bf16[2,320,768]{2,1,0:T(8,128)(2,1)S(1)}, bf16[2,320,768]{2,1,0:T(8,128)(2,1)}, u32[]{:S(2)}, u32[]{:S(2)}) collective-permute-start(bf16[2,320,768]{2,1,0:T(8,128)(2,1)S(1)} %get-tuple-element.31), channel_id=1, source_target_pairs={{0,24},{8,0},{16,8},{24,16},{1,25},{9,1},{17,9},{25,17},{2,26},{10... | collective-permute-start | bytes 2949128 | tf_op jit(solution)/shard_map/ppermute | solution.py:77
  259.9 148.2 %collective-permute-start.1 = (bf16[2,320,768]{2,1,0:T(8,128)(2,1)S(1)}, bf16[2,320,768]{2,1,0:T(8,128)(2,1)}, u32[]{:S(2)}, u32[]{:S(2)}) collective-permute-start(bf16[2,320,768]{2,1,0:T(8,128)(2,1)S(1)} %get-tuple-element.32), channel_id=1, source_target_pairs={{0,16},{8,24},{16,0},{24,8},{1,17},{9,25},{17,1},{25,9},{2,18},{10... | collective-permute-start | bytes 2949128 | tf_op jit(solution)/shard_map/ppermute | solution.py:77
  413.2 12.3 %all-to-all-start.4 = ((f32[4,4,80]{2,0,1:T(4,128)}), f32[4,4,80]{2,0,1:T(4,128)S(1)}, u32[]{:S(2)}, u32[]{:S(2)}) async-start(f32[4,4,80]{2,0,1:T(4,128)} %copy.80), calls=%async_computation.4 | async-start | bytes 16384 | tf_op jit(solution)/shard_map/all_to_all | solution.py:100
Sparse Core Ops, SparseCore 0:
  42.3 142.1 all-gather.1

commit v9 on v6

--- a/solution.py
+++ b/solution.py
@@ -58,8 +58,6 @@
             preferred_element_type=jnp.float32,
         ).astype(columns.dtype)
         received = lax.all_to_all(picked, "expert", split_axis=0, concat_axis=0, tiled=True)
-        if c == chunks - 1:
-            hidden_all, received = lax.optimization_barrier((hidden_all, received))
         partial = jnp.einsum(
             "qglsd,lfd->glqsf", received, down_weight[local], preferred_element_type=jnp.float32
         ).reshape(groups, per, slot_rows_all, ff_part)

time: 413 us -> 435 us (1.053)
  waiting for transfers between devices: 193 us -> 238 us
  starting transfers between devices: 61.4 us -> 48.7 us
    all_to_all x2, waiting for transfers between devices: 47.1 us -> 91.2 us  [body(): lax.all_to_all(picked, 'expert', split_axis=0, concat_axis=0, tiled=True)]
    ppermute x6, waiting for transfers between devices: 107 us -> 146 us  [body(): lax.ppermute(chunk, 'dp', pairs).astype(jnp.float32)]
    ppermute x3, waiting for transfers between devices: 38.9 us -> 0.01 us  [body(): own_dots = own_dots + lax.ppermute(chunk, 'dp', pairs)]
    ppermute x3, starting transfers between devices: 24.7 us -> 3.81 us  [body(): own_dots = own_dots + lax.ppermute(chunk, 'dp', pairs)]
    ppermute x6, starting transfers between devices: 5.25 us -> 15.1 us  [body(): lax.ppermute(chunk, 'dp', pairs).astype(jnp.float32)]
    convert_element_type x2 -> x1, other arithmetic: 8.27 us -> 9.62 us  [body(): (jnp.moveaxis(slot_gates[local], 0, 1)[..., None] * hidden_rows).astype(j...]
  transfers between devices with their start and end apart: 16 -> 16, of which waited for: 5 -> 5; matrix products, arithmetic and copies ran while one was open for 22% -> 16% of each run, Pallas kernels for 0% -> 0%
where the time goes in v9:
time: 435 us; the launch traced here: 432 us
  waiting for transfers between devices  238 us (55%)
  starting transfers between devices  48.7 us (11%)
  other arithmetic  41.2 us (9%)
  matrix products  37.7 us (9%)
  blocking collectives  26.2 us (6%)
  local copies, waits for them, and re-layouts  25.4 us (6%)
  between operations  14.3 us (3%)
    ppermute x6, waiting for transfers between devices, body(): lax.ppermute(chunk, 'dp', pairs).astype(jnp.float32)  146 us
    all_to_all x2, waiting for transfers between devices, body(): lax.all_to_all(picked, 'expert', split_axis=0, concat_axis=0, tiled=True)  91.2 us
    all_gather x1, blocking collectives, body(): all_meta = lax.all_gather(meta, 'dp', axis=0, tiled=True)  26.2 us
    ppermute x6, starting transfers between devices, body(): lax.ppermute(chunk, 'dp', pairs).astype(jnp.float32)  15.1 us
    dot_general x2, matrix products, body(): jnp.einsum('qglsd,lfd->glqsf', received, down_weight[local], preferred_el...  14.3 us
    dot_general x2, matrix products, body(): jnp.einsum('glqsf,qglsd->lfd', scaled, received, preferred_element_type=j...  14.1 us
    all_to_all x2, starting transfers between devices, body(): lax.all_to_all(picked, 'expert', split_axis=0, concat_axis=0, tiled=True)  12.1 us
    convert_element_type x2, local copies, waits for them, and re-layouts, body(): picked = jnp.einsum('gtlqs,gtd->qglsd', token_select[:, :, local], token_...  11.5 us
  transfers between devices with their start and end apart: 16, of which 5 were waited for; matrix products, arithmetic and copies ran while one was open for 16% of the time, Pallas kernels for 0%

profile of v9, /device:TPU:29, one launch (start us, length us, event | category | flops | bytes accessed | tf_op | source)
XLA Modules:
  0.0 431.9 jit_solution(12465872905366875267)
XLA Ops:
  9.4 4.5 %all-to-all-start = ((bf16[128,4,1024]{0,2,1:T(8,128)(2,1)}), bf16[128,4,1024]{0,2,1:T(8,128)(2,1)S(1)}, u32[]{:S(2)}, u32[]{:S(2)}) async-start(bf16[128,4,1024]{0,2,1:T(8,128)(2,1)} %bitcast), calls=%async_computation | async-start | bytes 2097152 | tf_op jit(solution)/shard_map/all_to_all | solution.py:18
  15.3 26.2 %all_gather.6 = f32[512,16]{0,1:T(8,128)S(1)} all-gather(f32[128,16]{0,1:T(8,128)S(1)} %pad_maximum_fusion.1), channel_id=1, replica_groups=mesh['dp'=4,'expert'=4,'etp'=2] {'dp'}, dimensions={0}, use_global_device_ids=true | all-gather | bytes 40960 | tf_op jit(solution)/shard_map/all_gather | solution.py:17
  43.5 7.4 %fusion.33 = bf16[4,128,1280]{2,1,0:T(8,128)(2,1)} fusion(s32[4,128,8]{2,1,0:T(8,128)S(1)} %fusion.58), kind=kLoop, calls=%fused_computation.36 | loop fusion | flops 15073280 | bytes 1327104 | tf_op jit(solution)/shard_map/reduce_sum | solution.py:38
  53.8 5.6 %fusion.1 = bf16[4,1,1280,1]{2,1,3,0:T(2,128)(2,1)S(1)} fusion(bf16[4,128,8,1]{2,3,1,0:T(2,128)(2,1)S(1)} %copy.83, s32[4,128,8]{2,1,0:T(8,128)S(1)} %fusion.58), kind=kOutput, calls=%fused_computation.2 | convolution fusion | flops 15728640 | bytes 34816 | tf_op jit(solution)/shard_map/gtk,gtkr->gr/dot_general | solution.py:37
  60.1 6.8 %all-to-all-start.1 = ((bf16[4,4,4,80]{3,0,1,2:T(4,128)(2,1)}), bf16[4,4,4,80]{3,0,1,2:T(4,128)(2,1)S(1)}, u32[]{:S(2)}, u32[]{:S(2)}) async-start(bf16[4,4,4,80]{3,0,1,2:T(4,128)(2,1)} %copy.67), calls=%async_computation.1 | async-start | bytes 32768 | tf_op jit(solution)/shard_map/all_to_all | solution.py:44
  69.2 3.2 convert_bitcast_fusion.1
  72.4 5.8 %copy.70 = bf16[4,4,2,80,1024]{4,3,2,1,0:T(8,128)(2,1)} copy(bf16[4,4,2,80,1024]{4,3,0,2,1:T(8,128)(2,1)} %convert_bitcast_fusion.1) | data formatting | bytes 10485760 | tf_op jit(solution)/shard_map/convert_element_type | solution.py:59
  78.2 5.2 %all-to-all-start.2 = ((bf16[4,4,2,80,1024]{4,3,2,1,0:T(8,128)(2,1)}), bf16[4,4,2,80,1024]{4,3,2,1,0:T(8,128)(2,1)}, u32[]{:S(2)}, u32[]{:S(2)}) async-start(bf16[4,4,2,80,1024]{4,3,2,1,0:T(8,128)(2,1)} %copy.70), calls=%async_computation.2 | async-start | bytes 10485760 | tf_op jit(solution)/shard_map/all_to_all | solution.py:60
  88.1 5.7 %copy.73 = bf16[4,4,2,80,1024]{4,3,2,1,0:T(8,128)(2,1)} copy(bf16[4,4,2,80,1024]{4,3,0,2,1:T(8,128)(2,1)} %convert_bitcast_fusion) | data formatting | bytes 10485760 | tf_op jit(solution)/shard_map/convert_element_type | solution.py:59
  93.8 47.2 %all-to-all-done.2 = bf16[4,4,2,80,1024]{4,3,2,1,0:T(8,128)(2,1)} async-done(((bf16[4,4,2,80,1024]{4,3,2,1,0:T(8,128)(2,1)}), bf16[4,4,2,80,1024]{4,3,2,1,0:T(8,128)(2,1)}, u32[]{:S(2)}, u32[]{:S(2)}) %all-to-all-start.2) | async-done | bytes 5242912 | tf_op jit(solution)/shard_map/all_to_all | solution.py:60
  141.0 6.9 %all-to-all-start.3 = ((bf16[4,4,2,80,1024]{4,3,2,1,0:T(8,128)(2,1)}), bf16[4,4,2,80,1024]{4,3,2,1,0:T(8,128)(2,1)}, u32[]{:S(2)}, u32[]{:S(2)}) async-start(bf16[4,4,2,80,1024]{4,3,2,1,0:T(8,128)(2,1)} %copy.73), calls=%async_computation.3 | async-start | bytes 10485760 | tf_op jit(solution)/shard_map/all_to_all | solution.py:60
  148.1 7.2 %fusion.23 = f32[4,2,4,80,768]{4,3,0,2,1:T(8,128)S(1)} fusion(bf16[4,768,1024]{2,1,0:T(8,128)(2,1)} %param.9, bf16[4,4,2,80,1024]{4,3,2,1,0:T(8,128)(2,1)} %all-to-all-done.2), kind=kOutput, calls=%fused_computation.34 | convolution fusion | flops 4026531840 | bytes 16252928 | tf_op jit(solution)/shard_map/qglsd,lfd->glqsf/dot_general | solution.py:61
  161.6 43.9 %all-to-all-done.3 = bf16[4,4,2,80,1024]{4,3,2,1,0:T(8,128)(2,1)} async-done(((bf16[4,4,2,80,1024]{4,3,2,1,0:T(8,128)(2,1)}), bf16[4,4,2,80,1024]{4,3,2,1,0:T(8,128)(2,1)}, u32[]{:S(2)}, u32[]{:S(2)}) %all-to-all-start.3) | async-done | bytes 5242912 | tf_op jit(solution)/shard_map/all_to_all | solution.py:60
  205.5 7.2 %fusion.28 = f32[4,2,4,80,768]{4,3,0,2,1:T(8,128)S(1)} fusion(bf16[4,768,1024]{2,1,0:T(8,128)(2,1)} %param.9, bf16[4,4,2,80,1024]{4,3,2,1,0:T(8,128)(2,1)} %all-to-all-done.3), kind=kOutput, calls=%fused_computation.35 | convolution fusion | flops 4026531840 | bytes 16252928 | tf_op jit(solution)/shard_map/qglsd,lfd->glqsf/dot_general | solution.py:61
  218.0 6.5 %collective-permute-done = bf16[2,320,768]{2,1,0:T(8,128)(2,1)S(1)} collective-permute-done((bf16[2,320,768]{2,1,0:T(8,128)(2,1)}, bf16[2,320,768]{2,1,0:T(8,128)(2,1)S(1)}, u32[]{:S(2)}, u32[]{:S(2)}) %collective-permute-start) | collective-permute-done | bytes 983072 | tf_op jit(solution)/shard_map/ppermute | solution.py:69
  224.5 9.8 %collective-permute-start.5 = (bf16[2,320,768]{2,1,0:T(8,128)(2,1)S(1)}, bf16[2,320,768]{2,1,0:T(8,128)(2,1)S(1)}, u32[]{:S(2)}, u32[]{:S(2)}) collective-permute-start(bf16[2,320,768]{2,1,0:T(8,128)(2,1)S(1)} %get-tuple-element.28), channel_id=1, source_target_pairs={{0,24},{8,0},{16,8},{24,16},{1,25},{9,1},{17,9},{25,17},{2,26},{10... | collective-permute-start | bytes 2949128 | tf_op jit(solution)/shard_map/ppermute | solution.py:69
  234.4 57.7 %collective-permute-done.1 = bf16[2,320,768]{2,1,0:T(8,128)(2,1)S(1)} collective-permute-done((bf16[2,320,768]{2,1,0:T(8,128)(2,1)S(1)}, bf16[2,320,768]{2,1,0:T(8,128)(2,1)S(1)}, u32[]{:S(2)}, u32[]{:S(2)}) %collective-permute-start.1) | collective-permute-done | bytes 983072 | tf_op jit(solution)/shard_map/ppermute | solution.py:69
  294.1 82.2 %collective-permute-done.4 = bf16[2,320,768]{2,1,0:T(8,128)(2,1)S(1)} collective-permute-done((bf16[2,320,768]{2,1,0:T(8,128)(2,1)S(1)}, bf16[2,320,768]{2,1,0:T(8,128)(2,1)S(1)}, u32[]{:S(2)}, u32[]{:S(2)}) %collective-permute-start.4) | collective-permute-done | bytes 983072 | tf_op jit(solution)/shard_map/ppermute | solution.py:69
  378.2 9.6 %fusion.4 = (bf16[4,2,320,768]{3,2,1,0:T(8,128)(2,1)S(1)}, bf16[4,2,320,768]{3,2,1,0:T(8,128)(2,1)S(1)}, f32[4,2,320]{2,1,0:T(2,128)S(1)}, f32[4,2,320]{2,1,0:T(2,128)S(1)}) fusion(f32[4,2,320]{2,1,0:T(2,128)S(1)} %copy.76, bf16[4,4,320,768]{3,2,1,0:T(8,128)(2,1)} %all-gather.2.cloned.1.call-done, f32[4,2,320]{2,1,0:T(2,128)S(1)} %copy.78, ...), kind=kLoop, calls=%fused_computation.9 | loop fusion | flops 19655680 | bytes 31498240 | tf_op jit(solution)/shard_map/convert_element_type | solution.py:72
  391.7 7.0 %bitcast_convert_fusion.1 = bf16[2,768,1024]{2,1,0:T(8,128)(2,1)S(1)} fusion(bf16[4,2,4,80,768]{4,3,2,1,0:T(8,128)(2,1)S(1)} %bitcast.146, bf16[4,4,2,80,1024]{4,3,2,1,0:T(8,128)(2,1)} %all-to-all-done.2), kind=kOutput, calls=%fused_computation.14 | convolution fusion | flops 4028104704 | bytes 12320768 | tf_op jit(solution)/shard_map/glqsf,qglsd->lfd/dot_general | solution.py:74
  398.8 7.1 %bitcast_convert_fusion = bf16[2,768,1024]{2,1,0:T(8,128)(2,1)S(1)} fusion(bf16[4,2,4,80,768]{4,3,2,1,0:T(8,128)(2,1)S(1)} %bitcast.145, bf16[4,4,2,80,1024]{4,3,2,1,0:T(8,128)(2,1)} %all-to-all-done.3), kind=kOutput, calls=%fused_computation.13 | convolution fusion | flops 4028104704 | bytes 12320768 | tf_op jit(solution)/shard_map/glqsf,qglsd->lfd/dot_general | solution.py:74
  407.1 3.2 pad_maximum_fusion
  411.1 5.1 %all-to-all-start.4 = ((f32[4,4,80]{2,0,1:T(4,128)}), f32[4,4,80]{2,0,1:T(4,128)S(1)}, u32[]{:S(2)}, u32[]{:S(2)}) async-start(f32[4,4,80]{2,0,1:T(4,128)} %copy.80), calls=%async_computation.4 | async-start | bytes 16384 | tf_op jit(solution)/shard_map/all_to_all | solution.py:92
  416.2 5.8 %fusion = bf16[4,128,8,1280]{3,2,1,0:T(8,128)(2,1)} fusion(s32[4,128,8]{2,1,0:T(8,128)S(1)} %fusion.58), kind=kLoop, calls=%fused_computation.1 | loop fusion | flops 10485760 | bytes 10502144 | tf_op jit(solution)/shard_map/convert_element_type | solution.py:35
  (77 shorter events, 40.6 us)
Async XLA Ops:
  9.4 32.2 %all-to-all-start = ((bf16[128,4,1024]{0,2,1:T(8,128)(2,1)}), bf16[128,4,1024]{0,2,1:T(8,128)(2,1)S(1)}, u32[]{:S(2)}, u32[]{:S(2)}) async-start(bf16[128,4,1024]{0,2,1:T(8,128)(2,1)} %bitcast), calls=%async_computation | async-start | bytes 2097152 | tf_op jit(solution)/shard_map/all_to_all | solution.py:18
  53.8 13.9 %copy-start.2 = (bf16[4,128,2,4,80]{1,4,3,2,0:T(8,128)(2,1)S(1)}, bf16[4,128,2,4,80]{1,4,3,2,0:T(8,128)(2,1)}, u32[]{:S(2)}) copy-start(bf16[4,128,2,4,80]{1,4,3,2,0:T(8,128)(2,1)} %get-tuple-element.30) | copy-start | bytes 1966084
  60.1 18.0 %all-to-all-start.1 = ((bf16[4,4,4,80]{3,0,1,2:T(4,128)(2,1)}), bf16[4,4,4,80]{3,0,1,2:T(4,128)(2,1)S(1)}, u32[]{:S(2)}, u32[]{:S(2)}) async-start(bf16[4,4,4,80]{3,0,1,2:T(4,128)(2,1)} %copy.67), calls=%async_computation.1 | async-start | bytes 32768 | tf_op jit(solution)/shard_map/all_to_all | solution.py:44
  67.0 311.3 %all-gather.2.cloned.1.call-start = ((), (), s32[]{:S(2)}) async-start(), calls=%async_computation.5 | async-start | bytes 9830400 | tf_op jit(solution)/shard_map/all_gather | solution.py:20
  78.2 62.8 %all-to-all-start.2 = ((bf16[4,4,2,80,1024]{4,3,2,1,0:T(8,128)(2,1)}), bf16[4,4,2,80,1024]{4,3,2,1,0:T(8,128)(2,1)}, u32[]{:S(2)}, u32[]{:S(2)}) async-start(bf16[4,4,2,80,1024]{4,3,2,1,0:T(8,128)(2,1)} %copy.70), calls=%async_computation.2 | async-start | bytes 10485760 | tf_op jit(solution)/shard_map/all_to_all | solution.py:60
  141.0 64.5 %all-to-all-start.3 = ((bf16[4,4,2,80,1024]{4,3,2,1,0:T(8,128)(2,1)}), bf16[4,4,2,80,1024]{4,3,2,1,0:T(8,128)(2,1)}, u32[]{:S(2)}, u32[]{:S(2)}) async-start(bf16[4,4,2,80,1024]{4,3,2,1,0:T(8,128)(2,1)} %copy.73), calls=%async_computation.3 | async-start | bytes 10485760 | tf_op jit(solution)/shard_map/all_to_all | solution.py:60
  156.0 3.2 copy-start
  160.3 64.3 %collective-permute-start = (bf16[2,320,768]{2,1,0:T(8,128)(2,1)}, bf16[2,320,768]{2,1,0:T(8,128)(2,1)S(1)}, u32[]{:S(2)}, u32[]{:S(2)}) collective-permute-start(bf16[2,320,768]{2,1,0:T(8,128)(2,1)} %get-tuple-element.24), channel_id=1, source_target_pairs={{0,8},{8,16},{16,24},{24,0},{1,9},{9,17},{17,25},{25,1},{2,10},{10... | collective-permute-start | bytes 2949128 | tf_op jit(solution)/shard_map/ppermute | solution.py:69
  213.4 162.9 %copy-start.1 = (f32[4,2,4,80,768]{4,3,2,1,0:T(8,128)}, f32[4,2,4,80,768]{4,3,2,1,0:T(8,128)S(1)}, u32[]{:S(2)}) copy-start(f32[4,2,4,80,768]{4,3,2,1,0:T(8,128)S(1)} %copy.75) | copy-start | bytes 23592964
  213.4 78.6 %collective-permute-start.1 = (bf16[2,320,768]{2,1,0:T(8,128)(2,1)S(1)}, bf16[2,320,768]{2,1,0:T(8,128)(2,1)S(1)}, u32[]{:S(2)}, u32[]{:S(2)}) collective-permute-start(bf16[2,320,768]{2,1,0:T(8,128)(2,1)S(1)} %get-tuple-element.26), channel_id=1, source_target_pairs={{0,16},{8,24},{16,0},{24,8},{1,17},{9,25},{17,1},{25,9},{2,18},{10... | collective-permute-start | bytes 2949128 | tf_op jit(solution)/shard_map/ppermute | solution.py:69
  213.8 78.3 %collective-permute-start.2 = (bf16[2,320,768]{2,1,0:T(8,128)(2,1)S(1)}, bf16[2,320,768]{2,1,0:T(8,128)(2,1)S(1)}, u32[]{:S(2)}, u32[]{:S(2)}) collective-permute-start(bf16[2,320,768]{2,1,0:T(8,128)(2,1)S(1)} %get-tuple-element.25), channel_id=1, source_target_pairs={{0,24},{8,0},{16,8},{24,16},{1,25},{9,1},{17,9},{25,17},{2,26},{10... | collective-permute-start | bytes 2949128 | tf_op jit(solution)/shard_map/ppermute | solution.py:69
  215.7 78.4 %collective-permute-start.3 = (bf16[2,320,768]{2,1,0:T(8,128)(2,1)S(1)}, bf16[2,320,768]{2,1,0:T(8,128)(2,1)S(1)}, u32[]{:S(2)}, u32[]{:S(2)}) collective-permute-start(bf16[2,320,768]{2,1,0:T(8,128)(2,1)S(1)} %get-tuple-element.27), channel_id=1, source_target_pairs={{0,8},{8,16},{16,24},{24,0},{1,9},{9,17},{17,25},{25,1},{2,10},{10... | collective-permute-start | bytes 2949128 | tf_op jit(solution)/shard_map/ppermute | solution.py:69
  217.7 158.6 %collective-permute-start.4 = (bf16[2,320,768]{2,1,0:T(8,128)(2,1)S(1)}, bf16[2,320,768]{2,1,0:T(8,128)(2,1)S(1)}, u32[]{:S(2)}, u32[]{:S(2)}) collective-permute-start(bf16[2,320,768]{2,1,0:T(8,128)(2,1)S(1)} %get-tuple-element.29), channel_id=1, source_target_pairs={{0,16},{8,24},{16,0},{24,8},{1,17},{9,25},{17,1},{25,9},{2,18},{10... | collective-permute-start | bytes 2949128 | tf_op jit(solution)/shard_map/ppermute | solution.py:69
  224.5 151.8 %collective-permute-start.5 = (bf16[2,320,768]{2,1,0:T(8,128)(2,1)S(1)}, bf16[2,320,768]{2,1,0:T(8,128)(2,1)S(1)}, u32[]{:S(2)}, u32[]{:S(2)}) collective-permute-start(bf16[2,320,768]{2,1,0:T(8,128)(2,1)S(1)} %get-tuple-element.28), channel_id=1, source_target_pairs={{0,24},{8,0},{16,8},{24,16},{1,25},{9,1},{17,9},{25,17},{2,26},{10... | collective-permute-start | bytes 2949128 | tf_op jit(solution)/shard_map/ppermute | solution.py:69
  387.9 17.9 %collective-permute-start.6 = (f32[4,320]{1,0:T(4,128)S(1)}, f32[4,320]{1,0:T(4,128)S(1)}, u32[]{:S(2)}, u32[]{:S(2)}) collective-permute-start(f32[4,320]{1,0:T(4,128)S(1)} %get-tuple-element.34), channel_id=1, source_target_pairs={{0,8},{8,16},{16,24},{24,0},{1,9},{9,17},{17,25},{25,1},{2,10},{10... | collective-permute-start | bytes 15368 | tf_op jit(solution)/shard_map/ppermute | solution.py:84
  387.9 17.9 %collective-permute-start.7 = (f32[4,320]{1,0:T(4,128)S(1)}, f32[4,320]{1,0:T(4,128)S(1)}, u32[]{:S(2)}, u32[]{:S(2)}) collective-permute-start(f32[4,320]{1,0:T(4,128)S(1)} %get-tuple-element.35), channel_id=1, source_target_pairs={{0,16},{8,24},{16,0},{24,8},{1,17},{9,25},{17,1},{25,9},{2,18},{10... | collective-permute-start | bytes 15368 | tf_op jit(solution)/shard_map/ppermute | solution.py:84
  390.3 15.5 %collective-permute-start.8 = (f32[4,320]{1,0:T(4,128)S(1)}, f32[4,320]{1,0:T(4,128)S(1)}, u32[]{:S(2)}, u32[]{:S(2)}) collective-permute-start(f32[4,320]{1,0:T(4,128)S(1)} %get-tuple-element.36), channel_id=1, source_target_pairs={{0,24},{8,0},{16,8},{24,16},{1,25},{9,1},{17,9},{25,17},{2,26},{10... | collective-permute-start | bytes 15368 | tf_op jit(solution)/shard_map/ppermute | solution.py:84
  405.9 4.5 %collective-permute-start.9 = (f32[4,320]{1,0:T(4,128)S(1)}, f32[4,320]{1,0:T(4,128)S(1)}, u32[]{:S(2)}, u32[]{:S(2)}) collective-permute-start(f32[4,320]{1,0:T(4,128)S(1)} %fusion.72), channel_id=1, source_target_pairs={{0,1},{1,0},{2,3},{3,2},{4,5},{5,4},{6,7},{7,6},{8,9},{9,8},{10,11... | collective-permute-start | bytes 15368 | tf_op jit(solution)/shard_map/ppermute | solution.py:89
  411.1 10.9 %all-to-all-start.4 = ((f32[4,4,80]{2,0,1:T(4,128)}), f32[4,4,80]{2,0,1:T(4,128)S(1)}, u32[]{:S(2)}, u32[]{:S(2)}) async-start(f32[4,4,80]{2,0,1:T(4,128)} %copy.80), calls=%async_computation.4 | async-start | bytes 16384 | tf_op jit(solution)/shard_map/all_to_all | solution.py:92
Sparse Core Ops, SparseCore 0:
  69.3 205.4 all-gather.1

commit v10 on v6

--- a/solution.py
+++ b/solution.py
@@ -13,10 +13,19 @@
     slot_rows_all = hidden_saved.shape[2]
     capacity = slot_rows_all // senders
     experts = exp_dev * senders
-    meta = jnp.concatenate([routes.astype(jnp.float32), gates.astype(jnp.float32)], axis=1)
-    all_meta = lax.all_gather(meta, "dp", axis=0, tiled=True)
-    columns = lax.all_to_all(grad_out, "dp", split_axis=1, concat_axis=0, tiled=True)
-    hidden_saved, all_meta, columns = lax.optimization_barrier((hidden_saved, all_meta, columns))
+    quarter_cols = grad_out.shape[1] // groups
+    meta = jnp.concatenate([routes.astype(grad_out.dtype), gates.astype(grad_out.dtype)], axis=1)
+    packed = jnp.concatenate(
+        [
+            grad_out.reshape(token_count, groups, quarter_cols),
+            jnp.broadcast_to(meta[:, None, :], (token_count, groups, 2 * top_count)),
+        ],
+        axis=2,
+    )
+    moved = lax.all_to_all(packed, "dp", split_axis=1, concat_axis=0, tiled=True)
+    hidden_saved, moved = lax.optimization_barrier((hidden_saved, moved))
+    columns = moved[:, 0, :quarter_cols]
+    all_meta = moved[:, 0, quarter_cols:]
     hidden_all = lax.all_gather(hidden_saved, "dp", axis=0, tiled=True)
     all_routes = all_meta[:, :top_count].astype(jnp.int32)
     all_gates = all_meta[:, top_count:].astype(gates.dtype)

time: 413 us -> 407 us (0.985)
  starting transfers between devices: 61.4 us -> 55.4 us
    all_to_all x0 -> x1, blocking collectives: none -> 28.1 us  [body(): lax.all_to_all(packed, 'dp', split_axis=1, concat_axis=0, tiled=True)]
    all_gather x1 -> x0, blocking collectives: 26.2 us -> none  [body(): all_meta = lax.all_gather(meta, 'dp', axis=0, tiled=True)]
    all_to_all x1 -> x0, starting transfers between devices: 4.53 us -> none  [body(): lax.all_to_all(grad_out, 'dp', split_axis=1, concat_axis=0, tiled=True)]
  transfers between devices with their start and end apart: 16 -> 15, of which waited for: 5 -> 5; matrix products, arithmetic and copies ran while one was open for 22% -> 22% of each run, Pallas kernels for 0% -> 0%
where the time goes in v10:
time: 407 us; the launch traced here: 404 us
  waiting for transfers between devices  192 us (47%)
  starting transfers between devices  55.4 us (14%)
  other arithmetic  44.9 us (11%)
  matrix products  41.6 us (10%)
  blocking collectives  28.1 us (7%)
  local copies, waits for them, and re-layouts  27.4 us (7%)
  between operations  14.7 us (4%)
    ppermute x6, waiting for transfers between devices, body(): lax.ppermute(chunk, 'dp', pairs).astype(jnp.float32)  106 us
    all_to_all x2, waiting for transfers between devices, body(): lax.all_to_all(picked, 'expert', split_axis=0, concat_axis=0, tiled=True)  47.1 us
    ppermute x3, waiting for transfers between devices, body(): own_dots = own_dots + lax.ppermute(chunk, 'dp', pairs)  38.9 us
    all_to_all x1, blocking collectives, body(): lax.all_to_all(packed, 'dp', split_axis=1, concat_axis=0, tiled=True)  28.1 us
    ppermute x3, starting transfers between devices, body(): own_dots = own_dots + lax.ppermute(chunk, 'dp', pairs)  24.7 us
    dot_general x2, matrix products, body(): jnp.einsum('glqsf,qglsd->lfd', scaled, received, preferred_element_type=j...  18 us
    dot_general x2, matrix products, body(): jnp.einsum('qglsd,lfd->glqsf', received, down_weight[local], preferred_el...  14.4 us
    all_to_all x2, starting transfers between devices, body(): lax.all_to_all(picked, 'expert', split_axis=0, concat_axis=0, tiled=True)  12.2 us
  transfers between devices with their start and end apart: 15, of which 5 were waited for; matrix products, arithmetic and copies ran while one was open for 22% of the time, Pallas kernels for 0%

profile of v10, /device:TPU:29, one launch (start us, length us, event | category | flops | bytes accessed | tf_op | source)
XLA Modules:
  0.0 403.6 jit_solution(9667012312741765412)
XLA Ops:
  10.3 28.1 %all_to_all.38 = bf16[128,4,1040]{0,2,1:T(8,128)(2,1)S(1)} all-to-all(bf16[128,4,1040]{0,2,1:T(8,128)(2,1)S(1)} %pad_maximum_fusion.1), channel_id=1, replica_groups=mesh['dp'=4,'expert'=4,'etp'=2] {'dp'}, dimensions={1} | all-to-all | bytes 2129920 | tf_op jit(solution)/shard_map/all_to_all | solution.py:25
  40.8 5.6 %fusion.1 = bf16[4,1,1280,1]{2,1,3,0:T(2,128)(2,1)S(1)} fusion(bf16[4,128,8,1]{2,3,1,0:T(2,128)(2,1)S(1)} %copy.81, s32[4,128,8]{2,1,0:T(8,128)S(1)} %fusion.58), kind=kOutput, calls=%fused_computation.2 | convolution fusion | flops 15728640 | bytes 34816 | tf_op jit(solution)/shard_map/gtk,gtkr->gr/dot_general | solution.py:46
  47.1 5.1 %all-to-all-start.1 = ((bf16[4,4,4,80]{3,0,1,2:T(4,128)(2,1)}), bf16[4,4,4,80]{3,0,1,2:T(4,128)(2,1)S(1)}, u32[]{:S(2)}, u32[]{:S(2)}) async-start(bf16[4,4,4,80]{3,0,1,2:T(4,128)(2,1)} %copy.64), calls=%async_computation.1 | async-start | bytes 32768 | tf_op jit(solution)/shard_map/all_to_all | solution.py:53
  52.2 7.4 %fusion.33 = bf16[4,128,1280]{2,1,0:T(8,128)(2,1)} fusion(s32[4,128,8]{2,1,0:T(8,128)S(1)} %fusion.58), kind=kLoop, calls=%fused_computation.36 | loop fusion | flops 15073280 | bytes 1327104 | tf_op jit(solution)/shard_map/reduce_sum | solution.py:47
  63.0 3.2 convert_bitcast_fusion.1
  66.2 5.8 %copy.68 = bf16[4,4,2,80,1024]{4,3,2,1,0:T(8,128)(2,1)} copy(bf16[4,4,2,80,1024]{4,3,0,2,1:T(8,128)(2,1)} %convert_bitcast_fusion.1) | data formatting | bytes 10485760 | tf_op jit(solution)/shard_map/convert_element_type | solution.py:68
  72.0 5.2 %all-to-all-start.2 = ((bf16[4,4,2,80,1024]{4,3,2,1,0:T(8,128)(2,1)}), bf16[4,4,2,80,1024]{4,3,2,1,0:T(8,128)(2,1)}, u32[]{:S(2)}, u32[]{:S(2)}) async-start(bf16[4,4,2,80,1024]{4,3,2,1,0:T(8,128)(2,1)} %copy.68), calls=%async_computation.2 | async-start | bytes 10485760 | tf_op jit(solution)/shard_map/all_to_all | solution.py:69
  81.9 5.8 %copy.71 = bf16[4,4,2,80,1024]{4,3,2,1,0:T(8,128)(2,1)} copy(bf16[4,4,2,80,1024]{4,3,0,2,1:T(8,128)(2,1)} %convert_bitcast_fusion) | data formatting | bytes 10485760 | tf_op jit(solution)/shard_map/convert_element_type | solution.py:68
  87.8 47.1 %all-to-all-done.2 = bf16[4,4,2,80,1024]{4,3,2,1,0:T(8,128)(2,1)} async-done(((bf16[4,4,2,80,1024]{4,3,2,1,0:T(8,128)(2,1)}), bf16[4,4,2,80,1024]{4,3,2,1,0:T(8,128)(2,1)}, u32[]{:S(2)}, u32[]{:S(2)}) %all-to-all-start.2) | async-done | bytes 5242912 | tf_op jit(solution)/shard_map/all_to_all | solution.py:69
  134.8 6.9 %all-to-all-start.3 = ((bf16[4,4,2,80,1024]{4,3,2,1,0:T(8,128)(2,1)}), bf16[4,4,2,80,1024]{4,3,2,1,0:T(8,128)(2,1)}, u32[]{:S(2)}, u32[]{:S(2)}) async-start(bf16[4,4,2,80,1024]{4,3,2,1,0:T(8,128)(2,1)} %copy.71), calls=%async_computation.3 | async-start | bytes 10485760 | tf_op jit(solution)/shard_map/all_to_all | solution.py:69
  141.8 7.2 %fusion.23 = f32[4,2,4,80,768]{4,3,0,2,1:T(8,128)S(1)} fusion(bf16[4,768,1024]{2,1,0:T(8,128)(2,1)} %param.9, bf16[4,4,2,80,1024]{4,3,2,1,0:T(8,128)(2,1)} %all-to-all-done.2), kind=kOutput, calls=%fused_computation.34 | convolution fusion | flops 4026531840 | bytes 16252928 | tf_op jit(solution)/shard_map/qglsd,lfd->glqsf/dot_general | solution.py:72
  156.7 42.1 %collective-permute-done = bf16[2,320,768]{2,1,0:T(8,128)(2,1)S(1)} collective-permute-done((bf16[2,320,768]{2,1,0:T(8,128)(2,1)}, bf16[2,320,768]{2,1,0:T(8,128)(2,1)S(1)}, u32[]{:S(2)}, u32[]{:S(2)}) %collective-permute-start) | collective-permute-done | bytes 983072 | tf_op jit(solution)/shard_map/ppermute | solution.py:80
  198.8 21.4 %collective-permute-done.2 = bf16[2,320,768]{2,1,0:T(8,128)(2,1)} collective-permute-done((bf16[2,320,768]{2,1,0:T(8,128)(2,1)S(1)}, bf16[2,320,768]{2,1,0:T(8,128)(2,1)}, u32[]{:S(2)}, u32[]{:S(2)}) %collective-permute-start.2) | collective-permute-done | bytes 983072 | tf_op jit(solution)/shard_map/ppermute | solution.py:80
  220.2 42.2 %collective-permute-done.1 = bf16[2,320,768]{2,1,0:T(8,128)(2,1)} collective-permute-done((bf16[2,320,768]{2,1,0:T(8,128)(2,1)S(1)}, bf16[2,320,768]{2,1,0:T(8,128)(2,1)}, u32[]{:S(2)}, u32[]{:S(2)}) %collective-permute-start.1) | collective-permute-done | bytes 983072 | tf_op jit(solution)/shard_map/ppermute | solution.py:80
  265.1 7.2 %fusion.28 = f32[4,2,4,80,768]{4,3,0,2,1:T(8,128)S(1)} fusion(bf16[4,768,1024]{2,1,0:T(8,128)(2,1)} %param.9, bf16[4,4,2,80,1024]{4,3,2,1,0:T(8,128)(2,1)} %all-to-all-done.3), kind=kOutput, calls=%fused_computation.35 | convolution fusion | flops 4026531840 | bytes 16252928 | tf_op jit(solution)/shard_map/qglsd,lfd->glqsf/dot_general | solution.py:72
  278.1 4.9 %fusion.6 = (bf16[4,2,320,768]{3,2,1,0:T(8,128)(2,1)}, f32[4,2,320]{2,1,0:T(2,128)S(1)}) fusion(f32[4,2,320]{2,1,0:T(2,128)S(1)} %copy.76, bf16[4,4,320,768]{3,2,1,0:T(8,128)(2,1)} %all-gather.2.cloned.1.call-done, f32[4,2,320,768]{3,2,1,0:T(8,128)S(1)} %bitcast.148), kind=kLoop, calls=%fused_computation.11 | loop fusion | flops 9827840 | bytes 15749120 | tf_op jit(solution)/shard_map/convert_element_type | solution.py:83
  284.0 3.4 fusion.4
  290.5 9.8 %bitcast_convert_fusion = bf16[2,768,1024]{2,1,0:T(8,128)(2,1)} fusion(bf16[4,2,4,80,768]{4,3,2,1,0:T(8,128)(2,1)} %bitcast.161, bf16[4,4,2,80,1024]{4,3,2,1,0:T(8,128)(2,1)} %all-to-all-done.3), kind=kOutput, calls=%fused_computation.13 | convolution fusion | flops 4028104704 | bytes 12320768 | tf_op jit(solution)/shard_map/glqsf,qglsd->lfd/dot_general | solution.py:85
  301.7 38.9 %collective-permute-done.6 = f32[4,320]{1,0:T(4,128)S(1)} collective-permute-done((f32[4,320]{1,0:T(4,128)S(1)}, f32[4,320]{1,0:T(4,128)S(1)}, u32[]{:S(2)}, u32[]{:S(2)}) %collective-permute-start.6) | collective-permute-done | bytes 5152 | tf_op jit(solution)/shard_map/ppermute | solution.py:95
  340.6 20.2 %collective-permute-start.8 = (f32[4,320]{1,0:T(4,128)S(1)}, f32[4,320]{1,0:T(4,128)S(1)}, u32[]{:S(2)}, u32[]{:S(2)}) collective-permute-start(f32[4,320]{1,0:T(4,128)S(1)} %get-tuple-element.36), channel_id=1, source_target_pairs={{0,24},{8,0},{16,8},{24,16},{1,25},{9,1},{17,9},{25,17},{2,26},{10... | collective-permute-start | bytes 15368 | tf_op jit(solution)/shard_map/ppermute | solution.py:95
  360.7 8.2 %bitcast_convert_fusion.1 = bf16[2,768,1024]{2,1,0:T(8,128)(2,1)} fusion(bf16[4,2,4,80,768]{4,3,2,1,0:T(8,128)(2,1)S(1)} %bitcast.160, bf16[4,4,2,80,1024]{4,3,2,1,0:T(8,128)(2,1)} %all-to-all-done.2), kind=kOutput, calls=%fused_computation.14 | convolution fusion | flops 4028104704 | bytes 12320768 | tf_op jit(solution)/shard_map/glqsf,qglsd->lfd/dot_general | solution.py:85
  370.2 6.1 %pad_maximum_fusion = bf16[4,768,1024]{2,1,0:T(8,128)(2,1)} fusion(bf16[2,768,1024]{2,1,0:T(8,128)(2,1)} %bitcast_convert_fusion, bf16[2,768,1024]{2,1,0:T(8,128)(2,1)} %bitcast_convert_fusion.1), kind=kLoop, calls=%fused_computation.12 | loop fusion | flops 3145728 | bytes 12582912 | tf_op jit(solution)/shard_map/concatenate | solution.py:88
  381.4 6.2 %all-to-all-start.4 = ((f32[4,4,80]{2,0,1:T(4,128)}), f32[4,4,80]{2,0,1:T(4,128)S(1)}, u32[]{:S(2)}, u32[]{:S(2)}) async-start(f32[4,4,80]{2,0,1:T(4,128)} %copy.78), calls=%async_computation.4 | async-start | bytes 16384 | tf_op jit(solution)/shard_map/all_to_all | solution.py:103
  387.7 5.8 %fusion = bf16[4,128,8,1280]{3,2,1,0:T(8,128)(2,1)} fusion(s32[4,128,8]{2,1,0:T(8,128)S(1)} %fusion.58), kind=kLoop, calls=%fused_computation.1 | loop fusion | flops 10485760 | bytes 10502144 | tf_op jit(solution)/shard_map/convert_element_type | solution.py:44
  (90 shorter events, 45.3 us)
Async XLA Ops:
  7.2 257.9 %all-gather.2.cloned.1.call-start = ((), (), s32[]{:S(2)}) async-start(), calls=%async_computation.5 | async-start | bytes 9830400 | tf_op jit(solution)/shard_map/all_gather | solution.py:29
  47.1 24.9 %all-to-all-start.1 = ((bf16[4,4,4,80]{3,0,1,2:T(4,128)(2,1)}), bf16[4,4,4,80]{3,0,1,2:T(4,128)(2,1)S(1)}, u32[]{:S(2)}, u32[]{:S(2)}) async-start(bf16[4,4,4,80]{3,0,1,2:T(4,128)(2,1)} %copy.64), calls=%async_computation.1 | async-start | bytes 32768 | tf_op jit(solution)/shard_map/all_to_all | solution.py:53
  72.0 62.8 %all-to-all-start.2 = ((bf16[4,4,2,80,1024]{4,3,2,1,0:T(8,128)(2,1)}), bf16[4,4,2,80,1024]{4,3,2,1,0:T(8,128)(2,1)}, u32[]{:S(2)}, u32[]{:S(2)}) async-start(bf16[4,4,2,80,1024]{4,3,2,1,0:T(8,128)(2,1)} %copy.68), calls=%async_computation.2 | async-start | bytes 10485760 | tf_op jit(solution)/shard_map/all_to_all | solution.py:69
  134.8 130.2 %all-to-all-start.3 = ((bf16[4,4,2,80,1024]{4,3,2,1,0:T(8,128)(2,1)}), bf16[4,4,2,80,1024]{4,3,2,1,0:T(8,128)(2,1)}, u32[]{:S(2)}, u32[]{:S(2)}) async-start(bf16[4,4,2,80,1024]{4,3,2,1,0:T(8,128)(2,1)} %copy.71), calls=%async_computation.3 | async-start | bytes 10485760 | tf_op jit(solution)/shard_map/all_to_all | solution.py:69
  149.7 3.1 copy-start
  154.0 44.9 %collective-permute-start = (bf16[2,320,768]{2,1,0:T(8,128)(2,1)}, bf16[2,320,768]{2,1,0:T(8,128)(2,1)S(1)}, u32[]{:S(2)}, u32[]{:S(2)}) collective-permute-start(bf16[2,320,768]{2,1,0:T(8,128)(2,1)} %get-tuple-element.24), channel_id=1, source_target_pairs={{0,8},{8,16},{16,24},{24,0},{1,9},{9,17},{17,25},{25,1},{2,10},{10... | collective-permute-start | bytes 2949128 | tf_op jit(solution)/shard_map/ppermute | solution.py:80
  156.0 64.2 %collective-permute-start.2 = (bf16[2,320,768]{2,1,0:T(8,128)(2,1)S(1)}, bf16[2,320,768]{2,1,0:T(8,128)(2,1)}, u32[]{:S(2)}, u32[]{:S(2)}) collective-permute-start(bf16[2,320,768]{2,1,0:T(8,128)(2,1)S(1)} %get-tuple-element.25), channel_id=1, source_target_pairs={{0,24},{8,0},{16,8},{24,16},{1,25},{9,1},{17,9},{25,17},{2,26},{10... | collective-permute-start | bytes 2949128 | tf_op jit(solution)/shard_map/ppermute | solution.py:80
  156.0 106.4 %collective-permute-start.1 = (bf16[2,320,768]{2,1,0:T(8,128)(2,1)S(1)}, bf16[2,320,768]{2,1,0:T(8,128)(2,1)}, u32[]{:S(2)}, u32[]{:S(2)}) collective-permute-start(bf16[2,320,768]{2,1,0:T(8,128)(2,1)S(1)} %get-tuple-element.26), channel_id=1, source_target_pairs={{0,16},{8,24},{16,0},{24,8},{1,17},{9,25},{17,1},{25,9},{2,18},{10... | collective-permute-start | bytes 2949128 | tf_op jit(solution)/shard_map/ppermute | solution.py:80
  272.8 10.1 %slice-start.2 = ((s8[7864320]{0:T(1024)(128)(4,1)}), s8[4194304]{0:T(1024)(128)(4,1)S(1)}, s32[]{:S(2)}) async-start(s8[7864320]{0:T(1024)(128)(4,1)} %bitcast.154), calls=%async_computation.8 | async-start | bytes 8388608
  273.3 9.7 %slice-start.3 = ((s8[7864320]{0:T(1024)(128)(4,1)}), s8[3670016]{0:T(1024)(128)(4,1)S(1)}, s32[]{:S(2)}) async-start(s8[7864320]{0:T(1024)(128)(4,1)} %bitcast.154), calls=%async_computation.9 | async-start | bytes 7340032
  274.8 101.6 %collective-permute-start.3 = (bf16[2,320,768]{2,1,0:T(8,128)(2,1)}, bf16[2,320,768]{2,1,0:T(8,128)(2,1)S(1)}, u32[]{:S(2)}, u32[]{:S(2)}) collective-permute-start(bf16[2,320,768]{2,1,0:T(8,128)(2,1)} %get-tuple-element.27), channel_id=1, source_target_pairs={{0,8},{8,16},{16,24},{24,0},{1,9},{9,17},{17,25},{25,1},{2,10},{10... | collective-permute-start | bytes 2949128 | tf_op jit(solution)/shard_map/ppermute | solution.py:80
  277.6 98.7 %collective-permute-start.5 = (bf16[2,320,768]{2,1,0:T(8,128)(2,1)}, bf16[2,320,768]{2,1,0:T(8,128)(2,1)S(1)}, u32[]{:S(2)}, u32[]{:S(2)}) collective-permute-start(bf16[2,320,768]{2,1,0:T(8,128)(2,1)} %get-tuple-element.28), channel_id=1, source_target_pairs={{0,24},{8,0},{16,8},{24,16},{1,25},{9,1},{17,9},{25,17},{2,26},{10... | collective-permute-start | bytes 2949128 | tf_op jit(solution)/shard_map/ppermute | solution.py:80
  277.8 98.6 %collective-permute-start.4 = (bf16[2,320,768]{2,1,0:T(8,128)(2,1)S(1)}, bf16[2,320,768]{2,1,0:T(8,128)(2,1)}, u32[]{:S(2)}, u32[]{:S(2)}) collective-permute-start(bf16[2,320,768]{2,1,0:T(8,128)(2,1)S(1)} %get-tuple-element.29), channel_id=1, source_target_pairs={{0,16},{8,24},{16,0},{24,8},{1,17},{9,25},{17,1},{25,9},{2,18},{10... | collective-permute-start | bytes 2949128 | tf_op jit(solution)/shard_map/ppermute | solution.py:80
  278.1 4.9 %slice-start = ((s8[7864320]{0:T(1024)(128)(4,1)}), s8[4194304]{0:T(1024)(128)(4,1)S(1)}, s32[]{:S(2)}) async-start(s8[7864320]{0:T(1024)(128)(4,1)} %bitcast.145), calls=%async_computation.6 | async-start | bytes 8388608
  278.1 5.9 %slice-start.1 = ((s8[7864320]{0:T(1024)(128)(4,1)}), s8[3670016]{0:T(1024)(128)(4,1)S(1)}, s32[]{:S(2)}) async-start(s8[7864320]{0:T(1024)(128)(4,1)} %bitcast.145), calls=%async_computation.7 | async-start | bytes 7340032
  287.4 53.1 %collective-permute-start.6 = (f32[4,320]{1,0:T(4,128)S(1)}, f32[4,320]{1,0:T(4,128)S(1)}, u32[]{:S(2)}, u32[]{:S(2)}) collective-permute-start(f32[4,320]{1,0:T(4,128)S(1)} %get-tuple-element.34), channel_id=1, source_target_pairs={{0,8},{8,16},{16,24},{24,0},{1,9},{9,17},{17,25},{25,1},{2,10},{10... | collective-permute-start | bytes 15368 | tf_op jit(solution)/shard_map/ppermute | solution.py:95
  290.5 70.3 %copy-start.1 = (bf16[4,2,320,768]{3,2,1,0:T(8,128)(2,1)S(1)}, bf16[4,2,320,768]{3,2,1,0:T(8,128)(2,1)}, u32[]{:S(2)}) copy-start(bf16[4,2,320,768]{3,2,1,0:T(8,128)(2,1)} %get-tuple-element.20) | copy-start | bytes 11796484
  300.2 68.7 %collective-permute-start.7 = (f32[4,320]{1,0:T(4,128)S(1)}, f32[4,320]{1,0:T(4,128)S(1)}, u32[]{:S(2)}, u32[]{:S(2)}) collective-permute-start(f32[4,320]{1,0:T(4,128)S(1)} %get-tuple-element.35), channel_id=1, source_target_pairs={{0,16},{8,24},{16,0},{24,8},{1,17},{9,25},{17,1},{25,9},{2,18},{10... | collective-permute-start | bytes 15368 | tf_op jit(solution)/shard_map/ppermute | solution.py:95
  340.6 28.4 %collective-permute-start.8 = (f32[4,320]{1,0:T(4,128)S(1)}, f32[4,320]{1,0:T(4,128)S(1)}, u32[]{:S(2)}, u32[]{:S(2)}) collective-permute-start(f32[4,320]{1,0:T(4,128)S(1)} %get-tuple-element.36), channel_id=1, source_target_pairs={{0,24},{8,0},{16,8},{24,16},{1,25},{9,1},{17,9},{25,17},{2,26},{10... | collective-permute-start | bytes 15368 | tf_op jit(solution)/shard_map/ppermute | solution.py:95
  369.0 7.4 %collective-permute-start.9 = (f32[4,320]{1,0:T(4,128)S(1)}, f32[4,320]{1,0:T(4,128)S(1)}, u32[]{:S(2)}, u32[]{:S(2)}) collective-permute-start(f32[4,320]{1,0:T(4,128)S(1)} %fusion.71), channel_id=1, source_target_pairs={{0,1},{1,0},{2,3},{3,2},{4,5},{5,4},{6,7},{7,6},{8,9},{9,8},{10,11... | collective-permute-start | bytes 15368 | tf_op jit(solution)/shard_map/ppermute | solution.py:100
  376.4 0.9 copy-start.2
  381.4 12.0 %all-to-all-start.4 = ((f32[4,4,80]{2,0,1:T(4,128)}), f32[4,4,80]{2,0,1:T(4,128)S(1)}, u32[]{:S(2)}, u32[]{:S(2)}) async-start(f32[4,4,80]{2,0,1:T(4,128)} %copy.78), calls=%async_computation.4 | async-start | bytes 16384 | tf_op jit(solution)/shard_map/all_to_all | solution.py:103
Sparse Core Ops, SparseCore 0:
  38.6 158.6 all-gather.1

commit v11 on v10

--- a/solution.py
+++ b/solution.py
@@ -67,11 +67,11 @@
             preferred_element_type=jnp.float32,
         ).astype(columns.dtype)
         received = lax.all_to_all(picked, "expert", split_axis=0, concat_axis=0, tiled=True)
-        if c == chunks - 1:
-            hidden_all, received = lax.optimization_barrier((hidden_all, received))
         partial = jnp.einsum(
             "qglsd,lfd->glqsf", received, down_weight[local], preferred_element_type=jnp.float32
         ).reshape(groups, per, slot_rows_all, ff_part)
+        if c == chunks - 1:
+            hidden_all, partial = lax.optimization_barrier((hidden_all, partial))
         sent = partial.astype(jnp.bfloat16)
         expert_grad = lax.dynamic_index_in_dim(partial, me, 0, keepdims=False)
         for shift in range(1, groups):

time: 407 us -> 403 us (level)
    ppermute x6, waiting for transfers between devices: 106 us -> 52.8 us  [body(): lax.ppermute(chunk, 'dp', pairs).astype(jnp.float32)]
    all_to_all x2, waiting for transfers between devices: 47.1 us -> 89.7 us  [body(): lax.all_to_all(picked, 'expert', split_axis=0, concat_axis=0, tiled=True)]
    ppermute x3, waiting for transfers between devices: 38.9 us -> 47.6 us  [body(): own_dots = own_dots + lax.ppermute(chunk, 'dp', pairs)]
  transfers between devices with their start and end apart: 15 -> 15, of which waited for: 5 -> 5; matrix products, arithmetic and copies ran while one was open for 22% -> 23% of each run, Pallas kernels for 0% -> 0%
where the time goes in v11:
time: 403 us
  waiting for transfers between devices  190 us (47%)
  starting transfers between devices  54.6 us (14%)
  other arithmetic  46.8 us (12%)
  matrix products  40.2 us (10%)
  local copies, waits for them, and re-layouts  28.4 us (7%)
  blocking collectives  28.1 us (7%)
  between operations  14.4 us (4%)
    all_to_all x2, waiting for transfers between devices, body(): lax.all_to_all(picked, 'expert', split_axis=0, concat_axis=0, tiled=True)  89.7 us
    ppermute x6, waiting for transfers between devices, body(): lax.ppermute(chunk, 'dp', pairs).astype(jnp.float32)  52.8 us
    ppermute x3, waiting for transfers between devices, body(): own_dots = own_dots + lax.ppermute(chunk, 'dp', pairs)  47.6 us
    all_to_all x1, blocking collectives, body(): lax.all_to_all(packed, 'dp', split_axis=1, concat_axis=0, tiled=True)  28.1 us
    ppermute x3, starting transfers between devices, body(): own_dots = own_dots + lax.ppermute(chunk, 'dp', pairs)  24.7 us
    dot_general x2, matrix products, body(): jnp.einsum('glqsf,qglsd->lfd', scaled, received, preferred_element_type=j...  16.6 us
    dot_general x2, matrix products, body(): jnp.einsum('qglsd,lfd->glqsf', received, down_weight[local], preferred_el...  14.4 us
    all_to_all x2, starting transfers between devices, body(): lax.all_to_all(picked, 'expert', split_axis=0, concat_axis=0, tiled=True)  12.2 us
  transfers between devices with their start and end apart: 15, of which 5 were waited for; matrix products, arithmetic and copies ran while one was open for 23% of the time, Pallas kernels for 0%

profile of v11, /device:TPU:29, one launch (start us, length us, event | category | flops | bytes accessed | tf_op | source)
XLA Modules:
  0.0 402.6 jit_solution(14683617745274715366)
XLA Ops:
  10.3 28.1 %all_to_all.38 = bf16[128,4,1040]{0,2,1:T(8,128)(2,1)S(1)} all-to-all(bf16[128,4,1040]{0,2,1:T(8,128)(2,1)S(1)} %pad_maximum_fusion.1), channel_id=1, replica_groups=mesh['dp'=4,'expert'=4,'etp'=2] {'dp'}, dimensions={1} | all-to-all | bytes 2129920 | tf_op jit(solution)/shard_map/all_to_all | solution.py:25
  40.8 5.6 %fusion.1 = bf16[4,1,1280,1]{2,1,3,0:T(2,128)(2,1)S(1)} fusion(bf16[4,128,8,1]{2,3,1,0:T(2,128)(2,1)S(1)} %copy.81, s32[4,128,8]{2,1,0:T(8,128)S(1)} %fusion.58), kind=kOutput, calls=%fused_computation.2 | convolution fusion | flops 15728640 | bytes 34816 | tf_op jit(solution)/shard_map/gtk,gtkr->gr/dot_general | solution.py:46
  47.1 4.6 %all-to-all-start.1 = ((bf16[4,4,4,80]{3,0,1,2:T(4,128)(2,1)}), bf16[4,4,4,80]{3,0,1,2:T(4,128)(2,1)S(1)}, u32[]{:S(2)}, u32[]{:S(2)}) async-start(bf16[4,4,4,80]{3,0,1,2:T(4,128)(2,1)} %copy.64), calls=%async_computation.1 | async-start | bytes 32768 | tf_op jit(solution)/shard_map/all_to_all | solution.py:53
  51.7 7.4 %fusion.33 = bf16[4,128,1280]{2,1,0:T(8,128)(2,1)} fusion(s32[4,128,8]{2,1,0:T(8,128)S(1)} %fusion.58), kind=kLoop, calls=%fused_computation.36 | loop fusion | flops 15073280 | bytes 1327104 | tf_op jit(solution)/shard_map/reduce_sum | solution.py:47
  62.5 3.2 convert_bitcast_fusion.1
  65.7 5.7 %copy.68 = bf16[4,4,2,80,1024]{4,3,2,1,0:T(8,128)(2,1)} copy(bf16[4,4,2,80,1024]{4,3,0,2,1:T(8,128)(2,1)} %convert_bitcast_fusion.1) | data formatting | bytes 10485760 | tf_op jit(solution)/shard_map/convert_element_type | solution.py:68
  71.4 5.2 %all-to-all-start.2 = ((bf16[4,4,2,80,1024]{4,3,2,1,0:T(8,128)(2,1)}), bf16[4,4,2,80,1024]{4,3,2,1,0:T(8,128)(2,1)}, u32[]{:S(2)}, u32[]{:S(2)}) async-start(bf16[4,4,2,80,1024]{4,3,2,1,0:T(8,128)(2,1)} %copy.68), calls=%async_computation.2 | async-start | bytes 10485760 | tf_op jit(solution)/shard_map/all_to_all | solution.py:69
  81.3 5.8 %copy.71 = bf16[4,4,2,80,1024]{4,3,2,1,0:T(8,128)(2,1)} copy(bf16[4,4,2,80,1024]{4,3,0,2,1:T(8,128)(2,1)} %convert_bitcast_fusion) | data formatting | bytes 10485760 | tf_op jit(solution)/shard_map/convert_element_type | solution.py:68
  87.1 47.1 %all-to-all-done.2 = bf16[4,4,2,80,1024]{4,3,2,1,0:T(8,128)(2,1)} async-done(((bf16[4,4,2,80,1024]{4,3,2,1,0:T(8,128)(2,1)}), bf16[4,4,2,80,1024]{4,3,2,1,0:T(8,128)(2,1)}, u32[]{:S(2)}, u32[]{:S(2)}) %all-to-all-start.2) | async-done | bytes 5242912 | tf_op jit(solution)/shard_map/all_to_all | solution.py:69
  134.2 7.0 %all-to-all-start.3 = ((bf16[4,4,2,80,1024]{4,3,2,1,0:T(8,128)(2,1)}), bf16[4,4,2,80,1024]{4,3,2,1,0:T(8,128)(2,1)}, u32[]{:S(2)}, u32[]{:S(2)}) async-start(bf16[4,4,2,80,1024]{4,3,2,1,0:T(8,128)(2,1)} %copy.71), calls=%async_computation.3 | async-start | bytes 10485760 | tf_op jit(solution)/shard_map/all_to_all | solution.py:69
  141.4 7.2 %fusion.23 = f32[4,2,4,80,768]{4,3,0,2,1:T(8,128)S(1)} fusion(bf16[4,768,1024]{2,1,0:T(8,128)(2,1)} %param.9, bf16[4,4,2,80,1024]{4,3,2,1,0:T(8,128)(2,1)} %all-to-all-done.2), kind=kOutput, calls=%fused_computation.34 | convolution fusion | flops 4026531840 | bytes 16252928 | tf_op jit(solution)/shard_map/qglsd,lfd->glqsf/dot_general | solution.py:70
  156.2 42.6 %all-to-all-done.3 = bf16[4,4,2,80,1024]{4,3,2,1,0:T(8,128)(2,1)} async-done(((bf16[4,4,2,80,1024]{4,3,2,1,0:T(8,128)(2,1)}), bf16[4,4,2,80,1024]{4,3,2,1,0:T(8,128)(2,1)}, u32[]{:S(2)}, u32[]{:S(2)}) %all-to-all-start.3) | async-done | bytes 5242912 | tf_op jit(solution)/shard_map/all_to_all | solution.py:69
  198.8 7.2 %fusion.28 = f32[4,2,4,80,768]{4,3,0,2,1:T(8,128)S(1)} fusion(bf16[4,768,1024]{2,1,0:T(8,128)(2,1)} %param.9, bf16[4,4,2,80,1024]{4,3,2,1,0:T(8,128)(2,1)} %all-to-all-done.3), kind=kOutput, calls=%fused_computation.35 | convolution fusion | flops 4026531840 | bytes 16252928 | tf_op jit(solution)/shard_map/qglsd,lfd->glqsf/dot_general | solution.py:70
  206.0 3.7 copy.73
  209.7 10.7 %collective-permute-done.2 = bf16[2,320,768]{2,1,0:T(8,128)(2,1)} collective-permute-done((bf16[2,320,768]{2,1,0:T(8,128)(2,1)S(1)}, bf16[2,320,768]{2,1,0:T(8,128)(2,1)}, u32[]{:S(2)}, u32[]{:S(2)}) %collective-permute-start.2) | collective-permute-done | bytes 983072 | tf_op jit(solution)/shard_map/ppermute | solution.py:80
  220.3 42.1 %collective-permute-done.1 = bf16[2,320,768]{2,1,0:T(8,128)(2,1)} collective-permute-done((bf16[2,320,768]{2,1,0:T(8,128)(2,1)S(1)}, bf16[2,320,768]{2,1,0:T(8,128)(2,1)}, u32[]{:S(2)}, u32[]{:S(2)}) %collective-permute-start.1) | collective-permute-done | bytes 983072 | tf_op jit(solution)/shard_map/ppermute | solution.py:80
  265.1 8.9 %fusion.6 = (bf16[4,2,320,768]{3,2,1,0:T(8,128)(2,1)S(1)}, f32[4,2,320]{2,1,0:T(2,128)S(1)}, bf16[4,2,320,768]{3,2,1,0:T(8,128)(2,1)S(1)}) fusion(f32[4,2,320]{2,1,0:T(2,128)S(1)} %copy.76, bf16[4,4,320,768]{3,2,1,0:T(8,128)(2,1)} %all-gather.2.cloned.1.call-done, f32[4,2,320,768]{3,2,1,0:T(8,128)} %bitcast.149), kind=kLoop, calls=%fused_computation.11 | loop fusion | flops 11793920 | bytes 19681280 | tf_op jit(solution)/shard_map/convert_element_type | solution.py:83
  285.6 8.2 %bitcast_convert_fusion = bf16[2,768,1024]{2,1,0:T(8,128)(2,1)} fusion(bf16[4,2,4,80,768]{4,3,2,1,0:T(8,128)(2,1)S(1)} %bitcast.157, bf16[4,4,2,80,1024]{4,3,2,1,0:T(8,128)(2,1)} %all-to-all-done.3), kind=kOutput, calls=%fused_computation.13 | convolution fusion | flops 4028104704 | bytes 12320768 | tf_op jit(solution)/shard_map/glqsf,qglsd->lfd/dot_general | solution.py:85
  293.8 47.6 %collective-permute-done.6 = f32[4,320]{1,0:T(4,128)S(1)} collective-permute-done((f32[4,320]{1,0:T(4,128)S(1)}, f32[4,320]{1,0:T(4,128)S(1)}, u32[]{:S(2)}, u32[]{:S(2)}) %collective-permute-start.6) | collective-permute-done | bytes 5152 | tf_op jit(solution)/shard_map/ppermute | solution.py:95
  341.4 20.2 %collective-permute-start.8 = (f32[4,320]{1,0:T(4,128)S(1)}, f32[4,320]{1,0:T(4,128)S(1)}, u32[]{:S(2)}, u32[]{:S(2)}) collective-permute-start(f32[4,320]{1,0:T(4,128)S(1)} %get-tuple-element.37), channel_id=1, source_target_pairs={{0,24},{8,0},{16,8},{24,16},{1,25},{9,1},{17,9},{25,17},{2,26},{10... | collective-permute-start | bytes 15368 | tf_op jit(solution)/shard_map/ppermute | solution.py:95
  361.6 8.4 %bitcast_convert_fusion.1 = bf16[2,768,1024]{2,1,0:T(8,128)(2,1)} fusion(bf16[4,2,4,80,768]{4,3,2,1,0:T(8,128)(2,1)S(1)} %bitcast.158, bf16[4,4,2,80,1024]{4,3,2,1,0:T(8,128)(2,1)} %all-to-all-done.2), kind=kOutput, calls=%fused_computation.14 | convolution fusion | flops 4028104704 | bytes 12320768 | tf_op jit(solution)/shard_map/glqsf,qglsd->lfd/dot_general | solution.py:85
  371.2 5.1 %pad_maximum_fusion = bf16[4,768,1024]{2,1,0:T(8,128)(2,1)} fusion(bf16[2,768,1024]{2,1,0:T(8,128)(2,1)S(1)} %copy-done.2, bf16[2,768,1024]{2,1,0:T(8,128)(2,1)} %bitcast_convert_fusion.1), kind=kLoop, calls=%fused_computation.12 | loop fusion | flops 3145728 | bytes 12582912 | tf_op jit(solution)/shard_map/concatenate | solution.py:88
  380.9 6.0 %all-to-all-start.4 = ((f32[4,4,80]{2,0,1:T(4,128)}), f32[4,4,80]{2,0,1:T(4,128)S(1)}, u32[]{:S(2)}, u32[]{:S(2)}) async-start(f32[4,4,80]{2,0,1:T(4,128)} %copy.78), calls=%async_computation.4 | async-start | bytes 16384 | tf_op jit(solution)/shard_map/all_to_all | solution.py:103
  386.9 5.8 %fusion = bf16[4,128,8,1280]{3,2,1,0:T(8,128)(2,1)} fusion(s32[4,128,8]{2,1,0:T(8,128)S(1)} %fusion.58), kind=kLoop, calls=%fused_computation.1 | loop fusion | flops 10485760 | bytes 10502144 | tf_op jit(solution)/shard_map/convert_element_type | solution.py:44
  (84 shorter events, 44.9 us)
Async XLA Ops:
  7.2 257.9 %all-gather.2.cloned.1.call-start = ((), (), s32[]{:S(2)}) async-start(), calls=%async_computation.5 | async-start | bytes 9830400 | tf_op jit(solution)/shard_map/all_gather | solution.py:29
  47.1 24.3 %all-to-all-start.1 = ((bf16[4,4,4,80]{3,0,1,2:T(4,128)(2,1)}), bf16[4,4,4,80]{3,0,1,2:T(4,128)(2,1)S(1)}, u32[]{:S(2)}, u32[]{:S(2)}) async-start(bf16[4,4,4,80]{3,0,1,2:T(4,128)(2,1)} %copy.64), calls=%async_computation.1 | async-start | bytes 32768 | tf_op jit(solution)/shard_map/all_to_all | solution.py:53
  71.4 62.9 %all-to-all-start.2 = ((bf16[4,4,2,80,1024]{4,3,2,1,0:T(8,128)(2,1)}), bf16[4,4,2,80,1024]{4,3,2,1,0:T(8,128)(2,1)}, u32[]{:S(2)}, u32[]{:S(2)}) async-start(bf16[4,4,2,80,1024]{4,3,2,1,0:T(8,128)(2,1)} %copy.68), calls=%async_computation.2 | async-start | bytes 10485760 | tf_op jit(solution)/shard_map/all_to_all | solution.py:69
  134.2 64.6 %all-to-all-start.3 = ((bf16[4,4,2,80,1024]{4,3,2,1,0:T(8,128)(2,1)}), bf16[4,4,2,80,1024]{4,3,2,1,0:T(8,128)(2,1)}, u32[]{:S(2)}, u32[]{:S(2)}) async-start(bf16[4,4,2,80,1024]{4,3,2,1,0:T(8,128)(2,1)} %copy.71), calls=%async_computation.3 | async-start | bytes 10485760 | tf_op jit(solution)/shard_map/all_to_all | solution.py:69
  149.3 3.1 copy-start
  153.6 56.1 %collective-permute-start = (bf16[2,320,768]{2,1,0:T(8,128)(2,1)}, bf16[2,320,768]{2,1,0:T(8,128)(2,1)S(1)}, u32[]{:S(2)}, u32[]{:S(2)}) collective-permute-start(bf16[2,320,768]{2,1,0:T(8,128)(2,1)} %get-tuple-element.25), channel_id=1, source_target_pairs={{0,8},{8,16},{16,24},{24,0},{1,9},{9,17},{17,25},{25,1},{2,10},{10... | collective-permute-start | bytes 2949128 | tf_op jit(solution)/shard_map/ppermute | solution.py:80
  155.7 64.7 %collective-permute-start.2 = (bf16[2,320,768]{2,1,0:T(8,128)(2,1)S(1)}, bf16[2,320,768]{2,1,0:T(8,128)(2,1)}, u32[]{:S(2)}, u32[]{:S(2)}) collective-permute-start(bf16[2,320,768]{2,1,0:T(8,128)(2,1)S(1)} %get-tuple-element.26), channel_id=1, source_target_pairs={{0,24},{8,0},{16,8},{24,16},{1,25},{9,1},{17,9},{25,17},{2,26},{10... | collective-permute-start | bytes 2949128 | tf_op jit(solution)/shard_map/ppermute | solution.py:80
  155.7 106.8 %collective-permute-start.1 = (bf16[2,320,768]{2,1,0:T(8,128)(2,1)S(1)}, bf16[2,320,768]{2,1,0:T(8,128)(2,1)}, u32[]{:S(2)}, u32[]{:S(2)}) collective-permute-start(bf16[2,320,768]{2,1,0:T(8,128)(2,1)S(1)} %get-tuple-element.27), channel_id=1, source_target_pairs={{0,16},{8,24},{16,0},{24,8},{1,17},{9,25},{17,1},{25,9},{2,18},{10... | collective-permute-start | bytes 2949128 | tf_op jit(solution)/shard_map/ppermute | solution.py:80
  265.1 13.7 %slice-start = ((s8[7864320]{0:T(1024)(128)(4,1)}), s8[4194304]{0:T(1024)(128)(4,1)S(1)}, s32[]{:S(2)}) async-start(s8[7864320]{0:T(1024)(128)(4,1)} %bitcast.144), calls=%async_computation.6 | async-start | bytes 8388608
  265.1 13.7 %slice-start.1 = ((s8[7864320]{0:T(1024)(128)(4,1)}), s8[3670016]{0:T(1024)(128)(4,1)S(1)}, s32[]{:S(2)}) async-start(s8[7864320]{0:T(1024)(128)(4,1)} %bitcast.144), calls=%async_computation.7 | async-start | bytes 7340032
  265.1 13.7 %copy-start.1 = (bf16[4,4,320,768]{3,2,1,0:T(8,128)(2,1)S(1)}, bf16[4,4,320,768]{3,2,1,0:T(8,128)(2,1)}, u32[]{:S(2)}) copy-start(bf16[4,4,320,768]{3,2,1,0:T(8,128)(2,1)} %all-gather.2.cloned.1.call-done) | copy-start | bytes 23592964
  275.6 100.8 %collective-permute-start.3 = (bf16[2,320,768]{2,1,0:T(8,128)(2,1)}, bf16[2,320,768]{2,1,0:T(8,128)(2,1)S(1)}, u32[]{:S(2)}, u32[]{:S(2)}) collective-permute-start(bf16[2,320,768]{2,1,0:T(8,128)(2,1)} %get-tuple-element.28), channel_id=1, source_target_pairs={{0,8},{8,16},{16,24},{24,0},{1,9},{9,17},{17,25},{25,1},{2,10},{10... | collective-permute-start | bytes 2949128 | tf_op jit(solution)/shard_map/ppermute | solution.py:80
  278.5 97.9 %collective-permute-start.5 = (bf16[2,320,768]{2,1,0:T(8,128)(2,1)}, bf16[2,320,768]{2,1,0:T(8,128)(2,1)S(1)}, u32[]{:S(2)}, u32[]{:S(2)}) collective-permute-start(bf16[2,320,768]{2,1,0:T(8,128)(2,1)} %get-tuple-element.29), channel_id=1, source_target_pairs={{0,24},{8,0},{16,8},{24,16},{1,25},{9,1},{17,9},{25,17},{2,26},{10... | collective-permute-start | bytes 2949128 | tf_op jit(solution)/shard_map/ppermute | solution.py:80
  278.5 97.9 %collective-permute-start.4 = (bf16[2,320,768]{2,1,0:T(8,128)(2,1)S(1)}, bf16[2,320,768]{2,1,0:T(8,128)(2,1)}, u32[]{:S(2)}, u32[]{:S(2)}) collective-permute-start(bf16[2,320,768]{2,1,0:T(8,128)(2,1)S(1)} %get-tuple-element.30), channel_id=1, source_target_pairs={{0,16},{8,24},{16,0},{24,8},{1,17},{9,25},{17,1},{25,9},{2,18},{10... | collective-permute-start | bytes 2949128 | tf_op jit(solution)/shard_map/ppermute | solution.py:80
  281.1 60.3 %collective-permute-start.6 = (f32[4,320]{1,0:T(4,128)S(1)}, f32[4,320]{1,0:T(4,128)S(1)}, u32[]{:S(2)}, u32[]{:S(2)}) collective-permute-start(f32[4,320]{1,0:T(4,128)S(1)} %get-tuple-element.35), channel_id=1, source_target_pairs={{0,8},{8,16},{16,24},{24,0},{1,9},{9,17},{17,25},{25,1},{2,10},{10... | collective-permute-start | bytes 15368 | tf_op jit(solution)/shard_map/ppermute | solution.py:95
  284.2 85.8 %collective-permute-start.7 = (f32[4,320]{1,0:T(4,128)S(1)}, f32[4,320]{1,0:T(4,128)S(1)}, u32[]{:S(2)}, u32[]{:S(2)}) collective-permute-start(f32[4,320]{1,0:T(4,128)S(1)} %get-tuple-element.36), channel_id=1, source_target_pairs={{0,16},{8,24},{16,0},{24,8},{1,17},{9,25},{17,1},{25,9},{2,18},{10... | collective-permute-start | bytes 15368 | tf_op jit(solution)/shard_map/ppermute | solution.py:95
  341.4 28.6 %collective-permute-start.8 = (f32[4,320]{1,0:T(4,128)S(1)}, f32[4,320]{1,0:T(4,128)S(1)}, u32[]{:S(2)}, u32[]{:S(2)}) collective-permute-start(f32[4,320]{1,0:T(4,128)S(1)} %get-tuple-element.37), channel_id=1, source_target_pairs={{0,24},{8,0},{16,8},{24,16},{1,25},{9,1},{17,9},{25,17},{2,26},{10... | collective-permute-start | bytes 15368 | tf_op jit(solution)/shard_map/ppermute | solution.py:95
  361.6 9.6 %copy-start.2 = (bf16[2,768,1024]{2,1,0:T(8,128)(2,1)S(1)}, bf16[2,768,1024]{2,1,0:T(8,128)(2,1)}, u32[]{:S(2)}) copy-start(bf16[2,768,1024]{2,1,0:T(8,128)(2,1)} %bitcast_convert_fusion) | copy-start | bytes 9437188
  370.0 6.3 %collective-permute-start.9 = (f32[4,320]{1,0:T(4,128)S(1)}, f32[4,320]{1,0:T(4,128)S(1)}, u32[]{:S(2)}, u32[]{:S(2)}) collective-permute-start(f32[4,320]{1,0:T(4,128)S(1)} %fusion.71), channel_id=1, source_target_pairs={{0,1},{1,0},{2,3},{3,2},{4,5},{5,4},{6,7},{7,6},{8,9},{9,8},{10,11... | collective-permute-start | bytes 15368 | tf_op jit(solution)/shard_map/ppermute | solution.py:100
  380.9 11.8 %all-to-all-start.4 = ((f32[4,4,80]{2,0,1:T(4,128)}), f32[4,4,80]{2,0,1:T(4,128)S(1)}, u32[]{:S(2)}, u32[]{:S(2)}) async-start(f32[4,4,80]{2,0,1:T(4,128)} %copy.78), calls=%async_computation.4 | async-start | bytes 16384 | tf_op jit(solution)/shard_map/all_to_all | solution.py:103
Sparse Core Ops, SparseCore 0:
  38.7 159.2 all-gather.1

commit v12 on v11

--- a/solution.py
+++ b/solution.py
@@ -73,19 +73,24 @@
         if c == chunks - 1:
             hidden_all, partial = lax.optimization_barrier((hidden_all, partial))
         sent = partial.astype(jnp.bfloat16)
-        expert_grad = lax.dynamic_index_in_dim(partial, me, 0, keepdims=False)
+        arrivals = []
         for shift in range(1, groups):
             chunk = lax.dynamic_index_in_dim(sent, (me + shift) % groups, 0, keepdims=False)
             pairs = [(i, (i + shift) % groups) for i in range(groups)]
-            expert_grad = expert_grad + lax.ppermute(chunk, "dp", pairs).astype(jnp.float32)
+            arrivals.append(lax.ppermute(chunk, "dp", pairs))
         hidden_rows = hidden_all[:, local].astype(jnp.float32)
         dots.append(jnp.sum(hidden_rows * partial, axis=3))
         scaled = (jnp.moveaxis(slot_gates[local], 0, 1)[..., None] * hidden_rows).astype(jnp.bfloat16)
         scaled = scaled.reshape(groups, per, senders, capacity, ff_part)
         weight_sum = jnp.einsum("glqsf,qglsd->lfd", scaled, received, preferred_element_type=jnp.float32)
         grads.append(weight_sum.astype(jnp.bfloat16))
+        expert_grad = lax.dynamic_index_in_dim(partial, me, 0, keepdims=False)
+        if c == chunks - 1:
+            weight_grad = jnp.concatenate(grads, axis=0)
+            weight_grad, expert_grad = lax.optimization_barrier((weight_grad, expert_grad))
+        for arrived in arrivals:
+            expert_grad = expert_grad + arrived.astype(jnp.float32)
         hidden_parts.append((own_gates[local][..., None] * expert_grad).astype(jnp.bfloat16))
-    weight_grad = jnp.concatenate(grads, axis=0)
     dot_part = jnp.concatenate(dots, axis=1)
     hidden_grad = jnp.concatenate(hidden_parts, axis=0)[None]
     own_dots = lax.dynamic_index_in_dim(dot_part, me, 0, keepdims=False)

time: 403 us -> 395 us (0.980)
  waiting for transfers between devices: 190 us -> 182 us
    convert_element_type x2 -> x0, other arithmetic: 11.2 us -> none  [body(): (jnp.moveaxis(slot_gates[local], 0, 1)[..., None] * hidden_rows).astype(j...]
    reduce_sum x0 -> x2, other arithmetic: none -> 10.3 us  [body(): dots.append(jnp.sum(hidden_rows * partial, axis=3))]
    ppermute x3, waiting for transfers between devices: 47.6 us -> 39 us  [body(): own_dots = own_dots + lax.ppermute(chunk, 'dp', pairs)]
  transfers between devices with their start and end apart: 15 -> 15, of which waited for: 5 -> 5; matrix products, arithmetic and copies ran while one was open for 23% -> 24% of each run, Pallas kernels for 0% -> 0%
where the time goes in v12:
time: 395 us; the launch traced here: 394 us
  waiting for transfers between devices  182 us (46%)
  starting transfers between devices  55.1 us (14%)
  other arithmetic  45.9 us (12%)
  matrix products  40.2 us (10%)
  local copies, waits for them, and re-layouts  28.8 us (7%)
  blocking collectives  28.1 us (7%)
  between operations  14.4 us (4%)
    all_to_all x2, waiting for transfers between devices, body(): lax.all_to_all(picked, 'expert', split_axis=0, concat_axis=0, tiled=True)  89.7 us
    ppermute x6, waiting for transfers between devices, body(): arrivals.append(lax.ppermute(chunk, 'dp', pairs))  52.8 us
    ppermute x3, waiting for transfers between devices, body(): own_dots = own_dots + lax.ppermute(chunk, 'dp', pairs)  39 us
    all_to_all x1, blocking collectives, body(): lax.all_to_all(packed, 'dp', split_axis=1, concat_axis=0, tiled=True)  28.1 us
    ppermute x3, starting transfers between devices, body(): own_dots = own_dots + lax.ppermute(chunk, 'dp', pairs)  24.4 us
    dot_general x2, matrix products, body(): jnp.einsum('glqsf,qglsd->lfd', scaled, received, preferred_element_type=j...  16.6 us
    dot_general x2, matrix products, body(): jnp.einsum('qglsd,lfd->glqsf', received, down_weight[local], preferred_el...  14.4 us
    all_to_all x2, starting transfers between devices, body(): lax.all_to_all(picked, 'expert', split_axis=0, concat_axis=0, tiled=True)  12.2 us
  transfers between devices with their start and end apart: 15, of which 5 were waited for; matrix products, arithmetic and copies ran while one was open for 24% of the time, Pallas kernels for 0%

profile of v12, /device:TPU:29, one launch (start us, length us, event | category | flops | bytes accessed | tf_op | source)
XLA Modules:
  0.0 394.0 jit_solution(10784708245323259568)
XLA Ops:
  10.3 28.1 %all_to_all.38 = bf16[128,4,1040]{0,2,1:T(8,128)(2,1)S(1)} all-to-all(bf16[128,4,1040]{0,2,1:T(8,128)(2,1)S(1)} %pad_maximum_fusion.1), channel_id=1, replica_groups=mesh['dp'=4,'expert'=4,'etp'=2] {'dp'}, dimensions={1} | all-to-all | bytes 2129920 | tf_op jit(solution)/shard_map/all_to_all | solution.py:25
  40.8 5.6 %fusion.1 = bf16[4,1,1280,1]{2,1,3,0:T(2,128)(2,1)S(1)} fusion(bf16[4,128,8,1]{2,3,1,0:T(2,128)(2,1)S(1)} %copy.81, s32[4,128,8]{2,1,0:T(8,128)S(1)} %fusion.54), kind=kOutput, calls=%fused_computation.2 | convolution fusion | flops 15728640 | bytes 34816 | tf_op jit(solution)/shard_map/gtk,gtkr->gr/dot_general | solution.py:46
  47.1 4.6 %all-to-all-start.1 = ((bf16[4,4,4,80]{3,0,1,2:T(4,128)(2,1)}), bf16[4,4,4,80]{3,0,1,2:T(4,128)(2,1)S(1)}, u32[]{:S(2)}, u32[]{:S(2)}) async-start(bf16[4,4,4,80]{3,0,1,2:T(4,128)(2,1)} %copy.64), calls=%async_computation.1 | async-start | bytes 32768 | tf_op jit(solution)/shard_map/all_to_all | solution.py:53
  51.7 7.4 %fusion.33 = bf16[4,128,1280]{2,1,0:T(8,128)(2,1)} fusion(s32[4,128,8]{2,1,0:T(8,128)S(1)} %fusion.54), kind=kLoop, calls=%fused_computation.36 | loop fusion | flops 15073280 | bytes 1327104 | tf_op jit(solution)/shard_map/reduce_sum | solution.py:47
  62.5 3.2 convert_bitcast_fusion.1
  65.7 5.7 %copy.68 = bf16[4,4,2,80,1024]{4,3,2,1,0:T(8,128)(2,1)} copy(bf16[4,4,2,80,1024]{4,3,0,2,1:T(8,128)(2,1)} %convert_bitcast_fusion.1) | data formatting | bytes 10485760 | tf_op jit(solution)/shard_map/convert_element_type | solution.py:68
  71.4 5.2 %all-to-all-start.2 = ((bf16[4,4,2,80,1024]{4,3,2,1,0:T(8,128)(2,1)}), bf16[4,4,2,80,1024]{4,3,2,1,0:T(8,128)(2,1)}, u32[]{:S(2)}, u32[]{:S(2)}) async-start(bf16[4,4,2,80,1024]{4,3,2,1,0:T(8,128)(2,1)} %copy.68), calls=%async_computation.2 | async-start | bytes 10485760 | tf_op jit(solution)/shard_map/all_to_all | solution.py:69
  81.3 5.8 %copy.74 = bf16[4,4,2,80,1024]{4,3,2,1,0:T(8,128)(2,1)} copy(bf16[4,4,2,80,1024]{4,3,0,2,1:T(8,128)(2,1)} %convert_bitcast_fusion) | data formatting | bytes 10485760 | tf_op jit(solution)/shard_map/convert_element_type | solution.py:68
  87.1 47.1 %all-to-all-done.2 = bf16[4,4,2,80,1024]{4,3,2,1,0:T(8,128)(2,1)} async-done(((bf16[4,4,2,80,1024]{4,3,2,1,0:T(8,128)(2,1)}), bf16[4,4,2,80,1024]{4,3,2,1,0:T(8,128)(2,1)}, u32[]{:S(2)}, u32[]{:S(2)}) %all-to-all-start.2) | async-done | bytes 5242912 | tf_op jit(solution)/shard_map/all_to_all | solution.py:69
  134.2 7.0 %all-to-all-start.3 = ((bf16[4,4,2,80,1024]{4,3,2,1,0:T(8,128)(2,1)}), bf16[4,4,2,80,1024]{4,3,2,1,0:T(8,128)(2,1)}, u32[]{:S(2)}, u32[]{:S(2)}) async-start(bf16[4,4,2,80,1024]{4,3,2,1,0:T(8,128)(2,1)} %copy.74), calls=%async_computation.3 | async-start | bytes 10485760 | tf_op jit(solution)/shard_map/all_to_all | solution.py:69
  141.4 7.2 %fusion.23 = f32[4,2,4,80,768]{4,3,0,2,1:T(8,128)S(1)} fusion(bf16[4,768,1024]{2,1,0:T(8,128)(2,1)} %param.9, bf16[4,4,2,80,1024]{4,3,2,1,0:T(8,128)(2,1)} %all-to-all-done.2), kind=kOutput, calls=%fused_computation.34 | convolution fusion | flops 4026531840 | bytes 16252928 | tf_op jit(solution)/shard_map/qglsd,lfd->glqsf/dot_general | solution.py:70
  156.2 42.6 %all-to-all-done.3 = bf16[4,4,2,80,1024]{4,3,2,1,0:T(8,128)(2,1)} async-done(((bf16[4,4,2,80,1024]{4,3,2,1,0:T(8,128)(2,1)}), bf16[4,4,2,80,1024]{4,3,2,1,0:T(8,128)(2,1)}, u32[]{:S(2)}, u32[]{:S(2)}) %all-to-all-start.3) | async-done | bytes 5242912 | tf_op jit(solution)/shard_map/all_to_all | solution.py:69
  198.8 7.2 %fusion.28 = f32[4,2,4,80,768]{4,3,0,2,1:T(8,128)S(1)} fusion(bf16[4,768,1024]{2,1,0:T(8,128)(2,1)} %param.9, bf16[4,4,2,80,1024]{4,3,2,1,0:T(8,128)(2,1)} %all-to-all-done.3), kind=kOutput, calls=%fused_computation.35 | convolution fusion | flops 4026531840 | bytes 16252928 | tf_op jit(solution)/shard_map/qglsd,lfd->glqsf/dot_general | solution.py:70
  206.0 3.7 copy.76
  209.7 10.7 %collective-permute-done.2 = bf16[2,320,768]{2,1,0:T(8,128)(2,1)} collective-permute-done((bf16[2,320,768]{2,1,0:T(8,128)(2,1)S(1)}, bf16[2,320,768]{2,1,0:T(8,128)(2,1)}, u32[]{:S(2)}, u32[]{:S(2)}) %collective-permute-start.2) | collective-permute-done | bytes 983072 | tf_op jit(solution)/shard_map/ppermute | solution.py:80
  220.3 42.1 %collective-permute-done.1 = bf16[2,320,768]{2,1,0:T(8,128)(2,1)} collective-permute-done((bf16[2,320,768]{2,1,0:T(8,128)(2,1)S(1)}, bf16[2,320,768]{2,1,0:T(8,128)(2,1)}, u32[]{:S(2)}, u32[]{:S(2)}) %collective-permute-start.1) | collective-permute-done | bytes 983072 | tf_op jit(solution)/shard_map/ppermute | solution.py:80
  265.1 8.0 %fusion.6 = (f32[4,2,320]{2,1,0:T(2,128)S(1)}, bf16[4,2,320,768]{3,2,1,0:T(8,128)(2,1)S(1)}, bf16[4,2,320,768]{3,2,1,0:T(8,128)(2,1)S(1)}) fusion(f32[4,2,320,768]{3,2,1,0:T(8,128)} %bitcast.141, bf16[4,4,320,768]{3,2,1,0:T(8,128)(2,1)} %all-gather.2.cloned.1.call-done, f32[4,2,320]{2,1,0:T(2,128)S(1)} %copy.73), kind=kLoop, calls=%fused_computation.11 | loop fusion | flops 11793920 | bytes 19681280 | tf_op jit(solution)/shard_map/reduce_sum | solution.py:82
  283.5 8.2 %bitcast_convert_fusion = bf16[2,768,1024]{2,1,0:T(8,128)(2,1)} fusion(bf16[4,2,4,80,768]{4,3,2,1,0:T(8,128)(2,1)S(1)} %bitcast.149, bf16[4,4,2,80,1024]{4,3,2,1,0:T(8,128)(2,1)} %all-to-all-done.3), kind=kOutput, calls=%fused_computation.13 | convolution fusion | flops 4028104704 | bytes 12320768 | tf_op jit(solution)/shard_map/glqsf,qglsd->lfd/dot_general | solution.py:85
  291.7 8.4 %bitcast_convert_fusion.1 = bf16[2,768,1024]{2,1,0:T(8,128)(2,1)} fusion(bf16[4,2,4,80,768]{4,3,2,1,0:T(8,128)(2,1)S(1)} %bitcast.150, bf16[4,4,2,80,1024]{4,3,2,1,0:T(8,128)(2,1)} %all-to-all-done.2), kind=kOutput, calls=%fused_computation.14 | convolution fusion | flops 4028104704 | bytes 12320768 | tf_op jit(solution)/shard_map/glqsf,qglsd->lfd/dot_general | solution.py:85
  300.0 39.0 %collective-permute-done.6 = f32[4,320]{1,0:T(4,128)S(1)} collective-permute-done((f32[4,320]{1,0:T(4,128)S(1)}, f32[4,320]{1,0:T(4,128)S(1)}, u32[]{:S(2)}, u32[]{:S(2)}) %collective-permute-start.6) | collective-permute-done | bytes 5152 | tf_op jit(solution)/shard_map/ppermute | solution.py:100
  339.1 20.2 %collective-permute-start.8 = (f32[4,320]{1,0:T(4,128)S(1)}, f32[4,320]{1,0:T(4,128)S(1)}, u32[]{:S(2)}, u32[]{:S(2)}) collective-permute-start(f32[4,320]{1,0:T(4,128)S(1)} %get-tuple-element.39), channel_id=1, source_target_pairs={{0,24},{8,0},{16,8},{24,16},{1,25},{9,1},{17,9},{25,17},{2,26},{10... | collective-permute-start | bytes 15368 | tf_op jit(solution)/shard_map/ppermute | solution.py:100
  359.2 5.1 %pad_maximum_fusion = bf16[4,768,1024]{2,1,0:T(8,128)(2,1)} fusion(bf16[2,768,1024]{2,1,0:T(8,128)(2,1)S(1)} %copy-done.2, bf16[2,768,1024]{2,1,0:T(8,128)(2,1)} %bitcast_convert_fusion.1), kind=kLoop, calls=%fused_computation.12 | loop fusion | flops 3145728 | bytes 12582912 | tf_op jit(solution)/shard_map/concatenate | solution.py:89
  371.8 6.5 %all-to-all-start.4 = ((f32[4,4,80]{2,0,1:T(4,128)}), f32[4,4,80]{2,0,1:T(4,128)S(1)}, u32[]{:S(2)}, u32[]{:S(2)}) async-start(f32[4,4,80]{2,0,1:T(4,128)} %copy.78), calls=%async_computation.4 | async-start | bytes 16384 | tf_op jit(solution)/shard_map/all_to_all | solution.py:108
  378.3 5.8 %fusion = bf16[4,128,8,1280]{3,2,1,0:T(8,128)(2,1)} fusion(s32[4,128,8]{2,1,0:T(8,128)S(1)} %fusion.54), kind=kLoop, calls=%fused_computation.1 | loop fusion | flops 10485760 | bytes 10502144 | tf_op jit(solution)/shard_map/convert_element_type | solution.py:44
  (85 shorter events, 45.4 us)
Async XLA Ops:
  7.2 257.9 %all-gather.2.cloned.1.call-start = ((), (), s32[]{:S(2)}) async-start(), calls=%async_computation.5 | async-start | bytes 9830400 | tf_op jit(solution)/shard_map/all_gather | solution.py:29
  47.1 24.3 %all-to-all-start.1 = ((bf16[4,4,4,80]{3,0,1,2:T(4,128)(2,1)}), bf16[4,4,4,80]{3,0,1,2:T(4,128)(2,1)S(1)}, u32[]{:S(2)}, u32[]{:S(2)}) async-start(bf16[4,4,4,80]{3,0,1,2:T(4,128)(2,1)} %copy.64), calls=%async_computation.1 | async-start | bytes 32768 | tf_op jit(solution)/shard_map/all_to_all | solution.py:53
  71.4 62.9 %all-to-all-start.2 = ((bf16[4,4,2,80,1024]{4,3,2,1,0:T(8,128)(2,1)}), bf16[4,4,2,80,1024]{4,3,2,1,0:T(8,128)(2,1)}, u32[]{:S(2)}, u32[]{:S(2)}) async-start(bf16[4,4,2,80,1024]{4,3,2,1,0:T(8,128)(2,1)} %copy.68), calls=%async_computation.2 | async-start | bytes 10485760 | tf_op jit(solution)/shard_map/all_to_all | solution.py:69
  134.2 64.6 %all-to-all-start.3 = ((bf16[4,4,2,80,1024]{4,3,2,1,0:T(8,128)(2,1)}), bf16[4,4,2,80,1024]{4,3,2,1,0:T(8,128)(2,1)}, u32[]{:S(2)}, u32[]{:S(2)}) async-start(bf16[4,4,2,80,1024]{4,3,2,1,0:T(8,128)(2,1)} %copy.74), calls=%async_computation.3 | async-start | bytes 10485760 | tf_op jit(solution)/shard_map/all_to_all | solution.py:69
  149.3 3.1 copy-start
  153.6 56.1 %collective-permute-start = (bf16[2,320,768]{2,1,0:T(8,128)(2,1)}, bf16[2,320,768]{2,1,0:T(8,128)(2,1)S(1)}, u32[]{:S(2)}, u32[]{:S(2)}) collective-permute-start(bf16[2,320,768]{2,1,0:T(8,128)(2,1)} %get-tuple-element.29), channel_id=1, source_target_pairs={{0,8},{8,16},{16,24},{24,0},{1,9},{9,17},{17,25},{25,1},{2,10},{10... | collective-permute-start | bytes 2949128 | tf_op jit(solution)/shard_map/ppermute | solution.py:80
  155.7 64.7 %collective-permute-start.2 = (bf16[2,320,768]{2,1,0:T(8,128)(2,1)S(1)}, bf16[2,320,768]{2,1,0:T(8,128)(2,1)}, u32[]{:S(2)}, u32[]{:S(2)}) collective-permute-start(bf16[2,320,768]{2,1,0:T(8,128)(2,1)S(1)} %get-tuple-element.30), channel_id=1, source_target_pairs={{0,24},{8,0},{16,8},{24,16},{1,25},{9,1},{17,9},{25,17},{2,26},{10... | collective-permute-start | bytes 2949128 | tf_op jit(solution)/shard_map/ppermute | solution.py:80
  155.7 106.8 %collective-permute-start.1 = (bf16[2,320,768]{2,1,0:T(8,128)(2,1)S(1)}, bf16[2,320,768]{2,1,0:T(8,128)(2,1)}, u32[]{:S(2)}, u32[]{:S(2)}) collective-permute-start(bf16[2,320,768]{2,1,0:T(8,128)(2,1)S(1)} %get-tuple-element.31), channel_id=1, source_target_pairs={{0,16},{8,24},{16,0},{24,8},{1,17},{9,25},{17,1},{25,9},{2,18},{10... | collective-permute-start | bytes 2949128 | tf_op jit(solution)/shard_map/ppermute | solution.py:80
  265.1 11.8 %slice-start = ((s8[7864320]{0:T(1024)(128)(4,1)}), s8[4194304]{0:T(1024)(128)(4,1)S(1)}, s32[]{:S(2)}) async-start(s8[7864320]{0:T(1024)(128)(4,1)} %bitcast.136), calls=%async_computation.6 | async-start | bytes 8388608
  265.1 11.8 %slice-start.1 = ((s8[7864320]{0:T(1024)(128)(4,1)}), s8[3670016]{0:T(1024)(128)(4,1)S(1)}, s32[]{:S(2)}) async-start(s8[7864320]{0:T(1024)(128)(4,1)} %bitcast.136), calls=%async_computation.7 | async-start | bytes 7340032
  265.1 11.8 %copy-start.1 = (bf16[4,4,320,768]{3,2,1,0:T(8,128)(2,1)S(1)}, bf16[4,4,320,768]{3,2,1,0:T(8,128)(2,1)}, u32[]{:S(2)}) copy-start(bf16[4,4,320,768]{3,2,1,0:T(8,128)(2,1)} %all-gather.2.cloned.1.call-done) | copy-start | bytes 23592964
  273.3 94.0 %collective-permute-start.3 = (bf16[2,320,768]{2,1,0:T(8,128)(2,1)S(1)}, bf16[2,320,768]{2,1,0:T(8,128)(2,1)}, u32[]{:S(2)}, u32[]{:S(2)}) collective-permute-start(bf16[2,320,768]{2,1,0:T(8,128)(2,1)S(1)} %get-tuple-element.32), channel_id=1, source_target_pairs={{0,8},{8,16},{16,24},{24,0},{1,9},{9,17},{17,25},{25,1},{2,10},{10... | collective-permute-start | bytes 2949128 | tf_op jit(solution)/shard_map/ppermute | solution.py:80
  276.3 91.0 %collective-permute-start.5 = (bf16[2,320,768]{2,1,0:T(8,128)(2,1)S(1)}, bf16[2,320,768]{2,1,0:T(8,128)(2,1)}, u32[]{:S(2)}, u32[]{:S(2)}) collective-permute-start(bf16[2,320,768]{2,1,0:T(8,128)(2,1)S(1)} %get-tuple-element.33), channel_id=1, source_target_pairs={{0,24},{8,0},{16,8},{24,16},{1,25},{9,1},{17,9},{25,17},{2,26},{10... | collective-permute-start | bytes 2949128 | tf_op jit(solution)/shard_map/ppermute | solution.py:80
  276.3 91.0 %collective-permute-start.4 = (bf16[2,320,768]{2,1,0:T(8,128)(2,1)S(1)}, bf16[2,320,768]{2,1,0:T(8,128)(2,1)}, u32[]{:S(2)}, u32[]{:S(2)}) collective-permute-start(bf16[2,320,768]{2,1,0:T(8,128)(2,1)S(1)} %get-tuple-element.34), channel_id=1, source_target_pairs={{0,16},{8,24},{16,0},{24,8},{1,17},{9,25},{17,1},{25,9},{2,18},{10... | collective-permute-start | bytes 2949128 | tf_op jit(solution)/shard_map/ppermute | solution.py:80
  279.3 59.8 %collective-permute-start.6 = (f32[4,320]{1,0:T(4,128)S(1)}, f32[4,320]{1,0:T(4,128)S(1)}, u32[]{:S(2)}, u32[]{:S(2)}) collective-permute-start(f32[4,320]{1,0:T(4,128)S(1)} %get-tuple-element.37), channel_id=1, source_target_pairs={{0,8},{8,16},{16,24},{24,0},{1,9},{9,17},{17,25},{25,1},{2,10},{10... | collective-permute-start | bytes 15368 | tf_op jit(solution)/shard_map/ppermute | solution.py:100
  282.0 82.4 %collective-permute-start.7 = (f32[4,320]{1,0:T(4,128)S(1)}, f32[4,320]{1,0:T(4,128)S(1)}, u32[]{:S(2)}, u32[]{:S(2)}) collective-permute-start(f32[4,320]{1,0:T(4,128)S(1)} %get-tuple-element.38), channel_id=1, source_target_pairs={{0,16},{8,24},{16,0},{24,8},{1,17},{9,25},{17,1},{25,9},{2,18},{10... | collective-permute-start | bytes 15368 | tf_op jit(solution)/shard_map/ppermute | solution.py:100
  291.7 67.6 %copy-start.2 = (bf16[2,768,1024]{2,1,0:T(8,128)(2,1)S(1)}, bf16[2,768,1024]{2,1,0:T(8,128)(2,1)}, u32[]{:S(2)}) copy-start(bf16[2,768,1024]{2,1,0:T(8,128)(2,1)} %bitcast_convert_fusion) | copy-start | bytes 9437188
  339.1 25.3 %collective-permute-start.8 = (f32[4,320]{1,0:T(4,128)S(1)}, f32[4,320]{1,0:T(4,128)S(1)}, u32[]{:S(2)}, u32[]{:S(2)}) collective-permute-start(f32[4,320]{1,0:T(4,128)S(1)} %get-tuple-element.39), channel_id=1, source_target_pairs={{0,24},{8,0},{16,8},{24,16},{1,25},{9,1},{17,9},{25,17},{2,26},{10... | collective-permute-start | bytes 15368 | tf_op jit(solution)/shard_map/ppermute | solution.py:100
  364.4 2.9 collective-permute-start.9
  371.8 12.2 %all-to-all-start.4 = ((f32[4,4,80]{2,0,1:T(4,128)}), f32[4,4,80]{2,0,1:T(4,128)S(1)}, u32[]{:S(2)}, u32[]{:S(2)}) async-start(f32[4,4,80]{2,0,1:T(4,128)} %copy.78), calls=%async_computation.4 | async-start | bytes 16384 | tf_op jit(solution)/shard_map/all_to_all | solution.py:108
Sparse Core Ops, SparseCore 0:
  38.7 159.2 all-gather.1

commit v13 on v12

--- a/solution.py
+++ b/solution.py
@@ -87,7 +87,10 @@
         expert_grad = lax.dynamic_index_in_dim(partial, me, 0, keepdims=False)
         if c == chunks - 1:
             weight_grad = jnp.concatenate(grads, axis=0)
-            weight_grad, expert_grad = lax.optimization_barrier((weight_grad, expert_grad))
+            own_select = lax.dynamic_index_in_dim(select, me, 0, keepdims=False).astype(jnp.float32)
+            weight_grad, expert_grad, own_select = lax.optimization_barrier(
+                (weight_grad, expert_grad, own_select)
+            )
         for arrived in arrivals:
             expert_grad = expert_grad + arrived.astype(jnp.float32)
         hidden_parts.append((own_gates[local][..., None] * expert_grad).astype(jnp.bfloat16))
@@ -106,7 +109,6 @@
     hidden_grad, own_dots, weight_grad = lax.optimization_barrier((hidden_grad, own_dots, weight_grad))
     slot_dots = own_dots.reshape(exp_dev, senders, capacity)
     returned = lax.all_to_all(slot_dots, "expert", split_axis=1, concat_axis=1, tiled=True)
-    own_select = lax.dynamic_index_in_dim(select, me, 0, keepdims=False).astype(jnp.float32)
     gate_grad = jnp.sum(own_select * returned.reshape(1, 1, rows), axis=2)
     return (weight_grad, hidden_grad, gate_grad)
 

time: 395 us -> 392 us (level)
  blocking collectives: 28.1 us -> 35 us
  starting transfers between devices: 55.1 us -> 49 us
  waiting for transfers between devices: 182 us -> 177 us
    all_to_all x0 -> x1, blocking collectives: none -> 6.92 us  [body(): lax.all_to_all(slot_dots, 'expert', split_axis=1, concat_axis=1, tiled=True)]
    all_to_all x1 -> x0, starting transfers between devices: 6.46 us -> none  [body(): lax.all_to_all(slot_dots, 'expert', split_axis=1, concat_axis=1, tiled=True)]
    all_to_all x2, waiting for transfers between devices: 89.7 us -> 85 us  [body(): lax.all_to_all(picked, 'expert', split_axis=0, concat_axis=0, tiled=True)]
    convert_element_type x1, other arithmetic: 5.77 us -> 1.75 us  [body(): select = (position[..., None] == row_ids).astype(jnp.bfloat16)]
  transfers between devices with their start and end apart: 15 -> 14, of which waited for: 5 -> 5; matrix products, arithmetic and copies ran while one was open for 24% -> 24% of each run, Pallas kernels for 0% -> 0%
where the time goes in v13:
time: 392 us; the launch traced here: 389 us
  waiting for transfers between devices  177 us (45%)
  starting transfers between devices  49 us (12%)
  other arithmetic  45.1 us (12%)
  matrix products  40.2 us (10%)
  blocking collectives  35 us (9%)
  local copies, waits for them, and re-layouts  28.2 us (7%)
  between operations  14.4 us (4%)
    all_to_all x2, waiting for transfers between devices, body(): lax.all_to_all(picked, 'expert', split_axis=0, concat_axis=0, tiled=True)  85 us
    ppermute x6, waiting for transfers between devices, body(): arrivals.append(lax.ppermute(chunk, 'dp', pairs))  53 us
    ppermute x3, waiting for transfers between devices, body(): own_dots = own_dots + lax.ppermute(chunk, 'dp', pairs)  39.4 us
    all_to_all x1, blocking collectives, body(): lax.all_to_all(packed, 'dp', split_axis=1, concat_axis=0, tiled=True)  28.1 us
    ppermute x3, starting transfers between devices, body(): own_dots = own_dots + lax.ppermute(chunk, 'dp', pairs)  24.7 us
    dot_general x2, matrix products, body(): jnp.einsum('glqsf,qglsd->lfd', scaled, received, preferred_element_type=j...  16.6 us
    dot_general x2, matrix products, body(): jnp.einsum('qglsd,lfd->glqsf', received, down_weight[local], preferred_el...  14.4 us
    all_to_all x2, starting transfers between devices, body(): lax.all_to_all(picked, 'expert', split_axis=0, concat_axis=0, tiled=True)  12.4 us
  transfers between devices with their start and end apart: 14, of which 5 were waited for; matrix products, arithmetic and copies ran while one was open for 24% of the time, Pallas kernels for 0%

profile of v13, /device:TPU:29, one launch (start us, length us, event | category | flops | bytes accessed | tf_op | source)
XLA Modules:
  0.0 389.5 jit_solution(12794413390614591350)
XLA Ops:
  10.3 28.1 %all_to_all.38 = bf16[128,4,1040]{0,2,1:T(8,128)(2,1)S(1)} all-to-all(bf16[128,4,1040]{0,2,1:T(8,128)(2,1)S(1)} %pad_maximum_fusion.1), channel_id=1, replica_groups=mesh['dp'=4,'expert'=4,'etp'=2] {'dp'}, dimensions={1} | all-to-all | bytes 2129920 | tf_op jit(solution)/shard_map/all_to_all | solution.py:25
  40.8 5.6 %fusion.1 = bf16[4,1,1280,1]{2,1,3,0:T(2,128)(2,1)S(1)} fusion(bf16[4,128,8,1]{2,3,1,0:T(2,128)(2,1)S(1)} %copy.81, s32[4,128,8]{2,1,0:T(8,128)S(1)} %fusion.53), kind=kOutput, calls=%fused_computation.2 | convolution fusion | flops 15728640 | bytes 34816 | tf_op jit(solution)/shard_map/gtk,gtkr->gr/dot_general | solution.py:46
  47.1 4.6 %all-to-all-start.1 = ((bf16[4,4,4,80]{3,0,1,2:T(4,128)(2,1)}), bf16[4,4,4,80]{3,0,1,2:T(4,128)(2,1)S(1)}, u32[]{:S(2)}, u32[]{:S(2)}) async-start(bf16[4,4,4,80]{3,0,1,2:T(4,128)(2,1)} %copy.64), calls=%async_computation.1 | async-start | bytes 32768 | tf_op jit(solution)/shard_map/all_to_all | solution.py:53
  51.7 7.4 %fusion.32 = bf16[4,128,1280]{2,1,0:T(8,128)(2,1)} fusion(s32[4,128,8]{2,1,0:T(8,128)S(1)} %fusion.53), kind=kLoop, calls=%fused_computation.35 | loop fusion | flops 15073280 | bytes 1327104 | tf_op jit(solution)/shard_map/reduce_sum | solution.py:47
  62.5 3.2 convert_bitcast_fusion.1
  65.7 5.7 %copy.68 = bf16[4,4,2,80,1024]{4,3,2,1,0:T(8,128)(2,1)} copy(bf16[4,4,2,80,1024]{4,3,0,2,1:T(8,128)(2,1)} %convert_bitcast_fusion.1) | data formatting | bytes 10485760 | tf_op jit(solution)/shard_map/convert_element_type | solution.py:68
  71.4 5.3 %all-to-all-start.2 = ((bf16[4,4,2,80,1024]{4,3,2,1,0:T(8,128)(2,1)}), bf16[4,4,2,80,1024]{4,3,2,1,0:T(8,128)(2,1)}, u32[]{:S(2)}, u32[]{:S(2)}) async-start(bf16[4,4,2,80,1024]{4,3,2,1,0:T(8,128)(2,1)} %copy.68), calls=%async_computation.2 | async-start | bytes 10485760 | tf_op jit(solution)/shard_map/all_to_all | solution.py:69
  78.2 3.2 convert_bitcast_fusion
  81.4 5.8 %copy.74 = bf16[4,4,2,80,1024]{4,3,2,1,0:T(8,128)(2,1)} copy(bf16[4,4,2,80,1024]{4,3,0,2,1:T(8,128)(2,1)} %convert_bitcast_fusion) | data formatting | bytes 10485760 | tf_op jit(solution)/shard_map/convert_element_type | solution.py:68
  87.2 46.9 %all-to-all-done.2 = bf16[4,4,2,80,1024]{4,3,2,1,0:T(8,128)(2,1)} async-done(((bf16[4,4,2,80,1024]{4,3,2,1,0:T(8,128)(2,1)}), bf16[4,4,2,80,1024]{4,3,2,1,0:T(8,128)(2,1)}, u32[]{:S(2)}, u32[]{:S(2)}) %all-to-all-start.2) | async-done | bytes 5242912 | tf_op jit(solution)/shard_map/all_to_all | solution.py:69
  134.1 7.1 %all-to-all-start.3 = ((bf16[4,4,2,80,1024]{4,3,2,1,0:T(8,128)(2,1)}), bf16[4,4,2,80,1024]{4,3,2,1,0:T(8,128)(2,1)}, u32[]{:S(2)}, u32[]{:S(2)}) async-start(bf16[4,4,2,80,1024]{4,3,2,1,0:T(8,128)(2,1)} %copy.74), calls=%async_computation.3 | async-start | bytes 10485760 | tf_op jit(solution)/shard_map/all_to_all | solution.py:69
  145.9 7.2 %fusion.22 = f32[4,2,4,80,768]{4,3,0,2,1:T(8,128)S(1)} fusion(bf16[4,768,1024]{2,1,0:T(8,128)(2,1)} %param.9, bf16[4,4,2,80,1024]{4,3,2,1,0:T(8,128)(2,1)} %all-to-all-done.2), kind=kOutput, calls=%fused_computation.33 | convolution fusion | flops 4026531840 | bytes 16252928 | tf_op jit(solution)/shard_map/qglsd,lfd->glqsf/dot_general | solution.py:70
  160.7 38.1 %all-to-all-done.3 = bf16[4,4,2,80,1024]{4,3,2,1,0:T(8,128)(2,1)} async-done(((bf16[4,4,2,80,1024]{4,3,2,1,0:T(8,128)(2,1)}), bf16[4,4,2,80,1024]{4,3,2,1,0:T(8,128)(2,1)}, u32[]{:S(2)}, u32[]{:S(2)}) %all-to-all-start.3) | async-done | bytes 5242912 | tf_op jit(solution)/shard_map/all_to_all | solution.py:69
  198.8 7.2 %fusion.27 = f32[4,2,4,80,768]{4,3,0,2,1:T(8,128)S(1)} fusion(bf16[4,768,1024]{2,1,0:T(8,128)(2,1)} %param.9, bf16[4,4,2,80,1024]{4,3,2,1,0:T(8,128)(2,1)} %all-to-all-done.3), kind=kOutput, calls=%fused_computation.34 | convolution fusion | flops 4026531840 | bytes 16252928 | tf_op jit(solution)/shard_map/qglsd,lfd->glqsf/dot_general | solution.py:70
  206.0 3.7 copy.76
  209.7 10.7 %collective-permute-done.2 = bf16[2,320,768]{2,1,0:T(8,128)(2,1)} collective-permute-done((bf16[2,320,768]{2,1,0:T(8,128)(2,1)S(1)}, bf16[2,320,768]{2,1,0:T(8,128)(2,1)}, u32[]{:S(2)}, u32[]{:S(2)}) %collective-permute-start.2) | collective-permute-done | bytes 983072 | tf_op jit(solution)/shard_map/ppermute | solution.py:80
  220.4 42.3 %collective-permute-done.1 = bf16[2,320,768]{2,1,0:T(8,128)(2,1)} collective-permute-done((bf16[2,320,768]{2,1,0:T(8,128)(2,1)S(1)}, bf16[2,320,768]{2,1,0:T(8,128)(2,1)}, u32[]{:S(2)}, u32[]{:S(2)}) %collective-permute-start.1) | collective-permute-done | bytes 983072 | tf_op jit(solution)/shard_map/ppermute | solution.py:80
  265.4 8.0 %fusion.6 = (f32[4,2,320]{2,1,0:T(2,128)S(1)}, bf16[4,2,320,768]{3,2,1,0:T(8,128)(2,1)S(1)}, bf16[4,2,320,768]{3,2,1,0:T(8,128)(2,1)S(1)}) fusion(f32[4,2,320,768]{3,2,1,0:T(8,128)} %bitcast.141, bf16[4,4,320,768]{3,2,1,0:T(8,128)(2,1)} %all-gather.2.cloned.1.call-done, f32[4,2,320]{2,1,0:T(2,128)S(1)} %copy.73), kind=kLoop, calls=%fused_computation.11 | loop fusion | flops 11793920 | bytes 19681280 | tf_op jit(solution)/shard_map/reduce_sum | solution.py:82
  283.8 8.2 %bitcast_convert_fusion = bf16[2,768,1024]{2,1,0:T(8,128)(2,1)} fusion(bf16[4,2,4,80,768]{4,3,2,1,0:T(8,128)(2,1)S(1)} %bitcast.149, bf16[4,4,2,80,1024]{4,3,2,1,0:T(8,128)(2,1)} %all-to-all-done.3), kind=kOutput, calls=%fused_computation.13 | convolution fusion | flops 4028104704 | bytes 12320768 | tf_op jit(solution)/shard_map/glqsf,qglsd->lfd/dot_general | solution.py:85
  292.0 8.4 %bitcast_convert_fusion.1 = bf16[2,768,1024]{2,1,0:T(8,128)(2,1)} fusion(bf16[4,2,4,80,768]{4,3,2,1,0:T(8,128)(2,1)S(1)} %bitcast.150, bf16[4,4,2,80,1024]{4,3,2,1,0:T(8,128)(2,1)} %all-to-all-done.2), kind=kOutput, calls=%fused_computation.14 | convolution fusion | flops 4028104704 | bytes 12320768 | tf_op jit(solution)/shard_map/glqsf,qglsd->lfd/dot_general | solution.py:85
  300.4 39.4 %collective-permute-done.6 = f32[4,320]{1,0:T(4,128)S(1)} collective-permute-done((f32[4,320]{1,0:T(4,128)S(1)}, f32[4,320]{1,0:T(4,128)S(1)}, u32[]{:S(2)}, u32[]{:S(2)}) %collective-permute-start.6) | collective-permute-done | bytes 5152 | tf_op jit(solution)/shard_map/ppermute | solution.py:103
  339.8 20.3 %collective-permute-start.8 = (f32[4,320]{1,0:T(4,128)S(1)}, f32[4,320]{1,0:T(4,128)S(1)}, u32[]{:S(2)}, u32[]{:S(2)}) collective-permute-start(f32[4,320]{1,0:T(4,128)S(1)} %get-tuple-element.41), channel_id=1, source_target_pairs={{0,24},{8,0},{16,8},{24,16},{1,25},{9,1},{17,9},{25,17},{2,26},{10... | collective-permute-start | bytes 15368 | tf_op jit(solution)/shard_map/ppermute | solution.py:103
  360.1 5.1 %pad_maximum_fusion = bf16[4,768,1024]{2,1,0:T(8,128)(2,1)} fusion(bf16[2,768,1024]{2,1,0:T(8,128)(2,1)S(1)} %copy-done.2, bf16[2,768,1024]{2,1,0:T(8,128)(2,1)} %bitcast_convert_fusion.1), kind=kLoop, calls=%fused_computation.12 | loop fusion | flops 3145728 | bytes 12582912 | tf_op jit(solution)/shard_map/concatenate | solution.py:89
  372.0 6.9 %all_to_all.39 = f32[4,4,80]{2,0,1:T(4,128)S(1)} all-to-all(f32[4,4,80]{2,0,1:T(4,128)S(1)} %copy.78), channel_id=1, replica_groups=mesh['dp'=4,'expert'=4,'etp'=2] {'expert'}, dimensions={1} | all-to-all | bytes 10240 | tf_op jit(solution)/shard_map/all_to_all | solution.py:111
  (85 shorter events, 46.8 us)
Async XLA Ops:
  7.2 258.2 %all-gather.2.cloned.1.call-start = ((), (), s32[]{:S(2)}) async-start(), calls=%async_computation.5 | async-start | bytes 9830400 | tf_op jit(solution)/shard_map/all_gather | solution.py:29
  47.1 24.3 %all-to-all-start.1 = ((bf16[4,4,4,80]{3,0,1,2:T(4,128)(2,1)}), bf16[4,4,4,80]{3,0,1,2:T(4,128)(2,1)S(1)}, u32[]{:S(2)}, u32[]{:S(2)}) async-start(bf16[4,4,4,80]{3,0,1,2:T(4,128)(2,1)} %copy.64), calls=%async_computation.1 | async-start | bytes 32768 | tf_op jit(solution)/shard_map/all_to_all | solution.py:53
  71.4 62.7 %all-to-all-start.2 = ((bf16[4,4,2,80,1024]{4,3,2,1,0:T(8,128)(2,1)}), bf16[4,4,2,80,1024]{4,3,2,1,0:T(8,128)(2,1)}, u32[]{:S(2)}, u32[]{:S(2)}) async-start(bf16[4,4,2,80,1024]{4,3,2,1,0:T(8,128)(2,1)} %copy.68), calls=%async_computation.2 | async-start | bytes 10485760 | tf_op jit(solution)/shard_map/all_to_all | solution.py:69
  134.1 64.7 %all-to-all-start.3 = ((bf16[4,4,2,80,1024]{4,3,2,1,0:T(8,128)(2,1)}), bf16[4,4,2,80,1024]{4,3,2,1,0:T(8,128)(2,1)}, u32[]{:S(2)}, u32[]{:S(2)}) async-start(bf16[4,4,2,80,1024]{4,3,2,1,0:T(8,128)(2,1)} %copy.74), calls=%async_computation.3 | async-start | bytes 10485760 | tf_op jit(solution)/shard_map/all_to_all | solution.py:69
  153.8 3.2 copy-start
  158.1 51.6 %collective-permute-start = (bf16[2,320,768]{2,1,0:T(8,128)(2,1)}, bf16[2,320,768]{2,1,0:T(8,128)(2,1)S(1)}, u32[]{:S(2)}, u32[]{:S(2)}) collective-permute-start(bf16[2,320,768]{2,1,0:T(8,128)(2,1)} %get-tuple-element.31), channel_id=1, source_target_pairs={{0,8},{8,16},{16,24},{24,0},{1,9},{9,17},{17,25},{25,1},{2,10},{10... | collective-permute-start | bytes 2949128 | tf_op jit(solution)/shard_map/ppermute | solution.py:80
  160.2 60.2 %collective-permute-start.2 = (bf16[2,320,768]{2,1,0:T(8,128)(2,1)S(1)}, bf16[2,320,768]{2,1,0:T(8,128)(2,1)}, u32[]{:S(2)}, u32[]{:S(2)}) collective-permute-start(bf16[2,320,768]{2,1,0:T(8,128)(2,1)S(1)} %get-tuple-element.32), channel_id=1, source_target_pairs={{0,24},{8,0},{16,8},{24,16},{1,25},{9,1},{17,9},{25,17},{2,26},{10... | collective-permute-start | bytes 2949128 | tf_op jit(solution)/shard_map/ppermute | solution.py:80
  160.2 102.5 %collective-permute-start.1 = (bf16[2,320,768]{2,1,0:T(8,128)(2,1)S(1)}, bf16[2,320,768]{2,1,0:T(8,128)(2,1)}, u32[]{:S(2)}, u32[]{:S(2)}) collective-permute-start(bf16[2,320,768]{2,1,0:T(8,128)(2,1)S(1)} %get-tuple-element.33), channel_id=1, source_target_pairs={{0,16},{8,24},{16,0},{24,8},{1,17},{9,25},{17,1},{25,9},{2,18},{10... | collective-permute-start | bytes 2949128 | tf_op jit(solution)/shard_map/ppermute | solution.py:80
  265.3 11.7 %slice-start = ((s8[7864320]{0:T(1024)(128)(4,1)}), s8[4194304]{0:T(1024)(128)(4,1)S(1)}, s32[]{:S(2)}) async-start(s8[7864320]{0:T(1024)(128)(4,1)} %bitcast.136), calls=%async_computation.6 | async-start | bytes 8388608
  265.3 11.7 %slice-start.1 = ((s8[7864320]{0:T(1024)(128)(4,1)}), s8[3670016]{0:T(1024)(128)(4,1)S(1)}, s32[]{:S(2)}) async-start(s8[7864320]{0:T(1024)(128)(4,1)} %bitcast.136), calls=%async_computation.7 | async-start | bytes 7340032
  265.4 11.7 %copy-start.1 = (bf16[4,4,320,768]{3,2,1,0:T(8,128)(2,1)S(1)}, bf16[4,4,320,768]{3,2,1,0:T(8,128)(2,1)}, u32[]{:S(2)}) copy-start(bf16[4,4,320,768]{3,2,1,0:T(8,128)(2,1)} %all-gather.2.cloned.1.call-done) | copy-start | bytes 23592964
  273.5 94.6 %collective-permute-start.3 = (bf16[2,320,768]{2,1,0:T(8,128)(2,1)S(1)}, bf16[2,320,768]{2,1,0:T(8,128)(2,1)}, u32[]{:S(2)}, u32[]{:S(2)}) collective-permute-start(bf16[2,320,768]{2,1,0:T(8,128)(2,1)S(1)} %get-tuple-element.34), channel_id=1, source_target_pairs={{0,8},{8,16},{16,24},{24,0},{1,9},{9,17},{17,25},{25,1},{2,10},{10... | collective-permute-start | bytes 2949128 | tf_op jit(solution)/shard_map/ppermute | solution.py:80
  276.7 91.5 %collective-permute-start.5 = (bf16[2,320,768]{2,1,0:T(8,128)(2,1)S(1)}, bf16[2,320,768]{2,1,0:T(8,128)(2,1)}, u32[]{:S(2)}, u32[]{:S(2)}) collective-permute-start(bf16[2,320,768]{2,1,0:T(8,128)(2,1)S(1)} %get-tuple-element.35), channel_id=1, source_target_pairs={{0,24},{8,0},{16,8},{24,16},{1,25},{9,1},{17,9},{25,17},{2,26},{10... | collective-permute-start | bytes 2949128 | tf_op jit(solution)/shard_map/ppermute | solution.py:80
  276.7 91.5 %collective-permute-start.4 = (bf16[2,320,768]{2,1,0:T(8,128)(2,1)S(1)}, bf16[2,320,768]{2,1,0:T(8,128)(2,1)}, u32[]{:S(2)}, u32[]{:S(2)}) collective-permute-start(bf16[2,320,768]{2,1,0:T(8,128)(2,1)S(1)} %get-tuple-element.36), channel_id=1, source_target_pairs={{0,16},{8,24},{16,0},{24,8},{1,17},{9,25},{17,1},{25,9},{2,18},{10... | collective-permute-start | bytes 2949128 | tf_op jit(solution)/shard_map/ppermute | solution.py:80
  279.4 60.4 %collective-permute-start.6 = (f32[4,320]{1,0:T(4,128)S(1)}, f32[4,320]{1,0:T(4,128)S(1)}, u32[]{:S(2)}, u32[]{:S(2)}) collective-permute-start(f32[4,320]{1,0:T(4,128)S(1)} %get-tuple-element.39), channel_id=1, source_target_pairs={{0,8},{8,16},{16,24},{24,0},{1,9},{9,17},{17,25},{25,1},{2,10},{10... | collective-permute-start | bytes 15368 | tf_op jit(solution)/shard_map/ppermute | solution.py:103
  282.4 82.8 %collective-permute-start.7 = (f32[4,320]{1,0:T(4,128)S(1)}, f32[4,320]{1,0:T(4,128)S(1)}, u32[]{:S(2)}, u32[]{:S(2)}) collective-permute-start(f32[4,320]{1,0:T(4,128)S(1)} %get-tuple-element.40), channel_id=1, source_target_pairs={{0,16},{8,24},{16,0},{24,8},{1,17},{9,25},{17,1},{25,9},{2,18},{10... | collective-permute-start | bytes 15368 | tf_op jit(solution)/shard_map/ppermute | solution.py:103
  292.0 68.1 %copy-start.2 = (bf16[2,768,1024]{2,1,0:T(8,128)(2,1)S(1)}, bf16[2,768,1024]{2,1,0:T(8,128)(2,1)}, u32[]{:S(2)}) copy-start(bf16[2,768,1024]{2,1,0:T(8,128)(2,1)} %bitcast_convert_fusion) | copy-start | bytes 9437188
  339.8 25.4 %collective-permute-start.8 = (f32[4,320]{1,0:T(4,128)S(1)}, f32[4,320]{1,0:T(4,128)S(1)}, u32[]{:S(2)}, u32[]{:S(2)}) collective-permute-start(f32[4,320]{1,0:T(4,128)S(1)} %get-tuple-element.41), channel_id=1, source_target_pairs={{0,24},{8,0},{16,8},{24,16},{1,25},{9,1},{17,9},{25,17},{2,26},{10... | collective-permute-start | bytes 15368 | tf_op jit(solution)/shard_map/ppermute | solution.py:103
  365.2 2.9 collective-permute-start.9
Sparse Core Ops, SparseCore 0:
  38.7 154.7 all-gather.1

commit v14 on v13

--- a/solution.py
+++ b/solution.py
@@ -2,6 +2,20 @@
 import jax.numpy as jnp
 from jax import lax
 from jax.sharding import PartitionSpec as P
+
+
+def reduce_dots(dot_part, me, groups):
+    own_dots = lax.dynamic_index_in_dim(dot_part, me, 0, keepdims=False)
+    for shift in range(1, groups):
+        chunk = lax.dynamic_index_in_dim(dot_part, (me + shift) % groups, 0, keepdims=False)
+        pairs = [(i, (i + shift) % groups) for i in range(groups)]
+        own_dots = own_dots + lax.ppermute(chunk, "dp", pairs)
+    halves = lax.axis_size("etp")
+    half_dots = own_dots
+    for shift in range(1, halves):
+        pairs = [(i, (i + shift) % halves) for i in range(halves)]
+        own_dots = own_dots + lax.ppermute(half_dots, "etp", pairs)
+    return own_dots
 
 
 def body(grad_out, routes, gates, hidden_saved, down_weight):
@@ -72,14 +86,17 @@
         ).reshape(groups, per, slot_rows_all, ff_part)
         if c == chunks - 1:
             hidden_all, partial = lax.optimization_barrier((hidden_all, partial))
+        hidden_rows = hidden_all[:, local].astype(jnp.float32)
+        dots.append(jnp.sum(hidden_rows * partial, axis=3))
+        if c == chunks - 1:
+            own_dots = reduce_dots(jnp.concatenate(dots, axis=1), me, groups)
+            partial, own_dots = lax.optimization_barrier((partial, own_dots))
         sent = partial.astype(jnp.bfloat16)
         arrivals = []
         for shift in range(1, groups):
             chunk = lax.dynamic_index_in_dim(sent, (me + shift) % groups, 0, keepdims=False)
             pairs = [(i, (i + shift) % groups) for i in range(groups)]
             arrivals.append(lax.ppermute(chunk, "dp", pairs))
-        hidden_rows = hidden_all[:, local].astype(jnp.float32)
-        dots.append(jnp.sum(hidden_rows * partial, axis=3))
         scaled = (jnp.moveaxis(slot_gates[local], 0, 1)[..., None] * hidden_rows).astype(jnp.bfloat16)
         scaled = scaled.reshape(groups, per, senders, capacity, ff_part)
         weight_sum = jnp.einsum("glqsf,qglsd->lfd", scaled, received, preferred_element_type=jnp.float32)
@@ -94,18 +111,7 @@
         for arrived in arrivals:
             expert_grad = expert_grad + arrived.astype(jnp.float32)
         hidden_parts.append((own_gates[local][..., None] * expert_grad).astype(jnp.bfloat16))
-    dot_part = jnp.concatenate(dots, axis=1)
     hidden_grad = jnp.concatenate(hidden_parts, axis=0)[None]
-    own_dots = lax.dynamic_index_in_dim(dot_part, me, 0, keepdims=False)
-    for shift in range(1, groups):
-        chunk = lax.dynamic_index_in_dim(dot_part, (me + shift) % groups, 0, keepdims=False)
-        pairs = [(i, (i + shift) % groups) for i in range(groups)]
-        own_dots = own_dots + lax.ppermute(chunk, "dp", pairs)
-    halves = lax.axis_size("etp")
-    half_dots = own_dots
-    for shift in range(1, halves):
-        pairs = [(i, (i + shift) % halves) for i in range(halves)]
-        own_dots = own_dots + lax.ppermute(half_dots, "etp", pairs)
     hidden_grad, own_dots, weight_grad = lax.optimization_barrier((hidden_grad, own_dots, weight_grad))
     slot_dots = own_dots.reshape(exp_dev, senders, capacity)
     returned = lax.all_to_all(slot_dots, "expert", split_axis=1, concat_axis=1, tiled=True)

time: 392 us -> 424 us (1.082)
  waiting for transfers between devices: 177 us -> 225 us
  starting transfers between devices: 49 us -> 27.8 us
    ppermute x6, waiting for transfers between devices: 53 us -> 136 us  [body(): arrivals.append(lax.ppermute(chunk, 'dp', pairs))]
    ppermute x4, waiting for transfers between devices: 39.4 us -> 0.01 us  [the longest x3 0.01 us: reduce_dots(): own_dots = own_dots + lax.ppermute(chunk, 'dp', pairs)]
    ppermute x4, starting transfers between devices: 25.9 us -> 5.79 us  [the longest x3 4.52 us: reduce_dots(): own_dots = own_dots + lax.ppermute(chunk, 'dp', pairs)]
    reduce_sum x2 -> x0, other arithmetic: 10.3 us -> none  [body(): dots.append(jnp.sum(hidden_rows * partial, axis=3))]
    convert_element_type x0 -> x2, other arithmetic: none -> 7.83 us  [body(): (jnp.moveaxis(slot_gates[local], 0, 1)[..., None] * hidden_rows).astype(j...]
  transfers between devices with their start and end apart: 14 -> 14, of which waited for: 5 -> 8; matrix products, arithmetic and copies ran while one was open for 24% -> 23% of each run, Pallas kernels for 0% -> 0%
where the time goes in v14:
time: 424 us; the launch traced here: 418 us
  waiting for transfers between devices  225 us (53%)
  other arithmetic  42.8 us (10%)
  matrix products  40.2 us (9%)
  blocking collectives  35.8 us (8%)
  local copies, waits for them, and re-layouts  31.9 us (8%)
  starting transfers between devices  27.8 us (7%)
  between operations  14.4 us (3%)
    ppermute x6, waiting for transfers between devices, body(): arrivals.append(lax.ppermute(chunk, 'dp', pairs))  136 us
    all_to_all x2, waiting for transfers between devices, body(): lax.all_to_all(picked, 'expert', split_axis=0, concat_axis=0, tiled=True)  89.2 us
    all_to_all x1, blocking collectives, body(): lax.all_to_all(packed, 'dp', split_axis=1, concat_axis=0, tiled=True)  28.1 us
    dot_general x2, matrix products, body(): jnp.einsum('glqsf,qglsd->lfd', scaled, received, preferred_element_type=j...  16.6 us
    dot_general x2, matrix products, body(): jnp.einsum('qglsd,lfd->glqsf', received, down_weight[local], preferred_el...  14.3 us
    all_to_all x2, starting transfers between devices, body(): lax.all_to_all(picked, 'expert', split_axis=0, concat_axis=0, tiled=True)  12.4 us
    convert_element_type x2, local copies, waits for them, and re-layouts, body(): picked = jnp.einsum('gtlqs,gtd->qglsd', token_select[:, :, local], token_...  11.5 us
  transfers between devices with their start and end apart: 14, of which 8 were waited for; matrix products, arithmetic and copies ran while one was open for 23% of the time, Pallas kernels for 0%

profile of v14, /device:TPU:29, one launch (start us, length us, event | category | flops | bytes accessed | tf_op | source)
XLA Modules:
  0.0 417.7 jit_solution(317737851194215864)
XLA Ops:
  10.3 28.1 %all_to_all.38 = bf16[128,4,1040]{0,2,1:T(8,128)(2,1)S(1)} all-to-all(bf16[128,4,1040]{0,2,1:T(8,128)(2,1)S(1)} %pad_maximum_fusion.1), channel_id=1, replica_groups=mesh['dp'=4,'expert'=4,'etp'=2] {'dp'}, dimensions={1} | all-to-all | bytes 2129920 | tf_op jit(solution)/shard_map/all_to_all | solution.py:39
  40.8 5.6 %fusion.1 = bf16[4,1,1280,1]{2,1,3,0:T(2,128)(2,1)S(1)} fusion(bf16[4,128,8,1]{2,3,1,0:T(2,128)(2,1)S(1)} %copy.81, s32[4,128,8]{2,1,0:T(8,128)S(1)} %fusion.53), kind=kOutput, calls=%fused_computation.2 | convolution fusion | flops 15728640 | bytes 34816 | tf_op jit(solution)/shard_map/gtk,gtkr->gr/dot_general | solution.py:60
  47.1 4.6 %all-to-all-start.1 = ((bf16[4,4,4,80]{3,0,1,2:T(4,128)(2,1)}), bf16[4,4,4,80]{3,0,1,2:T(4,128)(2,1)S(1)}, u32[]{:S(2)}, u32[]{:S(2)}) async-start(bf16[4,4,4,80]{3,0,1,2:T(4,128)(2,1)} %copy.64), calls=%async_computation.1 | async-start | bytes 32768 | tf_op jit(solution)/shard_map/all_to_all | solution.py:67
  51.7 7.4 %fusion.32 = bf16[4,128,1280]{2,1,0:T(8,128)(2,1)} fusion(s32[4,128,8]{2,1,0:T(8,128)S(1)} %fusion.53), kind=kLoop, calls=%fused_computation.35 | loop fusion | flops 15073280 | bytes 1327104 | tf_op jit(solution)/shard_map/reduce_sum | solution.py:61
  65.7 5.8 %copy.74 = bf16[4,4,2,80,1024]{4,3,2,1,0:T(8,128)(2,1)} copy(bf16[4,4,2,80,1024]{4,3,0,2,1:T(8,128)(2,1)} %convert_bitcast_fusion) | data formatting | bytes 10485760 | tf_op jit(solution)/shard_map/convert_element_type | solution.py:82
  71.5 5.3 %all-to-all-start.3 = ((bf16[4,4,2,80,1024]{4,3,2,1,0:T(8,128)(2,1)}), bf16[4,4,2,80,1024]{4,3,2,1,0:T(8,128)(2,1)}, u32[]{:S(2)}, u32[]{:S(2)}) async-start(bf16[4,4,2,80,1024]{4,3,2,1,0:T(8,128)(2,1)} %copy.74), calls=%async_computation.3 | async-start | bytes 10485760 | tf_op jit(solution)/shard_map/all_to_all | solution.py:83
  81.5 5.7 %copy.68 = bf16[4,4,2,80,1024]{4,3,2,1,0:T(8,128)(2,1)} copy(bf16[4,4,2,80,1024]{4,3,0,2,1:T(8,128)(2,1)} %convert_bitcast_fusion.1) | data formatting | bytes 10485760 | tf_op jit(solution)/shard_map/convert_element_type | solution.py:82
  87.1 47.1 %all-to-all-done.3 = bf16[4,4,2,80,1024]{4,3,2,1,0:T(8,128)(2,1)} async-done(((bf16[4,4,2,80,1024]{4,3,2,1,0:T(8,128)(2,1)}), bf16[4,4,2,80,1024]{4,3,2,1,0:T(8,128)(2,1)}, u32[]{:S(2)}, u32[]{:S(2)}) %all-to-all-start.3) | async-done | bytes 5242912 | tf_op jit(solution)/shard_map/all_to_all | solution.py:83
  134.2 7.1 %all-to-all-start.2 = ((bf16[4,4,2,80,1024]{4,3,2,1,0:T(8,128)(2,1)}), bf16[4,4,2,80,1024]{4,3,2,1,0:T(8,128)(2,1)}, u32[]{:S(2)}, u32[]{:S(2)}) async-start(bf16[4,4,2,80,1024]{4,3,2,1,0:T(8,128)(2,1)} %copy.68), calls=%async_computation.2 | async-start | bytes 10485760 | tf_op jit(solution)/shard_map/all_to_all | solution.py:83
  146.0 7.2 %fusion.27 = f32[4,2,4,80,768]{4,3,0,2,1:T(8,128)S(1)} fusion(bf16[4,768,1024]{2,1,0:T(8,128)(2,1)} %param.9, bf16[4,4,2,80,1024]{4,3,2,1,0:T(8,128)(2,1)} %all-to-all-done.3), kind=kOutput, calls=%fused_computation.34 | convolution fusion | flops 4026531840 | bytes 16252928 | tf_op jit(solution)/shard_map/qglsd,lfd->glqsf/dot_general | solution.py:84
  153.2 3.7 copy.76
  156.9 42.1 %all-to-all-done.2 = bf16[4,4,2,80,1024]{4,3,2,1,0:T(8,128)(2,1)} async-done(((bf16[4,4,2,80,1024]{4,3,2,1,0:T(8,128)(2,1)}), bf16[4,4,2,80,1024]{4,3,2,1,0:T(8,128)(2,1)}, u32[]{:S(2)}, u32[]{:S(2)}) %all-to-all-start.2) | async-done | bytes 5242912 | tf_op jit(solution)/shard_map/all_to_all | solution.py:83
  199.0 7.2 %fusion.22 = f32[4,2,4,80,768]{4,3,0,2,1:T(8,128)S(1)} fusion(bf16[4,768,1024]{2,1,0:T(8,128)(2,1)} %param.9, bf16[4,4,2,80,1024]{4,3,2,1,0:T(8,128)(2,1)} %all-to-all-done.2), kind=kOutput, calls=%fused_computation.33 | convolution fusion | flops 4026531840 | bytes 16252928 | tf_op jit(solution)/shard_map/qglsd,lfd->glqsf/dot_general | solution.py:84
  214.3 5.6 %fusion.5 = (bf16[4,2,320,768]{3,2,1,0:T(8,128)(2,1)S(1)}, f32[4,2,320]{2,1,0:T(2,128)S(1)}) fusion(f32[4,2,320]{2,1,0:T(2,128)S(1)} %copy.73, bf16[4,4,320,768]{3,2,1,0:T(8,128)(2,1)} %all-gather.2.cloned.1.call-done, f32[4,2,320,768]{3,2,1,0:T(8,128)} %bitcast.135), kind=kLoop, calls=%fused_computation.10 | loop fusion | flops 9827840 | bytes 15749120 | tf_op jit(solution)/shard_map/convert_element_type | solution.py:100
  229.9 4.9 %collective-permute-done = bf16[2,320,768]{2,1,0:T(8,128)(2,1)} collective-permute-done((bf16[2,320,768]{2,1,0:T(8,128)(2,1)}, bf16[2,320,768]{2,1,0:T(8,128)(2,1)}, u32[]{:S(2)}, u32[]{:S(2)}) %collective-permute-start) | collective-permute-done | bytes 983072 | tf_op jit(solution)/shard_map/ppermute | solution.py:99
  235.0 21.7 %collective-permute-done.2 = bf16[2,320,768]{2,1,0:T(8,128)(2,1)} collective-permute-done((bf16[2,320,768]{2,1,0:T(8,128)(2,1)}, bf16[2,320,768]{2,1,0:T(8,128)(2,1)}, u32[]{:S(2)}, u32[]{:S(2)}) %collective-permute-start.2) | collective-permute-done | bytes 983072 | tf_op jit(solution)/shard_map/ppermute | solution.py:99
  256.7 41.5 %collective-permute-done.1 = bf16[2,320,768]{2,1,0:T(8,128)(2,1)} collective-permute-done((bf16[2,320,768]{2,1,0:T(8,128)(2,1)}, bf16[2,320,768]{2,1,0:T(8,128)(2,1)}, u32[]{:S(2)}, u32[]{:S(2)}) %collective-permute-start.1) | collective-permute-done | bytes 983072 | tf_op jit(solution)/shard_map/ppermute | solution.py:99
  301.8 8.3 %bitcast_convert_fusion = bf16[2,768,1024]{2,1,0:T(8,128)(2,1)} fusion(bf16[4,2,4,80,768]{4,3,2,1,0:T(8,128)(2,1)S(1)} %bitcast.153, bf16[4,4,2,80,1024]{4,3,2,1,0:T(8,128)(2,1)} %all-to-all-done.3), kind=kOutput, calls=%fused_computation.13 | convolution fusion | flops 4028104704 | bytes 12320768 | tf_op jit(solution)/shard_map/glqsf,qglsd->lfd/dot_general | solution.py:102
  314.4 8.3 %bitcast_convert_fusion.1 = bf16[2,768,1024]{2,1,0:T(8,128)(2,1)} fusion(bf16[4,2,4,80,768]{4,3,2,1,0:T(8,128)(2,1)S(1)} %bitcast.152, bf16[4,4,2,80,1024]{4,3,2,1,0:T(8,128)(2,1)} %all-to-all-done.2), kind=kOutput, calls=%fused_computation.14 | convolution fusion | flops 4028104704 | bytes 12320768 | tf_op jit(solution)/shard_map/glqsf,qglsd->lfd/dot_general | solution.py:102
  322.7 5.1 %pad_maximum_fusion = bf16[4,768,1024]{2,1,0:T(8,128)(2,1)} fusion(bf16[2,768,1024]{2,1,0:T(8,128)(2,1)S(1)} %copy-done.2, bf16[2,768,1024]{2,1,0:T(8,128)(2,1)} %bitcast_convert_fusion.1), kind=kLoop, calls=%fused_computation.12 | loop fusion | flops 3145728 | bytes 12582912 | tf_op jit(solution)/shard_map/concatenate | solution.py:106
  328.0 7.9 %collective-permute-done.7 = bf16[2,320,768]{2,1,0:T(8,128)(2,1)} collective-permute-done((bf16[2,320,768]{2,1,0:T(8,128)(2,1)}, bf16[2,320,768]{2,1,0:T(8,128)(2,1)}, u32[]{:S(2)}, u32[]{:S(2)}) %collective-permute-start.7) | collective-permute-done | bytes 983072 | tf_op jit(solution)/shard_map/ppermute | solution.py:99
  335.9 19.5 %collective-permute-done.9 = bf16[2,320,768]{2,1,0:T(8,128)(2,1)} collective-permute-done((bf16[2,320,768]{2,1,0:T(8,128)(2,1)}, bf16[2,320,768]{2,1,0:T(8,128)(2,1)}, u32[]{:S(2)}, u32[]{:S(2)}) %collective-permute-start.9) | collective-permute-done | bytes 983072 | tf_op jit(solution)/shard_map/ppermute | solution.py:99
  355.4 40.2 %collective-permute-done.8 = bf16[2,320,768]{2,1,0:T(8,128)(2,1)} collective-permute-done((bf16[2,320,768]{2,1,0:T(8,128)(2,1)S(1)}, bf16[2,320,768]{2,1,0:T(8,128)(2,1)}, u32[]{:S(2)}, u32[]{:S(2)}) %collective-permute-start.8) | collective-permute-done | bytes 983072 | tf_op jit(solution)/shard_map/ppermute | solution.py:99
  399.4 7.8 %all_to_all.39 = f32[4,4,80]{2,0,1:T(4,128)S(1)} all-to-all(f32[4,4,80]{2,0,1:T(4,128)S(1)} %copy.78), channel_id=1, replica_groups=mesh['dp'=4,'expert'=4,'etp'=2] {'expert'}, dimensions={1} | all-to-all | bytes 10240 | tf_op jit(solution)/shard_map/all_to_all | solution.py:117
  (91 shorter events, 55.8 us)
Async XLA Ops:
  7.2 207.1 %all-gather.2.cloned.1.call-start = ((), (), s32[]{:S(2)}) async-start(), calls=%async_computation.5 | async-start | bytes 9830400 | tf_op jit(solution)/shard_map/all_gather | solution.py:43
  47.1 24.4 %all-to-all-start.1 = ((bf16[4,4,4,80]{3,0,1,2:T(4,128)(2,1)}), bf16[4,4,4,80]{3,0,1,2:T(4,128)(2,1)S(1)}, u32[]{:S(2)}, u32[]{:S(2)}) async-start(bf16[4,4,4,80]{3,0,1,2:T(4,128)(2,1)} %copy.64), calls=%async_computation.1 | async-start | bytes 32768 | tf_op jit(solution)/shard_map/all_to_all | solution.py:67
  71.5 62.7 %all-to-all-start.3 = ((bf16[4,4,2,80,1024]{4,3,2,1,0:T(8,128)(2,1)}), bf16[4,4,2,80,1024]{4,3,2,1,0:T(8,128)(2,1)}, u32[]{:S(2)}, u32[]{:S(2)}) async-start(bf16[4,4,2,80,1024]{4,3,2,1,0:T(8,128)(2,1)} %copy.74), calls=%async_computation.3 | async-start | bytes 10485760 | tf_op jit(solution)/shard_map/all_to_all | solution.py:83
  134.2 64.7 %all-to-all-start.2 = ((bf16[4,4,2,80,1024]{4,3,2,1,0:T(8,128)(2,1)}), bf16[4,4,2,80,1024]{4,3,2,1,0:T(8,128)(2,1)}, u32[]{:S(2)}, u32[]{:S(2)}) async-start(bf16[4,4,2,80,1024]{4,3,2,1,0:T(8,128)(2,1)} %copy.68), calls=%async_computation.2 | async-start | bytes 10485760 | tf_op jit(solution)/shard_map/all_to_all | solution.py:83
  206.8 3.1 copy-start
  211.7 23.0 %collective-permute-start = (bf16[2,320,768]{2,1,0:T(8,128)(2,1)}, bf16[2,320,768]{2,1,0:T(8,128)(2,1)}, u32[]{:S(2)}, u32[]{:S(2)}) collective-permute-start(bf16[2,320,768]{2,1,0:T(8,128)(2,1)} %get-tuple-element.34), channel_id=1, source_target_pairs={{0,8},{8,16},{16,24},{24,0},{1,9},{9,17},{17,25},{25,1},{2,10},{10... | collective-permute-start | bytes 2949128 | tf_op jit(solution)/shard_map/ppermute | solution.py:99
  213.8 42.9 %collective-permute-start.2 = (bf16[2,320,768]{2,1,0:T(8,128)(2,1)}, bf16[2,320,768]{2,1,0:T(8,128)(2,1)}, u32[]{:S(2)}, u32[]{:S(2)}) collective-permute-start(bf16[2,320,768]{2,1,0:T(8,128)(2,1)} %get-tuple-element.35), channel_id=1, source_target_pairs={{0,24},{8,0},{16,8},{24,16},{1,25},{9,1},{17,9},{25,17},{2,26},{10... | collective-permute-start | bytes 2949128 | tf_op jit(solution)/shard_map/ppermute | solution.py:99
  213.8 84.3 %collective-permute-start.1 = (bf16[2,320,768]{2,1,0:T(8,128)(2,1)}, bf16[2,320,768]{2,1,0:T(8,128)(2,1)}, u32[]{:S(2)}, u32[]{:S(2)}) collective-permute-start(bf16[2,320,768]{2,1,0:T(8,128)(2,1)} %get-tuple-element.36), channel_id=1, source_target_pairs={{0,16},{8,24},{16,0},{24,8},{1,17},{9,25},{17,1},{25,9},{2,18},{10... | collective-permute-start | bytes 2949128 | tf_op jit(solution)/shard_map/ppermute | solution.py:99
  214.3 5.6 %slice-start.2 = ((s8[7864320]{0:T(1024)(128)(4,1)}), s8[4194304]{0:T(1024)(128)(4,1)S(1)}, s32[]{:S(2)}) async-start(s8[7864320]{0:T(1024)(128)(4,1)} %bitcast.140), calls=%async_computation.8 | async-start | bytes 8388608
  214.3 6.7 %slice-start.3 = ((s8[7864320]{0:T(1024)(128)(4,1)}), s8[3670016]{0:T(1024)(128)(4,1)S(1)}, s32[]{:S(2)}) async-start(s8[7864320]{0:T(1024)(128)(4,1)} %bitcast.140), calls=%async_computation.9 | async-start | bytes 7340032
  214.3 9.0 %copy-start.1 = (bf16[4,4,320,768]{3,2,1,0:T(8,128)(2,1)S(1)}, bf16[4,4,320,768]{3,2,1,0:T(8,128)(2,1)}, u32[]{:S(2)}) copy-start(bf16[4,4,320,768]{3,2,1,0:T(8,128)(2,1)} %all-gather.2.cloned.1.call-done) | copy-start | bytes 23592964
  225.6 74.9 %collective-permute-start.3 = (f32[4,320]{1,0:T(4,128)S(1)}, f32[4,320]{1,0:T(4,128)S(1)}, u32[]{:S(2)}, u32[]{:S(2)}) collective-permute-start(f32[4,320]{1,0:T(4,128)S(1)} %get-tuple-element.44), channel_id=1, source_target_pairs={{0,8},{8,16},{16,24},{24,0},{1,9},{9,17},{17,25},{25,1},{2,10},{10... | collective-permute-start | bytes 15368 | tf_op jit(solution)/shard_map/ppermute | solution.py:12
  228.4 72.1 %collective-permute-start.4 = (f32[4,320]{1,0:T(4,128)S(1)}, f32[4,320]{1,0:T(4,128)S(1)}, u32[]{:S(2)}, u32[]{:S(2)}) collective-permute-start(f32[4,320]{1,0:T(4,128)S(1)} %get-tuple-element.45), channel_id=1, source_target_pairs={{0,16},{8,24},{16,0},{24,8},{1,17},{9,25},{17,1},{25,9},{2,18},{10... | collective-permute-start | bytes 15368 | tf_op jit(solution)/shard_map/ppermute | solution.py:12
  234.7 65.8 %collective-permute-start.5 = (f32[4,320]{1,0:T(4,128)S(1)}, f32[4,320]{1,0:T(4,128)S(1)}, u32[]{:S(2)}, u32[]{:S(2)}) collective-permute-start(f32[4,320]{1,0:T(4,128)S(1)} %get-tuple-element.46), channel_id=1, source_target_pairs={{0,24},{8,0},{16,8},{24,16},{1,25},{9,1},{17,9},{25,17},{2,26},{10... | collective-permute-start | bytes 15368 | tf_op jit(solution)/shard_map/ppermute | solution.py:12
  300.5 9.6 %collective-permute-start.6 = (f32[4,320]{1,0:T(4,128)S(1)}, f32[4,320]{1,0:T(4,128)S(1)}, u32[]{:S(2)}, u32[]{:S(2)}) collective-permute-start(f32[4,320]{1,0:T(4,128)S(1)} %fusion.66), channel_id=1, source_target_pairs={{0,1},{1,0},{2,3},{3,2},{4,5},{5,4},{6,7},{7,6},{8,9},{9,8},{10,11... | collective-permute-start | bytes 15368 | tf_op jit(solution)/shard_map/ppermute | solution.py:17
  301.8 8.3 %slice-start = ((s8[7864320]{0:T(1024)(128)(4,1)}), s8[4194304]{0:T(1024)(128)(4,1)S(1)}, s32[]{:S(2)}) async-start(s8[7864320]{0:T(1024)(128)(4,1)} %bitcast.136), calls=%async_computation.6 | async-start | bytes 8388608
  301.8 8.3 %slice-start.1 = ((s8[7864320]{0:T(1024)(128)(4,1)}), s8[3670016]{0:T(1024)(128)(4,1)S(1)}, s32[]{:S(2)}) async-start(s8[7864320]{0:T(1024)(128)(4,1)} %bitcast.136), calls=%async_computation.7 | async-start | bytes 7340032
  312.0 23.9 %collective-permute-start.7 = (bf16[2,320,768]{2,1,0:T(8,128)(2,1)}, bf16[2,320,768]{2,1,0:T(8,128)(2,1)}, u32[]{:S(2)}, u32[]{:S(2)}) collective-permute-start(bf16[2,320,768]{2,1,0:T(8,128)(2,1)} %get-tuple-element.37), channel_id=1, source_target_pairs={{0,8},{8,16},{16,24},{24,0},{1,9},{9,17},{17,25},{25,1},{2,10},{10... | collective-permute-start | bytes 2949128 | tf_op jit(solution)/shard_map/ppermute | solution.py:99
  314.1 41.3 %collective-permute-start.9 = (bf16[2,320,768]{2,1,0:T(8,128)(2,1)}, bf16[2,320,768]{2,1,0:T(8,128)(2,1)}, u32[]{:S(2)}, u32[]{:S(2)}) collective-permute-start(bf16[2,320,768]{2,1,0:T(8,128)(2,1)} %get-tuple-element.38), channel_id=1, source_target_pairs={{0,24},{8,0},{16,8},{24,16},{1,25},{9,1},{17,9},{25,17},{2,26},{10... | collective-permute-start | bytes 2949128 | tf_op jit(solution)/shard_map/ppermute | solution.py:99
  314.1 81.4 %collective-permute-start.8 = (bf16[2,320,768]{2,1,0:T(8,128)(2,1)S(1)}, bf16[2,320,768]{2,1,0:T(8,128)(2,1)}, u32[]{:S(2)}, u32[]{:S(2)}) collective-permute-start(bf16[2,320,768]{2,1,0:T(8,128)(2,1)S(1)} %get-tuple-element.39), channel_id=1, source_target_pairs={{0,16},{8,24},{16,0},{24,8},{1,17},{9,25},{17,1},{25,9},{2,18},{10... | collective-permute-start | bytes 2949128 | tf_op jit(solution)/shard_map/ppermute | solution.py:99
  314.4 8.3 %copy-start.2 = (bf16[2,768,1024]{2,1,0:T(8,128)(2,1)S(1)}, bf16[2,768,1024]{2,1,0:T(8,128)(2,1)}, u32[]{:S(2)}) copy-start(bf16[2,768,1024]{2,1,0:T(8,128)(2,1)} %bitcast_convert_fusion) | copy-start | bytes 9437188
Sparse Core Ops, SparseCore 0:
  38.7 139.9 all-gather.1

commit v15 on v12

--- a/solution.py
+++ b/solution.py
@@ -57,7 +57,7 @@
     own_gates = lax.dynamic_index_in_dim(got_gates, me, 1, keepdims=False).astype(jnp.float32)
     chunks = 2 if exp_dev % 2 == 0 else 1
     per = exp_dev // chunks
-    grads, dots, hidden_parts = [], [], []
+    grads, dots, hidden_parts, owns, pending = [], [], [], [], []
     for c in range(chunks):
         local = slice(c * per, (c + 1) * per)
         picked = jnp.einsum(
@@ -84,11 +84,15 @@
         scaled = scaled.reshape(groups, per, senders, capacity, ff_part)
         weight_sum = jnp.einsum("glqsf,qglsd->lfd", scaled, received, preferred_element_type=jnp.float32)
         grads.append(weight_sum.astype(jnp.bfloat16))
-        expert_grad = lax.dynamic_index_in_dim(partial, me, 0, keepdims=False)
-        if c == chunks - 1:
-            weight_grad = jnp.concatenate(grads, axis=0)
-            weight_grad, expert_grad = lax.optimization_barrier((weight_grad, expert_grad))
-        for arrived in arrivals:
+        owns.append(lax.dynamic_index_in_dim(partial, me, 0, keepdims=False))
+        pending.append(arrivals)
+    weight_grad = jnp.concatenate(grads, axis=0)
+    own_select = lax.dynamic_index_in_dim(select, me, 0, keepdims=False).astype(jnp.float32)
+    weight_grad, owns, own_select = lax.optimization_barrier((weight_grad, tuple(owns), own_select))
+    for c in range(chunks):
+        local = slice(c * per, (c + 1) * per)
+        expert_grad = owns[c]
+        for arrived in pending[c]:
             expert_grad = expert_grad + arrived.astype(jnp.float32)
         hidden_parts.append((own_gates[local][..., None] * expert_grad).astype(jnp.bfloat16))
     dot_part = jnp.concatenate(dots, axis=1)
@@ -106,7 +110,6 @@
     hidden_grad, own_dots, weight_grad = lax.optimization_barrier((hidden_grad, own_dots, weight_grad))
     slot_dots = own_dots.reshape(exp_dev, senders, capacity)
     returned = lax.all_to_all(slot_dots, "expert", split_axis=1, concat_axis=1, tiled=True)
-    own_select = lax.dynamic_index_in_dim(select, me, 0, keepdims=False).astype(jnp.float32)
     gate_grad = jnp.sum(own_select * returned.reshape(1, 1, rows), axis=2)
     return (weight_grad, hidden_grad, gate_grad)
 

time: 395 us -> 407 us (1.030)
  waiting for transfers between devices: 182 us -> 189 us
  blocking collectives: 28.1 us -> 33.2 us
    ppermute x6, starting transfers between devices: 6.22 us -> 29.6 us  [body(): arrivals.append(lax.ppermute(chunk, 'dp', pairs))]
    ppermute x3, starting transfers between devices: 24.4 us -> 4.34 us  [body(): own_dots = own_dots + lax.ppermute(chunk, 'dp', pairs)]
    all_to_all x1 -> x0, starting transfers between devices: 6.46 us -> none  [body(): lax.all_to_all(slot_dots, 'expert', split_axis=1, concat_axis=1, tiled=True)]
    ppermute x3, waiting for transfers between devices: 39 us -> 44.3 us  [body(): own_dots = own_dots + lax.ppermute(chunk, 'dp', pairs)]
    all_to_all x0 -> x1, blocking collectives: none -> 5.13 us  [body(): lax.all_to_all(slot_dots, 'expert', split_axis=1, concat_axis=1, tiled=True)]
  transfers between devices with their start and end apart: 15 -> 14, of which waited for: 5 -> 6; matrix products, arithmetic and copies ran while one was open for 24% -> 25% of each run, Pallas kernels for 0% -> 0%
where the time goes in v15:
time: 407 us; the launch traced here: 403 us
  waiting for transfers between devices  189 us (46%)
  starting transfers between devices  52.3 us (13%)
  other arithmetic  43.9 us (11%)
  matrix products  39 us (10%)
  blocking collectives  33.2 us (8%)
  local copies, waits for them, and re-layouts  30.8 us (8%)
  between operations  14.4 us (4%)
    all_to_all x2, waiting for transfers between devices, body(): lax.all_to_all(picked, 'expert', split_axis=0, concat_axis=0, tiled=True)  89.2 us
    ppermute x6, waiting for transfers between devices, body(): arrivals.append(lax.ppermute(chunk, 'dp', pairs))  55.9 us
    ppermute x3, waiting for transfers between devices, body(): own_dots = own_dots + lax.ppermute(chunk, 'dp', pairs)  44.3 us
    ppermute x6, starting transfers between devices, body(): arrivals.append(lax.ppermute(chunk, 'dp', pairs))  29.6 us
    all_to_all x1, blocking collectives, body(): lax.all_to_all(packed, 'dp', split_axis=1, concat_axis=0, tiled=True)  28.1 us
    dot_general x2, matrix products, body(): jnp.einsum('glqsf,qglsd->lfd', scaled, received, preferred_element_type=j...  15.4 us
    dot_general x2, matrix products, body(): jnp.einsum('qglsd,lfd->glqsf', received, down_weight[local], preferred_el...  14.3 us
    all_to_all x2, starting transfers between devices, body(): lax.all_to_all(picked, 'expert', split_axis=0, concat_axis=0, tiled=True)  12.4 us
  transfers between devices with their start and end apart: 14, of which 6 were waited for; matrix products, arithmetic and copies ran while one was open for 25% of the time, Pallas kernels for 0%

profile of v15, /device:TPU:29, one launch (start us, length us, event | category | flops | bytes accessed | tf_op | source)
XLA Modules:
  0.0 402.9 jit_solution(10634854687230112313)
XLA Ops:
  10.3 28.1 %all_to_all.38 = bf16[128,4,1040]{0,2,1:T(8,128)(2,1)S(1)} all-to-all(bf16[128,4,1040]{0,2,1:T(8,128)(2,1)S(1)} %pad_maximum_fusion.1), channel_id=1, replica_groups=mesh['dp'=4,'expert'=4,'etp'=2] {'dp'}, dimensions={1} | all-to-all | bytes 2129920 | tf_op jit(solution)/shard_map/all_to_all | solution.py:25
  40.8 5.6 %fusion.1 = bf16[4,1,1280,1]{2,1,3,0:T(2,128)(2,1)S(1)} fusion(bf16[4,128,8,1]{2,3,1,0:T(2,128)(2,1)S(1)} %copy.81, s32[4,128,8]{2,1,0:T(8,128)S(1)} %fusion.49), kind=kOutput, calls=%fused_computation.2 | convolution fusion | flops 15728640 | bytes 34816 | tf_op jit(solution)/shard_map/gtk,gtkr->gr/dot_general | solution.py:46
  47.1 4.6 %all-to-all-start.1 = ((bf16[4,4,4,80]{3,0,1,2:T(4,128)(2,1)}), bf16[4,4,4,80]{3,0,1,2:T(4,128)(2,1)S(1)}, u32[]{:S(2)}, u32[]{:S(2)}) async-start(bf16[4,4,4,80]{3,0,1,2:T(4,128)(2,1)} %copy.64), calls=%async_computation.1 | async-start | bytes 32768 | tf_op jit(solution)/shard_map/all_to_all | solution.py:53
  51.7 7.4 %fusion.32 = bf16[4,128,1280]{2,1,0:T(8,128)(2,1)} fusion(s32[4,128,8]{2,1,0:T(8,128)S(1)} %fusion.49), kind=kLoop, calls=%fused_computation.35 | loop fusion | flops 15073280 | bytes 1327104 | tf_op jit(solution)/shard_map/reduce_sum | solution.py:47
  65.7 5.8 %copy.72 = bf16[4,4,2,80,1024]{4,3,2,1,0:T(8,128)(2,1)} copy(bf16[4,4,2,80,1024]{4,3,0,2,1:T(8,128)(2,1)} %convert_bitcast_fusion) | data formatting | bytes 10485760 | tf_op jit(solution)/shard_map/convert_element_type | solution.py:68
  71.5 5.3 %all-to-all-start.3 = ((bf16[4,4,2,80,1024]{4,3,2,1,0:T(8,128)(2,1)}), bf16[4,4,2,80,1024]{4,3,2,1,0:T(8,128)(2,1)}, u32[]{:S(2)}, u32[]{:S(2)}) async-start(bf16[4,4,2,80,1024]{4,3,2,1,0:T(8,128)(2,1)} %copy.72), calls=%async_computation.3 | async-start | bytes 10485760 | tf_op jit(solution)/shard_map/all_to_all | solution.py:69
  81.5 5.7 %copy.69 = bf16[4,4,2,80,1024]{4,3,2,1,0:T(8,128)(2,1)} copy(bf16[4,4,2,80,1024]{4,3,0,2,1:T(8,128)(2,1)} %convert_bitcast_fusion.1) | data formatting | bytes 10485760 | tf_op jit(solution)/shard_map/convert_element_type | solution.py:68
  87.2 47.1 %all-to-all-done.3 = bf16[4,4,2,80,1024]{4,3,2,1,0:T(8,128)(2,1)} async-done(((bf16[4,4,2,80,1024]{4,3,2,1,0:T(8,128)(2,1)}), bf16[4,4,2,80,1024]{4,3,2,1,0:T(8,128)(2,1)}, u32[]{:S(2)}, u32[]{:S(2)}) %all-to-all-start.3) | async-done | bytes 5242912 | tf_op jit(solution)/shard_map/all_to_all | solution.py:69
  134.3 7.1 %all-to-all-start.2 = ((bf16[4,4,2,80,1024]{4,3,2,1,0:T(8,128)(2,1)}), bf16[4,4,2,80,1024]{4,3,2,1,0:T(8,128)(2,1)}, u32[]{:S(2)}, u32[]{:S(2)}) async-start(bf16[4,4,2,80,1024]{4,3,2,1,0:T(8,128)(2,1)} %copy.69), calls=%async_computation.2 | async-start | bytes 10485760 | tf_op jit(solution)/shard_map/all_to_all | solution.py:69
  146.0 7.2 %fusion.22 = f32[4,2,4,80,768]{4,3,0,2,1:T(8,128)S(1)} fusion(bf16[4,768,1024]{2,1,0:T(8,128)(2,1)} %param.9, bf16[4,4,2,80,1024]{4,3,2,1,0:T(8,128)(2,1)} %all-to-all-done.3), kind=kOutput, calls=%fused_computation.33 | convolution fusion | flops 4026531840 | bytes 16252928 | tf_op jit(solution)/shard_map/qglsd,lfd->glqsf/dot_general | solution.py:70
  153.2 3.7 copy.74
  156.9 42.1 %all-to-all-done.2 = bf16[4,4,2,80,1024]{4,3,2,1,0:T(8,128)(2,1)} async-done(((bf16[4,4,2,80,1024]{4,3,2,1,0:T(8,128)(2,1)}), bf16[4,4,2,80,1024]{4,3,2,1,0:T(8,128)(2,1)}, u32[]{:S(2)}, u32[]{:S(2)}) %all-to-all-start.2) | async-done | bytes 5242912 | tf_op jit(solution)/shard_map/all_to_all | solution.py:69
  199.0 7.2 %fusion.27 = f32[4,2,4,80,768]{4,3,0,2,1:T(8,128)S(1)} fusion(bf16[4,768,1024]{2,1,0:T(8,128)(2,1)} %param.9, bf16[4,4,2,80,1024]{4,3,2,1,0:T(8,128)(2,1)} %all-to-all-done.2), kind=kOutput, calls=%fused_computation.34 | convolution fusion | flops 4026531840 | bytes 16252928 | tf_op jit(solution)/shard_map/qglsd,lfd->glqsf/dot_general | solution.py:70
  211.9 8.0 %fusion.6 = (f32[4,2,320]{2,1,0:T(2,128)S(1)}, bf16[4,2,320,768]{3,2,1,0:T(8,128)(2,1)S(1)}, bf16[4,2,320,768]{3,2,1,0:T(8,128)(2,1)S(1)}) fusion(f32[4,2,320,768]{3,2,1,0:T(8,128)} %bitcast.133, bf16[4,4,320,768]{3,2,1,0:T(8,128)(2,1)} %all-gather.2.cloned.1.call-done, f32[4,2,320]{2,1,0:T(2,128)S(1)} %copy.71), kind=kLoop, calls=%fused_computation.11 | loop fusion | flops 11793920 | bytes 19681280 | tf_op jit(solution)/shard_map/reduce_sum | solution.py:82
  223.1 3.3 fusion.4
  230.7 8.4 %bitcast_convert_fusion = bf16[2,768,1024]{2,1,0:T(8,128)(2,1)} fusion(bf16[4,2,4,80,768]{4,3,2,1,0:T(8,128)(2,1)S(1)} %bitcast.141, bf16[4,4,2,80,1024]{4,3,2,1,0:T(8,128)(2,1)} %all-to-all-done.3), kind=kOutput, calls=%fused_computation.13 | convolution fusion | flops 4028104704 | bytes 12320768 | tf_op jit(solution)/shard_map/glqsf,qglsd->lfd/dot_general | solution.py:85
  239.1 7.0 %bitcast_convert_fusion.1 = bf16[2,768,1024]{2,1,0:T(8,128)(2,1)S(1)} fusion(bf16[4,2,4,80,768]{4,3,2,1,0:T(8,128)(2,1)S(1)} %bitcast.142, bf16[4,4,2,80,1024]{4,3,2,1,0:T(8,128)(2,1)} %all-to-all-done.2), kind=kOutput, calls=%fused_computation.14 | convolution fusion | flops 4028104704 | bytes 12320768 | tf_op jit(solution)/shard_map/glqsf,qglsd->lfd/dot_general | solution.py:85
  247.8 26.6 %collective-permute-done.6 = f32[4,320]{1,0:T(4,128)S(1)} collective-permute-done((f32[4,320]{1,0:T(4,128)S(1)}, f32[4,320]{1,0:T(4,128)S(1)}, u32[]{:S(2)}, u32[]{:S(2)}) %collective-permute-start.6) | collective-permute-done | bytes 5152 | tf_op jit(solution)/shard_map/ppermute | solution.py:104
  274.3 3.8 collective-permute-start.3
  278.1 17.7 %collective-permute-done.7 = f32[4,320]{1,0:T(4,128)S(1)} collective-permute-done((f32[4,320]{1,0:T(4,128)S(1)}, f32[4,320]{1,0:T(4,128)S(1)}, u32[]{:S(2)}, u32[]{:S(2)}) %collective-permute-start.7) | collective-permute-done | bytes 5152 | tf_op jit(solution)/shard_map/ppermute | solution.py:104
  295.9 20.1 %collective-permute-start.5 = (bf16[2,320,768]{2,1,0:T(8,128)(2,1)}, bf16[2,320,768]{2,1,0:T(8,128)(2,1)}, u32[]{:S(2)}, u32[]{:S(2)}) collective-permute-start(bf16[2,320,768]{2,1,0:T(8,128)(2,1)} %get-tuple-element.37), channel_id=1, source_target_pairs={{0,24},{8,0},{16,8},{24,16},{1,25},{9,1},{17,9},{25,17},{2,26},{10... | collective-permute-start | bytes 2949128 | tf_op jit(solution)/shard_map/ppermute | solution.py:80
  327.7 11.2 %collective-permute-done.5 = bf16[2,320,768]{2,1,0:T(8,128)(2,1)} collective-permute-done((bf16[2,320,768]{2,1,0:T(8,128)(2,1)}, bf16[2,320,768]{2,1,0:T(8,128)(2,1)}, u32[]{:S(2)}, u32[]{:S(2)}) %collective-permute-start.5) | collective-permute-done | bytes 983072 | tf_op jit(solution)/shard_map/ppermute | solution.py:80
  338.9 44.6 %collective-permute-done.4 = bf16[2,320,768]{2,1,0:T(8,128)(2,1)} collective-permute-done((bf16[2,320,768]{2,1,0:T(8,128)(2,1)S(1)}, bf16[2,320,768]{2,1,0:T(8,128)(2,1)}, u32[]{:S(2)}, u32[]{:S(2)}) %collective-permute-start.4) | collective-permute-done | bytes 983072 | tf_op jit(solution)/shard_map/ppermute | solution.py:80
  387.3 5.1 %all_to_all.39 = f32[4,4,80]{2,0,1:T(4,128)S(1)} all-to-all(f32[4,4,80]{2,0,1:T(4,128)S(1)} %copy.78), channel_id=1, replica_groups=mesh['dp'=4,'expert'=4,'etp'=2] {'expert'}, dimensions={1} | all-to-all | bytes 10240 | tf_op jit(solution)/shard_map/all_to_all | solution.py:112
  (88 shorter events, 56.0 us)
Async XLA Ops:
  7.2 204.7 %all-gather.2.cloned.1.call-start = ((), (), s32[]{:S(2)}) async-start(), calls=%async_computation.5 | async-start | bytes 9830400 | tf_op jit(solution)/shard_map/all_gather | solution.py:29
  47.1 24.4 %all-to-all-start.1 = ((bf16[4,4,4,80]{3,0,1,2:T(4,128)(2,1)}), bf16[4,4,4,80]{3,0,1,2:T(4,128)(2,1)S(1)}, u32[]{:S(2)}, u32[]{:S(2)}) async-start(bf16[4,4,4,80]{3,0,1,2:T(4,128)(2,1)} %copy.64), calls=%async_computation.1 | async-start | bytes 32768 | tf_op jit(solution)/shard_map/all_to_all | solution.py:53
  71.5 62.8 %all-to-all-start.3 = ((bf16[4,4,2,80,1024]{4,3,2,1,0:T(8,128)(2,1)}), bf16[4,4,2,80,1024]{4,3,2,1,0:T(8,128)(2,1)}, u32[]{:S(2)}, u32[]{:S(2)}) async-start(bf16[4,4,2,80,1024]{4,3,2,1,0:T(8,128)(2,1)} %copy.72), calls=%async_computation.3 | async-start | bytes 10485760 | tf_op jit(solution)/shard_map/all_to_all | solution.py:69
  134.3 64.7 %all-to-all-start.2 = ((bf16[4,4,2,80,1024]{4,3,2,1,0:T(8,128)(2,1)}), bf16[4,4,2,80,1024]{4,3,2,1,0:T(8,128)(2,1)}, u32[]{:S(2)}, u32[]{:S(2)}) async-start(bf16[4,4,2,80,1024]{4,3,2,1,0:T(8,128)(2,1)} %copy.69), calls=%async_computation.2 | async-start | bytes 10485760 | tf_op jit(solution)/shard_map/all_to_all | solution.py:69
  206.9 4.9 %copy-start = (f32[4,2,4,80,768]{4,3,2,1,0:T(8,128)}, f32[4,2,4,80,768]{4,3,2,1,0:T(8,128)S(1)}, u32[]{:S(2)}) copy-start(f32[4,2,4,80,768]{4,3,2,1,0:T(8,128)S(1)} %copy.77) | copy-start | bytes 23592964
  209.1 37.1 %collective-permute-start = (bf16[2,320,768]{2,1,0:T(8,128)(2,1)}, bf16[2,320,768]{2,1,0:T(8,128)(2,1)}, u32[]{:S(2)}, u32[]{:S(2)}) collective-permute-start(bf16[2,320,768]{2,1,0:T(8,128)(2,1)} %get-tuple-element.33), channel_id=1, source_target_pairs={{0,8},{8,16},{16,24},{24,0},{1,9},{9,17},{17,25},{25,1},{2,10},{10... | collective-permute-start | bytes 2949128 | tf_op jit(solution)/shard_map/ppermute | solution.py:80
  211.2 112.8 %collective-permute-start.2 = (bf16[2,320,768]{2,1,0:T(8,128)(2,1)}, bf16[2,320,768]{2,1,0:T(8,128)(2,1)}, u32[]{:S(2)}, u32[]{:S(2)}) collective-permute-start(bf16[2,320,768]{2,1,0:T(8,128)(2,1)} %get-tuple-element.34), channel_id=1, source_target_pairs={{0,24},{8,0},{16,8},{24,16},{1,25},{9,1},{17,9},{25,17},{2,26},{10... | collective-permute-start | bytes 2949128 | tf_op jit(solution)/shard_map/ppermute | solution.py:80
  211.2 114.1 %collective-permute-start.1 = (bf16[2,320,768]{2,1,0:T(8,128)(2,1)S(1)}, bf16[2,320,768]{2,1,0:T(8,128)(2,1)}, u32[]{:S(2)}, u32[]{:S(2)}) collective-permute-start(bf16[2,320,768]{2,1,0:T(8,128)(2,1)S(1)} %get-tuple-element.35), channel_id=1, source_target_pairs={{0,16},{8,24},{16,0},{24,8},{1,17},{9,25},{17,1},{25,9},{2,18},{10... | collective-permute-start | bytes 2949128 | tf_op jit(solution)/shard_map/ppermute | solution.py:80
  211.9 8.0 %slice-start = ((s8[7864320]{0:T(1024)(128)(4,1)}), s8[4194304]{0:T(1024)(128)(4,1)S(1)}, s32[]{:S(2)}) async-start(s8[7864320]{0:T(1024)(128)(4,1)} %bitcast.128), calls=%async_computation.6 | async-start | bytes 8388608
  211.9 9.0 %slice-start.1 = ((s8[7864320]{0:T(1024)(128)(4,1)}), s8[3670016]{0:T(1024)(128)(4,1)S(1)}, s32[]{:S(2)}) async-start(s8[7864320]{0:T(1024)(128)(4,1)} %bitcast.128), calls=%async_computation.7 | async-start | bytes 7340032
  211.9 11.2 %copy-start.1 = (bf16[4,4,320,768]{3,2,1,0:T(8,128)(2,1)S(1)}, bf16[4,4,320,768]{3,2,1,0:T(8,128)(2,1)}, u32[]{:S(2)}) copy-start(bf16[4,4,320,768]{3,2,1,0:T(8,128)(2,1)} %all-gather.2.cloned.1.call-done) | copy-start | bytes 23592964
  226.5 47.9 %collective-permute-start.6 = (f32[4,320]{1,0:T(4,128)S(1)}, f32[4,320]{1,0:T(4,128)S(1)}, u32[]{:S(2)}, u32[]{:S(2)}) collective-permute-start(f32[4,320]{1,0:T(4,128)S(1)} %get-tuple-element.41), channel_id=1, source_target_pairs={{0,8},{8,16},{16,24},{24,0},{1,9},{9,17},{17,25},{25,1},{2,10},{10... | collective-permute-start | bytes 15368 | tf_op jit(solution)/shard_map/ppermute | solution.py:104
  229.3 66.6 %collective-permute-start.7 = (f32[4,320]{1,0:T(4,128)S(1)}, f32[4,320]{1,0:T(4,128)S(1)}, u32[]{:S(2)}, u32[]{:S(2)}) collective-permute-start(f32[4,320]{1,0:T(4,128)S(1)} %get-tuple-element.42), channel_id=1, source_target_pairs={{0,16},{8,24},{16,0},{24,8},{1,17},{9,25},{17,1},{25,9},{2,18},{10... | collective-permute-start | bytes 15368 | tf_op jit(solution)/shard_map/ppermute | solution.py:104
  230.7 8.4 %copy-start.2 = (bf16[4,2,320,768]{3,2,1,0:T(8,128)(2,1)S(1)}, bf16[4,2,320,768]{3,2,1,0:T(8,128)(2,1)}, u32[]{:S(2)}) copy-start(bf16[4,2,320,768]{3,2,1,0:T(8,128)(2,1)} %get-tuple-element.32) | copy-start | bytes 11796484
  246.2 74.6 %copy-start.3 = (bf16[2,768,1024]{2,1,0:T(8,128)(2,1)S(1)}, bf16[2,768,1024]{2,1,0:T(8,128)(2,1)}, u32[]{:S(2)}) copy-start(bf16[2,768,1024]{2,1,0:T(8,128)(2,1)} %bitcast_convert_fusion) | copy-start | bytes 9437188
  246.2 69.7 %collective-permute-start.8 = (f32[4,320]{1,0:T(4,128)S(1)}, f32[4,320]{1,0:T(4,128)S(1)}, u32[]{:S(2)}, u32[]{:S(2)}) collective-permute-start(f32[4,320]{1,0:T(4,128)S(1)} %get-tuple-element.43), channel_id=1, source_target_pairs={{0,24},{8,0},{16,8},{24,16},{1,25},{9,1},{17,9},{25,17},{2,26},{10... | collective-permute-start | bytes 15368 | tf_op jit(solution)/shard_map/ppermute | solution.py:104
  274.3 53.3 %collective-permute-start.3 = (bf16[2,320,768]{2,1,0:T(8,128)(2,1)}, bf16[2,320,768]{2,1,0:T(8,128)(2,1)}, u32[]{:S(2)}, u32[]{:S(2)}) collective-permute-start(bf16[2,320,768]{2,1,0:T(8,128)(2,1)} %get-tuple-element.36), channel_id=1, source_target_pairs={{0,8},{8,16},{16,24},{24,0},{1,9},{9,17},{17,25},{25,1},{2,10},{10... | collective-permute-start | bytes 2949128 | tf_op jit(solution)/shard_map/ppermute | solution.py:80
  295.9 43.0 %collective-permute-start.5 = (bf16[2,320,768]{2,1,0:T(8,128)(2,1)}, bf16[2,320,768]{2,1,0:T(8,128)(2,1)}, u32[]{:S(2)}, u32[]{:S(2)}) collective-permute-start(bf16[2,320,768]{2,1,0:T(8,128)(2,1)} %get-tuple-element.37), channel_id=1, source_target_pairs={{0,24},{8,0},{16,8},{24,16},{1,25},{9,1},{17,9},{25,17},{2,26},{10... | collective-permute-start | bytes 2949128 | tf_op jit(solution)/shard_map/ppermute | solution.py:80
  315.9 67.6 %collective-permute-start.4 = (bf16[2,320,768]{2,1,0:T(8,128)(2,1)S(1)}, bf16[2,320,768]{2,1,0:T(8,128)(2,1)}, u32[]{:S(2)}, u32[]{:S(2)}) collective-permute-start(bf16[2,320,768]{2,1,0:T(8,128)(2,1)S(1)} %get-tuple-element.38), channel_id=1, source_target_pairs={{0,16},{8,24},{16,0},{24,8},{1,17},{9,25},{17,1},{25,9},{2,18},{10... | collective-permute-start | bytes 2949128 | tf_op jit(solution)/shard_map/ppermute | solution.py:80
  324.1 3.5 collective-permute-start.9
Sparse Core Ops, SparseCore 0:
  38.7 139.9 all-gather.1

commit v16 on v13

--- a/solution.py
+++ b/solution.py
@@ -96,16 +96,16 @@
         hidden_parts.append((own_gates[local][..., None] * expert_grad).astype(jnp.bfloat16))
     dot_part = jnp.concatenate(dots, axis=1)
     hidden_grad = jnp.concatenate(hidden_parts, axis=0)[None]
+    halves = lax.axis_size("etp")
+    half_dots = dot_part
+    for shift in range(1, halves):
+        pairs = [(i, (i + shift) % halves) for i in range(halves)]
+        dot_part = dot_part + lax.ppermute(half_dots, "etp", pairs)
     own_dots = lax.dynamic_index_in_dim(dot_part, me, 0, keepdims=False)
     for shift in range(1, groups):
         chunk = lax.dynamic_index_in_dim(dot_part, (me + shift) % groups, 0, keepdims=False)
         pairs = [(i, (i + shift) % groups) for i in range(groups)]
         own_dots = own_dots + lax.ppermute(chunk, "dp", pairs)
-    halves = lax.axis_size("etp")
-    half_dots = own_dots
-    for shift in range(1, halves):
-        pairs = [(i, (i + shift) % halves) for i in range(halves)]
-        own_dots = own_dots + lax.ppermute(half_dots, "etp", pairs)
     hidden_grad, own_dots, weight_grad = lax.optimization_barrier((hidden_grad, own_dots, weight_grad))
     slot_dots = own_dots.reshape(exp_dev, senders, capacity)
     returned = lax.all_to_all(slot_dots, "expert", split_axis=1, concat_axis=1, tiled=True)

time: 392 us -> 388 us (0.990); the launches traced: 389 us -> 381 us
  waiting for transfers between devices: 177 us -> 172 us
    ppermute x3, waiting for transfers between devices: 39.4 us -> 34.2 us  [body(): own_dots = own_dots + lax.ppermute(chunk, 'dp', pairs)]
where the time goes in v16:
time: 388 us; the launch traced here: 381 us
  waiting for transfers between devices  172 us (44%)
  starting transfers between devices  47 us (12%)
  other arithmetic  45.2 us (12%)
  matrix products  40.2 us (10%)
  blocking collectives  33.9 us (9%)
  local copies, waits for them, and re-layouts  28.2 us (7%)
  between operations  14.5 us (4%)
    all_to_all x2, waiting for transfers between devices, body(): lax.all_to_all(picked, 'expert', split_axis=0, concat_axis=0, tiled=True)  85 us
    ppermute x6, waiting for transfers between devices, body(): arrivals.append(lax.ppermute(chunk, 'dp', pairs))  53 us
    ppermute x3, waiting for transfers between devices, body(): own_dots = own_dots + lax.ppermute(chunk, 'dp', pairs)  34.2 us
    all_to_all x1, blocking collectives, body(): lax.all_to_all(packed, 'dp', split_axis=1, concat_axis=0, tiled=True)  28.1 us
    ppermute x3, starting transfers between devices, body(): own_dots = own_dots + lax.ppermute(chunk, 'dp', pairs)  22.7 us
    dot_general x2, matrix products, body(): jnp.einsum('glqsf,qglsd->lfd', scaled, received, preferred_element_type=j...  16.6 us
    dot_general x2, matrix products, body(): jnp.einsum('qglsd,lfd->glqsf', received, down_weight[local], preferred_el...  14.3 us
    all_to_all x2, starting transfers between devices, body(): lax.all_to_all(picked, 'expert', split_axis=0, concat_axis=0, tiled=True)  12.4 us
  transfers between devices with their start and end apart: 14, of which 5 were waited for; matrix products, arithmetic and copies ran while one was open for 24% of the time, Pallas kernels for 0%

profile of v16, /device:TPU:29, one launch (start us, length us, event | category | flops | bytes accessed | tf_op | source)
XLA Modules:
  0.0 381.2 jit_solution(16083456852259124732)
XLA Ops:
  10.3 28.1 %all_to_all.38 = bf16[128,4,1040]{0,2,1:T(8,128)(2,1)S(1)} all-to-all(bf16[128,4,1040]{0,2,1:T(8,128)(2,1)S(1)} %pad_maximum_fusion.1), channel_id=1, replica_groups=mesh['dp'=4,'expert'=4,'etp'=2] {'dp'}, dimensions={1} | all-to-all | bytes 2129920 | tf_op jit(solution)/shard_map/all_to_all | solution.py:25
  40.8 5.6 %fusion.1 = bf16[4,1,1280,1]{2,1,3,0:T(2,128)(2,1)S(1)} fusion(bf16[4,128,8,1]{2,3,1,0:T(2,128)(2,1)S(1)} %copy.81, s32[4,128,8]{2,1,0:T(8,128)S(1)} %fusion.53), kind=kOutput, calls=%fused_computation.2 | convolution fusion | flops 15728640 | bytes 34816 | tf_op jit(solution)/shard_map/gtk,gtkr->gr/dot_general | solution.py:46
  47.1 4.6 %all-to-all-start.1 = ((bf16[4,4,4,80]{3,0,1,2:T(4,128)(2,1)}), bf16[4,4,4,80]{3,0,1,2:T(4,128)(2,1)S(1)}, u32[]{:S(2)}, u32[]{:S(2)}) async-start(bf16[4,4,4,80]{3,0,1,2:T(4,128)(2,1)} %copy.64), calls=%async_computation.1 | async-start | bytes 32768 | tf_op jit(solution)/shard_map/all_to_all | solution.py:53
  51.7 7.4 %fusion.32 = bf16[4,128,1280]{2,1,0:T(8,128)(2,1)} fusion(s32[4,128,8]{2,1,0:T(8,128)S(1)} %fusion.53), kind=kLoop, calls=%fused_computation.35 | loop fusion | flops 15073280 | bytes 1327104 | tf_op jit(solution)/shard_map/reduce_sum | solution.py:47
  62.5 3.2 convert_bitcast_fusion.1
  65.7 5.7 %copy.68 = bf16[4,4,2,80,1024]{4,3,2,1,0:T(8,128)(2,1)} copy(bf16[4,4,2,80,1024]{4,3,0,2,1:T(8,128)(2,1)} %convert_bitcast_fusion.1) | data formatting | bytes 10485760 | tf_op jit(solution)/shard_map/convert_element_type | solution.py:68
  71.4 5.3 %all-to-all-start.2 = ((bf16[4,4,2,80,1024]{4,3,2,1,0:T(8,128)(2,1)}), bf16[4,4,2,80,1024]{4,3,2,1,0:T(8,128)(2,1)}, u32[]{:S(2)}, u32[]{:S(2)}) async-start(bf16[4,4,2,80,1024]{4,3,2,1,0:T(8,128)(2,1)} %copy.68), calls=%async_computation.2 | async-start | bytes 10485760 | tf_op jit(solution)/shard_map/all_to_all | solution.py:69
  78.2 3.2 convert_bitcast_fusion
  81.4 5.8 %copy.74 = bf16[4,4,2,80,1024]{4,3,2,1,0:T(8,128)(2,1)} copy(bf16[4,4,2,80,1024]{4,3,0,2,1:T(8,128)(2,1)} %convert_bitcast_fusion) | data formatting | bytes 10485760 | tf_op jit(solution)/shard_map/convert_element_type | solution.py:68
  87.2 46.9 %all-to-all-done.2 = bf16[4,4,2,80,1024]{4,3,2,1,0:T(8,128)(2,1)} async-done(((bf16[4,4,2,80,1024]{4,3,2,1,0:T(8,128)(2,1)}), bf16[4,4,2,80,1024]{4,3,2,1,0:T(8,128)(2,1)}, u32[]{:S(2)}, u32[]{:S(2)}) %all-to-all-start.2) | async-done | bytes 5242912 | tf_op jit(solution)/shard_map/all_to_all | solution.py:69
  134.1 7.1 %all-to-all-start.3 = ((bf16[4,4,2,80,1024]{4,3,2,1,0:T(8,128)(2,1)}), bf16[4,4,2,80,1024]{4,3,2,1,0:T(8,128)(2,1)}, u32[]{:S(2)}, u32[]{:S(2)}) async-start(bf16[4,4,2,80,1024]{4,3,2,1,0:T(8,128)(2,1)} %copy.74), calls=%async_computation.3 | async-start | bytes 10485760 | tf_op jit(solution)/shard_map/all_to_all | solution.py:69
  145.9 7.2 %fusion.22 = f32[4,2,4,80,768]{4,3,0,2,1:T(8,128)S(1)} fusion(bf16[4,768,1024]{2,1,0:T(8,128)(2,1)} %param.9, bf16[4,4,2,80,1024]{4,3,2,1,0:T(8,128)(2,1)} %all-to-all-done.2), kind=kOutput, calls=%fused_computation.33 | convolution fusion | flops 4026531840 | bytes 16252928 | tf_op jit(solution)/shard_map/qglsd,lfd->glqsf/dot_general | solution.py:70
  160.7 38.1 %all-to-all-done.3 = bf16[4,4,2,80,1024]{4,3,2,1,0:T(8,128)(2,1)} async-done(((bf16[4,4,2,80,1024]{4,3,2,1,0:T(8,128)(2,1)}), bf16[4,4,2,80,1024]{4,3,2,1,0:T(8,128)(2,1)}, u32[]{:S(2)}, u32[]{:S(2)}) %all-to-all-start.3) | async-done | bytes 5242912 | tf_op jit(solution)/shard_map/all_to_all | solution.py:69
  198.8 7.2 %fusion.27 = f32[4,2,4,80,768]{4,3,0,2,1:T(8,128)S(1)} fusion(bf16[4,768,1024]{2,1,0:T(8,128)(2,1)} %param.9, bf16[4,4,2,80,1024]{4,3,2,1,0:T(8,128)(2,1)} %all-to-all-done.3), kind=kOutput, calls=%fused_computation.34 | convolution fusion | flops 4026531840 | bytes 16252928 | tf_op jit(solution)/shard_map/qglsd,lfd->glqsf/dot_general | solution.py:70
  206.0 3.7 copy.76
  209.7 10.7 %collective-permute-done.2 = bf16[2,320,768]{2,1,0:T(8,128)(2,1)} collective-permute-done((bf16[2,320,768]{2,1,0:T(8,128)(2,1)S(1)}, bf16[2,320,768]{2,1,0:T(8,128)(2,1)}, u32[]{:S(2)}, u32[]{:S(2)}) %collective-permute-start.2) | collective-permute-done | bytes 983072 | tf_op jit(solution)/shard_map/ppermute | solution.py:80
  220.4 42.3 %collective-permute-done.1 = bf16[2,320,768]{2,1,0:T(8,128)(2,1)} collective-permute-done((bf16[2,320,768]{2,1,0:T(8,128)(2,1)S(1)}, bf16[2,320,768]{2,1,0:T(8,128)(2,1)}, u32[]{:S(2)}, u32[]{:S(2)}) %collective-permute-start.1) | collective-permute-done | bytes 983072 | tf_op jit(solution)/shard_map/ppermute | solution.py:80
  265.4 8.0 %fusion.6 = (f32[4,2,320]{2,1,0:T(2,128)S(1)}, bf16[4,2,320,768]{3,2,1,0:T(8,128)(2,1)S(1)}, bf16[4,2,320,768]{3,2,1,0:T(8,128)(2,1)S(1)}) fusion(f32[4,2,320,768]{3,2,1,0:T(8,128)} %bitcast.139, bf16[4,4,320,768]{3,2,1,0:T(8,128)(2,1)} %all-gather.2.cloned.1.call-done, f32[4,2,320]{2,1,0:T(2,128)S(1)} %copy.73), kind=kLoop, calls=%fused_computation.11 | loop fusion | flops 11793920 | bytes 19681280 | tf_op jit(solution)/shard_map/reduce_sum | solution.py:82
  280.6 8.2 %bitcast_convert_fusion = bf16[2,768,1024]{2,1,0:T(8,128)(2,1)} fusion(bf16[4,2,4,80,768]{4,3,2,1,0:T(8,128)(2,1)S(1)} %bitcast.147, bf16[4,4,2,80,1024]{4,3,2,1,0:T(8,128)(2,1)} %all-to-all-done.3), kind=kOutput, calls=%fused_computation.13 | convolution fusion | flops 4028104704 | bytes 12320768 | tf_op jit(solution)/shard_map/glqsf,qglsd->lfd/dot_general | solution.py:85
  288.8 8.4 %bitcast_convert_fusion.1 = bf16[2,768,1024]{2,1,0:T(8,128)(2,1)} fusion(bf16[4,2,4,80,768]{4,3,2,1,0:T(8,128)(2,1)S(1)} %bitcast.148, bf16[4,4,2,80,1024]{4,3,2,1,0:T(8,128)(2,1)} %all-to-all-done.2), kind=kOutput, calls=%fused_computation.14 | convolution fusion | flops 4028104704 | bytes 12320768 | tf_op jit(solution)/shard_map/glqsf,qglsd->lfd/dot_general | solution.py:85
  300.2 5.1 %pad_maximum_fusion = bf16[4,768,1024]{2,1,0:T(8,128)(2,1)} fusion(bf16[2,768,1024]{2,1,0:T(8,128)(2,1)S(1)} %copy-done.2, bf16[2,768,1024]{2,1,0:T(8,128)(2,1)} %bitcast_convert_fusion.1), kind=kLoop, calls=%fused_computation.12 | loop fusion | flops 3145728 | bytes 12582912 | tf_op jit(solution)/shard_map/concatenate | solution.py:89
  305.6 34.2 %collective-permute-done.7 = f32[4,320]{1,0:T(4,128)S(1)} collective-permute-done((f32[4,320]{1,0:T(4,128)S(1)}, f32[4,320]{1,0:T(4,128)S(1)}, u32[]{:S(2)}, u32[]{:S(2)}) %collective-permute-start.7) | collective-permute-done | bytes 5152 | tf_op jit(solution)/shard_map/ppermute | solution.py:108
  339.8 19.4 %collective-permute-start.8 = (f32[4,320]{1,0:T(4,128)S(1)}, f32[4,320]{1,0:T(4,128)S(1)}, u32[]{:S(2)}, u32[]{:S(2)}) collective-permute-start(f32[4,320]{1,0:T(4,128)S(1)} %get-tuple-element.41), channel_id=1, source_target_pairs={{0,16},{8,24},{16,0},{24,8},{1,17},{9,25},{17,1},{25,9},{2,18},{10... | collective-permute-start | bytes 15368 | tf_op jit(solution)/shard_map/ppermute | solution.py:108
  364.8 5.8 %all_to_all.39 = f32[4,4,80]{2,0,1:T(4,128)S(1)} all-to-all(f32[4,4,80]{2,0,1:T(4,128)S(1)} %copy.78), channel_id=1, replica_groups=mesh['dp'=4,'expert'=4,'etp'=2] {'expert'}, dimensions={1} | all-to-all | bytes 10240 | tf_op jit(solution)/shard_map/all_to_all | solution.py:111
  (86 shorter events, 45.6 us)
Async XLA Ops:
  7.2 258.2 %all-gather.2.cloned.1.call-start = ((), (), s32[]{:S(2)}) async-start(), calls=%async_computation.5 | async-start | bytes 9830400 | tf_op jit(solution)/shard_map/all_gather | solution.py:29
  47.1 24.3 %all-to-all-start.1 = ((bf16[4,4,4,80]{3,0,1,2:T(4,128)(2,1)}), bf16[4,4,4,80]{3,0,1,2:T(4,128)(2,1)S(1)}, u32[]{:S(2)}, u32[]{:S(2)}) async-start(bf16[4,4,4,80]{3,0,1,2:T(4,128)(2,1)} %copy.64), calls=%async_computation.1 | async-start | bytes 32768 | tf_op jit(solution)/shard_map/all_to_all | solution.py:53
  71.4 62.7 %all-to-all-start.2 = ((bf16[4,4,2,80,1024]{4,3,2,1,0:T(8,128)(2,1)}), bf16[4,4,2,80,1024]{4,3,2,1,0:T(8,128)(2,1)}, u32[]{:S(2)}, u32[]{:S(2)}) async-start(bf16[4,4,2,80,1024]{4,3,2,1,0:T(8,128)(2,1)} %copy.68), calls=%async_computation.2 | async-start | bytes 10485760 | tf_op jit(solution)/shard_map/all_to_all | solution.py:69
  134.1 64.7 %all-to-all-start.3 = ((bf16[4,4,2,80,1024]{4,3,2,1,0:T(8,128)(2,1)}), bf16[4,4,2,80,1024]{4,3,2,1,0:T(8,128)(2,1)}, u32[]{:S(2)}, u32[]{:S(2)}) async-start(bf16[4,4,2,80,1024]{4,3,2,1,0:T(8,128)(2,1)} %copy.74), calls=%async_computation.3 | async-start | bytes 10485760 | tf_op jit(solution)/shard_map/all_to_all | solution.py:69
  153.8 3.2 copy-start
  158.1 51.6 %collective-permute-start = (bf16[2,320,768]{2,1,0:T(8,128)(2,1)}, bf16[2,320,768]{2,1,0:T(8,128)(2,1)S(1)}, u32[]{:S(2)}, u32[]{:S(2)}) collective-permute-start(bf16[2,320,768]{2,1,0:T(8,128)(2,1)} %get-tuple-element.31), channel_id=1, source_target_pairs={{0,8},{8,16},{16,24},{24,0},{1,9},{9,17},{17,25},{25,1},{2,10},{10... | collective-permute-start | bytes 2949128 | tf_op jit(solution)/shard_map/ppermute | solution.py:80
  160.2 60.2 %collective-permute-start.2 = (bf16[2,320,768]{2,1,0:T(8,128)(2,1)S(1)}, bf16[2,320,768]{2,1,0:T(8,128)(2,1)}, u32[]{:S(2)}, u32[]{:S(2)}) collective-permute-start(bf16[2,320,768]{2,1,0:T(8,128)(2,1)S(1)} %get-tuple-element.32), channel_id=1, source_target_pairs={{0,24},{8,0},{16,8},{24,16},{1,25},{9,1},{17,9},{25,17},{2,26},{10... | collective-permute-start | bytes 2949128 | tf_op jit(solution)/shard_map/ppermute | solution.py:80
  160.2 102.5 %collective-permute-start.1 = (bf16[2,320,768]{2,1,0:T(8,128)(2,1)S(1)}, bf16[2,320,768]{2,1,0:T(8,128)(2,1)}, u32[]{:S(2)}, u32[]{:S(2)}) collective-permute-start(bf16[2,320,768]{2,1,0:T(8,128)(2,1)S(1)} %get-tuple-element.33), channel_id=1, source_target_pairs={{0,16},{8,24},{16,0},{24,8},{1,17},{9,25},{17,1},{25,9},{2,18},{10... | collective-permute-start | bytes 2949128 | tf_op jit(solution)/shard_map/ppermute | solution.py:80
  265.3 11.7 %slice-start = ((s8[7864320]{0:T(1024)(128)(4,1)}), s8[4194304]{0:T(1024)(128)(4,1)S(1)}, s32[]{:S(2)}) async-start(s8[7864320]{0:T(1024)(128)(4,1)} %bitcast.134), calls=%async_computation.6 | async-start | bytes 8388608
  265.3 11.7 %slice-start.1 = ((s8[7864320]{0:T(1024)(128)(4,1)}), s8[3670016]{0:T(1024)(128)(4,1)S(1)}, s32[]{:S(2)}) async-start(s8[7864320]{0:T(1024)(128)(4,1)} %bitcast.134), calls=%async_computation.7 | async-start | bytes 7340032
  265.4 11.7 %copy-start.1 = (bf16[4,4,320,768]{3,2,1,0:T(8,128)(2,1)S(1)}, bf16[4,4,320,768]{3,2,1,0:T(8,128)(2,1)}, u32[]{:S(2)}) copy-start(bf16[4,4,320,768]{3,2,1,0:T(8,128)(2,1)} %all-gather.2.cloned.1.call-done) | copy-start | bytes 23592964
  273.5 87.4 %collective-permute-start.3 = (bf16[2,320,768]{2,1,0:T(8,128)(2,1)S(1)}, bf16[2,320,768]{2,1,0:T(8,128)(2,1)}, u32[]{:S(2)}, u32[]{:S(2)}) collective-permute-start(bf16[2,320,768]{2,1,0:T(8,128)(2,1)S(1)} %get-tuple-element.34), channel_id=1, source_target_pairs={{0,8},{8,16},{16,24},{24,0},{1,9},{9,17},{17,25},{25,1},{2,10},{10... | collective-permute-start | bytes 2949128 | tf_op jit(solution)/shard_map/ppermute | solution.py:80
  276.7 84.3 %collective-permute-start.5 = (bf16[2,320,768]{2,1,0:T(8,128)(2,1)S(1)}, bf16[2,320,768]{2,1,0:T(8,128)(2,1)}, u32[]{:S(2)}, u32[]{:S(2)}) collective-permute-start(bf16[2,320,768]{2,1,0:T(8,128)(2,1)S(1)} %get-tuple-element.35), channel_id=1, source_target_pairs={{0,24},{8,0},{16,8},{24,16},{1,25},{9,1},{17,9},{25,17},{2,26},{10... | collective-permute-start | bytes 2949128 | tf_op jit(solution)/shard_map/ppermute | solution.py:80
  276.7 84.3 %collective-permute-start.4 = (bf16[2,320,768]{2,1,0:T(8,128)(2,1)S(1)}, bf16[2,320,768]{2,1,0:T(8,128)(2,1)}, u32[]{:S(2)}, u32[]{:S(2)}) collective-permute-start(bf16[2,320,768]{2,1,0:T(8,128)(2,1)S(1)} %get-tuple-element.36), channel_id=1, source_target_pairs={{0,16},{8,24},{16,0},{24,8},{1,17},{9,25},{17,1},{25,9},{2,18},{10... | collective-permute-start | bytes 2949128 | tf_op jit(solution)/shard_map/ppermute | solution.py:80
  279.4 17.8 %collective-permute-start.6 = (f32[4,4,320]{2,1,0:T(4,128)S(1)}, f32[4,4,320]{2,1,0:T(4,128)S(1)}, u32[]{:S(2)}, u32[]{:S(2)}) collective-permute-start(f32[4,4,320]{2,1,0:T(4,128)S(1)} %pad_maximum_fusion.2), channel_id=1, source_target_pairs={{0,1},{1,0},{2,3},{3,2},{4,5},{5,4},{6,7},{7,6},{8,9},{9,8},{10,11... | collective-permute-start | bytes 61448 | tf_op jit(solution)/shard_map/ppermute | solution.py:103
  288.8 11.4 %copy-start.2 = (bf16[2,768,1024]{2,1,0:T(8,128)(2,1)S(1)}, bf16[2,768,1024]{2,1,0:T(8,128)(2,1)}, u32[]{:S(2)}) copy-start(bf16[2,768,1024]{2,1,0:T(8,128)(2,1)} %bitcast_convert_fusion) | copy-start | bytes 9437188
  297.2 42.6 %collective-permute-start.7 = (f32[4,320]{1,0:T(4,128)S(1)}, f32[4,320]{1,0:T(4,128)S(1)}, u32[]{:S(2)}, u32[]{:S(2)}) collective-permute-start(f32[4,320]{1,0:T(4,128)S(1)} %get-tuple-element.39), channel_id=1, source_target_pairs={{0,8},{8,16},{16,24},{24,0},{1,9},{9,17},{17,25},{25,1},{2,10},{10... | collective-permute-start | bytes 15368 | tf_op jit(solution)/shard_map/ppermute | solution.py:108
  305.3 55.6 %collective-permute-start.9 = (f32[4,320]{1,0:T(4,128)S(1)}, f32[4,320]{1,0:T(4,128)S(1)}, u32[]{:S(2)}, u32[]{:S(2)}) collective-permute-start(f32[4,320]{1,0:T(4,128)S(1)} %get-tuple-element.40), channel_id=1, source_target_pairs={{0,24},{8,0},{16,8},{24,16},{1,25},{9,1},{17,9},{25,17},{2,26},{10... | collective-permute-start | bytes 15368 | tf_op jit(solution)/shard_map/ppermute | solution.py:108
  339.8 21.1 %collective-permute-start.8 = (f32[4,320]{1,0:T(4,128)S(1)}, f32[4,320]{1,0:T(4,128)S(1)}, u32[]{:S(2)}, u32[]{:S(2)}) collective-permute-start(f32[4,320]{1,0:T(4,128)S(1)} %get-tuple-element.41), channel_id=1, source_target_pairs={{0,16},{8,24},{16,0},{24,8},{1,17},{9,25},{17,1},{25,9},{2,18},{10... | collective-permute-start | bytes 15368 | tf_op jit(solution)/shard_map/ppermute | solution.py:108
Sparse Core Ops, SparseCore 0:
  38.7 154.7 all-gather.1

commit v17 on v16

--- a/solution.py
+++ b/solution.py
@@ -101,11 +101,7 @@
     for shift in range(1, halves):
         pairs = [(i, (i + shift) % halves) for i in range(halves)]
         dot_part = dot_part + lax.ppermute(half_dots, "etp", pairs)
-    own_dots = lax.dynamic_index_in_dim(dot_part, me, 0, keepdims=False)
-    for shift in range(1, groups):
-        chunk = lax.dynamic_index_in_dim(dot_part, (me + shift) % groups, 0, keepdims=False)
-        pairs = [(i, (i + shift) % groups) for i in range(groups)]
-        own_dots = own_dots + lax.ppermute(chunk, "dp", pairs)
+    own_dots = jnp.sum(lax.all_to_all(dot_part, "dp", split_axis=0, concat_axis=0, tiled=True), axis=0)
     hidden_grad, own_dots, weight_grad = lax.optimization_barrier((hidden_grad, own_dots, weight_grad))
     slot_dots = own_dots.reshape(exp_dev, senders, capacity)
     returned = lax.all_to_all(slot_dots, "expert", split_axis=1, concat_axis=1, tiled=True)

time: 388 us -> 388 us (level)
  starting transfers between devices: 47 us -> 30.8 us
  waiting for transfers between devices: 172 us -> 187 us
    all_to_all x0 -> x1, waiting for transfers between devices: none -> 49.4 us  [body(): lax.all_to_all(dot_part, 'dp', split_axis=0, concat_axis=0, tiled=True)]
    ppermute x3 -> x0, waiting for transfers between devices: 34.2 us -> none  [body(): own_dots = own_dots + lax.ppermute(chunk, 'dp', pairs)]
    ppermute x3 -> x0, starting transfers between devices: 22.7 us -> none  [body(): own_dots = own_dots + lax.ppermute(chunk, 'dp', pairs)]
    all_to_all x0 -> x1, starting transfers between devices: none -> 6.6 us  [body(): lax.all_to_all(dot_part, 'dp', split_axis=0, concat_axis=0, tiled=True)]
  transfers between devices with their start and end apart: 14 -> 12, of which waited for: 5 -> 5; matrix products, arithmetic and copies ran while one was open for 24% -> 24% of each run, Pallas kernels for 0% -> 0%
where the time goes in v17:
time: 388 us; the launch traced here: 382 us
  waiting for transfers between devices  187 us (48%)
  other arithmetic  45.7 us (12%)
  matrix products  40.2 us (10%)
  blocking collectives  33.4 us (9%)
  starting transfers between devices  30.8 us (8%)
  local copies, waits for them, and re-layouts  29.7 us (8%)
  between operations  14.4 us (4%)
    all_to_all x2, waiting for transfers between devices, body(): lax.all_to_all(picked, 'expert', split_axis=0, concat_axis=0, tiled=True)  85.1 us
    ppermute x6, waiting for transfers between devices, body(): arrivals.append(lax.ppermute(chunk, 'dp', pairs))  53 us
    all_to_all x1, waiting for transfers between devices, body(): lax.all_to_all(dot_part, 'dp', split_axis=0, concat_axis=0, tiled=True)  49.4 us
    all_to_all x1, blocking collectives, body(): lax.all_to_all(packed, 'dp', split_axis=1, concat_axis=0, tiled=True)  28.1 us
    dot_general x2, matrix products, body(): jnp.einsum('glqsf,qglsd->lfd', scaled, received, preferred_element_type=j...  16.6 us
    dot_general x2, matrix products, body(): jnp.einsum('qglsd,lfd->glqsf', received, down_weight[local], preferred_el...  14.4 us
    all_to_all x2, starting transfers between devices, body(): lax.all_to_all(picked, 'expert', split_axis=0, concat_axis=0, tiled=True)  12.4 us
    convert_element_type x2, local copies, waits for them, and re-layouts, body(): picked = jnp.einsum('gtlqs,gtd->qglsd', token_select[:, :, local], token_...  11.5 us
  transfers between devices with their start and end apart: 12, of which 5 were waited for; matrix products, arithmetic and copies ran while one was open for 24% of the time, Pallas kernels for 0%

profile of v17, /device:TPU:29, one launch (start us, length us, event | category | flops | bytes accessed | tf_op | source)
XLA Modules:
  0.0 381.7 jit_solution(18319638936529385434)
XLA Ops:
  10.3 28.1 %all_to_all.43 = bf16[128,4,1040]{0,2,1:T(8,128)(2,1)S(1)} all-to-all(bf16[128,4,1040]{0,2,1:T(8,128)(2,1)S(1)} %pad_maximum_fusion.1), channel_id=1, replica_groups=mesh['dp'=4,'expert'=4,'etp'=2] {'dp'}, dimensions={1} | all-to-all | bytes 2129920 | tf_op jit(solution)/shard_map/all_to_all | solution.py:25
  40.8 5.6 %fusion.1 = bf16[4,1,1280,1]{2,1,3,0:T(2,128)(2,1)S(1)} fusion(bf16[4,128,8,1]{2,3,1,0:T(2,128)(2,1)S(1)} %copy.81, s32[4,128,8]{2,1,0:T(8,128)S(1)} %fusion.53), kind=kOutput, calls=%fused_computation.2 | convolution fusion | flops 15728640 | bytes 34816 | tf_op jit(solution)/shard_map/gtk,gtkr->gr/dot_general | solution.py:46
  47.1 4.6 %all-to-all-start.1 = ((bf16[4,4,4,80]{3,0,1,2:T(4,128)(2,1)}), bf16[4,4,4,80]{3,0,1,2:T(4,128)(2,1)S(1)}, u32[]{:S(2)}, u32[]{:S(2)}) async-start(bf16[4,4,4,80]{3,0,1,2:T(4,128)(2,1)} %copy.64), calls=%async_computation.1 | async-start | bytes 32768 | tf_op jit(solution)/shard_map/all_to_all | solution.py:53
  51.7 7.4 %fusion.32 = bf16[4,128,1280]{2,1,0:T(8,128)(2,1)} fusion(s32[4,128,8]{2,1,0:T(8,128)S(1)} %fusion.53), kind=kLoop, calls=%fused_computation.35 | loop fusion | flops 15073280 | bytes 1327104 | tf_op jit(solution)/shard_map/reduce_sum | solution.py:47
  62.5 3.2 convert_bitcast_fusion.1
  65.7 5.7 %copy.68 = bf16[4,4,2,80,1024]{4,3,2,1,0:T(8,128)(2,1)} copy(bf16[4,4,2,80,1024]{4,3,0,2,1:T(8,128)(2,1)} %convert_bitcast_fusion.1) | data formatting | bytes 10485760 | tf_op jit(solution)/shard_map/convert_element_type | solution.py:68
  71.4 5.3 %all-to-all-start.2 = ((bf16[4,4,2,80,1024]{4,3,2,1,0:T(8,128)(2,1)}), bf16[4,4,2,80,1024]{4,3,2,1,0:T(8,128)(2,1)}, u32[]{:S(2)}, u32[]{:S(2)}) async-start(bf16[4,4,2,80,1024]{4,3,2,1,0:T(8,128)(2,1)} %copy.68), calls=%async_computation.2 | async-start | bytes 10485760 | tf_op jit(solution)/shard_map/all_to_all | solution.py:69
  78.3 3.2 convert_bitcast_fusion
  81.5 5.8 %copy.74 = bf16[4,4,2,80,1024]{4,3,2,1,0:T(8,128)(2,1)} copy(bf16[4,4,2,80,1024]{4,3,0,2,1:T(8,128)(2,1)} %convert_bitcast_fusion) | data formatting | bytes 10485760 | tf_op jit(solution)/shard_map/convert_element_type | solution.py:68
  87.2 46.9 %all-to-all-done.2 = bf16[4,4,2,80,1024]{4,3,2,1,0:T(8,128)(2,1)} async-done(((bf16[4,4,2,80,1024]{4,3,2,1,0:T(8,128)(2,1)}), bf16[4,4,2,80,1024]{4,3,2,1,0:T(8,128)(2,1)}, u32[]{:S(2)}, u32[]{:S(2)}) %all-to-all-start.2) | async-done | bytes 5242912 | tf_op jit(solution)/shard_map/all_to_all | solution.py:69
  134.2 7.1 %all-to-all-start.3 = ((bf16[4,4,2,80,1024]{4,3,2,1,0:T(8,128)(2,1)}), bf16[4,4,2,80,1024]{4,3,2,1,0:T(8,128)(2,1)}, u32[]{:S(2)}, u32[]{:S(2)}) async-start(bf16[4,4,2,80,1024]{4,3,2,1,0:T(8,128)(2,1)} %copy.74), calls=%async_computation.3 | async-start | bytes 10485760 | tf_op jit(solution)/shard_map/all_to_all | solution.py:69
  145.9 7.2 %fusion.22 = f32[4,2,4,80,768]{4,3,0,2,1:T(8,128)S(1)} fusion(bf16[4,768,1024]{2,1,0:T(8,128)(2,1)} %param.9, bf16[4,4,2,80,1024]{4,3,2,1,0:T(8,128)(2,1)} %all-to-all-done.2), kind=kOutput, calls=%fused_computation.33 | convolution fusion | flops 4026531840 | bytes 16252928 | tf_op jit(solution)/shard_map/qglsd,lfd->glqsf/dot_general | solution.py:70
  160.7 38.2 %all-to-all-done.3 = bf16[4,4,2,80,1024]{4,3,2,1,0:T(8,128)(2,1)} async-done(((bf16[4,4,2,80,1024]{4,3,2,1,0:T(8,128)(2,1)}), bf16[4,4,2,80,1024]{4,3,2,1,0:T(8,128)(2,1)}, u32[]{:S(2)}, u32[]{:S(2)}) %all-to-all-start.3) | async-done | bytes 5242912 | tf_op jit(solution)/shard_map/all_to_all | solution.py:69
  198.8 7.2 %fusion.27 = f32[4,2,4,80,768]{4,3,0,2,1:T(8,128)S(1)} fusion(bf16[4,768,1024]{2,1,0:T(8,128)(2,1)} %param.9, bf16[4,4,2,80,1024]{4,3,2,1,0:T(8,128)(2,1)} %all-to-all-done.3), kind=kOutput, calls=%fused_computation.34 | convolution fusion | flops 4026531840 | bytes 16252928 | tf_op jit(solution)/shard_map/qglsd,lfd->glqsf/dot_general | solution.py:70
  206.0 3.7 copy.76
  209.7 10.6 %collective-permute-done.2 = bf16[2,320,768]{2,1,0:T(8,128)(2,1)} collective-permute-done((bf16[2,320,768]{2,1,0:T(8,128)(2,1)S(1)}, bf16[2,320,768]{2,1,0:T(8,128)(2,1)}, u32[]{:S(2)}, u32[]{:S(2)}) %collective-permute-start.2) | collective-permute-done | bytes 983072 | tf_op jit(solution)/shard_map/ppermute | solution.py:80
  220.4 42.3 %collective-permute-done.1 = bf16[2,320,768]{2,1,0:T(8,128)(2,1)} collective-permute-done((bf16[2,320,768]{2,1,0:T(8,128)(2,1)S(1)}, bf16[2,320,768]{2,1,0:T(8,128)(2,1)}, u32[]{:S(2)}, u32[]{:S(2)}) %collective-permute-start.1) | collective-permute-done | bytes 983072 | tf_op jit(solution)/shard_map/ppermute | solution.py:80
  265.4 8.0 %fusion.6 = (f32[4,2,320]{2,1,0:T(2,128)S(1)}, bf16[4,2,320,768]{3,2,1,0:T(8,128)(2,1)S(1)}, bf16[4,2,320,768]{3,2,1,0:T(8,128)(2,1)S(1)}) fusion(f32[4,2,320,768]{3,2,1,0:T(8,128)} %bitcast.127, bf16[4,4,320,768]{3,2,1,0:T(8,128)(2,1)} %all-gather.2.cloned.1.call-done, f32[4,2,320]{2,1,0:T(2,128)S(1)} %copy.73), kind=kLoop, calls=%fused_computation.11 | loop fusion | flops 11793920 | bytes 19681280 | tf_op jit(solution)/shard_map/reduce_sum | solution.py:82
  281.9 8.2 %bitcast_convert_fusion = bf16[2,768,1024]{2,1,0:T(8,128)(2,1)} fusion(bf16[4,2,4,80,768]{4,3,2,1,0:T(8,128)(2,1)S(1)} %bitcast.135, bf16[4,4,2,80,1024]{4,3,2,1,0:T(8,128)(2,1)} %all-to-all-done.3), kind=kOutput, calls=%fused_computation.13 | convolution fusion | flops 4028104704 | bytes 12320768 | tf_op jit(solution)/shard_map/glqsf,qglsd->lfd/dot_general | solution.py:85
  290.2 8.4 %bitcast_convert_fusion.1 = bf16[2,768,1024]{2,1,0:T(8,128)(2,1)} fusion(bf16[4,2,4,80,768]{4,3,2,1,0:T(8,128)(2,1)S(1)} %bitcast.136, bf16[4,4,2,80,1024]{4,3,2,1,0:T(8,128)(2,1)} %all-to-all-done.2), kind=kOutput, calls=%fused_computation.14 | convolution fusion | flops 4028104704 | bytes 12320768 | tf_op jit(solution)/shard_map/glqsf,qglsd->lfd/dot_general | solution.py:85
  298.5 5.1 %pad_maximum_fusion = bf16[4,768,1024]{2,1,0:T(8,128)(2,1)} fusion(bf16[2,768,1024]{2,1,0:T(8,128)(2,1)S(1)} %copy-done.2, bf16[2,768,1024]{2,1,0:T(8,128)(2,1)} %bitcast_convert_fusion.1), kind=kLoop, calls=%fused_computation.12 | loop fusion | flops 3145728 | bytes 12582912 | tf_op jit(solution)/shard_map/concatenate | solution.py:89
  304.3 6.6 %all-to-all-start.4 = ((f32[4,4,320]{2,1,0:T(4,128)}), f32[4,4,320]{2,1,0:T(4,128)S(1)}, u32[]{:S(2)}, u32[]{:S(2)}) async-start(f32[4,4,320]{2,1,0:T(4,128)} %fusion.61), calls=%async_computation.4 | async-start | bytes 49152 | tf_op jit(solution)/shard_map/all_to_all | solution.py:104
  312.6 49.4 %all-to-all-done.4 = f32[4,4,320]{2,1,0:T(4,128)S(1)} async-done(((f32[4,4,320]{2,1,0:T(4,128)}), f32[4,4,320]{2,1,0:T(4,128)S(1)}, u32[]{:S(2)}, u32[]{:S(2)}) %all-to-all-start.4) | async-done | bytes 20512 | tf_op jit(solution)/shard_map/all_to_all | solution.py:104
  365.8 5.4 %all_to_all.44 = f32[4,4,80]{2,0,1:T(4,128)S(1)} all-to-all(f32[4,4,80]{2,0,1:T(4,128)S(1)} %copy.78), channel_id=1, replica_groups=mesh['dp'=4,'expert'=4,'etp'=2] {'expert'}, dimensions={1} | all-to-all | bytes 10240 | tf_op jit(solution)/shard_map/all_to_all | solution.py:107
  (81 shorter events, 44.2 us)
Async XLA Ops:
  7.2 258.2 %all-gather.2.cloned.1.call-start = ((), (), s32[]{:S(2)}) async-start(), calls=%async_computation.6 | async-start | bytes 9830400 | tf_op jit(solution)/shard_map/all_gather | solution.py:29
  47.1 24.3 %all-to-all-start.1 = ((bf16[4,4,4,80]{3,0,1,2:T(4,128)(2,1)}), bf16[4,4,4,80]{3,0,1,2:T(4,128)(2,1)S(1)}, u32[]{:S(2)}, u32[]{:S(2)}) async-start(bf16[4,4,4,80]{3,0,1,2:T(4,128)(2,1)} %copy.64), calls=%async_computation.1 | async-start | bytes 32768 | tf_op jit(solution)/shard_map/all_to_all | solution.py:53
  71.4 62.7 %all-to-all-start.2 = ((bf16[4,4,2,80,1024]{4,3,2,1,0:T(8,128)(2,1)}), bf16[4,4,2,80,1024]{4,3,2,1,0:T(8,128)(2,1)}, u32[]{:S(2)}, u32[]{:S(2)}) async-start(bf16[4,4,2,80,1024]{4,3,2,1,0:T(8,128)(2,1)} %copy.68), calls=%async_computation.2 | async-start | bytes 10485760 | tf_op jit(solution)/shard_map/all_to_all | solution.py:69
  134.2 64.7 %all-to-all-start.3 = ((bf16[4,4,2,80,1024]{4,3,2,1,0:T(8,128)(2,1)}), bf16[4,4,2,80,1024]{4,3,2,1,0:T(8,128)(2,1)}, u32[]{:S(2)}, u32[]{:S(2)}) async-start(bf16[4,4,2,80,1024]{4,3,2,1,0:T(8,128)(2,1)} %copy.74), calls=%async_computation.3 | async-start | bytes 10485760 | tf_op jit(solution)/shard_map/all_to_all | solution.py:69
  153.8 3.1 copy-start
  158.1 51.7 %collective-permute-start = (bf16[2,320,768]{2,1,0:T(8,128)(2,1)}, bf16[2,320,768]{2,1,0:T(8,128)(2,1)S(1)}, u32[]{:S(2)}, u32[]{:S(2)}) collective-permute-start(bf16[2,320,768]{2,1,0:T(8,128)(2,1)} %get-tuple-element.31), channel_id=1, source_target_pairs={{0,8},{8,16},{16,24},{24,0},{1,9},{9,17},{17,25},{25,1},{2,10},{10... | collective-permute-start | bytes 2949128 | tf_op jit(solution)/shard_map/ppermute | solution.py:80
  160.2 60.2 %collective-permute-start.2 = (bf16[2,320,768]{2,1,0:T(8,128)(2,1)S(1)}, bf16[2,320,768]{2,1,0:T(8,128)(2,1)}, u32[]{:S(2)}, u32[]{:S(2)}) collective-permute-start(bf16[2,320,768]{2,1,0:T(8,128)(2,1)S(1)} %get-tuple-element.32), channel_id=1, source_target_pairs={{0,24},{8,0},{16,8},{24,16},{1,25},{9,1},{17,9},{25,17},{2,26},{10... | collective-permute-start | bytes 2949128 | tf_op jit(solution)/shard_map/ppermute | solution.py:80
  160.2 102.5 %collective-permute-start.1 = (bf16[2,320,768]{2,1,0:T(8,128)(2,1)S(1)}, bf16[2,320,768]{2,1,0:T(8,128)(2,1)}, u32[]{:S(2)}, u32[]{:S(2)}) collective-permute-start(bf16[2,320,768]{2,1,0:T(8,128)(2,1)S(1)} %get-tuple-element.33), channel_id=1, source_target_pairs={{0,16},{8,24},{16,0},{24,8},{1,17},{9,25},{17,1},{25,9},{2,18},{10... | collective-permute-start | bytes 2949128 | tf_op jit(solution)/shard_map/ppermute | solution.py:80
  265.3 13.1 %slice-start = ((s8[7864320]{0:T(1024)(128)(4,1)}), s8[4194304]{0:T(1024)(128)(4,1)S(1)}, s32[]{:S(2)}) async-start(s8[7864320]{0:T(1024)(128)(4,1)} %bitcast.122), calls=%async_computation.7 | async-start | bytes 8388608
  265.3 13.0 %slice-start.1 = ((s8[7864320]{0:T(1024)(128)(4,1)}), s8[3670016]{0:T(1024)(128)(4,1)S(1)}, s32[]{:S(2)}) async-start(s8[7864320]{0:T(1024)(128)(4,1)} %bitcast.122), calls=%async_computation.8 | async-start | bytes 7340032
  265.4 13.0 %copy-start.1 = (bf16[4,4,320,768]{3,2,1,0:T(8,128)(2,1)S(1)}, bf16[4,4,320,768]{3,2,1,0:T(8,128)(2,1)}, u32[]{:S(2)}) copy-start(bf16[4,4,320,768]{3,2,1,0:T(8,128)(2,1)} %all-gather.2.cloned.1.call-done) | copy-start | bytes 23592964
  275.0 87.0 %collective-permute-start.3 = (bf16[2,320,768]{2,1,0:T(8,128)(2,1)}, bf16[2,320,768]{2,1,0:T(8,128)(2,1)}, u32[]{:S(2)}, u32[]{:S(2)}) collective-permute-start(bf16[2,320,768]{2,1,0:T(8,128)(2,1)} %get-tuple-element.34), channel_id=1, source_target_pairs={{0,8},{8,16},{16,24},{24,0},{1,9},{9,17},{17,25},{25,1},{2,10},{10... | collective-permute-start | bytes 2949128 | tf_op jit(solution)/shard_map/ppermute | solution.py:80
  278.1 83.9 %collective-permute-start.5 = (bf16[2,320,768]{2,1,0:T(8,128)(2,1)}, bf16[2,320,768]{2,1,0:T(8,128)(2,1)}, u32[]{:S(2)}, u32[]{:S(2)}) collective-permute-start(bf16[2,320,768]{2,1,0:T(8,128)(2,1)} %get-tuple-element.35), channel_id=1, source_target_pairs={{0,24},{8,0},{16,8},{24,16},{1,25},{9,1},{17,9},{25,17},{2,26},{10... | collective-permute-start | bytes 2949128 | tf_op jit(solution)/shard_map/ppermute | solution.py:80
  278.1 83.9 %collective-permute-start.4 = (bf16[2,320,768]{2,1,0:T(8,128)(2,1)}, bf16[2,320,768]{2,1,0:T(8,128)(2,1)}, u32[]{:S(2)}, u32[]{:S(2)}) collective-permute-start(bf16[2,320,768]{2,1,0:T(8,128)(2,1)} %get-tuple-element.36), channel_id=1, source_target_pairs={{0,16},{8,24},{16,0},{24,8},{1,17},{9,25},{17,1},{25,9},{2,18},{10... | collective-permute-start | bytes 2949128 | tf_op jit(solution)/shard_map/ppermute | solution.py:80
  280.7 23.0 %collective-permute-start.6 = (f32[4,4,320]{2,1,0:T(4,128)S(1)}, f32[4,4,320]{2,1,0:T(4,128)S(1)}, u32[]{:S(2)}, u32[]{:S(2)}) collective-permute-start(f32[4,4,320]{2,1,0:T(4,128)S(1)} %pad_maximum_fusion.2), channel_id=1, source_target_pairs={{0,1},{1,0},{2,3},{3,2},{4,5},{5,4},{6,7},{7,6},{8,9},{9,8},{10,11... | collective-permute-start | bytes 61448 | tf_op jit(solution)/shard_map/ppermute | solution.py:103
  290.2 8.4 %copy-start.2 = (bf16[2,768,1024]{2,1,0:T(8,128)(2,1)S(1)}, bf16[2,768,1024]{2,1,0:T(8,128)(2,1)}, u32[]{:S(2)}) copy-start(bf16[2,768,1024]{2,1,0:T(8,128)(2,1)} %bitcast_convert_fusion) | copy-start | bytes 9437188
  304.3 57.6 %all-to-all-start.4 = ((f32[4,4,320]{2,1,0:T(4,128)}), f32[4,4,320]{2,1,0:T(4,128)S(1)}, u32[]{:S(2)}, u32[]{:S(2)}) async-start(f32[4,4,320]{2,1,0:T(4,128)} %fusion.61), calls=%async_computation.4 | async-start | bytes 49152 | tf_op jit(solution)/shard_map/all_to_all | solution.py:104
Sparse Core Ops, SparseCore 0:
  38.7 154.8 all-gather.1
